TPU v7x, 512 devices: a whole 4x8x8 slice. The times are simulated.
512 devices in a mesh: aux: 8 (over y), ao: 64 (over x, z, core).
Axes of the slice: x: 4, y: 8, z: 8, core: 2. Of those that a mesh axis runs over, the one named last changes fastest.
Arguments:
- pair_list: int32 [1536, 2], P('ao'), may hold values from 0 to 255, as said below
- pair_count: int32 [64], P('ao'), may hold values from 3 to 24, as said below
- tiles: bfloat16 [1536, 32, 128, 128], P('ao', 'aux'), may hold values from -6 to 6
- coeff: bfloat16 [32768, 512], P('ao'), may hold values from -0.25 to 0.25
Outputs:
- k_tiles: bfloat16 [1536, 128, 128], P('ao', 'aux')
Inputs may be any that keep to these rules, and one draw needn't show every extreme that they name: `pair_list`: each live row of owner o names i among its blocks and i < j < (o + 3) * 4; no live pair repeats; rows past an owner's count repeat that owner's first row. `pair_count`: some owner has exactly 24 live rows.
All inputs are finite; a program needn't handle non-finite values.
Results may differ from a plain program's by a relative error of at most 0.0067.
Values may be sent and summed in bfloat16 or wider, within the bound.
No kernel may reach another device: no remote copies, remote signals or barrier semaphores. Data moves between devices by JAX's collectives and lax.ppermute only.
A program may use at most 64 MiB of HBM per device.

v0:
```python
import jax
import jax.numpy as jnp
from jax import lax
from jax.sharding import PartitionSpec as P

BAND = 2


def passed_along(value, axis, steps):
    count = lax.axis_size(axis)
    first, last = (max(0, -steps), min(count, count - steps))
    return lax.ppermute(value, axis, [(source, source + steps) for source in range(first, last)])


def add_block(totals, position, update):
    current = lax.dynamic_index_in_dim(totals, position, 0, keepdims=False)
    return lax.dynamic_update_index_in_dim(totals, current + update, position, 0)


def on_device(pair_list, pair_count, tiles, coeff):
    pair_slots = pair_list.shape[0]
    aux_local = tiles.shape[1]
    block_size = tiles.shape[2]
    orbitals = coeff.shape[1]
    own_blocks = coeff.shape[0] // block_size
    window_blocks = (BAND + 1) * own_blocks
    owner_index = lax.axis_index("ao")
    first_block = owner_index * own_blocks
    live_count = pair_count[0]
    own_coeff = coeff.reshape(own_blocks, block_size, orbitals)
    ahead_coeff = [passed_along(own_coeff, "ao", -distance) for distance in range(1, BAND + 1)]
    window_coeff = jnp.concatenate([own_coeff] + ahead_coeff, 0)

    def accumulate(slot_index, totals):
        pair_row = lax.dynamic_index_in_dim(pair_list, slot_index, 0, keepdims=False)
        left_block = pair_row[0] - first_block
        right_block = pair_row[1] - first_block
        pair_tile = lax.dynamic_index_in_dim(tiles, slot_index, 0, keepdims=False)
        left_coeff = lax.dynamic_index_in_dim(window_coeff, left_block, 0, keepdims=False)
        right_coeff = lax.dynamic_index_in_dim(window_coeff, right_block, 0, keepdims=False)
        to_left = jnp.einsum(
            "pmn,nk->pmk", pair_tile, right_coeff, preferred_element_type=jnp.float32
        )
        to_right = jnp.einsum(
            "pmn,mk->pnk", pair_tile, left_coeff, preferred_element_type=jnp.float32
        )
        totals = add_block(totals, left_block, to_left)
        return add_block(totals, right_block, to_right)

    empty = jnp.zeros((window_blocks, aux_local, block_size, orbitals), jnp.float32)
    totals = lax.fori_loop(0, live_count, accumulate, empty)
    halves = totals.astype(jnp.bfloat16)
    fitted_sum = halves[:own_blocks].astype(jnp.float32)
    for distance in range(1, BAND + 1):
        outgoing = halves[distance * own_blocks : (distance + 1) * own_blocks]
        arriving = passed_along(outgoing, "ao", distance)
        fitted_sum = fitted_sum + arriving.astype(jnp.float32)
    fitted = fitted_sum.astype(jnp.bfloat16)
    ahead_fitted = [passed_along(fitted, "ao", -distance) for distance in range(1, BAND + 1)]
    window_fitted = jnp.concatenate([fitted] + ahead_fitted, 0)

    def contract(slot_index, result):
        pair_row = lax.dynamic_index_in_dim(pair_list, slot_index, 0, keepdims=False)
        left_rows = lax.dynamic_index_in_dim(
            window_fitted, pair_row[0] - first_block, 0, keepdims=False
        )
        right_rows = lax.dynamic_index_in_dim(
            window_fitted, pair_row[1] - first_block, 0, keepdims=False
        )
        pair_tile = jnp.einsum(
            "pmk,pnk->mn", left_rows, right_rows, preferred_element_type=jnp.float32
        )
        return lax.dynamic_update_index_in_dim(result, pair_tile, slot_index, 0)

    partial_tiles = lax.fori_loop(
        0, live_count, contract, jnp.zeros((pair_slots, block_size, block_size), jnp.float32)
    )
    summed = lax.psum_scatter(partial_tiles, "aux", scatter_dimension=1, tiled=True)
    norm_factor = (aux_local * lax.axis_size("aux") * orbitals) ** (-0.5)
    return (summed * norm_factor).astype(jnp.bfloat16)


def solution(mesh):
    in_specs = (P("ao", None), P("ao"), P("ao", "aux", None, None), P("ao", None))
    out_specs = P("ao", "aux", None)
    return jax.shard_map(
        on_device, mesh=mesh, in_specs=in_specs, out_specs=out_specs, check_vma=False
    )
```

profile of v0, /device:TPU:6, one launch (start us, length us, event | category | flops | bytes accessed | tf_op | source)
XLA Modules:
  0.0 588.1 jit_solution(7210815847886249985)
XLA Ops:
  6.5 10.6 %collective-permute-start = (bf16[4,128,512]{2,1,0:T(8,128)(2,1)}, bf16[4,128,512]{2,1,0:T(8,128)(2,1)S(1)}, u32[]{:S(2)}, u32[]{:S(2)}) collective-permute-start(bf16[4,128,512]{2,1,0:T(8,128)(2,1)} %bitcast.72), channel_id=1, source_target_pairs={{1,0},{2,1},{3,2},{4,3},{5,4},{6,5},{7,6},{8,7},{9,8},{10,9},{11,1... | collective-permute-start | bytes 1572872 | tf_op jit(solution)/shard_map/ppermute | solution.py:12
  17.2 2.5 collective-permute-start.1
  19.7 8.1 %collective-permute-done = bf16[4,128,512]{2,1,0:T(8,128)(2,1)S(1)} collective-permute-done((bf16[4,128,512]{2,1,0:T(8,128)(2,1)}, bf16[4,128,512]{2,1,0:T(8,128)(2,1)S(1)}, u32[]{:S(2)}, u32[]{:S(2)}) %collective-permute-start) | collective-permute-done | bytes 524320 | tf_op jit(solution)/shard_map/ppermute | solution.py:12
  27.8 7.6 %collective-permute-done.1 = bf16[4,128,512]{2,1,0:T(8,128)(2,1)S(1)} collective-permute-done((bf16[4,128,512]{2,1,0:T(8,128)(2,1)}, bf16[4,128,512]{2,1,0:T(8,128)(2,1)S(1)}, u32[]{:S(2)}, u32[]{:S(2)}) %collective-permute-start.1) | collective-permute-done | bytes 524320 | tf_op jit(solution)/shard_map/ppermute | solution.py:12
  36.6 6.1 %broadcast_in_dim.18 = f32[12,4,128,512]{3,2,1,0:T(8,128)} broadcast(f32[]{:T(128)} %constant.57.clone.1), dimensions={} | broadcast | bytes 12582916 | tf_op jit(solution)/shard_map/broadcast_in_dim | solution.py:50
  42.8 29.7 %while.20 = (s32[]{:T(128)}, f32[12,4,128,512]{3,2,1,0:T(8,128)}, s32[]{:T(128)}, s32[24,2]{0,1:T(2,128)S(1)}, s32[]{:T(128)}, /*index=5*/bf16[24,4,128,128]{3,2...) while((s32[]{:T(128)}, f32[12,4,128,512]{3,2,1,0:T(8,128)}, ...), condition=%wide.region_1.2_spmd, body=%wide.region_0.1_spmd.sunk | while | flops 134742032 | bytes 8913199 | solution.py:51
  44.8 1.3 constant_dynamic-slice_fusion.9
  46.7 2.2 fusion.39
  50.2 2.2 fusion.40
  54.5 1.3 constant_dynamic-slice_fusion.9
  56.4 2.2 fusion.39
  59.9 2.2 fusion.40
  64.1 1.3 constant_dynamic-slice_fusion.9
  66.0 2.2 fusion.39
  69.5 2.2 fusion.40
  72.4 5.5 convert_element_type.18
  78.3 27.2 %collective-permute-start.2 = (bf16[4,4,128,512]{3,2,1,0:T(8,128)(2,1)S(1)}, bf16[4,4,128,512]{3,2,1,0:T(8,128)(2,1)S(1)}, u32[]{:S(2)}, u32[]{:S(2)}) collective-permute-start(bf16[4,4,128,512]{3,2,1,0:T(8,128)(2,1)S(1)} %get-tuple-element.108), channel_id=1, source_target_pairs={{0,1},{1,2},{2,3},{3,4},{4,5},{5,6},{6,7},{7,8},{8,9},{9,10},{10,1... | collective-permute-start | bytes 6291464 | tf_op jit(solution)/shard_map/ppermute | solution.py:12
  105.5 1.9 collective-permute-start.3
  107.5 216.4 %collective-permute-done.2 = bf16[4,4,128,512]{3,2,1,0:T(8,128)(2,1)S(1)} collective-permute-done((bf16[4,4,128,512]{3,2,1,0:T(8,128)(2,1)S(1)}, bf16[4,4,128,512]{3,2,1,0:T(8,128)(2,1)S(1)}, u32[]{:S(2)}, u32[]{:S(2)}) %collective-permute-start.2) | collective-permute-done | bytes 2097184 | tf_op jit(solution)/shard_map/ppermute | solution.py:12
  323.8 12.4 %collective-permute-done.3 = bf16[4,4,128,512]{3,2,1,0:T(8,128)(2,1)S(1)} collective-permute-done((bf16[4,4,128,512]{3,2,1,0:T(8,128)(2,1)S(1)}, bf16[4,4,128,512]{3,2,1,0:T(8,128)(2,1)S(1)}, u32[]{:S(2)}, u32[]{:S(2)}) %collective-permute-start.3) | collective-permute-done | bytes 2097184 | tf_op jit(solution)/shard_map/ppermute | solution.py:12
  336.2 2.4 add_convert_fusion
  338.5 23.3 %collective-permute-start.4 = (bf16[4,4,128,512]{3,2,1,0:T(8,128)(2,1)}, bf16[4,4,128,512]{3,2,1,0:T(8,128)(2,1)S(1)}, u32[]{:S(2)}, u32[]{:S(2)}) collective-permute-start(bf16[4,4,128,512]{3,2,1,0:T(8,128)(2,1)} %add_convert_fusion), channel_id=1, source_target_pairs={{1,0},{2,1},{3,2},{4,3},{5,4},{6,5},{7,6},{8,7},{9,8},{10,9},{11,1... | collective-permute-start | bytes 6291464 | tf_op jit(solution)/shard_map/ppermute | solution.py:12
  361.8 1.9 collective-permute-start.5
  363.8 43.0 %collective-permute-done.4 = bf16[4,4,128,512]{3,2,1,0:T(8,128)(2,1)S(1)} collective-permute-done((bf16[4,4,128,512]{3,2,1,0:T(8,128)(2,1)}, bf16[4,4,128,512]{3,2,1,0:T(8,128)(2,1)S(1)}, u32[]{:S(2)}, u32[]{:S(2)}) %collective-permute-start.4) | collective-permute-done | bytes 2097184 | tf_op jit(solution)/shard_map/ppermute | solution.py:12
  406.8 23.8 %collective-permute-done.5 = bf16[4,4,128,512]{3,2,1,0:T(8,128)(2,1)} collective-permute-done((bf16[4,4,128,512]{3,2,1,0:T(8,128)(2,1)}, bf16[4,4,128,512]{3,2,1,0:T(8,128)(2,1)}, u32[]{:S(2)}, u32[]{:S(2)}) %collective-permute-start.5) | collective-permute-done | bytes 2097184 | tf_op jit(solution)/shard_map/ppermute | solution.py:12
  430.6 5.4 pad_maximum_fusion
  436.2 13.0 %while.21 = (s32[]{:T(128)}, f32[24,128,128]{2,1,0:T(8,128)S(1)}, s32[]{:T(128)}, s32[24,2]{0,1:T(2,128)S(1)}, s32[]{:T(128)}, /*index=5*/bf16[12,4,128,512]{3,2...) while((s32[]{:T(128)}, f32[24,128,128]{2,1,0:T(8,128)S(1)}, s32[]{:T(128)}, ...), condition=%wide.region_3.4_spmd, body=%wide.region_2.3_spmd.sunk | while | flops 67108880 | bytes 1114387 | solution.py:75
  438.8 1.5 fusion.44
  442.9 1.5 fusion.44
  447.0 1.5 fusion.44
  450.4 129.3 %reduce-scatter.2.cloned.1.call-done = f32[24,16,128]{2,1,0:T(8,128)} async-done(((f32[24,128,128]{2,1,0:T(8,128)}), f32[24,16,128]{2,1,0:T(8,128)}) %reduce-scatter.2.cloned.1.call-update) | async-done | bytes 196624 | tf_op jit(solution)/shard_map/reduce_scatter | solution.py:78
  579.7 1.6 multiply_convert_fusion
  (24 shorter events, 10.7 us)
Async XLA Ops:
  6.5 573.1 %reduce-scatter.2.cloned.1.call-start = ((), (), s32[]{:S(2)}) async-start(), calls=%async_computation.1 | async-start | bytes 1769472 | tf_op jit(solution)/shard_map/reduce_scatter | solution.py:78
  6.5 21.2 %collective-permute-start = (bf16[4,128,512]{2,1,0:T(8,128)(2,1)}, bf16[4,128,512]{2,1,0:T(8,128)(2,1)S(1)}, u32[]{:S(2)}, u32[]{:S(2)}) collective-permute-start(bf16[4,128,512]{2,1,0:T(8,128)(2,1)} %bitcast.72), channel_id=1, source_target_pairs={{1,0},{2,1},{3,2},{4,3},{5,4},{6,5},{7,6},{8,7},{9,8},{10,9},{11,1... | collective-permute-start | bytes 1572872 | tf_op jit(solution)/shard_map/ppermute | solution.py:12
  17.2 18.2 %collective-permute-start.1 = (bf16[4,128,512]{2,1,0:T(8,128)(2,1)}, bf16[4,128,512]{2,1,0:T(8,128)(2,1)S(1)}, u32[]{:S(2)}, u32[]{:S(2)}) collective-permute-start(bf16[4,128,512]{2,1,0:T(8,128)(2,1)} %bitcast.73), channel_id=1, source_target_pairs={{2,0},{3,1},{4,2},{5,3},{6,4},{7,5},{8,6},{9,7},{10,8},{11,9},{12,... | collective-permute-start | bytes 1572872 | tf_op jit(solution)/shard_map/ppermute | solution.py:12
  36.6 6.1 %copy-start.1 = (s32[24,2]{0,1:T(2,128)S(1)}, s32[24,2]{0,1:T(2,128)}, u32[]{:S(2)}) copy-start(s32[24,2]{0,1:T(2,128)} %param.8) | copy-start | bytes 580
  78.3 245.5 %collective-permute-start.2 = (bf16[4,4,128,512]{3,2,1,0:T(8,128)(2,1)S(1)}, bf16[4,4,128,512]{3,2,1,0:T(8,128)(2,1)S(1)}, u32[]{:S(2)}, u32[]{:S(2)}) collective-permute-start(bf16[4,4,128,512]{3,2,1,0:T(8,128)(2,1)S(1)} %get-tuple-element.108), channel_id=1, source_target_pairs={{0,1},{1,2},{2,3},{3,4},{4,5},{5,6},{6,7},{7,8},{8,9},{9,10},{10,1... | collective-permute-start | bytes 6291464 | tf_op jit(solution)/shard_map/ppermute | solution.py:12
  105.5 230.6 %collective-permute-start.3 = (bf16[4,4,128,512]{3,2,1,0:T(8,128)(2,1)S(1)}, bf16[4,4,128,512]{3,2,1,0:T(8,128)(2,1)S(1)}, u32[]{:S(2)}, u32[]{:S(2)}) collective-permute-start(bf16[4,4,128,512]{3,2,1,0:T(8,128)(2,1)S(1)} %get-tuple-element.109), channel_id=1, source_target_pairs={{0,2},{1,3},{2,4},{3,5},{4,6},{5,7},{6,8},{7,9},{8,10},{9,11},{10,... | collective-permute-start | bytes 6291464 | tf_op jit(solution)/shard_map/ppermute | solution.py:12
  338.5 68.3 %collective-permute-start.4 = (bf16[4,4,128,512]{3,2,1,0:T(8,128)(2,1)}, bf16[4,4,128,512]{3,2,1,0:T(8,128)(2,1)S(1)}, u32[]{:S(2)}, u32[]{:S(2)}) collective-permute-start(bf16[4,4,128,512]{3,2,1,0:T(8,128)(2,1)} %add_convert_fusion), channel_id=1, source_target_pairs={{1,0},{2,1},{3,2},{4,3},{5,4},{6,5},{7,6},{8,7},{9,8},{10,9},{11,1... | collective-permute-start | bytes 6291464 | tf_op jit(solution)/shard_map/ppermute | solution.py:12
  361.8 68.8 %collective-permute-start.5 = (bf16[4,4,128,512]{3,2,1,0:T(8,128)(2,1)}, bf16[4,4,128,512]{3,2,1,0:T(8,128)(2,1)}, u32[]{:S(2)}, u32[]{:S(2)}) collective-permute-start(bf16[4,4,128,512]{3,2,1,0:T(8,128)(2,1)} %add_convert_fusion), channel_id=1, source_target_pairs={{2,0},{3,1},{4,2},{5,3},{6,4},{7,5},{8,6},{9,7},{10,8},{11,9},{12,... | collective-permute-start | bytes 6291464 | tf_op jit(solution)/shard_map/ppermute | solution.py:12
  449.2 1.2 copy-start
Sparse Core Ops, SparseCore 0:
  450.5 129.1 reduce-scatter.1
where the time goes:
time: 593 us; the launch traced here: 588 us
  waiting for transfers between devices  441 us (74%)
  starting transfers between devices  67.5 us (11%)
  local copies, waits for them, and re-layouts  19.5 us (3%)
  matrix products  17.7 us (3%)
  other arithmetic  16.1 us (3%)
  between operations  13.5 us (2%)
  loops' own time  13.1 us (2%)
    ppermute x6, waiting for transfers between devices, passed_along(): lax.ppermute(value, axis, [(source, source + steps) for source in range(f...  311 us
    reduce_scatter x1, waiting for transfers between devices, on_device(): lax.psum_scatter(partial_tiles, 'aux', scatter_dimension=1, tiled=True)  129 us
    ppermute x6, starting transfers between devices, passed_along(): lax.ppermute(value, axis, [(source, source + steps) for source in range(f...  67.5 us
  transfers between devices with their start and end apart: 7, of which 7 were waited for; matrix products, arithmetic and copies ran while one was open for 0% of the time, Pallas kernels for 0%

commit v1 on v0

v1 whole, which is shorter than its diff:
```python
import jax
import jax.numpy as jnp
from jax import lax
from jax.experimental import pallas as pl
from jax.experimental.pallas import tpu as pltpu
from jax.sharding import PartitionSpec as P

BAND = 2


def passed_along(value, axis, steps):
    count = lax.axis_size(axis)
    first, last = (max(0, -steps), min(count, count - steps))
    return lax.ppermute(value, axis, [(source, source + steps) for source in range(first, last)])


def _half_kernel(left_ref, right_ref, count_ref, tile_ref, coeff_ref, out_ref, acc_ref):
    slot = pl.program_id(0)

    @pl.when(slot == 0)
    def _():
        acc_ref[...] = jnp.zeros_like(acc_ref)

    @pl.when(slot < count_ref[0])
    def _():
        left = left_ref[slot]
        right = right_ref[slot]
        tile = tile_ref[0]
        aux_local, block_size, _ = tile.shape
        right_coeff = coeff_ref[right]
        left_coeff = coeff_ref[left]
        to_left = jnp.dot(
            tile.reshape(aux_local * block_size, block_size),
            right_coeff,
            preferred_element_type=jnp.float32,
        ).reshape(aux_local, block_size, -1)
        acc_ref[left] += to_left
        parts = [
            lax.dot_general(
                tile[p], left_coeff, (((0,), (0,)), ((), ())),
                preferred_element_type=jnp.float32,
            )
            for p in range(aux_local)
        ]
        acc_ref[right] += jnp.stack(parts, 0)

    @pl.when(slot == pl.num_programs(0) - 1)
    def _():
        out_ref[...] = acc_ref[...].astype(out_ref.dtype)


def _contract_kernel(left_ref, right_ref, count_ref, fitted_ref, out_ref):
    slot = pl.program_id(0)
    live = slot < count_ref[0]

    @pl.when(live)
    def _():
        left_rows = fitted_ref[left_ref[slot]]
        right_rows = fitted_ref[right_ref[slot]]
        total = None
        for p in range(left_rows.shape[0]):
            part = lax.dot_general(
                left_rows[p], right_rows[p], (((1,), (1,)), ((), ())),
                preferred_element_type=jnp.float32,
            )
            total = part if total is None else total + part
        out_ref[0] = total

    @pl.when(jnp.logical_not(live))
    def _():
        out_ref[...] = jnp.zeros_like(out_ref)


def on_device(pair_list, pair_count, tiles, coeff):
    pair_slots = pair_list.shape[0]
    aux_local = tiles.shape[1]
    block_size = tiles.shape[2]
    orbitals = coeff.shape[1]
    own_blocks = coeff.shape[0] // block_size
    window_blocks = (BAND + 1) * own_blocks
    owner_index = lax.axis_index("ao")
    first_block = owner_index * own_blocks
    left_rel = (pair_list[:, 0] - first_block).astype(jnp.int32)
    right_rel = (pair_list[:, 1] - first_block).astype(jnp.int32)
    count = pair_count.astype(jnp.int32)
    own_coeff = coeff.reshape(own_blocks, block_size, orbitals)
    ahead_coeff = [passed_along(own_coeff, "ao", -distance) for distance in range(1, BAND + 1)]
    window_coeff = jnp.concatenate([own_coeff] + ahead_coeff, 0)

    def tile_map(slot, left, right, cnt):
        return (jnp.minimum(slot, jnp.maximum(cnt[0] - 1, 0)), 0, 0, 0)

    halves = pl.pallas_call(
        _half_kernel,
        grid_spec=pltpu.PrefetchScalarGridSpec(
            num_scalar_prefetch=3,
            grid=(pair_slots,),
            in_specs=[
                pl.BlockSpec((1, aux_local, block_size, block_size), tile_map),
                pl.BlockSpec(
                    (window_blocks, block_size, orbitals), lambda s, l, r, c: (0, 0, 0)
                ),
            ],
            out_specs=pl.BlockSpec(
                (window_blocks, aux_local, block_size, orbitals),
                lambda s, l, r, c: (0, 0, 0, 0),
            ),
            scratch_shapes=[
                pltpu.VMEM((window_blocks, aux_local, block_size, orbitals), jnp.float32)
            ],
        ),
        out_shape=jax.ShapeDtypeStruct(
            (window_blocks, aux_local, block_size, orbitals), jnp.bfloat16
        ),
        compiler_params=pltpu.CompilerParams(
            dimension_semantics=("arbitrary",), vmem_limit_bytes=48 * 1024 * 1024
        ),
    )(left_rel, right_rel, count, tiles, window_coeff)

    fitted_sum = halves[:own_blocks].astype(jnp.float32)
    for distance in range(1, BAND + 1):
        outgoing = halves[distance * own_blocks : (distance + 1) * own_blocks]
        arriving = passed_along(outgoing, "ao", distance)
        fitted_sum = fitted_sum + arriving.astype(jnp.float32)
    fitted = fitted_sum.astype(jnp.bfloat16)
    ahead_fitted = [passed_along(fitted, "ao", -distance) for distance in range(1, BAND + 1)]
    window_fitted = jnp.concatenate([fitted] + ahead_fitted, 0)

    partial_tiles = pl.pallas_call(
        _contract_kernel,
        grid_spec=pltpu.PrefetchScalarGridSpec(
            num_scalar_prefetch=3,
            grid=(pair_slots,),
            in_specs=[
                pl.BlockSpec(
                    (window_blocks, aux_local, block_size, orbitals),
                    lambda s, l, r, c: (0, 0, 0, 0),
                ),
            ],
            out_specs=pl.BlockSpec((1, block_size, block_size), lambda s, l, r, c: (s, 0, 0)),
        ),
        out_shape=jax.ShapeDtypeStruct((pair_slots, block_size, block_size), jnp.float32),
        compiler_params=pltpu.CompilerParams(
            dimension_semantics=("arbitrary",), vmem_limit_bytes=48 * 1024 * 1024
        ),
    )(left_rel, right_rel, count, window_fitted)

    summed = lax.psum_scatter(partial_tiles, "aux", scatter_dimension=1, tiled=True)
    norm_factor = (aux_local * lax.axis_size("aux") * orbitals) ** (-0.5)
    return (summed * norm_factor).astype(jnp.bfloat16)


def solution(mesh):
    in_specs = (P("ao", None), P("ao"), P("ao", "aux", None, None), P("ao", None))
    out_specs = P("ao", "aux", None)
    return jax.shard_map(
        on_device, mesh=mesh, in_specs=in_specs, out_specs=out_specs, check_vma=False
    )
```

time: 593 us -> 255 us (0.43)
  waiting for transfers between devices: 441 us -> 157 us
  Pallas kernels: 0 us -> 30.1 us
  starting transfers between devices: 67.5 us -> 40.2 us
  matrix products: 17.7 us -> 0 us
  local copies, waits for them, and re-layouts: 19.5 us -> 2.5 us
  loops' own time: 13.1 us -> 0 us
    ppermute x6, waiting for transfers between devices: 311 us -> 114 us  [passed_along(): lax.ppermute(value, axis, [(source, source + steps) for source in range(f...]
    reduce_scatter x1, waiting for transfers between devices: 129 us -> 42.5 us  [on_device(): lax.psum_scatter(partial_tiles, 'aux', scatter_dimension=1, tiled=True)]
    pallas_call x0 -> x2, Pallas kernels: none -> 30.1 us  [the longest x1 15.4 us: on_device(): pl.pallas_call(_half_kernel, grid_spec=pltpu.PrefetchScalarGridSpec(num_s...]
    ppermute x6, starting transfers between devices: 67.5 us -> 40.2 us  [passed_along(): lax.ppermute(value, axis, [(source, source + steps) for source in range(f...]
    dot_general x9 -> x0, matrix products: 17.7 us -> none  [the longest x3 6.66 us: accumulate(): jnp.einsum('pmn,mk->pnk', pair_tile, left_coeff, preferred_element_type=j...]
    another operation x2 -> x0, loops' own time: 13.1 us -> none  [the longest x1 6.62 us: on_device(): totals = lax.fori_loop(0, live_count, accumulate, empty)]
    dynamic_slice x12 -> x0, local copies, waits for them, and re-layouts: 8.22 us -> none  [the longest x6 7.78 us: add_block(): current = lax.dynamic_index_in_dim(totals, position, 0, keepdims=False)]
    broadcast_in_dim x2 -> x0, local copies, waits for them, and re-layouts: 6.29 us -> none  [the longest x1 6.13 us: on_device(): jnp.zeros((window_blocks, aux_local, block_size, orbitals), jnp.float32)]
where the time goes in v1:
time: 255 us
  waiting for transfers between devices  157 us (62%)
  starting transfers between devices  40.2 us (16%)
  Pallas kernels  30.1 us (12%)
  between operations  14.1 us (6%)
  other arithmetic  11.4 us (4%)
    ppermute x6, waiting for transfers between devices, passed_along(): lax.ppermute(value, axis, [(source, source + steps) for source in range(f...  114 us
    reduce_scatter x1, waiting for transfers between devices, on_device(): lax.psum_scatter(partial_tiles, 'aux', scatter_dimension=1, tiled=True)  42.5 us
    ppermute x6, starting transfers between devices, passed_along(): lax.ppermute(value, axis, [(source, source + steps) for source in range(f...  40.2 us
    pallas_call x1, Pallas kernels, on_device(): pl.pallas_call(_half_kernel, grid_spec=pltpu.PrefetchScalarGridSpec(num_s...  15.4 us
    pallas_call x1, Pallas kernels, on_device(): pl.pallas_call(_contract_kernel, grid_spec=pltpu.PrefetchScalarGridSpec(n...  14.7 us
  transfers between devices with their start and end apart: 7, of which 7 were waited for; matrix products, arithmetic and copies ran while one was open for 0% of the time, Pallas kernels for 0%

profile of v1, /device:TPU:6, one launch (start us, length us, event | category | flops | bytes accessed | tf_op | source)
XLA Modules:
  0.0 254.9 jit_solution(1268292035917092415)
XLA Ops:
  6.5 0.0 copy-start
  6.5 0.0 reduce-scatter.2.cloned.1.call-start
  6.5 11.5 %collective-permute-start.1 = (bf16[4,128,512]{2,1,0:T(8,128)(2,1)}, bf16[4,128,512]{2,1,0:T(8,128)(2,1)}, u32[]{:S(2)}, u32[]{:S(2)}) collective-permute-start(bf16[4,128,512]{2,1,0:T(8,128)(2,1)} %bitcast.5), channel_id=1, source_target_pairs={{2,0},{3,1},{4,2},{5,3},{6,4},{7,5},{8,6},{9,7},{10,8},{11,9},{12,... | collective-permute-start | bytes 1572872 | tf_op jit(solution)/shard_map/ppermute | solution.py:14
  18.0 1.9 collective-permute-start
  20.6 0.8 subtract_bitcast_fusion
  21.4 8.1 %collective-permute-done.1 = bf16[4,128,512]{2,1,0:T(8,128)(2,1)} collective-permute-done((bf16[4,128,512]{2,1,0:T(8,128)(2,1)}, bf16[4,128,512]{2,1,0:T(8,128)(2,1)}, u32[]{:S(2)}, u32[]{:S(2)}) %collective-permute-start.1) | collective-permute-done | bytes 524320 | tf_op jit(solution)/shard_map/ppermute | solution.py:14
  29.5 5.6 %collective-permute-done = bf16[4,128,512]{2,1,0:T(8,128)(2,1)} collective-permute-done((bf16[4,128,512]{2,1,0:T(8,128)(2,1)}, bf16[4,128,512]{2,1,0:T(8,128)(2,1)}, u32[]{:S(2)}, u32[]{:S(2)}) %collective-permute-start) | collective-permute-done | bytes 524320 | tf_op jit(solution)/shard_map/ppermute | solution.py:14
  35.1 1.5 pad_maximum_fusion.1.coeff_ref
  36.6 0.0 copy-done
  36.6 15.4 %shard_map.46 = bf16[12,4,128,512]{3,2,1,0:T(8,128)(2,1)} custom-call(s32[24]{0:T(128)S(1)} %get-tuple-element.8.left_ref, s32[24]{0:T(128)S(1)} %get-tuple-element.7.right_ref, s32[1]{0:T(128)S(6)} %copy.5.count_ref, bf16[24,4,128,128]{3,2,1,0:T(8,128)(2,1)S(1)} %copy-done, bf16[12,128,512]{2,1,0:T(8,128)(2,1)S(1)} %pad_maximum_fusion.1.coeff_ref), custom_call_target="tpu_custom_call" | custom-call | tf_op jit(solution)/shard_map/pallas_call | solution.py:93
  52.1 2.5 fusion
  54.6 1.9 collective-permute-start.2
  56.5 1.9 collective-permute-start.3
  58.4 45.6 %collective-permute-done.2 = bf16[4,4,128,512]{3,2,1,0:T(8,128)(2,1)S(1)} collective-permute-done((bf16[4,4,128,512]{3,2,1,0:T(8,128)(2,1)S(1)}, bf16[4,4,128,512]{3,2,1,0:T(8,128)(2,1)S(1)}, u32[]{:S(2)}, u32[]{:S(2)}) %collective-permute-start.2) | collective-permute-done | bytes 2097184 | tf_op jit(solution)/shard_map/ppermute | solution.py:14
  104.1 5.2 %collective-permute-done.3 = bf16[4,4,128,512]{3,2,1,0:T(8,128)(2,1)S(1)} collective-permute-done((bf16[4,4,128,512]{3,2,1,0:T(8,128)(2,1)S(1)}, bf16[4,4,128,512]{3,2,1,0:T(8,128)(2,1)S(1)}, u32[]{:S(2)}, u32[]{:S(2)}) %collective-permute-start.3) | collective-permute-done | bytes 2097184 | tf_op jit(solution)/shard_map/ppermute | solution.py:14
  109.3 2.6 %add_convert_fusion = bf16[4,4,128,512]{3,2,1,0:T(8,128)(2,1)S(1)} fusion(bf16[4,4,128,512]{3,2,1,0:T(8,128)(2,1)S(1)} %collective-permute-done.3, bf16[4,4,128,512]{3,2,1,0:T(8,128)(2,1)S(1)} %collective-permute-done.2, bf16[12,4,128,512]{3,2,1,0:T(8,128)(2,1)} %shard_map.46), kind=kLoop, calls=%fused_computation.1 | loop fusion | flops 6291456 | bytes 8388608 | tf_op jit(solution)/shard_map/convert_element_type | solution.py:125
  111.9 3.9 %collective-permute-start.5 = (bf16[4,4,128,512]{3,2,1,0:T(8,128)(2,1)S(1)}, bf16[4,4,128,512]{3,2,1,0:T(8,128)(2,1)S(1)}, u32[]{:S(2)}, u32[]{:S(2)}) collective-permute-start(bf16[4,4,128,512]{3,2,1,0:T(8,128)(2,1)S(1)} %add_convert_fusion), channel_id=1, source_target_pairs={{2,0},{3,1},{4,2},{5,3},{6,4},{7,5},{8,6},{9,7},{10,8},{11,9},{12,... | collective-permute-start | bytes 6291464 | tf_op jit(solution)/shard_map/ppermute | solution.py:14
  115.8 19.0 %collective-permute-start.4 = (bf16[4,4,128,512]{3,2,1,0:T(8,128)(2,1)S(1)}, bf16[4,4,128,512]{3,2,1,0:T(8,128)(2,1)S(1)}, u32[]{:S(2)}, u32[]{:S(2)}) collective-permute-start(bf16[4,4,128,512]{3,2,1,0:T(8,128)(2,1)S(1)} %add_convert_fusion), channel_id=1, source_target_pairs={{1,0},{2,1},{3,2},{4,3},{5,4},{6,5},{7,6},{8,7},{9,8},{10,9},{11,1... | collective-permute-start | bytes 6291464 | tf_op jit(solution)/shard_map/ppermute | solution.py:14
  134.9 10.0 %collective-permute-done.5 = bf16[4,4,128,512]{3,2,1,0:T(8,128)(2,1)S(1)} collective-permute-done((bf16[4,4,128,512]{3,2,1,0:T(8,128)(2,1)S(1)}, bf16[4,4,128,512]{3,2,1,0:T(8,128)(2,1)S(1)}, u32[]{:S(2)}, u32[]{:S(2)}) %collective-permute-start.5) | collective-permute-done | bytes 2097184 | tf_op jit(solution)/shard_map/ppermute | solution.py:14
  144.8 39.5 %collective-permute-done.4 = bf16[4,4,128,512]{3,2,1,0:T(8,128)(2,1)S(1)} collective-permute-done((bf16[4,4,128,512]{3,2,1,0:T(8,128)(2,1)S(1)}, bf16[4,4,128,512]{3,2,1,0:T(8,128)(2,1)S(1)}, u32[]{:S(2)}, u32[]{:S(2)}) %collective-permute-start.4) | collective-permute-done | bytes 2097184 | tf_op jit(solution)/shard_map/ppermute | solution.py:14
  184.3 5.0 %pad_maximum_fusion.fitted_ref = bf16[12,4,128,512]{3,2,1,0:T(8,128)(2,1)} fusion(bf16[4,4,128,512]{3,2,1,0:T(8,128)(2,1)S(1)} %collective-permute-done.5, bf16[4,4,128,512]{3,2,1,0:T(8,128)(2,1)S(1)} %collective-permute-done.4, bf16[4,4,128,512]{3,2,1,0:T(8,128)(2,1)S(1)} %add_convert_fusion), kind=kLoop, calls=%fused_computation | loop fusion | flops 6291456 | bytes 12582912 | tf_op jit(solution)/shard_map/concatenate | solution.py:127
  189.3 14.7 %shard_map.47 = f32[24,128,128]{2,1,0:T(8,128)} custom-call(s32[24]{0:T(128)S(1)} %get-tuple-element.8.left_ref, s32[24]{0:T(128)S(1)} %get-tuple-element.7.right_ref, s32[1]{0:T(128)S(6)} %copy.5.count_ref, bf16[12,4,128,512]{3,2,1,0:T(8,128)(2,1)} %pad_maximum_fusion.fitted_ref), custom_call_target="tpu_custom_call" | custom-call | tf_op jit(solution)/shard_map/pallas_call | solution.py:129
  203.9 0.0 reduce-scatter.2.cloned.1.call-update
  204.0 42.5 %reduce-scatter.2.cloned.1.call-done = f32[24,16,128]{2,1,0:T(8,128)} async-done(((f32[24,128,128]{2,1,0:T(8,128)}), f32[24,16,128]{2,1,0:T(8,128)}) %reduce-scatter.2.cloned.1.call-update) | async-done | bytes 196624 | tf_op jit(solution)/shard_map/reduce_scatter | solution.py:148
  246.4 1.6 multiply_convert_fusion
Async XLA Ops:
  6.5 30.1 %copy-start = (bf16[24,4,128,128]{3,2,1,0:T(8,128)(2,1)S(1)}, bf16[24,4,128,128]{3,2,1,0:T(8,128)(2,1)}, u32[]{:S(2)}) copy-start(bf16[24,4,128,128]{3,2,1,0:T(8,128)(2,1)} %tile_ref.1) | copy-start | bytes 9437188
  6.5 239.9 %reduce-scatter.2.cloned.1.call-start = ((), (), s32[]{:S(2)}) async-start(), calls=%async_computation.1 | async-start | bytes 1769472 | tf_op jit(solution)/shard_map/reduce_scatter | solution.py:148
  6.5 23.0 %collective-permute-start.1 = (bf16[4,128,512]{2,1,0:T(8,128)(2,1)}, bf16[4,128,512]{2,1,0:T(8,128)(2,1)}, u32[]{:S(2)}, u32[]{:S(2)}) collective-permute-start(bf16[4,128,512]{2,1,0:T(8,128)(2,1)} %bitcast.5), channel_id=1, source_target_pairs={{2,0},{3,1},{4,2},{5,3},{6,4},{7,5},{8,6},{9,7},{10,8},{11,9},{12,... | collective-permute-start | bytes 1572872 | tf_op jit(solution)/shard_map/ppermute | solution.py:14
  18.0 17.1 %collective-permute-start = (bf16[4,128,512]{2,1,0:T(8,128)(2,1)}, bf16[4,128,512]{2,1,0:T(8,128)(2,1)}, u32[]{:S(2)}, u32[]{:S(2)}) collective-permute-start(bf16[4,128,512]{2,1,0:T(8,128)(2,1)} %bitcast.6), channel_id=1, source_target_pairs={{1,0},{2,1},{3,2},{4,3},{5,4},{6,5},{7,6},{8,7},{9,8},{10,9},{11,1... | collective-permute-start | bytes 1572872 | tf_op jit(solution)/shard_map/ppermute | solution.py:14
  54.6 49.5 %collective-permute-start.2 = (bf16[4,4,128,512]{3,2,1,0:T(8,128)(2,1)S(1)}, bf16[4,4,128,512]{3,2,1,0:T(8,128)(2,1)S(1)}, u32[]{:S(2)}, u32[]{:S(2)}) collective-permute-start(bf16[4,4,128,512]{3,2,1,0:T(8,128)(2,1)S(1)} %get-tuple-element.5), channel_id=1, source_target_pairs={{0,1},{1,2},{2,3},{3,4},{4,5},{5,6},{6,7},{7,8},{8,9},{9,10},{10,1... | collective-permute-start | bytes 6291464 | tf_op jit(solution)/shard_map/ppermute | solution.py:14
  56.5 52.8 %collective-permute-start.3 = (bf16[4,4,128,512]{3,2,1,0:T(8,128)(2,1)S(1)}, bf16[4,4,128,512]{3,2,1,0:T(8,128)(2,1)S(1)}, u32[]{:S(2)}, u32[]{:S(2)}) collective-permute-start(bf16[4,4,128,512]{3,2,1,0:T(8,128)(2,1)S(1)} %get-tuple-element.6), channel_id=1, source_target_pairs={{0,2},{1,3},{2,4},{3,5},{4,6},{5,7},{6,8},{7,9},{8,10},{9,11},{10,... | collective-permute-start | bytes 6291464 | tf_op jit(solution)/shard_map/ppermute | solution.py:14
  111.9 32.9 %collective-permute-start.5 = (bf16[4,4,128,512]{3,2,1,0:T(8,128)(2,1)S(1)}, bf16[4,4,128,512]{3,2,1,0:T(8,128)(2,1)S(1)}, u32[]{:S(2)}, u32[]{:S(2)}) collective-permute-start(bf16[4,4,128,512]{3,2,1,0:T(8,128)(2,1)S(1)} %add_convert_fusion), channel_id=1, source_target_pairs={{2,0},{3,1},{4,2},{5,3},{6,4},{7,5},{8,6},{9,7},{10,8},{11,9},{12,... | collective-permute-start | bytes 6291464 | tf_op jit(solution)/shard_map/ppermute | solution.py:14
  115.8 68.5 %collective-permute-start.4 = (bf16[4,4,128,512]{3,2,1,0:T(8,128)(2,1)S(1)}, bf16[4,4,128,512]{3,2,1,0:T(8,128)(2,1)S(1)}, u32[]{:S(2)}, u32[]{:S(2)}) collective-permute-start(bf16[4,4,128,512]{3,2,1,0:T(8,128)(2,1)S(1)} %add_convert_fusion), channel_id=1, source_target_pairs={{1,0},{2,1},{3,2},{4,3},{5,4},{6,5},{7,6},{8,7},{9,8},{10,9},{11,1... | collective-permute-start | bytes 6291464 | tf_op jit(solution)/shard_map/ppermute | solution.py:14
Sparse Core Ops, SparseCore 0:
  204.1 42.2 reduce-scatter.1

commit v2 on v1

--- a/solution.py
+++ b/solution.py
@@ -46,29 +46,40 @@
 
     @pl.when(slot == pl.num_programs(0) - 1)
     def _():
-        out_ref[...] = acc_ref[...].astype(out_ref.dtype)
+        chunks = out_ref.shape[0]
+        width = out_ref.shape[-1]
+        for c in range(chunks):
+            out_ref[c] = acc_ref[:, :, :, c * width : (c + 1) * width].astype(out_ref.dtype)
 
 
-def _contract_kernel(left_ref, right_ref, count_ref, fitted_ref, out_ref):
+def _contract_kernel(left_ref, right_ref, count_ref, own_ref, near_ref, far_ref, prev_ref, out_ref):
     slot = pl.program_id(0)
     live = slot < count_ref[0]
+    own_blocks = own_ref.shape[0]
 
     @pl.when(live)
     def _():
-        left_rows = fitted_ref[left_ref[slot]]
-        right_rows = fitted_ref[right_ref[slot]]
-        total = None
+        left_rows = own_ref[left_ref[slot]]
+        right = right_ref[slot]
+        group = right // own_blocks
+        index = right % own_blocks
+        right_rows = jnp.where(
+            group == 0, own_ref[index], jnp.where(group == 1, near_ref[index], far_ref[index])
+        )
+        total = prev_ref[0]
         for p in range(left_rows.shape[0]):
-            part = lax.dot_general(
+            total = total + lax.dot_general(
                 left_rows[p], right_rows[p], (((1,), (1,)), ((), ())),
                 preferred_element_type=jnp.float32,
             )
-            total = part if total is None else total + part
         out_ref[0] = total
 
     @pl.when(jnp.logical_not(live))
     def _():
         out_ref[...] = jnp.zeros_like(out_ref)
+
+
+CHUNKS = 4
 
 
 def on_device(pair_list, pair_count, tiles, coeff):
@@ -78,6 +89,8 @@
     orbitals = coeff.shape[1]
     own_blocks = coeff.shape[0] // block_size
     window_blocks = (BAND + 1) * own_blocks
+    width = orbitals // CHUNKS
+    devices = lax.axis_size("ao")
     owner_index = lax.axis_index("ao")
     first_block = owner_index * own_blocks
     left_rel = (pair_list[:, 0] - first_block).astype(jnp.int32)
@@ -102,48 +115,60 @@
                 ),
             ],
             out_specs=pl.BlockSpec(
-                (window_blocks, aux_local, block_size, orbitals),
-                lambda s, l, r, c: (0, 0, 0, 0),
+                (CHUNKS, window_blocks, aux_local, block_size, width),
+                lambda s, l, r, c: (0, 0, 0, 0, 0),
             ),
             scratch_shapes=[
                 pltpu.VMEM((window_blocks, aux_local, block_size, orbitals), jnp.float32)
             ],
         ),
         out_shape=jax.ShapeDtypeStruct(
-            (window_blocks, aux_local, block_size, orbitals), jnp.bfloat16
+            (CHUNKS, window_blocks, aux_local, block_size, width), jnp.bfloat16
         ),
         compiler_params=pltpu.CompilerParams(
             dimension_semantics=("arbitrary",), vmem_limit_bytes=48 * 1024 * 1024
         ),
     )(left_rel, right_rel, count, tiles, window_coeff)
 
-    fitted_sum = halves[:own_blocks].astype(jnp.float32)
-    for distance in range(1, BAND + 1):
-        outgoing = halves[distance * own_blocks : (distance + 1) * own_blocks]
-        arriving = passed_along(outgoing, "ao", distance)
-        fitted_sum = fitted_sum + arriving.astype(jnp.float32)
-    fitted = fitted_sum.astype(jnp.bfloat16)
-    ahead_fitted = [passed_along(fitted, "ao", -distance) for distance in range(1, BAND + 1)]
-    window_fitted = jnp.concatenate([fitted] + ahead_fitted, 0)
-
-    partial_tiles = pl.pallas_call(
-        _contract_kernel,
-        grid_spec=pltpu.PrefetchScalarGridSpec(
-            num_scalar_prefetch=3,
-            grid=(pair_slots,),
-            in_specs=[
-                pl.BlockSpec(
-                    (window_blocks, aux_local, block_size, orbitals),
-                    lambda s, l, r, c: (0, 0, 0, 0),
+    odd_down_one = [(s, s - 1) for s in range(1, devices, 2)]
+    odd_down_two = [(s, s - 2) for s in range(3, devices, 2)]
+    is_even = (owner_index % 2) == 0
+    block_shape = (own_blocks, aux_local, block_size, width)
+    partial_tiles = jnp.zeros((pair_slots, block_size, block_size), jnp.float32)
+    pending = halves[0]
+    for c in range(CHUNKS):
+        chunk = pending
+        from_one = passed_along(chunk[own_blocks : 2 * own_blocks], "ao", 1)
+        from_two = passed_along(chunk[2 * own_blocks :], "ao", 2)
+        fitted = (
+            (from_two.astype(jnp.float32) + from_one.astype(jnp.float32))
+            + chunk[:own_blocks].astype(jnp.float32)
+        ).astype(jnp.bfloat16)
+        if c + 1 < CHUNKS:
+            fitted, pending = lax.optimization_barrier((fitted, halves[c + 1]))
+        near = passed_along(fitted, "ao", -1)
+        relayed = lax.ppermute(near, "ao", odd_down_one)
+        direct = lax.ppermute(fitted, "ao", odd_down_two)
+        far = jnp.where(is_even, relayed, direct)
+        partial_tiles = pl.pallas_call(
+            _contract_kernel,
+            grid_spec=pltpu.PrefetchScalarGridSpec(
+                num_scalar_prefetch=3,
+                grid=(pair_slots,),
+                in_specs=[
+                    pl.BlockSpec(block_shape, lambda s, l, r, n: (0, 0, 0, 0)),
+                    pl.BlockSpec(block_shape, lambda s, l, r, n: (0, 0, 0, 0)),
+                    pl.BlockSpec(block_shape, lambda s, l, r, n: (0, 0, 0, 0)),
+                    pl.BlockSpec((1, block_size, block_size), lambda s, l, r, n: (s, 0, 0)),
+                ],
+                out_specs=pl.BlockSpec(
+                    (1, block_size, block_size), lambda s, l, r, n: (s, 0, 0)
                 ),
-            ],
-            out_specs=pl.BlockSpec((1, block_size, block_size), lambda s, l, r, c: (s, 0, 0)),
-        ),
-        out_shape=jax.ShapeDtypeStruct((pair_slots, block_size, block_size), jnp.float32),
-        compiler_params=pltpu.CompilerParams(
-            dimension_semantics=("arbitrary",), vmem_limit_bytes=48 * 1024 * 1024
-        ),
-    )(left_rel, right_rel, count, window_fitted)
+            ),
+            out_shape=jax.ShapeDtypeStruct((pair_slots, block_size, block_size), jnp.float32),
+            input_output_aliases={6: 0},
+            compiler_params=pltpu.CompilerParams(dimension_semantics=("arbitrary",)),
+        )(left_rel, right_rel, count, fitted, near, far, partial_tiles)
 
     summed = lax.psum_scatter(partial_tiles, "aux", scatter_dimension=1, tiled=True)
     norm_factor = (aux_local * lax.axis_size("aux") * orbitals) ** (-0.5)

time: 255 us -> 278 us (1.090); the launches traced: 255 us -> 274 us
  waiting for transfers between devices: 157 us -> 106 us
  Pallas kernels: 30.1 us -> 79.5 us
  starting transfers between devices: 40.2 us -> 56.2 us
  local copies, waits for them, and re-layouts: 2.5 us -> 6.2 us
    ppermute x6 -> x14, waiting for transfers between devices: 114 us -> 61 us  [passed_along(): lax.ppermute(value, axis, [(source, source + steps) for source in range(f...]
    pallas_call x1 -> x4, Pallas kernels: 14.7 us -> 63.2 us  [on_device(): pl.pallas_call(_contract_kernel, grid_spec=pltpu.PrefetchScalarGridSpec(n...]
    ppermute x0 -> x8, starting transfers between devices: none -> 8.68 us  [the longest x4 5.14 us: on_device(): relayed = lax.ppermute(near, 'ao', odd_down_one)]
    ppermute x6 -> x14, starting transfers between devices: 40.2 us -> 47.5 us  [passed_along(): lax.ppermute(value, axis, [(source, source + steps) for source in range(f...]
    select_n x0 -> x4, other arithmetic: none -> 5.5 us  [on_device(): far = jnp.where(is_even, relayed, direct)]
    concatenate x1 -> x0, other arithmetic: 4.97 us -> none  [on_device(): window_fitted = jnp.concatenate([fitted] + ahead_fitted, 0)]
    squeeze x0 -> x1, local copies, waits for them, and re-layouts: none -> 3.31 us  [on_device(): fitted, pending = lax.optimization_barrier((fitted, halves[c + 1]))]
  transfers between devices with their start and end apart: 7 -> 23, of which waited for: 7 -> 12; matrix products, arithmetic and copies ran while one was open for 0% -> 4% of each run, Pallas kernels for 0% -> 17%
where the time goes in v2:
time: 278 us; the launch traced here: 274 us
  waiting for transfers between devices  106 us (38%)
  Pallas kernels  79.5 us (29%)
  starting transfers between devices  56.2 us (20%)
  between operations  14.4 us (5%)
  other arithmetic  11 us (4%)
  local copies, waits for them, and re-layouts  6.2 us (2%)
    pallas_call x4, Pallas kernels, on_device(): pl.pallas_call(_contract_kernel, grid_spec=pltpu.PrefetchScalarGridSpec(n...  63.2 us
    ppermute x14, waiting for transfers between devices, passed_along(): lax.ppermute(value, axis, [(source, source + steps) for source in range(f...  61 us
    ppermute x14, starting transfers between devices, passed_along(): lax.ppermute(value, axis, [(source, source + steps) for source in range(f...  47.5 us
    reduce_scatter x1, waiting for transfers between devices, on_device(): lax.psum_scatter(partial_tiles, 'aux', scatter_dimension=1, tiled=True)  45.2 us
    pallas_call x1, Pallas kernels, on_device(): pl.pallas_call(_half_kernel, grid_spec=pltpu.PrefetchScalarGridSpec(num_s...  16.4 us
  transfers between devices with their start and end apart: 23, of which 12 were waited for; matrix products, arithmetic and copies ran while one was open for 4% of the time, Pallas kernels for 17%

profile of v2, /device:TPU:6, one launch (start us, length us, event | category | flops | bytes accessed | tf_op | source)
XLA Modules:
  0.0 273.6 jit_solution(13905158716706184548)
XLA Ops:
  6.5 10.6 %collective-permute-start = (bf16[4,128,512]{2,1,0:T(8,128)(2,1)}, bf16[4,128,512]{2,1,0:T(8,128)(2,1)S(1)}, u32[]{:S(2)}, u32[]{:S(2)}) collective-permute-start(bf16[4,128,512]{2,1,0:T(8,128)(2,1)} %bitcast.20), channel_id=1, source_target_pairs={{1,0},{2,1},{3,2},{4,3},{5,4},{6,5},{7,6},{8,7},{9,8},{10,9},{11,1... | collective-permute-start | bytes 1572872 | tf_op jit(solution)/shard_map/ppermute | solution.py:14
  17.2 2.5 collective-permute-start.1
  21.1 6.7 %collective-permute-done = bf16[4,128,512]{2,1,0:T(8,128)(2,1)S(1)} collective-permute-done((bf16[4,128,512]{2,1,0:T(8,128)(2,1)}, bf16[4,128,512]{2,1,0:T(8,128)(2,1)S(1)}, u32[]{:S(2)}, u32[]{:S(2)}) %collective-permute-start) | collective-permute-done | bytes 524320 | tf_op jit(solution)/shard_map/ppermute | solution.py:14
  27.8 7.6 %collective-permute-done.1 = bf16[4,128,512]{2,1,0:T(8,128)(2,1)S(1)} collective-permute-done((bf16[4,128,512]{2,1,0:T(8,128)(2,1)}, bf16[4,128,512]{2,1,0:T(8,128)(2,1)S(1)}, u32[]{:S(2)}, u32[]{:S(2)}) %collective-permute-start.1) | collective-permute-done | bytes 524320 | tf_op jit(solution)/shard_map/ppermute | solution.py:14
  36.7 16.4 %shard_map.46 = bf16[4,12,4,128,128]{4,3,2,1,0:T(8,128)(2,1)} custom-call(s32[24]{0:T(128)S(1)} %get-tuple-element.29.left_ref, s32[24]{0:T(128)S(1)} %get-tuple-element.28.right_ref, s32[1]{0:T(128)S(6)} %copy.13.count_ref, bf16[24,4,128,128]{3,2,1,0:T(8,128)(2,1)S(1)} %copy-done, bf16[12,128,512]{2,1,0:T(8,128)(2,1)S(1)} %pad_maximum_fusion.coeff_ref), custom_call_target="tpu_custom_call" | custom-call | tf_op jit(solution)/shard_map/pallas_call | solution.py:106
  54.3 1.9 collective-permute-start.2
  56.2 1.9 collective-permute-start.3
  58.2 3.3 %slice_bitcast_fusion = (bf16[12,4,128,128]{3,2,1,0:T(8,128)(2,1)S(1)}, bf16[12,4,128,128]{3,2,1,0:T(8,128)(2,1)S(1)}, bf16[12,4,128,128]{3,2,1,0:T(8,128)(2,1)S(1)}) fusion(bf16[4,12,4,128,128]{4,3,2,1,0:T(8,128)(2,1)} %shard_map.46), kind=kLoop, calls=%fused_computation | loop fusion | bytes 9437184 | tf_op jit(solution)/shard_map/squeeze | solution.py:148
  61.5 11.0 %collective-permute-done.2 = bf16[4,4,128,128]{3,2,1,0:T(8,128)(2,1)S(1)} collective-permute-done((bf16[4,4,128,128]{3,2,1,0:T(8,128)(2,1)S(1)}, bf16[4,4,128,128]{3,2,1,0:T(8,128)(2,1)S(1)}, u32[]{:S(2)}, u32[]{:S(2)}) %collective-permute-start.2) | collective-permute-done | bytes 524320 | tf_op jit(solution)/shard_map/ppermute | solution.py:14
  74.8 1.9 collective-permute-start.4
  76.8 1.9 collective-permute-start.5
  78.7 14.5 %collective-permute-done.4 = bf16[4,4,128,128]{3,2,1,0:T(8,128)(2,1)S(1)} collective-permute-done((bf16[4,4,128,128]{3,2,1,0:T(8,128)(2,1)S(1)}, bf16[4,4,128,128]{3,2,1,0:T(8,128)(2,1)S(1)}, u32[]{:S(2)}, u32[]{:S(2)}) %collective-permute-start.4) | collective-permute-done | bytes 524320 | tf_op jit(solution)/shard_map/ppermute | solution.py:14
  94.4 1.9 collective-permute-start.6
  96.3 1.9 collective-permute-start.7
  98.3 5.8 %collective-permute-start.19 = (bf16[4,4,128,128]{3,2,1,0:T(8,128)(2,1)S(1)}, bf16[4,4,128,128]{3,2,1,0:T(8,128)(2,1)}, u32[]{:S(2)}, u32[]{:S(2)}) collective-permute-start(bf16[4,4,128,128]{3,2,1,0:T(8,128)(2,1)S(1)} %fusion.own_ref), channel_id=1, source_target_pairs={{1,0},{2,1},{3,2},{4,3},{5,4},{6,5},{7,6},{8,7},{9,8},{10,9},{11,1... | collective-permute-start | bytes 1572872 | tf_op jit(solution)/shard_map/ppermute | solution.py:14
  104.0 8.8 %collective-permute-done.6 = bf16[4,4,128,128]{3,2,1,0:T(8,128)(2,1)S(1)} collective-permute-done((bf16[4,4,128,128]{3,2,1,0:T(8,128)(2,1)S(1)}, bf16[4,4,128,128]{3,2,1,0:T(8,128)(2,1)S(1)}, u32[]{:S(2)}, u32[]{:S(2)}) %collective-permute-start.6) | collective-permute-done | bytes 524320 | tf_op jit(solution)/shard_map/ppermute | solution.py:14
  114.0 1.9 collective-permute-start.8
  115.9 1.9 collective-permute-start.9
  118.6 8.7 %collective-permute-start.16 = (bf16[4,4,128,128]{3,2,1,0:T(8,128)(2,1)S(1)}, bf16[4,4,128,128]{3,2,1,0:T(8,128)(2,1)}, u32[]{:S(2)}, u32[]{:S(2)}) collective-permute-start(bf16[4,4,128,128]{3,2,1,0:T(8,128)(2,1)S(1)} %add_convert_fusion.2.own_ref), channel_id=1, source_target_pairs={{1,0},{2,1},{3,2},{4,3},{5,4},{6,5},{7,6},{8,7},{9,8},{10,9},{11,1... | collective-permute-start | bytes 1572872 | tf_op jit(solution)/shard_map/ppermute | solution.py:14
  128.0 4.8 %collective-permute-done.8 = bf16[4,4,128,128]{3,2,1,0:T(8,128)(2,1)S(1)} collective-permute-done((bf16[4,4,128,128]{3,2,1,0:T(8,128)(2,1)S(1)}, bf16[4,4,128,128]{3,2,1,0:T(8,128)(2,1)S(1)}, u32[]{:S(2)}, u32[]{:S(2)}) %collective-permute-start.8) | collective-permute-done | bytes 524320 | tf_op jit(solution)/shard_map/ppermute | solution.py:14
  134.7 2.7 collective-permute-start.13
  137.6 1.9 collective-permute-start.10
  140.9 1.5 collective-permute-start.15
  142.4 4.2 %collective-permute-done.13.near_ref = bf16[4,4,128,128]{3,2,1,0:T(8,128)(2,1)} collective-permute-done((bf16[4,4,128,128]{3,2,1,0:T(8,128)(2,1)S(1)}, bf16[4,4,128,128]{3,2,1,0:T(8,128)(2,1)}, u32[]{:S(2)}, u32[]{:S(2)}) %collective-permute-start.13) | collective-permute-done | bytes 524320 | tf_op jit(solution)/shard_map/ppermute | solution.py:14
  147.9 1.9 broadcast_select_fusion.far_ref
  151.1 15.8 %shard_map.47.prev_ref = f32[24,128,128]{2,1,0:T(8,128)} custom-call(s32[24]{0:T(128)} %copy-done.2, s32[24]{0:T(128)} %copy-done.1, s32[1]{0:T(128)S(6)} %copy.13.count_ref, bf16[4,4,128,128]{3,2,1,0:T(8,128)(2,1)} %copy-done.4, bf16[4,4,128,128]{3,2,1,0:T(8,128)(2,1)} %collective-permute-done.19.near_ref, ...), custom_call_target="tpu_custom_call", output_to_operand_aliasing={{}: (6, {})} | custom-call | tf_op jit(solution)/shard_map/pallas_call | solution.py:153
  169.8 15.8 %shard_map.48.prev_ref = f32[24,128,128]{2,1,0:T(8,128)} custom-call(s32[24]{0:T(128)} %copy-done.2, s32[24]{0:T(128)} %copy-done.1, s32[1]{0:T(128)S(6)} %copy.13.count_ref, bf16[4,4,128,128]{3,2,1,0:T(8,128)(2,1)} %copy-done.3, bf16[4,4,128,128]{3,2,1,0:T(8,128)(2,1)} %collective-permute-done.16.near_ref, ...), custom_call_target="tpu_custom_call", output_to_operand_aliasing={{}: (6, {})} | custom-call | tf_op jit(solution)/shard_map/pallas_call | solution.py:153
  185.6 1.9 broadcast_select_fusion.2.far_ref
  187.5 15.8 %shard_map.49.prev_ref = f32[24,128,128]{2,1,0:T(8,128)} custom-call(s32[24]{0:T(128)} %copy-done.2, s32[24]{0:T(128)} %copy-done.1, s32[1]{0:T(128)S(6)} %copy.13.count_ref, bf16[4,4,128,128]{3,2,1,0:T(8,128)(2,1)} %copy-done.5, bf16[4,4,128,128]{3,2,1,0:T(8,128)(2,1)} %collective-permute-done.13.near_ref, ...), custom_call_target="tpu_custom_call", output_to_operand_aliasing={{}: (6, {})} | custom-call | tf_op jit(solution)/shard_map/pallas_call | solution.py:153
  204.1 15.8 %shard_map.50 = f32[24,128,128]{2,1,0:T(8,128)} custom-call(s32[24]{0:T(128)} %copy-done.2, s32[24]{0:T(128)} %copy-done.1, s32[1]{0:T(128)S(6)} %copy.13.count_ref, bf16[4,4,128,128]{3,2,1,0:T(8,128)(2,1)} %copy-done.6, bf16[4,4,128,128]{3,2,1,0:T(8,128)(2,1)} %collective-permute-done.10.near_ref, ...), custom_call_target="tpu_custom_call", output_to_operand_aliasing={{}: (6, {})} | custom-call | tf_op jit(solution)/shard_map/pallas_call | solution.py:153
  219.9 45.2 %reduce-scatter.2.cloned.1.call-done = f32[24,16,128]{2,1,0:T(8,128)} async-done(((f32[24,128,128]{2,1,0:T(8,128)}), f32[24,16,128]{2,1,0:T(8,128)}) %reduce-scatter.2.cloned.1.call-update) | async-done | bytes 196624 | tf_op jit(solution)/shard_map/reduce_scatter | solution.py:173
  265.2 1.6 multiply_convert_fusion
  (51 shorter events, 19.1 us)
Async XLA Ops:
  6.5 258.6 %reduce-scatter.2.cloned.1.call-start = ((), (), s32[]{:S(2)}) async-start(), calls=%async_computation.1 | async-start | bytes 1769472 | tf_op jit(solution)/shard_map/reduce_scatter | solution.py:173
  6.5 21.2 %collective-permute-start = (bf16[4,128,512]{2,1,0:T(8,128)(2,1)}, bf16[4,128,512]{2,1,0:T(8,128)(2,1)S(1)}, u32[]{:S(2)}, u32[]{:S(2)}) collective-permute-start(bf16[4,128,512]{2,1,0:T(8,128)(2,1)} %bitcast.20), channel_id=1, source_target_pairs={{1,0},{2,1},{3,2},{4,3},{5,4},{6,5},{7,6},{8,7},{9,8},{10,9},{11,1... | collective-permute-start | bytes 1572872 | tf_op jit(solution)/shard_map/ppermute | solution.py:14
  17.2 18.2 %collective-permute-start.1 = (bf16[4,128,512]{2,1,0:T(8,128)(2,1)}, bf16[4,128,512]{2,1,0:T(8,128)(2,1)S(1)}, u32[]{:S(2)}, u32[]{:S(2)}) collective-permute-start(bf16[4,128,512]{2,1,0:T(8,128)(2,1)} %bitcast.21), channel_id=1, source_target_pairs={{2,0},{3,1},{4,2},{5,3},{6,4},{7,5},{8,6},{9,7},{10,8},{11,9},{12,... | collective-permute-start | bytes 1572872 | tf_op jit(solution)/shard_map/ppermute | solution.py:14
  21.1 15.5 %copy-start.1 = (s32[24]{0:T(128)}, s32[24]{0:T(128)S(1)}, u32[]{:S(2)}) copy-start(s32[24]{0:T(128)S(1)} %get-tuple-element.28.right_ref) | copy-start | bytes 292
  21.1 15.6 %copy-start.2 = (s32[24]{0:T(128)}, s32[24]{0:T(128)S(1)}, u32[]{:S(2)}) copy-start(s32[24]{0:T(128)S(1)} %get-tuple-element.29.left_ref) | copy-start | bytes 292
  21.1 15.6 %copy-start = (bf16[24,4,128,128]{3,2,1,0:T(8,128)(2,1)S(1)}, bf16[24,4,128,128]{3,2,1,0:T(8,128)(2,1)}, u32[]{:S(2)}) copy-start(bf16[24,4,128,128]{3,2,1,0:T(8,128)(2,1)} %tile_ref.1) | copy-start | bytes 9437188
  54.3 18.2 %collective-permute-start.2 = (bf16[4,4,128,128]{3,2,1,0:T(8,128)(2,1)S(1)}, bf16[4,4,128,128]{3,2,1,0:T(8,128)(2,1)S(1)}, u32[]{:S(2)}, u32[]{:S(2)}) collective-permute-start(bf16[4,4,128,128]{3,2,1,0:T(8,128)(2,1)S(1)} %get-tuple-element.20), channel_id=1, source_target_pairs={{0,2},{1,3},{2,4},{3,5},{4,6},{5,7},{6,8},{7,9},{8,10},{9,11},{10,... | collective-permute-start | bytes 1572872 | tf_op jit(solution)/shard_map/ppermute | solution.py:14
  56.2 17.2 %collective-permute-start.3 = (bf16[4,4,128,128]{3,2,1,0:T(8,128)(2,1)S(1)}, bf16[4,4,128,128]{3,2,1,0:T(8,128)(2,1)S(1)}, u32[]{:S(2)}, u32[]{:S(2)}) collective-permute-start(bf16[4,4,128,128]{3,2,1,0:T(8,128)(2,1)S(1)} %get-tuple-element.21), channel_id=1, source_target_pairs={{0,1},{1,2},{2,3},{3,4},{4,5},{5,6},{6,7},{7,8},{8,9},{9,10},{10,1... | collective-permute-start | bytes 1572872 | tf_op jit(solution)/shard_map/ppermute | solution.py:14
  74.7 43.1 %copy-start.4 = (bf16[4,4,128,128]{3,2,1,0:T(8,128)(2,1)}, bf16[4,4,128,128]{3,2,1,0:T(8,128)(2,1)S(1)}, u32[]{:S(2)}) copy-start(bf16[4,4,128,128]{3,2,1,0:T(8,128)(2,1)S(1)} %fusion.own_ref) | copy-start | bytes 1572868
  74.8 18.4 %collective-permute-start.4 = (bf16[4,4,128,128]{3,2,1,0:T(8,128)(2,1)S(1)}, bf16[4,4,128,128]{3,2,1,0:T(8,128)(2,1)S(1)}, u32[]{:S(2)}, u32[]{:S(2)}) collective-permute-start(bf16[4,4,128,128]{3,2,1,0:T(8,128)(2,1)S(1)} %get-tuple-element.26), channel_id=1, source_target_pairs={{0,2},{1,3},{2,4},{3,5},{4,6},{5,7},{6,8},{7,9},{8,10},{9,11},{10,... | collective-permute-start | bytes 1572872 | tf_op jit(solution)/shard_map/ppermute | solution.py:14
  76.8 17.3 %collective-permute-start.5 = (bf16[4,4,128,128]{3,2,1,0:T(8,128)(2,1)S(1)}, bf16[4,4,128,128]{3,2,1,0:T(8,128)(2,1)S(1)}, u32[]{:S(2)}, u32[]{:S(2)}) collective-permute-start(bf16[4,4,128,128]{3,2,1,0:T(8,128)(2,1)S(1)} %get-tuple-element.27), channel_id=1, source_target_pairs={{0,1},{1,2},{2,3},{3,4},{4,5},{5,6},{6,7},{7,8},{8,9},{9,10},{10,1... | collective-permute-start | bytes 1572872 | tf_op jit(solution)/shard_map/ppermute | solution.py:14
  94.3 33.0 %copy-start.3 = (bf16[4,4,128,128]{3,2,1,0:T(8,128)(2,1)}, bf16[4,4,128,128]{3,2,1,0:T(8,128)(2,1)S(1)}, u32[]{:S(2)}) copy-start(bf16[4,4,128,128]{3,2,1,0:T(8,128)(2,1)S(1)} %add_convert_fusion.2.own_ref) | copy-start | bytes 1572868
  94.4 18.4 %collective-permute-start.6 = (bf16[4,4,128,128]{3,2,1,0:T(8,128)(2,1)S(1)}, bf16[4,4,128,128]{3,2,1,0:T(8,128)(2,1)S(1)}, u32[]{:S(2)}, u32[]{:S(2)}) collective-permute-start(bf16[4,4,128,128]{3,2,1,0:T(8,128)(2,1)S(1)} %get-tuple-element.24), channel_id=1, source_target_pairs={{0,2},{1,3},{2,4},{3,5},{4,6},{5,7},{6,8},{7,9},{8,10},{9,11},{10,... | collective-permute-start | bytes 1572872 | tf_op jit(solution)/shard_map/ppermute | solution.py:14
  96.3 17.3 %collective-permute-start.7 = (bf16[4,4,128,128]{3,2,1,0:T(8,128)(2,1)S(1)}, bf16[4,4,128,128]{3,2,1,0:T(8,128)(2,1)S(1)}, u32[]{:S(2)}, u32[]{:S(2)}) collective-permute-start(bf16[4,4,128,128]{3,2,1,0:T(8,128)(2,1)S(1)} %get-tuple-element.25), channel_id=1, source_target_pairs={{0,1},{1,2},{2,3},{3,4},{4,5},{5,6},{6,7},{7,8},{8,9},{9,10},{10,1... | collective-permute-start | bytes 1572872 | tf_op jit(solution)/shard_map/ppermute | solution.py:14
  98.3 29.0 %collective-permute-start.19 = (bf16[4,4,128,128]{3,2,1,0:T(8,128)(2,1)S(1)}, bf16[4,4,128,128]{3,2,1,0:T(8,128)(2,1)}, u32[]{:S(2)}, u32[]{:S(2)}) collective-permute-start(bf16[4,4,128,128]{3,2,1,0:T(8,128)(2,1)S(1)} %fusion.own_ref), channel_id=1, source_target_pairs={{1,0},{2,1},{3,2},{4,3},{5,4},{6,5},{7,6},{8,7},{9,8},{10,9},{11,1... | collective-permute-start | bytes 1572872 | tf_op jit(solution)/shard_map/ppermute | solution.py:14
  113.9 27.0 %copy-start.5 = (bf16[4,4,128,128]{3,2,1,0:T(8,128)(2,1)}, bf16[4,4,128,128]{3,2,1,0:T(8,128)(2,1)S(1)}, u32[]{:S(2)}) copy-start(bf16[4,4,128,128]{3,2,1,0:T(8,128)(2,1)S(1)} %add_convert_fusion.1.own_ref) | copy-start | bytes 1572868
  114.0 18.8 %collective-permute-start.8 = (bf16[4,4,128,128]{3,2,1,0:T(8,128)(2,1)S(1)}, bf16[4,4,128,128]{3,2,1,0:T(8,128)(2,1)S(1)}, u32[]{:S(2)}, u32[]{:S(2)}) collective-permute-start(bf16[4,4,128,128]{3,2,1,0:T(8,128)(2,1)S(1)} %get-tuple-element.22), channel_id=1, source_target_pairs={{0,2},{1,3},{2,4},{3,5},{4,6},{5,7},{6,8},{7,9},{8,10},{9,11},{10,... | collective-permute-start | bytes 1572872 | tf_op jit(solution)/shard_map/ppermute | solution.py:14
  115.9 18.8 %collective-permute-start.9 = (bf16[4,4,128,128]{3,2,1,0:T(8,128)(2,1)S(1)}, bf16[4,4,128,128]{3,2,1,0:T(8,128)(2,1)S(1)}, u32[]{:S(2)}, u32[]{:S(2)}) collective-permute-start(bf16[4,4,128,128]{3,2,1,0:T(8,128)(2,1)S(1)} %get-tuple-element.23), channel_id=1, source_target_pairs={{0,1},{1,2},{2,3},{3,4},{4,5},{5,6},{6,7},{7,8},{8,9},{9,10},{10,1... | collective-permute-start | bytes 1572872 | tf_op jit(solution)/shard_map/ppermute | solution.py:14
  117.9 19.8 %collective-permute-start.21 = (bf16[4,4,128,128]{3,2,1,0:T(8,128)(2,1)S(1)}, bf16[4,4,128,128]{3,2,1,0:T(8,128)(2,1)S(1)}, u32[]{:S(2)}, u32[]{:S(2)}) collective-permute-start(bf16[4,4,128,128]{3,2,1,0:T(8,128)(2,1)S(1)} %fusion.own_ref), channel_id=1, source_target_pairs={{3,1},{5,3},{7,5},{9,7},{11,9},{13,11},{15,13},{17,15},{19,17},{21... | collective-permute-start | bytes 1572872 | tf_op jit(solution)/shard_map/ppermute | solution.py:151
  118.6 21.0 %collective-permute-start.16 = (bf16[4,4,128,128]{3,2,1,0:T(8,128)(2,1)S(1)}, bf16[4,4,128,128]{3,2,1,0:T(8,128)(2,1)}, u32[]{:S(2)}, u32[]{:S(2)}) collective-permute-start(bf16[4,4,128,128]{3,2,1,0:T(8,128)(2,1)S(1)} %add_convert_fusion.2.own_ref), channel_id=1, source_target_pairs={{1,0},{2,1},{3,2},{4,3},{5,4},{6,5},{7,6},{8,7},{9,8},{10,9},{11,1... | collective-permute-start | bytes 1572872 | tf_op jit(solution)/shard_map/ppermute | solution.py:14
  127.3 39.6 %collective-permute-start.18 = (bf16[4,4,128,128]{3,2,1,0:T(8,128)(2,1)S(1)}, bf16[4,4,128,128]{3,2,1,0:T(8,128)(2,1)S(1)}, u32[]{:S(2)}, u32[]{:S(2)}) collective-permute-start(bf16[4,4,128,128]{3,2,1,0:T(8,128)(2,1)S(1)} %add_convert_fusion.2.own_ref), channel_id=1, source_target_pairs={{3,1},{5,3},{7,5},{9,7},{11,9},{13,11},{15,13},{17,15},{19,17},{21... | collective-permute-start | bytes 1572872 | tf_op jit(solution)/shard_map/ppermute | solution.py:151
  132.8 8.1 %collective-permute-start.20 = (bf16[4,4,128,128]{3,2,1,0:T(8,128)(2,1)}, bf16[4,4,128,128]{3,2,1,0:T(8,128)(2,1)}, u32[]{:S(2)}, u32[]{:S(2)}) collective-permute-start(bf16[4,4,128,128]{3,2,1,0:T(8,128)(2,1)} %collective-permute-done.19.near_ref), channel_id=1, source_target_pairs={{1,0},{3,2},{5,4},{7,6},{9,8},{11,10},{13,12},{15,14},{17,16},{19,... | collective-permute-start | bytes 1572872 | tf_op jit(solution)/shard_map/ppermute | solution.py:150
  134.7 11.9 %collective-permute-start.13 = (bf16[4,4,128,128]{3,2,1,0:T(8,128)(2,1)S(1)}, bf16[4,4,128,128]{3,2,1,0:T(8,128)(2,1)}, u32[]{:S(2)}, u32[]{:S(2)}) collective-permute-start(bf16[4,4,128,128]{3,2,1,0:T(8,128)(2,1)S(1)} %add_convert_fusion.1.own_ref), channel_id=1, source_target_pairs={{1,0},{2,1},{3,2},{4,3},{5,4},{6,5},{7,6},{8,7},{9,8},{10,9},{11,1... | collective-permute-start | bytes 1572872 | tf_op jit(solution)/shard_map/ppermute | solution.py:14
  137.6 29.3 %copy-start.6 = (bf16[4,4,128,128]{3,2,1,0:T(8,128)(2,1)}, bf16[4,4,128,128]{3,2,1,0:T(8,128)(2,1)S(1)}, u32[]{:S(2)}) copy-start(bf16[4,4,128,128]{3,2,1,0:T(8,128)(2,1)S(1)} %add_convert_fusion.own_ref) | copy-start | bytes 1572868
  137.6 30.0 %collective-permute-start.10 = (bf16[4,4,128,128]{3,2,1,0:T(8,128)(2,1)S(1)}, bf16[4,4,128,128]{3,2,1,0:T(8,128)(2,1)}, u32[]{:S(2)}, u32[]{:S(2)}) collective-permute-start(bf16[4,4,128,128]{3,2,1,0:T(8,128)(2,1)S(1)} %add_convert_fusion.own_ref), channel_id=1, source_target_pairs={{1,0},{2,1},{3,2},{4,3},{5,4},{6,5},{7,6},{8,7},{9,8},{10,9},{11,1... | collective-permute-start | bytes 1572872 | tf_op jit(solution)/shard_map/ppermute | solution.py:14
  139.6 29.3 %collective-permute-start.17 = (bf16[4,4,128,128]{3,2,1,0:T(8,128)(2,1)}, bf16[4,4,128,128]{3,2,1,0:T(8,128)(2,1)S(1)}, u32[]{:S(2)}, u32[]{:S(2)}) collective-permute-start(bf16[4,4,128,128]{3,2,1,0:T(8,128)(2,1)} %collective-permute-done.16.near_ref), channel_id=1, source_target_pairs={{1,0},{3,2},{5,4},{7,6},{9,8},{11,10},{13,12},{15,14},{17,16},{19,... | collective-permute-start | bytes 1572872 | tf_op jit(solution)/shard_map/ppermute | solution.py:150
  140.9 44.7 %collective-permute-start.15 = (bf16[4,4,128,128]{3,2,1,0:T(8,128)(2,1)S(1)}, bf16[4,4,128,128]{3,2,1,0:T(8,128)(2,1)}, u32[]{:S(2)}, u32[]{:S(2)}) collective-permute-start(bf16[4,4,128,128]{3,2,1,0:T(8,128)(2,1)S(1)} %add_convert_fusion.1.own_ref), channel_id=1, source_target_pairs={{3,1},{5,3},{7,5},{9,7},{11,9},{13,11},{15,13},{17,15},{19,17},{21... | collective-permute-start | bytes 1572872 | tf_op jit(solution)/shard_map/ppermute | solution.py:151
  146.6 39.0 %collective-permute-start.14 = (bf16[4,4,128,128]{3,2,1,0:T(8,128)(2,1)}, bf16[4,4,128,128]{3,2,1,0:T(8,128)(2,1)}, u32[]{:S(2)}, u32[]{:S(2)}) collective-permute-start(bf16[4,4,128,128]{3,2,1,0:T(8,128)(2,1)} %collective-permute-done.13.near_ref), channel_id=1, source_target_pairs={{1,0},{3,2},{5,4},{7,6},{9,8},{11,10},{13,12},{15,14},{17,16},{19,... | collective-permute-start | bytes 1572872 | tf_op jit(solution)/shard_map/ppermute | solution.py:150
  166.9 36.4 %collective-permute-start.12 = (bf16[4,4,128,128]{3,2,1,0:T(8,128)(2,1)S(1)}, bf16[4,4,128,128]{3,2,1,0:T(8,128)(2,1)S(1)}, u32[]{:S(2)}, u32[]{:S(2)}) collective-permute-start(bf16[4,4,128,128]{3,2,1,0:T(8,128)(2,1)S(1)} %add_convert_fusion.own_ref), channel_id=1, source_target_pairs={{3,1},{5,3},{7,5},{9,7},{11,9},{13,11},{15,13},{17,15},{19,17},{21... | collective-permute-start | bytes 1572872 | tf_op jit(solution)/shard_map/ppermute | solution.py:151
  167.6 35.7 %collective-permute-start.11 = (bf16[4,4,128,128]{3,2,1,0:T(8,128)(2,1)}, bf16[4,4,128,128]{3,2,1,0:T(8,128)(2,1)S(1)}, u32[]{:S(2)}, u32[]{:S(2)}) collective-permute-start(bf16[4,4,128,128]{3,2,1,0:T(8,128)(2,1)} %collective-permute-done.10.near_ref), channel_id=1, source_target_pairs={{1,0},{3,2},{5,4},{7,6},{9,8},{11,10},{13,12},{15,14},{17,16},{19,... | collective-permute-start | bytes 1572872 | tf_op jit(solution)/shard_map/ppermute | solution.py:150
Sparse Core Ops, SparseCore 0:
  220.1 45.0 reduce-scatter.1

commit v3 on v2

--- a/solution.py
+++ b/solution.py
@@ -52,26 +52,33 @@
             out_ref[c] = acc_ref[:, :, :, c * width : (c + 1) * width].astype(out_ref.dtype)
 
 
-def _contract_kernel(left_ref, right_ref, count_ref, own_ref, near_ref, far_ref, prev_ref, out_ref):
+def _contract_kernel(left_ref, right_ref, count_ref, *refs):
+    out_ref = refs[-1]
+    groups = refs[:-1]
+    chunks = len(groups) // 3
     slot = pl.program_id(0)
     live = slot < count_ref[0]
-    own_blocks = own_ref.shape[0]
+    own_blocks = groups[0].shape[0]
 
     @pl.when(live)
     def _():
-        left_rows = own_ref[left_ref[slot]]
+        left = left_ref[slot]
         right = right_ref[slot]
         group = right // own_blocks
         index = right % own_blocks
-        right_rows = jnp.where(
-            group == 0, own_ref[index], jnp.where(group == 1, near_ref[index], far_ref[index])
-        )
-        total = prev_ref[0]
-        for p in range(left_rows.shape[0]):
-            total = total + lax.dot_general(
-                left_rows[p], right_rows[p], (((1,), (1,)), ((), ())),
-                preferred_element_type=jnp.float32,
+        total = None
+        for c in range(chunks):
+            own_ref, near_ref, far_ref = groups[3 * c : 3 * c + 3]
+            left_rows = own_ref[left]
+            right_rows = jnp.where(
+                group == 0, own_ref[index], jnp.where(group == 1, near_ref[index], far_ref[index])
             )
+            for p in range(left_rows.shape[0]):
+                part = lax.dot_general(
+                    left_rows[p], right_rows[p], (((1,), (1,)), ((), ())),
+                    preferred_element_type=jnp.float32,
+                )
+                total = part if total is None else total + part
         out_ref[0] = total
 
     @pl.when(jnp.logical_not(live))
@@ -134,7 +141,7 @@
     odd_down_two = [(s, s - 2) for s in range(3, devices, 2)]
     is_even = (owner_index % 2) == 0
     block_shape = (own_blocks, aux_local, block_size, width)
-    partial_tiles = jnp.zeros((pair_slots, block_size, block_size), jnp.float32)
+    pieces = []
     pending = halves[0]
     for c in range(CHUNKS):
         chunk = pending
@@ -150,25 +157,21 @@
         relayed = lax.ppermute(near, "ao", odd_down_one)
         direct = lax.ppermute(fitted, "ao", odd_down_two)
         far = jnp.where(is_even, relayed, direct)
-        partial_tiles = pl.pallas_call(
-            _contract_kernel,
-            grid_spec=pltpu.PrefetchScalarGridSpec(
-                num_scalar_prefetch=3,
-                grid=(pair_slots,),
-                in_specs=[
-                    pl.BlockSpec(block_shape, lambda s, l, r, n: (0, 0, 0, 0)),
-                    pl.BlockSpec(block_shape, lambda s, l, r, n: (0, 0, 0, 0)),
-                    pl.BlockSpec(block_shape, lambda s, l, r, n: (0, 0, 0, 0)),
-                    pl.BlockSpec((1, block_size, block_size), lambda s, l, r, n: (s, 0, 0)),
-                ],
-                out_specs=pl.BlockSpec(
-                    (1, block_size, block_size), lambda s, l, r, n: (s, 0, 0)
-                ),
-            ),
-            out_shape=jax.ShapeDtypeStruct((pair_slots, block_size, block_size), jnp.float32),
-            input_output_aliases={6: 0},
-            compiler_params=pltpu.CompilerParams(dimension_semantics=("arbitrary",)),
-        )(left_rel, right_rel, count, fitted, near, far, partial_tiles)
+        pieces += [fitted, near, far]
+    whole = pl.BlockSpec(block_shape, lambda s, l, r, n: (0, 0, 0, 0))
+    partial_tiles = pl.pallas_call(
+        _contract_kernel,
+        grid_spec=pltpu.PrefetchScalarGridSpec(
+            num_scalar_prefetch=3,
+            grid=(pair_slots,),
+            in_specs=[whole] * len(pieces),
+            out_specs=pl.BlockSpec((1, block_size, block_size), lambda s, l, r, n: (s, 0, 0)),
+        ),
+        out_shape=jax.ShapeDtypeStruct((pair_slots, block_size, block_size), jnp.float32),
+        compiler_params=pltpu.CompilerParams(
+            dimension_semantics=("arbitrary",), vmem_limit_bytes=48 * 1024 * 1024
+        ),
+    )(left_rel, right_rel, count, *pieces)
 
     summed = lax.psum_scatter(partial_tiles, "aux", scatter_dimension=1, tiled=True)
     norm_factor = (aux_local * lax.axis_size("aux") * orbitals) ** (-0.5)

time: 278 us -> 231 us (0.83); the launches traced: 274 us -> 230 us
  Pallas kernels: 79.5 us -> 32.2 us
  waiting for transfers between devices: 106 us -> 113 us
    pallas_call x4 -> x1, Pallas kernels: 63.2 us -> 15.9 us  [on_device(): pl.pallas_call(_contract_kernel, grid_spec=pltpu.PrefetchScalarGridSpec(n...]
    ppermute x14, waiting for transfers between devices: 61 us -> 65.9 us  [passed_along(): lax.ppermute(value, axis, [(source, source + steps) for source in range(f...]
    ppermute x4, waiting for transfers between devices: 0.01 us -> 3.05 us  [on_device(): relayed = lax.ppermute(near, 'ao', odd_down_one)]
  transfers between devices with their start and end apart: 23 -> 23, of which waited for: 12 -> 14; matrix products, arithmetic and copies ran while one was open for 4% -> 3% of each run, Pallas kernels for 17% -> 0%
where the time goes in v3:
time: 231 us; the launch traced here: 230 us
  waiting for transfers between devices  113 us (49%)
  starting transfers between devices  57 us (25%)
  Pallas kernels  32.2 us (14%)
  between operations  14.4 us (6%)
  other arithmetic  8.59 us (4%)
  local copies, waits for them, and re-layouts  4.84 us (2%)
    ppermute x14, waiting for transfers between devices, passed_along(): lax.ppermute(value, axis, [(source, source + steps) for source in range(f...  65.9 us
    ppermute x14, starting transfers between devices, passed_along(): lax.ppermute(value, axis, [(source, source + steps) for source in range(f...  48.3 us
    reduce_scatter x1, waiting for transfers between devices, on_device(): lax.psum_scatter(partial_tiles, 'aux', scatter_dimension=1, tiled=True)  43.5 us
    pallas_call x1, Pallas kernels, on_device(): pl.pallas_call(_half_kernel, grid_spec=pltpu.PrefetchScalarGridSpec(num_s...  16.4 us
    pallas_call x1, Pallas kernels, on_device(): pl.pallas_call(_contract_kernel, grid_spec=pltpu.PrefetchScalarGridSpec(n...  15.9 us
    ppermute x4, starting transfers between devices, on_device(): relayed = lax.ppermute(near, 'ao', odd_down_one)  5.12 us
  transfers between devices with their start and end apart: 23, of which 14 were waited for; matrix products, arithmetic and copies ran while one was open for 3% of the time, Pallas kernels for 0%

profile of v3, /device:TPU:6, one launch (start us, length us, event | category | flops | bytes accessed | tf_op | source)
XLA Modules:
  0.0 229.6 jit_solution(11718746541698640694)
XLA Ops:
  6.5 11.2 %collective-permute-start.1 = (bf16[4,128,512]{2,1,0:T(8,128)(2,1)}, bf16[4,128,512]{2,1,0:T(8,128)(2,1)S(1)}, u32[]{:S(2)}, u32[]{:S(2)}) collective-permute-start(bf16[4,128,512]{2,1,0:T(8,128)(2,1)} %bitcast.20), channel_id=1, source_target_pairs={{2,0},{3,1},{4,2},{5,3},{6,4},{7,5},{8,6},{9,7},{10,8},{11,9},{12,... | collective-permute-start | bytes 1572872 | tf_op jit(solution)/shard_map/ppermute | solution.py:14
  17.7 1.9 collective-permute-start
  21.1 8.1 %collective-permute-done.1 = bf16[4,128,512]{2,1,0:T(8,128)(2,1)S(1)} collective-permute-done((bf16[4,128,512]{2,1,0:T(8,128)(2,1)}, bf16[4,128,512]{2,1,0:T(8,128)(2,1)S(1)}, u32[]{:S(2)}, u32[]{:S(2)}) %collective-permute-start.1) | collective-permute-done | bytes 524320 | tf_op jit(solution)/shard_map/ppermute | solution.py:14
  29.2 5.6 %collective-permute-done = bf16[4,128,512]{2,1,0:T(8,128)(2,1)S(1)} collective-permute-done((bf16[4,128,512]{2,1,0:T(8,128)(2,1)}, bf16[4,128,512]{2,1,0:T(8,128)(2,1)S(1)}, u32[]{:S(2)}, u32[]{:S(2)}) %collective-permute-start) | collective-permute-done | bytes 524320 | tf_op jit(solution)/shard_map/ppermute | solution.py:14
  36.1 16.4 %shard_map.46 = bf16[4,12,4,128,128]{4,3,2,1,0:T(8,128)(2,1)} custom-call(s32[24]{0:T(128)S(1)} %get-tuple-element.29.left_ref, s32[24]{0:T(128)S(1)} %get-tuple-element.28.right_ref, s32[1]{0:T(128)S(6)} %copy.5.count_ref, bf16[24,4,128,128]{3,2,1,0:T(8,128)(2,1)S(1)} %copy-done, bf16[12,128,512]{2,1,0:T(8,128)(2,1)S(1)} %pad_maximum_fusion.coeff_ref), custom_call_target="tpu_custom_call" | custom-call | tf_op jit(solution)/shard_map/pallas_call | solution.py:113
  52.4 1.3 slice_bitcast_fusion.5
  53.7 1.9 collective-permute-start.2
  55.7 1.9 collective-permute-start.3
  57.6 3.3 %slice_bitcast_fusion = (bf16[12,4,128,128]{3,2,1,0:T(8,128)(2,1)S(1)}, bf16[12,4,128,128]{3,2,1,0:T(8,128)(2,1)S(1)}, bf16[12,4,128,128]{3,2,1,0:T(8,128)(2,1)S(1)}) fusion(bf16[4,12,4,128,128]{4,3,2,1,0:T(8,128)(2,1)} %shard_map.46), kind=kLoop, calls=%fused_computation | loop fusion | bytes 9437184 | tf_op jit(solution)/shard_map/squeeze | solution.py:155
  60.9 10.3 %collective-permute-done.2 = bf16[4,4,128,128]{3,2,1,0:T(8,128)(2,1)S(1)} collective-permute-done((bf16[4,4,128,128]{3,2,1,0:T(8,128)(2,1)S(1)}, bf16[4,4,128,128]{3,2,1,0:T(8,128)(2,1)S(1)}, u32[]{:S(2)}, u32[]{:S(2)}) %collective-permute-start.2) | collective-permute-done | bytes 524320 | tf_op jit(solution)/shard_map/ppermute | solution.py:14
  71.2 1.4 collective-permute-done.3
  73.9 1.9 collective-permute-start.7
  75.8 1.9 collective-permute-start.8
  77.8 14.5 %collective-permute-done.7 = bf16[4,4,128,128]{3,2,1,0:T(8,128)(2,1)S(1)} collective-permute-done((bf16[4,4,128,128]{3,2,1,0:T(8,128)(2,1)S(1)}, bf16[4,4,128,128]{3,2,1,0:T(8,128)(2,1)S(1)}, u32[]{:S(2)}, u32[]{:S(2)}) %collective-permute-start.7) | collective-permute-done | bytes 524320 | tf_op jit(solution)/shard_map/ppermute | solution.py:14
  93.5 1.9 collective-permute-start.12
  95.4 1.9 collective-permute-start.13
  97.3 5.8 %collective-permute-start.4 = (bf16[4,4,128,128]{3,2,1,0:T(8,128)(2,1)S(1)}, bf16[4,4,128,128]{3,2,1,0:T(8,128)(2,1)S(1)}, u32[]{:S(2)}, u32[]{:S(2)}) collective-permute-start(bf16[4,4,128,128]{3,2,1,0:T(8,128)(2,1)S(1)} %fusion.refs_0_), channel_id=1, source_target_pairs={{1,0},{2,1},{3,2},{4,3},{5,4},{6,5},{7,6},{8,7},{9,8},{10,9},{11,1... | collective-permute-start | bytes 1572872 | tf_op jit(solution)/shard_map/ppermute | solution.py:14
  103.1 8.8 %collective-permute-done.12 = bf16[4,4,128,128]{3,2,1,0:T(8,128)(2,1)S(1)} collective-permute-done((bf16[4,4,128,128]{3,2,1,0:T(8,128)(2,1)S(1)}, bf16[4,4,128,128]{3,2,1,0:T(8,128)(2,1)S(1)}, u32[]{:S(2)}, u32[]{:S(2)}) %collective-permute-start.12) | collective-permute-done | bytes 524320 | tf_op jit(solution)/shard_map/ppermute | solution.py:14
  113.0 1.9 collective-permute-start.17
  115.0 1.9 collective-permute-start.18
  117.6 8.7 %collective-permute-start.9 = (bf16[4,4,128,128]{3,2,1,0:T(8,128)(2,1)S(1)}, bf16[4,4,128,128]{3,2,1,0:T(8,128)(2,1)S(1)}, u32[]{:S(2)}, u32[]{:S(2)}) collective-permute-start(bf16[4,4,128,128]{3,2,1,0:T(8,128)(2,1)S(1)} %add_convert_fusion.2.refs_3_), channel_id=1, source_target_pairs={{1,0},{2,1},{3,2},{4,3},{5,4},{6,5},{7,6},{8,7},{9,8},{10,9},{11,1... | collective-permute-start | bytes 1572872 | tf_op jit(solution)/shard_map/ppermute | solution.py:14
  126.3 1.5 collective-permute-start.11
  127.8 3.6 %collective-permute-done.17 = bf16[4,4,128,128]{3,2,1,0:T(8,128)(2,1)S(1)} collective-permute-done((bf16[4,4,128,128]{3,2,1,0:T(8,128)(2,1)S(1)}, bf16[4,4,128,128]{3,2,1,0:T(8,128)(2,1)S(1)}, u32[]{:S(2)}, u32[]{:S(2)}) %collective-permute-start.17) | collective-permute-done | bytes 524320 | tf_op jit(solution)/shard_map/ppermute | solution.py:14
  131.4 1.3 collective-permute-start.5
  132.7 3.5 %collective-permute-start.14 = (bf16[4,4,128,128]{3,2,1,0:T(8,128)(2,1)S(1)}, bf16[4,4,128,128]{3,2,1,0:T(8,128)(2,1)}, u32[]{:S(2)}, u32[]{:S(2)}) collective-permute-start(bf16[4,4,128,128]{3,2,1,0:T(8,128)(2,1)S(1)} %add_convert_fusion.1.refs_6_), channel_id=1, source_target_pairs={{1,0},{2,1},{3,2},{4,3},{5,4},{6,5},{7,6},{8,7},{9,8},{10,9},{11,1... | collective-permute-start | bytes 1572872 | tf_op jit(solution)/shard_map/ppermute | solution.py:14
  136.4 1.9 collective-permute-start.19
  140.6 5.0 %collective-permute-done.14.refs_7_ = bf16[4,4,128,128]{3,2,1,0:T(8,128)(2,1)} collective-permute-done((bf16[4,4,128,128]{3,2,1,0:T(8,128)(2,1)S(1)}, bf16[4,4,128,128]{3,2,1,0:T(8,128)(2,1)}, u32[]{:S(2)}, u32[]{:S(2)}) %collective-permute-start.14) | collective-permute-done | bytes 524320 | tf_op jit(solution)/shard_map/ppermute | solution.py:14
  148.7 6.6 %collective-permute-done.19.refs_10_ = bf16[4,4,128,128]{3,2,1,0:T(8,128)(2,1)} collective-permute-done((bf16[4,4,128,128]{3,2,1,0:T(8,128)(2,1)S(1)}, bf16[4,4,128,128]{3,2,1,0:T(8,128)(2,1)}, u32[]{:S(2)}, u32[]{:S(2)}) %collective-permute-start.19) | collective-permute-done | bytes 524320 | tf_op jit(solution)/shard_map/ppermute | solution.py:14
  157.9 3.0 %collective-permute-done.20 = bf16[4,4,128,128]{3,2,1,0:T(8,128)(2,1)S(1)} collective-permute-done((bf16[4,4,128,128]{3,2,1,0:T(8,128)(2,1)}, bf16[4,4,128,128]{3,2,1,0:T(8,128)(2,1)S(1)}, u32[]{:S(2)}, u32[]{:S(2)}) %collective-permute-start.20) | collective-permute-done | bytes 524320 | tf_op jit(solution)/shard_map/ppermute | solution.py:157
  161.7 15.9 %shard_map.47 = f32[24,128,128]{2,1,0:T(8,128)} custom-call(s32[24]{0:T(128)S(1)} %get-tuple-element.29.left_ref, s32[24]{0:T(128)S(1)} %get-tuple-element.28.right_ref, s32[1]{0:T(128)S(6)} %copy.5.count_ref, bf16[4,4,128,128]{3,2,1,0:T(8,128)(2,1)S(1)} %fusion.refs_0_, bf16[4,4,128,128]{3,2,1,0:T(8,128)(2,1)S(1)} %collective-permute-done.4.refs_1_, ...), custom_call_target="tpu_custom_call" | custom-call | tf_op jit(solution)/shard_map/pallas_call | solution.py:162
  177.7 43.5 %reduce-scatter.2.cloned.1.call-done = f32[24,16,128]{2,1,0:T(8,128)} async-done(((f32[24,128,128]{2,1,0:T(8,128)}), f32[24,16,128]{2,1,0:T(8,128)}) %reduce-scatter.2.cloned.1.call-update) | async-done | bytes 196624 | tf_op jit(solution)/shard_map/reduce_scatter | solution.py:176
  221.2 1.6 multiply_convert_fusion
  (37 shorter events, 15.2 us)
Async XLA Ops:
  6.5 214.6 %reduce-scatter.2.cloned.1.call-start = ((), (), s32[]{:S(2)}) async-start(), calls=%async_computation.1 | async-start | bytes 1769472 | tf_op jit(solution)/shard_map/reduce_scatter | solution.py:176
  6.5 22.7 %collective-permute-start.1 = (bf16[4,128,512]{2,1,0:T(8,128)(2,1)}, bf16[4,128,512]{2,1,0:T(8,128)(2,1)S(1)}, u32[]{:S(2)}, u32[]{:S(2)}) collective-permute-start(bf16[4,128,512]{2,1,0:T(8,128)(2,1)} %bitcast.20), channel_id=1, source_target_pairs={{2,0},{3,1},{4,2},{5,3},{6,4},{7,5},{8,6},{9,7},{10,8},{11,9},{12,... | collective-permute-start | bytes 1572872 | tf_op jit(solution)/shard_map/ppermute | solution.py:14
  17.7 17.1 %collective-permute-start = (bf16[4,128,512]{2,1,0:T(8,128)(2,1)}, bf16[4,128,512]{2,1,0:T(8,128)(2,1)S(1)}, u32[]{:S(2)}, u32[]{:S(2)}) collective-permute-start(bf16[4,128,512]{2,1,0:T(8,128)(2,1)} %bitcast.21), channel_id=1, source_target_pairs={{1,0},{2,1},{3,2},{4,3},{5,4},{6,5},{7,6},{8,7},{9,8},{10,9},{11,1... | collective-permute-start | bytes 1572872 | tf_op jit(solution)/shard_map/ppermute | solution.py:14
  21.1 15.0 %copy-start = (bf16[24,4,128,128]{3,2,1,0:T(8,128)(2,1)S(1)}, bf16[24,4,128,128]{3,2,1,0:T(8,128)(2,1)}, u32[]{:S(2)}) copy-start(bf16[24,4,128,128]{3,2,1,0:T(8,128)(2,1)} %tile_ref.1) | copy-start | bytes 9437188
  53.7 17.4 %collective-permute-start.2 = (bf16[4,4,128,128]{3,2,1,0:T(8,128)(2,1)S(1)}, bf16[4,4,128,128]{3,2,1,0:T(8,128)(2,1)S(1)}, u32[]{:S(2)}, u32[]{:S(2)}) collective-permute-start(bf16[4,4,128,128]{3,2,1,0:T(8,128)(2,1)S(1)} %get-tuple-element.20), channel_id=1, source_target_pairs={{0,2},{1,3},{2,4},{3,5},{4,6},{5,7},{6,8},{7,9},{8,10},{9,11},{10,... | collective-permute-start | bytes 1572872 | tf_op jit(solution)/shard_map/ppermute | solution.py:14
  55.7 16.9 %collective-permute-start.3 = (bf16[4,4,128,128]{3,2,1,0:T(8,128)(2,1)S(1)}, bf16[4,4,128,128]{3,2,1,0:T(8,128)(2,1)S(1)}, u32[]{:S(2)}, u32[]{:S(2)}) collective-permute-start(bf16[4,4,128,128]{3,2,1,0:T(8,128)(2,1)S(1)} %get-tuple-element.21), channel_id=1, source_target_pairs={{0,1},{1,2},{2,3},{3,4},{4,5},{5,6},{6,7},{7,8},{8,9},{9,10},{10,1... | collective-permute-start | bytes 1572872 | tf_op jit(solution)/shard_map/ppermute | solution.py:14
  73.9 18.4 %collective-permute-start.7 = (bf16[4,4,128,128]{3,2,1,0:T(8,128)(2,1)S(1)}, bf16[4,4,128,128]{3,2,1,0:T(8,128)(2,1)S(1)}, u32[]{:S(2)}, u32[]{:S(2)}) collective-permute-start(bf16[4,4,128,128]{3,2,1,0:T(8,128)(2,1)S(1)} %get-tuple-element.26), channel_id=1, source_target_pairs={{0,2},{1,3},{2,4},{3,5},{4,6},{5,7},{6,8},{7,9},{8,10},{9,11},{10,... | collective-permute-start | bytes 1572872 | tf_op jit(solution)/shard_map/ppermute | solution.py:14
  75.8 17.3 %collective-permute-start.8 = (bf16[4,4,128,128]{3,2,1,0:T(8,128)(2,1)S(1)}, bf16[4,4,128,128]{3,2,1,0:T(8,128)(2,1)S(1)}, u32[]{:S(2)}, u32[]{:S(2)}) collective-permute-start(bf16[4,4,128,128]{3,2,1,0:T(8,128)(2,1)S(1)} %get-tuple-element.27), channel_id=1, source_target_pairs={{0,1},{1,2},{2,3},{3,4},{4,5},{5,6},{6,7},{7,8},{8,9},{9,10},{10,1... | collective-permute-start | bytes 1572872 | tf_op jit(solution)/shard_map/ppermute | solution.py:14
  93.5 18.4 %collective-permute-start.12 = (bf16[4,4,128,128]{3,2,1,0:T(8,128)(2,1)S(1)}, bf16[4,4,128,128]{3,2,1,0:T(8,128)(2,1)S(1)}, u32[]{:S(2)}, u32[]{:S(2)}) collective-permute-start(bf16[4,4,128,128]{3,2,1,0:T(8,128)(2,1)S(1)} %get-tuple-element.24), channel_id=1, source_target_pairs={{0,2},{1,3},{2,4},{3,5},{4,6},{5,7},{6,8},{7,9},{8,10},{9,11},{10,... | collective-permute-start | bytes 1572872 | tf_op jit(solution)/shard_map/ppermute | solution.py:14
  95.4 17.3 %collective-permute-start.13 = (bf16[4,4,128,128]{3,2,1,0:T(8,128)(2,1)S(1)}, bf16[4,4,128,128]{3,2,1,0:T(8,128)(2,1)S(1)}, u32[]{:S(2)}, u32[]{:S(2)}) collective-permute-start(bf16[4,4,128,128]{3,2,1,0:T(8,128)(2,1)S(1)} %get-tuple-element.25), channel_id=1, source_target_pairs={{0,1},{1,2},{2,3},{3,4},{4,5},{5,6},{6,7},{7,8},{8,9},{9,10},{10,1... | collective-permute-start | bytes 1572872 | tf_op jit(solution)/shard_map/ppermute | solution.py:14
  97.3 29.0 %collective-permute-start.4 = (bf16[4,4,128,128]{3,2,1,0:T(8,128)(2,1)S(1)}, bf16[4,4,128,128]{3,2,1,0:T(8,128)(2,1)S(1)}, u32[]{:S(2)}, u32[]{:S(2)}) collective-permute-start(bf16[4,4,128,128]{3,2,1,0:T(8,128)(2,1)S(1)} %fusion.refs_0_), channel_id=1, source_target_pairs={{1,0},{2,1},{3,2},{4,3},{5,4},{6,5},{7,6},{8,7},{9,8},{10,9},{11,1... | collective-permute-start | bytes 1572872 | tf_op jit(solution)/shard_map/ppermute | solution.py:14
  113.0 18.4 %collective-permute-start.17 = (bf16[4,4,128,128]{3,2,1,0:T(8,128)(2,1)S(1)}, bf16[4,4,128,128]{3,2,1,0:T(8,128)(2,1)S(1)}, u32[]{:S(2)}, u32[]{:S(2)}) collective-permute-start(bf16[4,4,128,128]{3,2,1,0:T(8,128)(2,1)S(1)} %get-tuple-element.22), channel_id=1, source_target_pairs={{0,2},{1,3},{2,4},{3,5},{4,6},{5,7},{6,8},{7,9},{8,10},{9,11},{10,... | collective-permute-start | bytes 1572872 | tf_op jit(solution)/shard_map/ppermute | solution.py:14
  115.0 17.7 %collective-permute-start.18 = (bf16[4,4,128,128]{3,2,1,0:T(8,128)(2,1)S(1)}, bf16[4,4,128,128]{3,2,1,0:T(8,128)(2,1)S(1)}, u32[]{:S(2)}, u32[]{:S(2)}) collective-permute-start(bf16[4,4,128,128]{3,2,1,0:T(8,128)(2,1)S(1)} %get-tuple-element.23), channel_id=1, source_target_pairs={{0,1},{1,2},{2,3},{3,4},{4,5},{5,6},{6,7},{7,8},{8,9},{9,10},{10,1... | collective-permute-start | bytes 1572872 | tf_op jit(solution)/shard_map/ppermute | solution.py:14
  116.9 19.5 %collective-permute-start.6 = (bf16[4,4,128,128]{3,2,1,0:T(8,128)(2,1)S(1)}, bf16[4,4,128,128]{3,2,1,0:T(8,128)(2,1)S(1)}, u32[]{:S(2)}, u32[]{:S(2)}) collective-permute-start(bf16[4,4,128,128]{3,2,1,0:T(8,128)(2,1)S(1)} %fusion.refs_0_), channel_id=1, source_target_pairs={{3,1},{5,3},{7,5},{9,7},{11,9},{13,11},{15,13},{17,15},{19,17},{21... | collective-permute-start | bytes 1572872 | tf_op jit(solution)/shard_map/ppermute | solution.py:158
  117.6 21.0 %collective-permute-start.9 = (bf16[4,4,128,128]{3,2,1,0:T(8,128)(2,1)S(1)}, bf16[4,4,128,128]{3,2,1,0:T(8,128)(2,1)S(1)}, u32[]{:S(2)}, u32[]{:S(2)}) collective-permute-start(bf16[4,4,128,128]{3,2,1,0:T(8,128)(2,1)S(1)} %add_convert_fusion.2.refs_3_), channel_id=1, source_target_pairs={{1,0},{2,1},{3,2},{4,3},{5,4},{6,5},{7,6},{8,7},{9,8},{10,9},{11,1... | collective-permute-start | bytes 1572872 | tf_op jit(solution)/shard_map/ppermute | solution.py:14
  126.3 21.7 %collective-permute-start.11 = (bf16[4,4,128,128]{3,2,1,0:T(8,128)(2,1)S(1)}, bf16[4,4,128,128]{3,2,1,0:T(8,128)(2,1)}, u32[]{:S(2)}, u32[]{:S(2)}) collective-permute-start(bf16[4,4,128,128]{3,2,1,0:T(8,128)(2,1)S(1)} %add_convert_fusion.2.refs_3_), channel_id=1, source_target_pairs={{3,1},{5,3},{7,5},{9,7},{11,9},{13,11},{15,13},{17,15},{19,17},{21... | collective-permute-start | bytes 1572872 | tf_op jit(solution)/shard_map/ppermute | solution.py:158
  131.4 8.5 %collective-permute-start.5 = (bf16[4,4,128,128]{3,2,1,0:T(8,128)(2,1)S(1)}, bf16[4,4,128,128]{3,2,1,0:T(8,128)(2,1)}, u32[]{:S(2)}, u32[]{:S(2)}) collective-permute-start(bf16[4,4,128,128]{3,2,1,0:T(8,128)(2,1)S(1)} %collective-permute-done.4.refs_1_), channel_id=1, source_target_pairs={{1,0},{3,2},{5,4},{7,6},{9,8},{11,10},{13,12},{15,14},{17,16},{19,... | collective-permute-start | bytes 1572872 | tf_op jit(solution)/shard_map/ppermute | solution.py:157
  132.7 12.9 %collective-permute-start.14 = (bf16[4,4,128,128]{3,2,1,0:T(8,128)(2,1)S(1)}, bf16[4,4,128,128]{3,2,1,0:T(8,128)(2,1)}, u32[]{:S(2)}, u32[]{:S(2)}) collective-permute-start(bf16[4,4,128,128]{3,2,1,0:T(8,128)(2,1)S(1)} %add_convert_fusion.1.refs_6_), channel_id=1, source_target_pairs={{1,0},{2,1},{3,2},{4,3},{5,4},{6,5},{7,6},{8,7},{9,8},{10,9},{11,1... | collective-permute-start | bytes 1572872 | tf_op jit(solution)/shard_map/ppermute | solution.py:14
  136.4 2.2 copy-start.1
  136.4 18.9 %collective-permute-start.19 = (bf16[4,4,128,128]{3,2,1,0:T(8,128)(2,1)S(1)}, bf16[4,4,128,128]{3,2,1,0:T(8,128)(2,1)}, u32[]{:S(2)}, u32[]{:S(2)}) collective-permute-start(bf16[4,4,128,128]{3,2,1,0:T(8,128)(2,1)S(1)} %add_convert_fusion.refs_9_), channel_id=1, source_target_pairs={{1,0},{2,1},{3,2},{4,3},{5,4},{6,5},{7,6},{8,7},{9,8},{10,9},{11,1... | collective-permute-start | bytes 1572872 | tf_op jit(solution)/shard_map/ppermute | solution.py:14
  138.6 18.0 %collective-permute-start.10 = (bf16[4,4,128,128]{3,2,1,0:T(8,128)(2,1)S(1)}, bf16[4,4,128,128]{3,2,1,0:T(8,128)(2,1)}, u32[]{:S(2)}, u32[]{:S(2)}) collective-permute-start(bf16[4,4,128,128]{3,2,1,0:T(8,128)(2,1)S(1)} %collective-permute-done.9.refs_4_), channel_id=1, source_target_pairs={{1,0},{3,2},{5,4},{7,6},{9,8},{11,10},{13,12},{15,14},{17,16},{19,... | collective-permute-start | bytes 1572872 | tf_op jit(solution)/shard_map/ppermute | solution.py:157
  139.9 17.9 %collective-permute-start.16 = (bf16[4,4,128,128]{3,2,1,0:T(8,128)(2,1)S(1)}, bf16[4,4,128,128]{3,2,1,0:T(8,128)(2,1)S(1)}, u32[]{:S(2)}, u32[]{:S(2)}) collective-permute-start(bf16[4,4,128,128]{3,2,1,0:T(8,128)(2,1)S(1)} %add_convert_fusion.1.refs_6_), channel_id=1, source_target_pairs={{3,1},{5,3},{7,5},{9,7},{11,9},{13,11},{15,13},{17,15},{19,17},{21... | collective-permute-start | bytes 1572872 | tf_op jit(solution)/shard_map/ppermute | solution.py:158
  145.6 12.2 %collective-permute-start.15 = (bf16[4,4,128,128]{3,2,1,0:T(8,128)(2,1)}, bf16[4,4,128,128]{3,2,1,0:T(8,128)(2,1)S(1)}, u32[]{:S(2)}, u32[]{:S(2)}) collective-permute-start(bf16[4,4,128,128]{3,2,1,0:T(8,128)(2,1)} %collective-permute-done.14.refs_7_), channel_id=1, source_target_pairs={{1,0},{3,2},{5,4},{7,6},{9,8},{11,10},{13,12},{15,14},{17,16},{19,... | collective-permute-start | bytes 1572872 | tf_op jit(solution)/shard_map/ppermute | solution.py:157
  148.0 9.8 %collective-permute-start.21 = (bf16[4,4,128,128]{3,2,1,0:T(8,128)(2,1)S(1)}, bf16[4,4,128,128]{3,2,1,0:T(8,128)(2,1)S(1)}, u32[]{:S(2)}, u32[]{:S(2)}) collective-permute-start(bf16[4,4,128,128]{3,2,1,0:T(8,128)(2,1)S(1)} %add_convert_fusion.refs_9_), channel_id=1, source_target_pairs={{3,1},{5,3},{7,5},{9,7},{11,9},{13,11},{15,13},{17,15},{19,17},{21... | collective-permute-start | bytes 1572872 | tf_op jit(solution)/shard_map/ppermute | solution.py:158
  155.3 5.5 %collective-permute-start.20 = (bf16[4,4,128,128]{3,2,1,0:T(8,128)(2,1)}, bf16[4,4,128,128]{3,2,1,0:T(8,128)(2,1)S(1)}, u32[]{:S(2)}, u32[]{:S(2)}) collective-permute-start(bf16[4,4,128,128]{3,2,1,0:T(8,128)(2,1)} %collective-permute-done.19.refs_10_), channel_id=1, source_target_pairs={{1,0},{3,2},{5,4},{7,6},{9,8},{11,10},{13,12},{15,14},{17,16},{19,... | collective-permute-start | bytes 1572872 | tf_op jit(solution)/shard_map/ppermute | solution.py:157
Sparse Core Ops, SparseCore 0:
  177.8 43.3 reduce-scatter.1

commit v4 on v3

--- a/solution.py
+++ b/solution.py
@@ -86,7 +86,7 @@
         out_ref[...] = jnp.zeros_like(out_ref)
 
 
-CHUNKS = 4
+CHUNKS = 2
 
 
 def on_device(pair_list, pair_count, tiles, coeff):

time: 231 us -> 229 us (level)
  waiting for transfers between devices: 113 us -> 149 us
  starting transfers between devices: 57 us -> 34.6 us
  Pallas kernels: 32.2 us -> 17.2 us
    ppermute x14 -> x8, waiting for transfers between devices: 65.9 us -> 90.3 us  [passed_along(): lax.ppermute(value, axis, [(source, source + steps) for source in range(f...]
    ppermute x14 -> x8, starting transfers between devices: 48.3 us -> 28.7 us  [passed_along(): lax.ppermute(value, axis, [(source, source + steps) for source in range(f...]
    reduce_scatter x1, waiting for transfers between devices: 43.5 us -> 56 us  [on_device(): lax.psum_scatter(partial_tiles, 'aux', scatter_dimension=1, tiled=True)]
    pallas_call x1, Pallas kernels: 16.4 us -> 6.89 us  [on_device(): pl.pallas_call(_half_kernel, grid_spec=pltpu.PrefetchScalarGridSpec(num_s...]
    pallas_call x1, Pallas kernels: 15.9 us -> 10.3 us  [on_device(): pl.pallas_call(_contract_kernel, grid_spec=pltpu.PrefetchScalarGridSpec(n...]
    ppermute x4 -> x2, starting transfers between devices: 5.12 us -> 2.56 us  [on_device(): relayed = lax.ppermute(near, 'ao', odd_down_one)]
  transfers between devices with their start and end apart: 23 -> 13, of which waited for: 14 -> 9; matrix products, arithmetic and copies ran while one was open for 3% -> 2% of each run, Pallas kernels for 0% -> 0%
where the time goes in v4:
time: 229 us; the launch traced here: 228 us
  waiting for transfers between devices  149 us (65%)
  starting transfers between devices  34.6 us (15%)
  Pallas kernels  17.2 us (8%)
  between operations  14.2 us (6%)
  other arithmetic  9.77 us (4%)
  local copies, waits for them, and re-layouts  4.12 us (2%)
    ppermute x8, waiting for transfers between devices, passed_along(): lax.ppermute(value, axis, [(source, source + steps) for source in range(f...  90.3 us
    reduce_scatter x1, waiting for transfers between devices, on_device(): lax.psum_scatter(partial_tiles, 'aux', scatter_dimension=1, tiled=True)  56 us
    ppermute x8, starting transfers between devices, passed_along(): lax.ppermute(value, axis, [(source, source + steps) for source in range(f...  28.7 us
    pallas_call x1, Pallas kernels, on_device(): pl.pallas_call(_contract_kernel, grid_spec=pltpu.PrefetchScalarGridSpec(n...  10.3 us
    pallas_call x1, Pallas kernels, on_device(): pl.pallas_call(_half_kernel, grid_spec=pltpu.PrefetchScalarGridSpec(num_s...  6.89 us
  transfers between devices with their start and end apart: 13, of which 9 were waited for; matrix products, arithmetic and copies ran while one was open for 2% of the time, Pallas kernels for 0%

profile of v4, /device:TPU:6, one launch (start us, length us, event | category | flops | bytes accessed | tf_op | source)
XLA Modules:
  0.0 228.5 jit_solution(1240462800643390457)
XLA Ops:
  6.5 11.5 %collective-permute-start.1 = (bf16[4,128,512]{2,1,0:T(8,128)(2,1)}, bf16[4,128,512]{2,1,0:T(8,128)(2,1)}, u32[]{:S(2)}, u32[]{:S(2)}) collective-permute-start(bf16[4,128,512]{2,1,0:T(8,128)(2,1)} %bitcast.16), channel_id=1, source_target_pairs={{2,0},{3,1},{4,2},{5,3},{6,4},{7,5},{8,6},{9,7},{10,8},{11,9},{12,... | collective-permute-start | bytes 1572872 | tf_op jit(solution)/shard_map/ppermute | solution.py:14
  18.0 1.9 collective-permute-start
  20.6 0.8 subtract_bitcast_fusion
  21.4 8.1 %collective-permute-done.1 = bf16[4,128,512]{2,1,0:T(8,128)(2,1)} collective-permute-done((bf16[4,128,512]{2,1,0:T(8,128)(2,1)}, bf16[4,128,512]{2,1,0:T(8,128)(2,1)}, u32[]{:S(2)}, u32[]{:S(2)}) %collective-permute-start.1) | collective-permute-done | bytes 524320 | tf_op jit(solution)/shard_map/ppermute | solution.py:14
  29.5 5.6 %collective-permute-done = bf16[4,128,512]{2,1,0:T(8,128)(2,1)} collective-permute-done((bf16[4,128,512]{2,1,0:T(8,128)(2,1)}, bf16[4,128,512]{2,1,0:T(8,128)(2,1)}, u32[]{:S(2)}, u32[]{:S(2)}) %collective-permute-start) | collective-permute-done | bytes 524320 | tf_op jit(solution)/shard_map/ppermute | solution.py:14
  35.1 1.5 pad_maximum_fusion.coeff_ref
  36.6 6.9 %shard_map.46 = bf16[2,12,4,128,256]{4,3,2,1,0:T(8,128)(2,1)} custom-call(s32[24]{0:T(128)S(1)} %get-tuple-element.14.left_ref, s32[24]{0:T(128)S(1)} %get-tuple-element.13.right_ref, s32[1]{0:T(128)S(6)} %copy.5.count_ref, bf16[24,4,128,128]{3,2,1,0:T(8,128)(2,1)S(1)} %copy-done, bf16[12,128,512]{2,1,0:T(8,128)(2,1)S(1)} %pad_maximum_fusion.coeff_ref), custom_call_target="tpu_custom_call" | custom-call | tf_op jit(solution)/shard_map/pallas_call | solution.py:113
  43.5 1.7 slice_bitcast_fusion.3
  45.3 1.9 collective-permute-start.2
  47.2 1.9 collective-permute-start.3
  49.2 2.2 slice_bitcast_fusion
  51.4 23.1 %collective-permute-done.2 = bf16[4,4,128,256]{3,2,1,0:T(8,128)(2,1)S(1)} collective-permute-done((bf16[4,4,128,256]{3,2,1,0:T(8,128)(2,1)S(1)}, bf16[4,4,128,256]{3,2,1,0:T(8,128)(2,1)S(1)}, u32[]{:S(2)}, u32[]{:S(2)}) %collective-permute-start.2) | collective-permute-done | bytes 1048608 | tf_op jit(solution)/shard_map/ppermute | solution.py:14
  74.5 12.1 %collective-permute-done.3 = bf16[4,4,128,256]{3,2,1,0:T(8,128)(2,1)S(1)} collective-permute-done((bf16[4,4,128,256]{3,2,1,0:T(8,128)(2,1)S(1)}, bf16[4,4,128,256]{3,2,1,0:T(8,128)(2,1)S(1)}, u32[]{:S(2)}, u32[]{:S(2)}) %collective-permute-start.3) | collective-permute-done | bytes 1048608 | tf_op jit(solution)/shard_map/ppermute | solution.py:14
  86.6 1.7 fusion.refs_0_
  88.5 1.9 collective-permute-start.7
  90.4 1.9 collective-permute-start.8
  92.3 5.8 %collective-permute-start.4 = (bf16[4,4,128,256]{3,2,1,0:T(8,128)(2,1)S(1)}, bf16[4,4,128,256]{3,2,1,0:T(8,128)(2,1)S(1)}, u32[]{:S(2)}, u32[]{:S(2)}) collective-permute-start(bf16[4,4,128,256]{3,2,1,0:T(8,128)(2,1)S(1)} %fusion.refs_0_), channel_id=1, source_target_pairs={{1,0},{2,1},{3,2},{4,3},{5,4},{6,5},{7,6},{8,7},{9,8},{10,9},{11,1... | collective-permute-start | bytes 3145736 | tf_op jit(solution)/shard_map/ppermute | solution.py:14
  98.1 20.4 %collective-permute-done.7 = bf16[4,4,128,256]{3,2,1,0:T(8,128)(2,1)S(1)} collective-permute-done((bf16[4,4,128,256]{3,2,1,0:T(8,128)(2,1)S(1)}, bf16[4,4,128,256]{3,2,1,0:T(8,128)(2,1)S(1)}, u32[]{:S(2)}, u32[]{:S(2)}) %collective-permute-start.7) | collective-permute-done | bytes 1048608 | tf_op jit(solution)/shard_map/ppermute | solution.py:14
  118.5 6.1 %collective-permute-done.8 = bf16[4,4,128,256]{3,2,1,0:T(8,128)(2,1)S(1)} collective-permute-done((bf16[4,4,128,256]{3,2,1,0:T(8,128)(2,1)S(1)}, bf16[4,4,128,256]{3,2,1,0:T(8,128)(2,1)S(1)}, u32[]{:S(2)}, u32[]{:S(2)}) %collective-permute-start.8) | collective-permute-done | bytes 1048608 | tf_op jit(solution)/shard_map/ppermute | solution.py:14
  124.6 0.5 add_convert_fusion.refs_3_
  125.1 1.9 collective-permute-start.9
  127.0 1.7 collective-permute-start.6
  128.7 1.3 collective-permute-start.5
  130.0 1.6 collective-permute-start.11
  131.6 14.9 %collective-permute-done.9.refs_4_ = bf16[4,4,128,256]{3,2,1,0:T(8,128)(2,1)} collective-permute-done((bf16[4,4,128,256]{3,2,1,0:T(8,128)(2,1)S(1)}, bf16[4,4,128,256]{3,2,1,0:T(8,128)(2,1)}, u32[]{:S(2)}, u32[]{:S(2)}) %collective-permute-start.9) | collective-permute-done | bytes 1048608 | tf_op jit(solution)/shard_map/ppermute | solution.py:14
  146.5 1.3 collective-permute-start.10
  147.8 1.3 broadcast_select_fusion.1.refs_2_
  149.2 2.2 collective-permute-done.10
  151.4 2.3 %broadcast_select_fusion.refs_5_ = bf16[4,4,128,256]{3,2,1,0:T(8,128)(2,1)} fusion(bf16[4,4,128,256]{3,2,1,0:T(8,128)(2,1)} %collective-permute-done.10, bf16[4,4,128,256]{3,2,1,0:T(8,128)(2,1)} %collective-permute-done.11, pred[]{:T(512)S(6)} %eq.5), kind=kLoop, calls=%fused_computation.8 | loop fusion | flops 524288 | bytes 3145729 | tf_op jit(solution)/shard_map/jit(_where)/select_n | solution.py:159
  153.7 10.3 %shard_map.47 = f32[24,128,128]{2,1,0:T(8,128)} custom-call(s32[24]{0:T(128)S(1)} %get-tuple-element.14.left_ref, s32[24]{0:T(128)S(1)} %get-tuple-element.13.right_ref, s32[1]{0:T(128)S(6)} %copy.5.count_ref, bf16[4,4,128,256]{3,2,1,0:T(8,128)(2,1)S(1)} %fusion.refs_0_, bf16[4,4,128,256]{3,2,1,0:T(8,128)(2,1)S(1)} %collective-permute-done.4.refs_1_, ...), custom_call_target="tpu_custom_call" | custom-call | tf_op jit(solution)/shard_map/pallas_call | solution.py:162
  164.0 56.0 %reduce-scatter.2.cloned.1.call-done = f32[24,16,128]{2,1,0:T(8,128)} async-done(((f32[24,128,128]{2,1,0:T(8,128)}), f32[24,16,128]{2,1,0:T(8,128)}) %reduce-scatter.2.cloned.1.call-update) | async-done | bytes 196624 | tf_op jit(solution)/shard_map/reduce_scatter | solution.py:176
  220.0 1.6 multiply_convert_fusion
  (9 shorter events, 0.2 us)
Async XLA Ops:
  6.5 30.1 %copy-start = (bf16[24,4,128,128]{3,2,1,0:T(8,128)(2,1)S(1)}, bf16[24,4,128,128]{3,2,1,0:T(8,128)(2,1)}, u32[]{:S(2)}) copy-start(bf16[24,4,128,128]{3,2,1,0:T(8,128)(2,1)} %tile_ref.1) | copy-start | bytes 9437188
  6.5 213.5 %reduce-scatter.2.cloned.1.call-start = ((), (), s32[]{:S(2)}) async-start(), calls=%async_computation.1 | async-start | bytes 1769472 | tf_op jit(solution)/shard_map/reduce_scatter | solution.py:176
  6.5 23.0 %collective-permute-start.1 = (bf16[4,128,512]{2,1,0:T(8,128)(2,1)}, bf16[4,128,512]{2,1,0:T(8,128)(2,1)}, u32[]{:S(2)}, u32[]{:S(2)}) collective-permute-start(bf16[4,128,512]{2,1,0:T(8,128)(2,1)} %bitcast.16), channel_id=1, source_target_pairs={{2,0},{3,1},{4,2},{5,3},{6,4},{7,5},{8,6},{9,7},{10,8},{11,9},{12,... | collective-permute-start | bytes 1572872 | tf_op jit(solution)/shard_map/ppermute | solution.py:14
  18.0 17.1 %collective-permute-start = (bf16[4,128,512]{2,1,0:T(8,128)(2,1)}, bf16[4,128,512]{2,1,0:T(8,128)(2,1)}, u32[]{:S(2)}, u32[]{:S(2)}) collective-permute-start(bf16[4,128,512]{2,1,0:T(8,128)(2,1)} %bitcast.17), channel_id=1, source_target_pairs={{1,0},{2,1},{3,2},{4,3},{5,4},{6,5},{7,6},{8,7},{9,8},{10,9},{11,1... | collective-permute-start | bytes 1572872 | tf_op jit(solution)/shard_map/ppermute | solution.py:14
  45.3 29.2 %collective-permute-start.2 = (bf16[4,4,128,256]{3,2,1,0:T(8,128)(2,1)S(1)}, bf16[4,4,128,256]{3,2,1,0:T(8,128)(2,1)S(1)}, u32[]{:S(2)}, u32[]{:S(2)}) collective-permute-start(bf16[4,4,128,256]{3,2,1,0:T(8,128)(2,1)S(1)} %get-tuple-element.9), channel_id=1, source_target_pairs={{0,2},{1,3},{2,4},{3,5},{4,6},{5,7},{6,8},{7,9},{8,10},{9,11},{10,... | collective-permute-start | bytes 3145736 | tf_op jit(solution)/shard_map/ppermute | solution.py:14
  47.2 39.3 %collective-permute-start.3 = (bf16[4,4,128,256]{3,2,1,0:T(8,128)(2,1)S(1)}, bf16[4,4,128,256]{3,2,1,0:T(8,128)(2,1)S(1)}, u32[]{:S(2)}, u32[]{:S(2)}) collective-permute-start(bf16[4,4,128,256]{3,2,1,0:T(8,128)(2,1)S(1)} %get-tuple-element.10), channel_id=1, source_target_pairs={{0,1},{1,2},{2,3},{3,4},{4,5},{5,6},{6,7},{7,8},{8,9},{9,10},{10,1... | collective-permute-start | bytes 3145736 | tf_op jit(solution)/shard_map/ppermute | solution.py:14
  88.5 30.0 %collective-permute-start.7 = (bf16[4,4,128,256]{3,2,1,0:T(8,128)(2,1)S(1)}, bf16[4,4,128,256]{3,2,1,0:T(8,128)(2,1)S(1)}, u32[]{:S(2)}, u32[]{:S(2)}) collective-permute-start(bf16[4,4,128,256]{3,2,1,0:T(8,128)(2,1)S(1)} %get-tuple-element.11), channel_id=1, source_target_pairs={{0,2},{1,3},{2,4},{3,5},{4,6},{5,7},{6,8},{7,9},{8,10},{9,11},{10,... | collective-permute-start | bytes 3145736 | tf_op jit(solution)/shard_map/ppermute | solution.py:14
  90.4 34.2 %collective-permute-start.8 = (bf16[4,4,128,256]{3,2,1,0:T(8,128)(2,1)S(1)}, bf16[4,4,128,256]{3,2,1,0:T(8,128)(2,1)S(1)}, u32[]{:S(2)}, u32[]{:S(2)}) collective-permute-start(bf16[4,4,128,256]{3,2,1,0:T(8,128)(2,1)S(1)} %get-tuple-element.12), channel_id=1, source_target_pairs={{0,1},{1,2},{2,3},{3,4},{4,5},{5,6},{6,7},{7,8},{8,9},{9,10},{10,1... | collective-permute-start | bytes 3145736 | tf_op jit(solution)/shard_map/ppermute | solution.py:14
  92.3 36.4 %collective-permute-start.4 = (bf16[4,4,128,256]{3,2,1,0:T(8,128)(2,1)S(1)}, bf16[4,4,128,256]{3,2,1,0:T(8,128)(2,1)S(1)}, u32[]{:S(2)}, u32[]{:S(2)}) collective-permute-start(bf16[4,4,128,256]{3,2,1,0:T(8,128)(2,1)S(1)} %fusion.refs_0_), channel_id=1, source_target_pairs={{1,0},{2,1},{3,2},{4,3},{5,4},{6,5},{7,6},{8,7},{9,8},{10,9},{11,1... | collective-permute-start | bytes 3145736 | tf_op jit(solution)/shard_map/ppermute | solution.py:14
  125.1 21.4 %collective-permute-start.9 = (bf16[4,4,128,256]{3,2,1,0:T(8,128)(2,1)S(1)}, bf16[4,4,128,256]{3,2,1,0:T(8,128)(2,1)}, u32[]{:S(2)}, u32[]{:S(2)}) collective-permute-start(bf16[4,4,128,256]{3,2,1,0:T(8,128)(2,1)S(1)} %add_convert_fusion.refs_3_), channel_id=1, source_target_pairs={{1,0},{2,1},{3,2},{4,3},{5,4},{6,5},{7,6},{8,7},{9,8},{10,9},{11,1... | collective-permute-start | bytes 3145736 | tf_op jit(solution)/shard_map/ppermute | solution.py:14
  127.0 20.8 %collective-permute-start.6 = (bf16[4,4,128,256]{3,2,1,0:T(8,128)(2,1)S(1)}, bf16[4,4,128,256]{3,2,1,0:T(8,128)(2,1)}, u32[]{:S(2)}, u32[]{:S(2)}) collective-permute-start(bf16[4,4,128,256]{3,2,1,0:T(8,128)(2,1)S(1)} %fusion.refs_0_), channel_id=1, source_target_pairs={{3,1},{5,3},{7,5},{9,7},{11,9},{13,11},{15,13},{17,15},{19,17},{21... | collective-permute-start | bytes 3145736 | tf_op jit(solution)/shard_map/ppermute | solution.py:158
  128.7 19.1 %collective-permute-start.5 = (bf16[4,4,128,256]{3,2,1,0:T(8,128)(2,1)S(1)}, bf16[4,4,128,256]{3,2,1,0:T(8,128)(2,1)}, u32[]{:S(2)}, u32[]{:S(2)}) collective-permute-start(bf16[4,4,128,256]{3,2,1,0:T(8,128)(2,1)S(1)} %collective-permute-done.4.refs_1_), channel_id=1, source_target_pairs={{1,0},{3,2},{5,4},{7,6},{9,8},{11,10},{13,12},{15,14},{17,16},{19,... | collective-permute-start | bytes 3145736 | tf_op jit(solution)/shard_map/ppermute | solution.py:157
  130.0 19.2 %collective-permute-start.11 = (bf16[4,4,128,256]{3,2,1,0:T(8,128)(2,1)S(1)}, bf16[4,4,128,256]{3,2,1,0:T(8,128)(2,1)}, u32[]{:S(2)}, u32[]{:S(2)}) collective-permute-start(bf16[4,4,128,256]{3,2,1,0:T(8,128)(2,1)S(1)} %add_convert_fusion.refs_3_), channel_id=1, source_target_pairs={{3,1},{5,3},{7,5},{9,7},{11,9},{13,11},{15,13},{17,15},{19,17},{21... | collective-permute-start | bytes 3145736 | tf_op jit(solution)/shard_map/ppermute | solution.py:158
  146.5 4.9 %collective-permute-start.10 = (bf16[4,4,128,256]{3,2,1,0:T(8,128)(2,1)}, bf16[4,4,128,256]{3,2,1,0:T(8,128)(2,1)}, u32[]{:S(2)}, u32[]{:S(2)}) collective-permute-start(bf16[4,4,128,256]{3,2,1,0:T(8,128)(2,1)} %collective-permute-done.9.refs_4_), channel_id=1, source_target_pairs={{1,0},{3,2},{5,4},{7,6},{9,8},{11,10},{13,12},{15,14},{17,16},{19,... | collective-permute-start | bytes 3145736 | tf_op jit(solution)/shard_map/ppermute | solution.py:157
Sparse Core Ops, SparseCore 0:
  164.2 55.8 reduce-scatter.1

commit v5 on v4

--- a/solution.py
+++ b/solution.py
@@ -173,9 +173,11 @@
         ),
     )(left_rel, right_rel, count, *pieces)
 
-    summed = lax.psum_scatter(partial_tiles, "aux", scatter_dimension=1, tiled=True)
+    summed = lax.psum_scatter(
+        partial_tiles.astype(jnp.bfloat16), "aux", scatter_dimension=1, tiled=True
+    )
     norm_factor = (aux_local * lax.axis_size("aux") * orbitals) ** (-0.5)
-    return (summed * norm_factor).astype(jnp.bfloat16)
+    return (summed.astype(jnp.float32) * norm_factor).astype(jnp.bfloat16)
 
 
 def solution(mesh):

time: 229 us -> 236 us (1.031)
  Pallas kernels: 17.2 us -> 22.5 us
  waiting for transfers between devices: 149 us -> 146 us
  other arithmetic: 9.77 us -> 12.2 us
    pallas_call x1, Pallas kernels: 6.89 us -> 10.6 us  [on_device(): pl.pallas_call(_half_kernel, grid_spec=pltpu.PrefetchScalarGridSpec(num_s...]
    reduce_scatter x1, waiting for transfers between devices: 56 us -> 52.6 us  [on_device(): lax.psum_scatter(partial_tiles.astype(jnp.bfloat16), 'aux', scatter_dimen...]
    convert_element_type x1 -> x2, other arithmetic: 1.58 us -> 4 us  [the longest x1 2.45 us: on_device(): partial_tiles.astype(jnp.bfloat16)]
where the time goes in v5:
time: 236 us; the launch traced here: 235 us
  waiting for transfers between devices  146 us (62%)
  starting transfers between devices  36.1 us (15%)
  Pallas kernels  22.5 us (10%)
  between operations  14.2 us (6%)
  other arithmetic  12.2 us (5%)
  local copies, waits for them, and re-layouts  4.12 us (2%)
    ppermute x8, waiting for transfers between devices, passed_along(): lax.ppermute(value, axis, [(source, source + steps) for source in range(f...  90.8 us
    reduce_scatter x1, waiting for transfers between devices, on_device(): lax.psum_scatter(partial_tiles.astype(jnp.bfloat16), 'aux', scatter_dimen...  52.6 us
    ppermute x8, starting transfers between devices, passed_along(): lax.ppermute(value, axis, [(source, source + steps) for source in range(f...  30.2 us
    pallas_call x1, Pallas kernels, on_device(): pl.pallas_call(_contract_kernel, grid_spec=pltpu.PrefetchScalarGridSpec(n...  11.9 us
    pallas_call x1, Pallas kernels, on_device(): pl.pallas_call(_half_kernel, grid_spec=pltpu.PrefetchScalarGridSpec(num_s...  10.6 us
  transfers between devices with their start and end apart: 13, of which 9 were waited for; matrix products, arithmetic and copies ran while one was open for 2% of the time, Pallas kernels for 0%

profile of v5, /device:TPU:6, one launch (start us, length us, event | category | flops | bytes accessed | tf_op | source)
XLA Modules:
  0.0 234.8 jit_solution(9653199081214988247)
XLA Ops:
  6.5 11.5 %collective-permute-start.1 = (bf16[4,128,512]{2,1,0:T(8,128)(2,1)}, bf16[4,128,512]{2,1,0:T(8,128)(2,1)}, u32[]{:S(2)}, u32[]{:S(2)}) collective-permute-start(bf16[4,128,512]{2,1,0:T(8,128)(2,1)} %bitcast.16), channel_id=1, source_target_pairs={{2,0},{3,1},{4,2},{5,3},{6,4},{7,5},{8,6},{9,7},{10,8},{11,9},{12,... | collective-permute-start | bytes 1572872 | tf_op jit(solution)/shard_map/ppermute | solution.py:14
  18.0 1.9 collective-permute-start
  20.6 0.8 subtract_bitcast_fusion
  21.4 8.1 %collective-permute-done.1 = bf16[4,128,512]{2,1,0:T(8,128)(2,1)} collective-permute-done((bf16[4,128,512]{2,1,0:T(8,128)(2,1)}, bf16[4,128,512]{2,1,0:T(8,128)(2,1)}, u32[]{:S(2)}, u32[]{:S(2)}) %collective-permute-start.1) | collective-permute-done | bytes 524320 | tf_op jit(solution)/shard_map/ppermute | solution.py:14
  29.5 5.6 %collective-permute-done = bf16[4,128,512]{2,1,0:T(8,128)(2,1)} collective-permute-done((bf16[4,128,512]{2,1,0:T(8,128)(2,1)}, bf16[4,128,512]{2,1,0:T(8,128)(2,1)}, u32[]{:S(2)}, u32[]{:S(2)}) %collective-permute-start) | collective-permute-done | bytes 524320 | tf_op jit(solution)/shard_map/ppermute | solution.py:14
  35.1 1.5 pad_maximum_fusion.coeff_ref
  36.6 10.6 %shard_map.46 = bf16[2,12,4,128,256]{4,3,2,1,0:T(8,128)(2,1)} custom-call(s32[24]{0:T(128)S(1)} %get-tuple-element.14.left_ref, s32[24]{0:T(128)S(1)} %get-tuple-element.13.right_ref, s32[1]{0:T(128)S(6)} %copy.5.count_ref, bf16[24,4,128,128]{3,2,1,0:T(8,128)(2,1)S(1)} %copy-done, bf16[12,128,512]{2,1,0:T(8,128)(2,1)S(1)} %pad_maximum_fusion.coeff_ref), custom_call_target="tpu_custom_call" | custom-call | tf_op jit(solution)/shard_map/pallas_call | solution.py:113
  47.3 1.7 slice_bitcast_fusion.3
  49.0 1.9 collective-permute-start.2
  51.0 2.6 %collective-permute-start.3 = (bf16[4,4,128,256]{3,2,1,0:T(8,128)(2,1)S(1)}, bf16[4,4,128,256]{3,2,1,0:T(8,128)(2,1)S(1)}, u32[]{:S(2)}, u32[]{:S(2)}) collective-permute-start(bf16[4,4,128,256]{3,2,1,0:T(8,128)(2,1)S(1)} %get-tuple-element.10), channel_id=1, source_target_pairs={{0,1},{1,2},{2,3},{3,4},{4,5},{5,6},{6,7},{7,8},{8,9},{9,10},{10,1... | collective-permute-start | bytes 3145736 | tf_op jit(solution)/shard_map/ppermute | solution.py:14
  53.6 2.2 slice_bitcast_fusion
  55.8 23.2 %collective-permute-done.2 = bf16[4,4,128,256]{3,2,1,0:T(8,128)(2,1)S(1)} collective-permute-done((bf16[4,4,128,256]{3,2,1,0:T(8,128)(2,1)S(1)}, bf16[4,4,128,256]{3,2,1,0:T(8,128)(2,1)S(1)}, u32[]{:S(2)}, u32[]{:S(2)}) %collective-permute-start.2) | collective-permute-done | bytes 1048608 | tf_op jit(solution)/shard_map/ppermute | solution.py:14
  79.1 8.3 %collective-permute-done.3 = bf16[4,4,128,256]{3,2,1,0:T(8,128)(2,1)S(1)} collective-permute-done((bf16[4,4,128,256]{3,2,1,0:T(8,128)(2,1)S(1)}, bf16[4,4,128,256]{3,2,1,0:T(8,128)(2,1)S(1)}, u32[]{:S(2)}, u32[]{:S(2)}) %collective-permute-start.3) | collective-permute-done | bytes 1048608 | tf_op jit(solution)/shard_map/ppermute | solution.py:14
  87.4 1.7 fusion.refs_0_
  89.3 2.7 %collective-permute-start.7 = (bf16[4,4,128,256]{3,2,1,0:T(8,128)(2,1)S(1)}, bf16[4,4,128,256]{3,2,1,0:T(8,128)(2,1)S(1)}, u32[]{:S(2)}, u32[]{:S(2)}) collective-permute-start(bf16[4,4,128,256]{3,2,1,0:T(8,128)(2,1)S(1)} %get-tuple-element.11), channel_id=1, source_target_pairs={{0,2},{1,3},{2,4},{3,5},{4,6},{5,7},{6,8},{7,9},{8,10},{9,11},{10,... | collective-permute-start | bytes 3145736 | tf_op jit(solution)/shard_map/ppermute | solution.py:14
  92.0 1.9 collective-permute-start.8
  94.0 5.8 %collective-permute-start.4 = (bf16[4,4,128,256]{3,2,1,0:T(8,128)(2,1)S(1)}, bf16[4,4,128,256]{3,2,1,0:T(8,128)(2,1)S(1)}, u32[]{:S(2)}, u32[]{:S(2)}) collective-permute-start(bf16[4,4,128,256]{3,2,1,0:T(8,128)(2,1)S(1)} %fusion.refs_0_), channel_id=1, source_target_pairs={{1,0},{2,1},{3,2},{4,3},{5,4},{6,5},{7,6},{8,7},{9,8},{10,9},{11,1... | collective-permute-start | bytes 3145736 | tf_op jit(solution)/shard_map/ppermute | solution.py:14
  99.7 19.6 %collective-permute-done.7 = bf16[4,4,128,256]{3,2,1,0:T(8,128)(2,1)S(1)} collective-permute-done((bf16[4,4,128,256]{3,2,1,0:T(8,128)(2,1)S(1)}, bf16[4,4,128,256]{3,2,1,0:T(8,128)(2,1)S(1)}, u32[]{:S(2)}, u32[]{:S(2)}) %collective-permute-start.7) | collective-permute-done | bytes 1048608 | tf_op jit(solution)/shard_map/ppermute | solution.py:14
  119.3 8.7 %collective-permute-done.8 = bf16[4,4,128,256]{3,2,1,0:T(8,128)(2,1)S(1)} collective-permute-done((bf16[4,4,128,256]{3,2,1,0:T(8,128)(2,1)S(1)}, bf16[4,4,128,256]{3,2,1,0:T(8,128)(2,1)S(1)}, u32[]{:S(2)}, u32[]{:S(2)}) %collective-permute-start.8) | collective-permute-done | bytes 1048608 | tf_op jit(solution)/shard_map/ppermute | solution.py:14
  128.6 1.9 collective-permute-start.9
  130.5 1.7 collective-permute-start.6
  132.2 1.3 collective-permute-start.5
  133.4 1.6 collective-permute-start.11
  135.1 17.2 %collective-permute-done.9.refs_4_ = bf16[4,4,128,256]{3,2,1,0:T(8,128)(2,1)} collective-permute-done((bf16[4,4,128,256]{3,2,1,0:T(8,128)(2,1)S(1)}, bf16[4,4,128,256]{3,2,1,0:T(8,128)(2,1)}, u32[]{:S(2)}, u32[]{:S(2)}) %collective-permute-start.9) | collective-permute-done | bytes 1048608 | tf_op jit(solution)/shard_map/ppermute | solution.py:14
  152.3 1.3 collective-permute-start.10
  153.6 1.3 broadcast_select_fusion.1.refs_2_
  155.0 2.2 collective-permute-done.10
  157.2 2.3 broadcast_select_fusion.refs_5_
  159.5 11.9 %shard_map.47 = f32[24,128,128]{2,1,0:T(8,128)} custom-call(s32[24]{0:T(128)S(1)} %get-tuple-element.14.left_ref, s32[24]{0:T(128)S(1)} %get-tuple-element.13.right_ref, s32[1]{0:T(128)S(6)} %copy.5.count_ref, bf16[4,4,128,256]{3,2,1,0:T(8,128)(2,1)S(1)} %fusion.refs_0_, bf16[4,4,128,256]{3,2,1,0:T(8,128)(2,1)S(1)} %collective-permute-done.4.refs_1_, ...), custom_call_target="tpu_custom_call" | custom-call | tf_op jit(solution)/shard_map/pallas_call | solution.py:162
  171.3 2.4 %convert_element_type.45 = bf16[24,128,128]{2,1,0:T(8,128)(2,1)} convert(f32[24,128,128]{2,1,0:T(8,128)} %shard_map.47) | non-fusion elementwise | flops 393216 | bytes 2359296 | tf_op jit(solution)/shard_map/convert_element_type | solution.py:177
  173.8 52.6 %reduce-scatter.2.cloned.1.call-done = bf16[24,16,128]{2,1,0:T(8,128)(2,1)} async-done(((bf16[24,128,128]{2,1,0:T(8,128)(2,1)}), bf16[24,16,128]{2,1,0:T(8,128)(2,1)}) %reduce-scatter.2.cloned.1.call-update) | async-done | bytes 98320 | tf_op jit(solution)/shard_map/reduce_scatter | solution.py:176
  226.4 1.6 multiply_convert_fusion
  (10 shorter events, 0.7 us)
Async XLA Ops:
  6.5 30.1 %copy-start = (bf16[24,4,128,128]{3,2,1,0:T(8,128)(2,1)S(1)}, bf16[24,4,128,128]{3,2,1,0:T(8,128)(2,1)}, u32[]{:S(2)}) copy-start(bf16[24,4,128,128]{3,2,1,0:T(8,128)(2,1)} %tile_ref.1) | copy-start | bytes 9437188
  6.5 219.9 %reduce-scatter.2.cloned.1.call-start = ((), (), s32[]{:S(2)}) async-start(), calls=%async_computation.1 | async-start | bytes 884736 | tf_op jit(solution)/shard_map/reduce_scatter | solution.py:176
  6.5 23.0 %collective-permute-start.1 = (bf16[4,128,512]{2,1,0:T(8,128)(2,1)}, bf16[4,128,512]{2,1,0:T(8,128)(2,1)}, u32[]{:S(2)}, u32[]{:S(2)}) collective-permute-start(bf16[4,128,512]{2,1,0:T(8,128)(2,1)} %bitcast.16), channel_id=1, source_target_pairs={{2,0},{3,1},{4,2},{5,3},{6,4},{7,5},{8,6},{9,7},{10,8},{11,9},{12,... | collective-permute-start | bytes 1572872 | tf_op jit(solution)/shard_map/ppermute | solution.py:14
  18.0 17.1 %collective-permute-start = (bf16[4,128,512]{2,1,0:T(8,128)(2,1)}, bf16[4,128,512]{2,1,0:T(8,128)(2,1)}, u32[]{:S(2)}, u32[]{:S(2)}) collective-permute-start(bf16[4,128,512]{2,1,0:T(8,128)(2,1)} %bitcast.17), channel_id=1, source_target_pairs={{1,0},{2,1},{3,2},{4,3},{5,4},{6,5},{7,6},{8,7},{9,8},{10,9},{11,1... | collective-permute-start | bytes 1572872 | tf_op jit(solution)/shard_map/ppermute | solution.py:14
  49.0 30.0 %collective-permute-start.2 = (bf16[4,4,128,256]{3,2,1,0:T(8,128)(2,1)S(1)}, bf16[4,4,128,256]{3,2,1,0:T(8,128)(2,1)S(1)}, u32[]{:S(2)}, u32[]{:S(2)}) collective-permute-start(bf16[4,4,128,256]{3,2,1,0:T(8,128)(2,1)S(1)} %get-tuple-element.9), channel_id=1, source_target_pairs={{0,2},{1,3},{2,4},{3,5},{4,6},{5,7},{6,8},{7,9},{8,10},{9,11},{10,... | collective-permute-start | bytes 3145736 | tf_op jit(solution)/shard_map/ppermute | solution.py:14
  51.0 36.4 %collective-permute-start.3 = (bf16[4,4,128,256]{3,2,1,0:T(8,128)(2,1)S(1)}, bf16[4,4,128,256]{3,2,1,0:T(8,128)(2,1)S(1)}, u32[]{:S(2)}, u32[]{:S(2)}) collective-permute-start(bf16[4,4,128,256]{3,2,1,0:T(8,128)(2,1)S(1)} %get-tuple-element.10), channel_id=1, source_target_pairs={{0,1},{1,2},{2,3},{3,4},{4,5},{5,6},{6,7},{7,8},{8,9},{9,10},{10,1... | collective-permute-start | bytes 3145736 | tf_op jit(solution)/shard_map/ppermute | solution.py:14
  89.3 30.0 %collective-permute-start.7 = (bf16[4,4,128,256]{3,2,1,0:T(8,128)(2,1)S(1)}, bf16[4,4,128,256]{3,2,1,0:T(8,128)(2,1)S(1)}, u32[]{:S(2)}, u32[]{:S(2)}) collective-permute-start(bf16[4,4,128,256]{3,2,1,0:T(8,128)(2,1)S(1)} %get-tuple-element.11), channel_id=1, source_target_pairs={{0,2},{1,3},{2,4},{3,5},{4,6},{5,7},{6,8},{7,9},{8,10},{9,11},{10,... | collective-permute-start | bytes 3145736 | tf_op jit(solution)/shard_map/ppermute | solution.py:14
  92.0 36.0 %collective-permute-start.8 = (bf16[4,4,128,256]{3,2,1,0:T(8,128)(2,1)S(1)}, bf16[4,4,128,256]{3,2,1,0:T(8,128)(2,1)S(1)}, u32[]{:S(2)}, u32[]{:S(2)}) collective-permute-start(bf16[4,4,128,256]{3,2,1,0:T(8,128)(2,1)S(1)} %get-tuple-element.12), channel_id=1, source_target_pairs={{0,1},{1,2},{2,3},{3,4},{4,5},{5,6},{6,7},{7,8},{8,9},{9,10},{10,1... | collective-permute-start | bytes 3145736 | tf_op jit(solution)/shard_map/ppermute | solution.py:14
  94.0 38.2 %collective-permute-start.4 = (bf16[4,4,128,256]{3,2,1,0:T(8,128)(2,1)S(1)}, bf16[4,4,128,256]{3,2,1,0:T(8,128)(2,1)S(1)}, u32[]{:S(2)}, u32[]{:S(2)}) collective-permute-start(bf16[4,4,128,256]{3,2,1,0:T(8,128)(2,1)S(1)} %fusion.refs_0_), channel_id=1, source_target_pairs={{1,0},{2,1},{3,2},{4,3},{5,4},{6,5},{7,6},{8,7},{9,8},{10,9},{11,1... | collective-permute-start | bytes 3145736 | tf_op jit(solution)/shard_map/ppermute | solution.py:14
  128.6 23.7 %collective-permute-start.9 = (bf16[4,4,128,256]{3,2,1,0:T(8,128)(2,1)S(1)}, bf16[4,4,128,256]{3,2,1,0:T(8,128)(2,1)}, u32[]{:S(2)}, u32[]{:S(2)}) collective-permute-start(bf16[4,4,128,256]{3,2,1,0:T(8,128)(2,1)S(1)} %add_convert_fusion.refs_3_), channel_id=1, source_target_pairs={{1,0},{2,1},{3,2},{4,3},{5,4},{6,5},{7,6},{8,7},{9,8},{10,9},{11,1... | collective-permute-start | bytes 3145736 | tf_op jit(solution)/shard_map/ppermute | solution.py:14
  130.5 23.1 %collective-permute-start.6 = (bf16[4,4,128,256]{3,2,1,0:T(8,128)(2,1)S(1)}, bf16[4,4,128,256]{3,2,1,0:T(8,128)(2,1)}, u32[]{:S(2)}, u32[]{:S(2)}) collective-permute-start(bf16[4,4,128,256]{3,2,1,0:T(8,128)(2,1)S(1)} %fusion.refs_0_), channel_id=1, source_target_pairs={{3,1},{5,3},{7,5},{9,7},{11,9},{13,11},{15,13},{17,15},{19,17},{21... | collective-permute-start | bytes 3145736 | tf_op jit(solution)/shard_map/ppermute | solution.py:158
  132.2 21.4 %collective-permute-start.5 = (bf16[4,4,128,256]{3,2,1,0:T(8,128)(2,1)S(1)}, bf16[4,4,128,256]{3,2,1,0:T(8,128)(2,1)}, u32[]{:S(2)}, u32[]{:S(2)}) collective-permute-start(bf16[4,4,128,256]{3,2,1,0:T(8,128)(2,1)S(1)} %collective-permute-done.4.refs_1_), channel_id=1, source_target_pairs={{1,0},{3,2},{5,4},{7,6},{9,8},{11,10},{13,12},{15,14},{17,16},{19,... | collective-permute-start | bytes 3145736 | tf_op jit(solution)/shard_map/ppermute | solution.py:157
  133.4 21.5 %collective-permute-start.11 = (bf16[4,4,128,256]{3,2,1,0:T(8,128)(2,1)S(1)}, bf16[4,4,128,256]{3,2,1,0:T(8,128)(2,1)}, u32[]{:S(2)}, u32[]{:S(2)}) collective-permute-start(bf16[4,4,128,256]{3,2,1,0:T(8,128)(2,1)S(1)} %add_convert_fusion.refs_3_), channel_id=1, source_target_pairs={{3,1},{5,3},{7,5},{9,7},{11,9},{13,11},{15,13},{17,15},{19,17},{21... | collective-permute-start | bytes 3145736 | tf_op jit(solution)/shard_map/ppermute | solution.py:158
  152.3 4.9 %collective-permute-start.10 = (bf16[4,4,128,256]{3,2,1,0:T(8,128)(2,1)}, bf16[4,4,128,256]{3,2,1,0:T(8,128)(2,1)}, u32[]{:S(2)}, u32[]{:S(2)}) collective-permute-start(bf16[4,4,128,256]{3,2,1,0:T(8,128)(2,1)} %collective-permute-done.9.refs_4_), channel_id=1, source_target_pairs={{1,0},{3,2},{5,4},{7,6},{9,8},{11,10},{13,12},{15,14},{17,16},{19,... | collective-permute-start | bytes 3145736 | tf_op jit(solution)/shard_map/ppermute | solution.py:157
Sparse Core Ops, SparseCore 0:
  173.9 52.4 reduce-scatter.1

commit v6 on v4

--- a/solution.py
+++ b/solution.py
@@ -79,7 +79,7 @@
                     preferred_element_type=jnp.float32,
                 )
                 total = part if total is None else total + part
-        out_ref[0] = total
+        out_ref[:, 0] = total.reshape(out_ref.shape[0], out_ref.shape[2], out_ref.shape[3])
 
     @pl.when(jnp.logical_not(live))
     def _():
@@ -158,6 +158,8 @@
         direct = lax.ppermute(fitted, "ao", odd_down_two)
         far = jnp.where(is_even, relayed, direct)
         pieces += [fitted, near, far]
+    aux_devices = lax.axis_size("aux")
+    share = block_size // aux_devices
     whole = pl.BlockSpec(block_shape, lambda s, l, r, n: (0, 0, 0, 0))
     partial_tiles = pl.pallas_call(
         _contract_kernel,
@@ -165,15 +167,22 @@
             num_scalar_prefetch=3,
             grid=(pair_slots,),
             in_specs=[whole] * len(pieces),
-            out_specs=pl.BlockSpec((1, block_size, block_size), lambda s, l, r, n: (s, 0, 0)),
+            out_specs=pl.BlockSpec(
+                (aux_devices, 1, share, block_size), lambda s, l, r, n: (0, s, 0, 0)
+            ),
         ),
-        out_shape=jax.ShapeDtypeStruct((pair_slots, block_size, block_size), jnp.float32),
+        out_shape=jax.ShapeDtypeStruct(
+            (aux_devices, pair_slots, share, block_size), jnp.float32
+        ),
         compiler_params=pltpu.CompilerParams(
             dimension_semantics=("arbitrary",), vmem_limit_bytes=48 * 1024 * 1024
         ),
     )(left_rel, right_rel, count, *pieces)
 
-    summed = lax.psum_scatter(partial_tiles, "aux", scatter_dimension=1, tiled=True)
+    gathered = lax.all_to_all(partial_tiles, "aux", 0, 0, tiled=True)
+    summed = gathered[0]
+    for source in range(1, aux_devices):
+        summed = summed + gathered[source]
     norm_factor = (aux_local * lax.axis_size("aux") * orbitals) ** (-0.5)
     return (summed * norm_factor).astype(jnp.bfloat16)
 

time: 229 us -> 213 us (0.930)
  the two profiles are of different devices: /device:TPU:6 before, /device:TPU:5 now
where the time goes in v6:
time: 213 us; the launch traced here: 212 us
  starting transfers between devices  78.5 us (37%)
  waiting for transfers between devices  62.4 us (29%)
  blocking collectives  40.3 us (19%)
  Pallas kernels  17.4 us (8%)
  other arithmetic  8.9 us (4%)
  local copies, waits for them, and re-layouts  4.09 us (2%)
    ppermute x8, starting transfers between devices, passed_along(): lax.ppermute(value, axis, [(source, source + steps) for source in range(f...  55.2 us
    ppermute x8, waiting for transfers between devices, passed_along(): lax.ppermute(value, axis, [(source, source + steps) for source in range(f...  52.6 us
    all_to_all x1, blocking collectives, on_device(): gathered = lax.all_to_all(partial_tiles, 'aux', 0, 0, tiled=True)  40.3 us
    ppermute x2, starting transfers between devices, on_device(): relayed = lax.ppermute(near, 'ao', odd_down_one)  17.6 us
    pallas_call x1, Pallas kernels, on_device(): pl.pallas_call(_contract_kernel, grid_spec=pltpu.PrefetchScalarGridSpec(n...  10.5 us
    ppermute x2, waiting for transfers between devices, on_device(): direct = lax.ppermute(fitted, 'ao', odd_down_two)  9.79 us
    pallas_call x1, Pallas kernels, on_device(): pl.pallas_call(_half_kernel, grid_spec=pltpu.PrefetchScalarGridSpec(num_s...  6.88 us
    ppermute x2, starting transfers between devices, on_device(): direct = lax.ppermute(fitted, 'ao', odd_down_two)  5.62 us
  transfers between devices with their start and end apart: 12, of which 7 were waited for; matrix products, arithmetic and copies ran while one was open for 2% of the time, Pallas kernels for 0%

profile of v6, /device:TPU:5, one launch (start us, length us, event | category | flops | bytes accessed | tf_op | source)
XLA Modules:
  0.0 212.3 jit_solution(16724961744137603741)
XLA Ops:
  0.0 10.9 %collective-permute-start.1 = (bf16[4,128,512]{2,1,0:T(8,128)(2,1)}, bf16[4,128,512]{2,1,0:T(8,128)(2,1)}, u32[]{:S(2)}, u32[]{:S(2)}) collective-permute-start(bf16[4,128,512]{2,1,0:T(8,128)(2,1)} %bitcast.18), channel_id=1, source_target_pairs={{2,0},{3,1},{4,2},{5,3},{6,4},{7,5},{8,6},{9,7},{10,8},{11,9},{12,... | collective-permute-start | bytes 1572872 | tf_op jit(solution)/shard_map/ppermute | solution.py:14
  10.9 2.9 %collective-permute-start = (bf16[4,128,512]{2,1,0:T(8,128)(2,1)}, bf16[4,128,512]{2,1,0:T(8,128)(2,1)}, u32[]{:S(2)}, u32[]{:S(2)}) collective-permute-start(bf16[4,128,512]{2,1,0:T(8,128)(2,1)} %bitcast.19), channel_id=1, source_target_pairs={{1,0},{2,1},{3,2},{4,3},{5,4},{6,5},{7,6},{8,7},{9,8},{10,9},{11,1... | collective-permute-start | bytes 1572872 | tf_op jit(solution)/shard_map/ppermute | solution.py:14
  14.4 0.8 subtract_bitcast_fusion
  15.2 6.6 %collective-permute-done.1 = bf16[4,128,512]{2,1,0:T(8,128)(2,1)} collective-permute-done((bf16[4,128,512]{2,1,0:T(8,128)(2,1)}, bf16[4,128,512]{2,1,0:T(8,128)(2,1)}, u32[]{:S(2)}, u32[]{:S(2)}) %collective-permute-start.1) | collective-permute-done | bytes 524320 | tf_op jit(solution)/shard_map/ppermute | solution.py:14
  21.8 0.6 collective-permute-done
  22.4 1.5 pad_maximum_fusion.coeff_ref
  23.9 6.9 %shard_map.46 = bf16[2,12,4,128,256]{4,3,2,1,0:T(8,128)(2,1)} custom-call(s32[24]{0:T(128)S(1)} %get-tuple-element.14.left_ref, s32[24]{0:T(128)S(1)} %get-tuple-element.13.right_ref, s32[1]{0:T(128)S(6)} %copy.5.count_ref, bf16[24,4,128,128]{3,2,1,0:T(8,128)(2,1)S(1)} %copy-done, bf16[12,128,512]{2,1,0:T(8,128)(2,1)S(1)} %pad_maximum_fusion.coeff_ref), custom_call_target="tpu_custom_call" | custom-call | tf_op jit(solution)/shard_map/pallas_call | solution.py:113
  30.8 1.7 slice_bitcast_fusion.3
  32.5 5.2 %collective-permute-start.2 = (bf16[4,4,128,256]{3,2,1,0:T(8,128)(2,1)S(1)}, bf16[4,4,128,256]{3,2,1,0:T(8,128)(2,1)S(1)}, u32[]{:S(2)}, u32[]{:S(2)}) collective-permute-start(bf16[4,4,128,256]{3,2,1,0:T(8,128)(2,1)S(1)} %get-tuple-element.9), channel_id=1, source_target_pairs={{0,2},{1,3},{2,4},{3,5},{4,6},{5,7},{6,8},{7,9},{8,10},{9,11},{10,... | collective-permute-start | bytes 3145736 | tf_op jit(solution)/shard_map/ppermute | solution.py:14
  37.8 7.2 %collective-permute-start.3 = (bf16[4,4,128,256]{3,2,1,0:T(8,128)(2,1)S(1)}, bf16[4,4,128,256]{3,2,1,0:T(8,128)(2,1)S(1)}, u32[]{:S(2)}, u32[]{:S(2)}) collective-permute-start(bf16[4,4,128,256]{3,2,1,0:T(8,128)(2,1)S(1)} %get-tuple-element.10), channel_id=1, source_target_pairs={{0,1},{1,2},{2,3},{3,4},{4,5},{5,6},{6,7},{7,8},{8,9},{9,10},{10,1... | collective-permute-start | bytes 3145736 | tf_op jit(solution)/shard_map/ppermute | solution.py:14
  44.9 2.2 %slice_bitcast_fusion = bf16[12,4,128,256]{3,2,1,0:T(8,128)(2,1)S(1)} fusion(bf16[2,12,4,128,256]{4,3,2,1,0:T(8,128)(2,1)} %shard_map.46), kind=kLoop, calls=%fused_computation | loop fusion | bytes 6291456 | tf_op jit(solution)/shard_map/squeeze | solution.py:155
  47.2 24.5 %collective-permute-done.2 = bf16[4,4,128,256]{3,2,1,0:T(8,128)(2,1)S(1)} collective-permute-done((bf16[4,4,128,256]{3,2,1,0:T(8,128)(2,1)S(1)}, bf16[4,4,128,256]{3,2,1,0:T(8,128)(2,1)S(1)}, u32[]{:S(2)}, u32[]{:S(2)}) %collective-permute-start.2) | collective-permute-done | bytes 1048608 | tf_op jit(solution)/shard_map/ppermute | solution.py:14
  71.7 0.3 collective-permute-done.3
  72.0 1.7 fusion.refs_0_
  73.7 0.1 fusion.4
  73.8 4.0 %collective-permute-start.7 = (bf16[4,4,128,256]{3,2,1,0:T(8,128)(2,1)S(1)}, bf16[4,4,128,256]{3,2,1,0:T(8,128)(2,1)S(1)}, u32[]{:S(2)}, u32[]{:S(2)}) collective-permute-start(bf16[4,4,128,256]{3,2,1,0:T(8,128)(2,1)S(1)} %get-tuple-element.11), channel_id=1, source_target_pairs={{0,2},{1,3},{2,4},{3,5},{4,6},{5,7},{6,8},{7,9},{8,10},{9,11},{10,... | collective-permute-start | bytes 3145736 | tf_op jit(solution)/shard_map/ppermute | solution.py:14
  77.8 4.7 %collective-permute-start.8 = (bf16[4,4,128,256]{3,2,1,0:T(8,128)(2,1)S(1)}, bf16[4,4,128,256]{3,2,1,0:T(8,128)(2,1)S(1)}, u32[]{:S(2)}, u32[]{:S(2)}) collective-permute-start(bf16[4,4,128,256]{3,2,1,0:T(8,128)(2,1)S(1)} %get-tuple-element.12), channel_id=1, source_target_pairs={{0,1},{1,2},{2,3},{3,4},{4,5},{5,6},{6,7},{7,8},{8,9},{9,10},{10,1... | collective-permute-start | bytes 3145736 | tf_op jit(solution)/shard_map/ppermute | solution.py:14
  82.5 8.8 %collective-permute-start.4 = (bf16[4,4,128,256]{3,2,1,0:T(8,128)(2,1)S(1)}, bf16[4,4,128,256]{3,2,1,0:T(8,128)(2,1)S(1)}, u32[]{:S(2)}, u32[]{:S(2)}) collective-permute-start(bf16[4,4,128,256]{3,2,1,0:T(8,128)(2,1)S(1)} %fusion.refs_0_), channel_id=1, source_target_pairs={{1,0},{2,1},{3,2},{4,3},{5,4},{6,5},{7,6},{8,7},{9,8},{10,9},{11,1... | collective-permute-start | bytes 3145736 | tf_op jit(solution)/shard_map/ppermute | solution.py:14
  91.3 13.6 %collective-permute-done.7 = bf16[4,4,128,256]{3,2,1,0:T(8,128)(2,1)S(1)} collective-permute-done((bf16[4,4,128,256]{3,2,1,0:T(8,128)(2,1)S(1)}, bf16[4,4,128,256]{3,2,1,0:T(8,128)(2,1)S(1)}, u32[]{:S(2)}, u32[]{:S(2)}) %collective-permute-start.7) | collective-permute-done | bytes 1048608 | tf_op jit(solution)/shard_map/ppermute | solution.py:14
  104.9 7.1 %collective-permute-done.8 = bf16[4,4,128,256]{3,2,1,0:T(8,128)(2,1)S(1)} collective-permute-done((bf16[4,4,128,256]{3,2,1,0:T(8,128)(2,1)S(1)}, bf16[4,4,128,256]{3,2,1,0:T(8,128)(2,1)S(1)}, u32[]{:S(2)}, u32[]{:S(2)}) %collective-permute-start.8) | collective-permute-done | bytes 1048608 | tf_op jit(solution)/shard_map/ppermute | solution.py:14
  112.0 0.5 add_convert_fusion.refs_3_
  112.5 11.6 %collective-permute-start.9 = (bf16[4,4,128,256]{3,2,1,0:T(8,128)(2,1)S(1)}, bf16[4,4,128,256]{3,2,1,0:T(8,128)(2,1)}, u32[]{:S(2)}, u32[]{:S(2)}) collective-permute-start(bf16[4,4,128,256]{3,2,1,0:T(8,128)(2,1)S(1)} %add_convert_fusion.refs_3_), channel_id=1, source_target_pairs={{1,0},{2,1},{3,2},{4,3},{5,4},{6,5},{7,6},{8,7},{9,8},{10,9},{11,1... | collective-permute-start | bytes 3145736 | tf_op jit(solution)/shard_map/ppermute | solution.py:14
  124.1 3.4 %collective-permute-start.6 = (bf16[4,4,128,256]{3,2,1,0:T(8,128)(2,1)S(1)}, bf16[4,4,128,256]{3,2,1,0:T(8,128)(2,1)}, u32[]{:S(2)}, u32[]{:S(2)}) collective-permute-start(bf16[4,4,128,256]{3,2,1,0:T(8,128)(2,1)S(1)} %fusion.refs_0_), channel_id=1, source_target_pairs={{3,1},{5,3},{7,5},{9,7},{11,9},{13,11},{15,13},{17,15},{19,17},{21... | collective-permute-start | bytes 3145736 | tf_op jit(solution)/shard_map/ppermute | solution.py:158
  127.5 2.3 %collective-permute-start.5 = (bf16[4,4,128,256]{3,2,1,0:T(8,128)(2,1)S(1)}, bf16[4,4,128,256]{3,2,1,0:T(8,128)(2,1)}, u32[]{:S(2)}, u32[]{:S(2)}) collective-permute-start(bf16[4,4,128,256]{3,2,1,0:T(8,128)(2,1)S(1)} %collective-permute-done.4.refs_1_), channel_id=1, source_target_pairs={{1,0},{3,2},{5,4},{7,6},{9,8},{11,10},{13,12},{15,14},{17,16},{19,... | collective-permute-start | bytes 3145736 | tf_op jit(solution)/shard_map/ppermute | solution.py:157
  129.8 2.3 %collective-permute-start.11 = (bf16[4,4,128,256]{3,2,1,0:T(8,128)(2,1)S(1)}, bf16[4,4,128,256]{3,2,1,0:T(8,128)(2,1)}, u32[]{:S(2)}, u32[]{:S(2)}) collective-permute-start(bf16[4,4,128,256]{3,2,1,0:T(8,128)(2,1)S(1)} %add_convert_fusion.refs_3_), channel_id=1, source_target_pairs={{3,1},{5,3},{7,5},{9,7},{11,9},{13,11},{15,13},{17,15},{19,17},{21... | collective-permute-start | bytes 3145736 | tf_op jit(solution)/shard_map/ppermute | solution.py:158
  132.1 15.3 %collective-permute-start.10 = (bf16[4,4,128,256]{3,2,1,0:T(8,128)(2,1)}, bf16[4,4,128,256]{3,2,1,0:T(8,128)(2,1)}, u32[]{:S(2)}, u32[]{:S(2)}) collective-permute-start(bf16[4,4,128,256]{3,2,1,0:T(8,128)(2,1)} %collective-permute-done.9.refs_4_), channel_id=1, source_target_pairs={{1,0},{3,2},{5,4},{7,6},{9,8},{11,10},{13,12},{15,14},{17,16},{19,... | collective-permute-start | bytes 3145736 | tf_op jit(solution)/shard_map/ppermute | solution.py:157
  147.4 1.3 broadcast_select_fusion.1.refs_2_
  148.7 9.8 %collective-permute-done.11 = bf16[4,4,128,256]{3,2,1,0:T(8,128)(2,1)} collective-permute-done((bf16[4,4,128,256]{3,2,1,0:T(8,128)(2,1)S(1)}, bf16[4,4,128,256]{3,2,1,0:T(8,128)(2,1)}, u32[]{:S(2)}, u32[]{:S(2)}) %collective-permute-start.11) | collective-permute-done | bytes 1048608 | tf_op jit(solution)/shard_map/ppermute | solution.py:158
  158.5 2.3 %broadcast_select_fusion.refs_5_ = bf16[4,4,128,256]{3,2,1,0:T(8,128)(2,1)} fusion(bf16[4,4,128,256]{3,2,1,0:T(8,128)(2,1)} %collective-permute-done.10, bf16[4,4,128,256]{3,2,1,0:T(8,128)(2,1)} %collective-permute-done.11, pred[]{:T(512)S(6)} %eq.5), kind=kLoop, calls=%fused_computation.8 | loop fusion | flops 524288 | bytes 3145729 | tf_op jit(solution)/shard_map/jit(_where)/select_n | solution.py:159
  160.8 10.5 %shard_map.47 = f32[8,24,16,128]{3,2,1,0:T(8,128)} custom-call(s32[24]{0:T(128)S(1)} %get-tuple-element.14.left_ref, s32[24]{0:T(128)S(1)} %get-tuple-element.13.right_ref, s32[1]{0:T(128)S(6)} %copy.5.count_ref, bf16[4,4,128,256]{3,2,1,0:T(8,128)(2,1)S(1)} %fusion.refs_0_, bf16[4,4,128,256]{3,2,1,0:T(8,128)(2,1)S(1)} %collective-permute-done.4.refs_1_, ...), custom_call_target="tpu_custom_call" | custom-call | tf_op jit(solution)/shard_map/pallas_call | solution.py:164
  171.3 40.3 %all_to_all.5 = f32[8,24,16,128]{3,2,1,0:T(8,128)S(1)} all-to-all(f32[8,24,16,128]{3,2,1,0:T(8,128)} %shard_map.47), channel_id=1, replica_groups=mesh['aux'=8,'ao'=64] {'aux'}, dimensions={0} | all-to-all | bytes 3145728 | tf_op jit(solution)/shard_map/all_to_all | solution.py:182
  211.6 0.7 fusion.3
  (7 shorter events, 0.0 us)
Async XLA Ops:
  0.0 23.9 %copy-start = (bf16[24,4,128,128]{3,2,1,0:T(8,128)(2,1)S(1)}, bf16[24,4,128,128]{3,2,1,0:T(8,128)(2,1)}, u32[]{:S(2)}) copy-start(bf16[24,4,128,128]{3,2,1,0:T(8,128)(2,1)} %tile_ref.1) | copy-start | bytes 9437188
  0.0 21.8 %collective-permute-start.1 = (bf16[4,128,512]{2,1,0:T(8,128)(2,1)}, bf16[4,128,512]{2,1,0:T(8,128)(2,1)}, u32[]{:S(2)}, u32[]{:S(2)}) collective-permute-start(bf16[4,128,512]{2,1,0:T(8,128)(2,1)} %bitcast.18), channel_id=1, source_target_pairs={{2,0},{3,1},{4,2},{5,3},{6,4},{7,5},{8,6},{9,7},{10,8},{11,9},{12,... | collective-permute-start | bytes 1572872 | tf_op jit(solution)/shard_map/ppermute | solution.py:14
  10.9 11.5 %collective-permute-start = (bf16[4,128,512]{2,1,0:T(8,128)(2,1)}, bf16[4,128,512]{2,1,0:T(8,128)(2,1)}, u32[]{:S(2)}, u32[]{:S(2)}) collective-permute-start(bf16[4,128,512]{2,1,0:T(8,128)(2,1)} %bitcast.19), channel_id=1, source_target_pairs={{1,0},{2,1},{3,2},{4,3},{5,4},{6,5},{7,6},{8,7},{9,8},{10,9},{11,1... | collective-permute-start | bytes 1572872 | tf_op jit(solution)/shard_map/ppermute | solution.py:14
  32.5 39.2 %collective-permute-start.2 = (bf16[4,4,128,256]{3,2,1,0:T(8,128)(2,1)S(1)}, bf16[4,4,128,256]{3,2,1,0:T(8,128)(2,1)S(1)}, u32[]{:S(2)}, u32[]{:S(2)}) collective-permute-start(bf16[4,4,128,256]{3,2,1,0:T(8,128)(2,1)S(1)} %get-tuple-element.9), channel_id=1, source_target_pairs={{0,2},{1,3},{2,4},{3,5},{4,6},{5,7},{6,8},{7,9},{8,10},{9,11},{10,... | collective-permute-start | bytes 3145736 | tf_op jit(solution)/shard_map/ppermute | solution.py:14
  37.8 34.2 %collective-permute-start.3 = (bf16[4,4,128,256]{3,2,1,0:T(8,128)(2,1)S(1)}, bf16[4,4,128,256]{3,2,1,0:T(8,128)(2,1)S(1)}, u32[]{:S(2)}, u32[]{:S(2)}) collective-permute-start(bf16[4,4,128,256]{3,2,1,0:T(8,128)(2,1)S(1)} %get-tuple-element.10), channel_id=1, source_target_pairs={{0,1},{1,2},{2,3},{3,4},{4,5},{5,6},{6,7},{7,8},{8,9},{9,10},{10,1... | collective-permute-start | bytes 3145736 | tf_op jit(solution)/shard_map/ppermute | solution.py:14
  73.8 31.1 %collective-permute-start.7 = (bf16[4,4,128,256]{3,2,1,0:T(8,128)(2,1)S(1)}, bf16[4,4,128,256]{3,2,1,0:T(8,128)(2,1)S(1)}, u32[]{:S(2)}, u32[]{:S(2)}) collective-permute-start(bf16[4,4,128,256]{3,2,1,0:T(8,128)(2,1)S(1)} %get-tuple-element.11), channel_id=1, source_target_pairs={{0,2},{1,3},{2,4},{3,5},{4,6},{5,7},{6,8},{7,9},{8,10},{9,11},{10,... | collective-permute-start | bytes 3145736 | tf_op jit(solution)/shard_map/ppermute | solution.py:14
  77.8 34.2 %collective-permute-start.8 = (bf16[4,4,128,256]{3,2,1,0:T(8,128)(2,1)S(1)}, bf16[4,4,128,256]{3,2,1,0:T(8,128)(2,1)S(1)}, u32[]{:S(2)}, u32[]{:S(2)}) collective-permute-start(bf16[4,4,128,256]{3,2,1,0:T(8,128)(2,1)S(1)} %get-tuple-element.12), channel_id=1, source_target_pairs={{0,1},{1,2},{2,3},{3,4},{4,5},{5,6},{6,7},{7,8},{8,9},{9,10},{10,1... | collective-permute-start | bytes 3145736 | tf_op jit(solution)/shard_map/ppermute | solution.py:14
  82.5 45.0 %collective-permute-start.4 = (bf16[4,4,128,256]{3,2,1,0:T(8,128)(2,1)S(1)}, bf16[4,4,128,256]{3,2,1,0:T(8,128)(2,1)S(1)}, u32[]{:S(2)}, u32[]{:S(2)}) collective-permute-start(bf16[4,4,128,256]{3,2,1,0:T(8,128)(2,1)S(1)} %fusion.refs_0_), channel_id=1, source_target_pairs={{1,0},{2,1},{3,2},{4,3},{5,4},{6,5},{7,6},{8,7},{9,8},{10,9},{11,1... | collective-permute-start | bytes 3145736 | tf_op jit(solution)/shard_map/ppermute | solution.py:14
  112.5 19.5 %collective-permute-start.9 = (bf16[4,4,128,256]{3,2,1,0:T(8,128)(2,1)S(1)}, bf16[4,4,128,256]{3,2,1,0:T(8,128)(2,1)}, u32[]{:S(2)}, u32[]{:S(2)}) collective-permute-start(bf16[4,4,128,256]{3,2,1,0:T(8,128)(2,1)S(1)} %add_convert_fusion.refs_3_), channel_id=1, source_target_pairs={{1,0},{2,1},{3,2},{4,3},{5,4},{6,5},{7,6},{8,7},{9,8},{10,9},{11,1... | collective-permute-start | bytes 3145736 | tf_op jit(solution)/shard_map/ppermute | solution.py:14
  124.1 23.2 %collective-permute-start.6 = (bf16[4,4,128,256]{3,2,1,0:T(8,128)(2,1)S(1)}, bf16[4,4,128,256]{3,2,1,0:T(8,128)(2,1)}, u32[]{:S(2)}, u32[]{:S(2)}) collective-permute-start(bf16[4,4,128,256]{3,2,1,0:T(8,128)(2,1)S(1)} %fusion.refs_0_), channel_id=1, source_target_pairs={{3,1},{5,3},{7,5},{9,7},{11,9},{13,11},{15,13},{17,15},{19,17},{21... | collective-permute-start | bytes 3145736 | tf_op jit(solution)/shard_map/ppermute | solution.py:158
  127.5 19.9 %collective-permute-start.5 = (bf16[4,4,128,256]{3,2,1,0:T(8,128)(2,1)S(1)}, bf16[4,4,128,256]{3,2,1,0:T(8,128)(2,1)}, u32[]{:S(2)}, u32[]{:S(2)}) collective-permute-start(bf16[4,4,128,256]{3,2,1,0:T(8,128)(2,1)S(1)} %collective-permute-done.4.refs_1_), channel_id=1, source_target_pairs={{1,0},{3,2},{5,4},{7,6},{9,8},{11,10},{13,12},{15,14},{17,16},{19,... | collective-permute-start | bytes 3145736 | tf_op jit(solution)/shard_map/ppermute | solution.py:157
  129.8 28.7 %collective-permute-start.11 = (bf16[4,4,128,256]{3,2,1,0:T(8,128)(2,1)S(1)}, bf16[4,4,128,256]{3,2,1,0:T(8,128)(2,1)}, u32[]{:S(2)}, u32[]{:S(2)}) collective-permute-start(bf16[4,4,128,256]{3,2,1,0:T(8,128)(2,1)S(1)} %add_convert_fusion.refs_3_), channel_id=1, source_target_pairs={{3,1},{5,3},{7,5},{9,7},{11,9},{13,11},{15,13},{17,15},{19,17},{21... | collective-permute-start | bytes 3145736 | tf_op jit(solution)/shard_map/ppermute | solution.py:158
  132.1 26.5 %collective-permute-start.10 = (bf16[4,4,128,256]{3,2,1,0:T(8,128)(2,1)}, bf16[4,4,128,256]{3,2,1,0:T(8,128)(2,1)}, u32[]{:S(2)}, u32[]{:S(2)}) collective-permute-start(bf16[4,4,128,256]{3,2,1,0:T(8,128)(2,1)} %collective-permute-done.9.refs_4_), channel_id=1, source_target_pairs={{1,0},{3,2},{5,4},{7,6},{9,8},{11,10},{13,12},{15,14},{17,16},{19,... | collective-permute-start | bytes 3145736 | tf_op jit(solution)/shard_map/ppermute | solution.py:157

commit v7 on v6

--- a/solution.py
+++ b/solution.py
@@ -86,7 +86,7 @@
         out_ref[...] = jnp.zeros_like(out_ref)
 
 
-CHUNKS = 2
+CHUNKS = 1
 
 
 def on_device(pair_list, pair_count, tiles, coeff):

time: 213 us -> 228 us (1.070)
  the two profiles are of different devices: /device:TPU:5 before, /device:TPU:6 now
where the time goes in v7:
time: 228 us; the launch traced here: 227 us
  waiting for transfers between devices  132 us (58%)
  blocking collectives  47.2 us (21%)
  starting transfers between devices  22.5 us (10%)
  Pallas kernels  13.4 us (6%)
  other arithmetic  8.76 us (4%)
  local copies, waits for them, and re-layouts  2.5 us (1%)
    ppermute x5, waiting for transfers between devices, passed_along(): lax.ppermute(value, axis, [(source, source + steps) for source in range(f...  127 us
    all_to_all x1, blocking collectives, on_device(): gathered = lax.all_to_all(partial_tiles, 'aux', 0, 0, tiled=True)  47.2 us
    ppermute x5, starting transfers between devices, passed_along(): lax.ppermute(value, axis, [(source, source + steps) for source in range(f...  19.2 us
    pallas_call x1, Pallas kernels, on_device(): pl.pallas_call(_half_kernel, grid_spec=pltpu.PrefetchScalarGridSpec(num_s...  7.95 us
    pallas_call x1, Pallas kernels, on_device(): pl.pallas_call(_contract_kernel, grid_spec=pltpu.PrefetchScalarGridSpec(n...  5.49 us
    ppermute x1, waiting for transfers between devices, on_device(): relayed = lax.ppermute(near, 'ao', odd_down_one)  5.08 us
  transfers between devices with their start and end apart: 7, of which 6 were waited for; matrix products, arithmetic and copies ran while one was open for 0% of the time, Pallas kernels for 0%

profile of v7, /device:TPU:6, one launch (start us, length us, event | category | flops | bytes accessed | tf_op | source)
XLA Modules:
  0.0 227.3 jit_solution(755645496117451709)
XLA Ops:
  0.0 0.0 copy-start
  0.0 11.5 %collective-permute-start.1 = (bf16[4,128,512]{2,1,0:T(8,128)(2,1)}, bf16[4,128,512]{2,1,0:T(8,128)(2,1)}, u32[]{:S(2)}, u32[]{:S(2)}) collective-permute-start(bf16[4,128,512]{2,1,0:T(8,128)(2,1)} %bitcast.16), channel_id=1, source_target_pairs={{2,0},{3,1},{4,2},{5,3},{6,4},{7,5},{8,6},{9,7},{10,8},{11,9},{12,... | collective-permute-start | bytes 1572872 | tf_op jit(solution)/shard_map/ppermute | solution.py:14
  11.5 1.9 collective-permute-start
  14.1 0.8 subtract_bitcast_fusion
  14.8 8.1 %collective-permute-done.1 = bf16[4,128,512]{2,1,0:T(8,128)(2,1)} collective-permute-done((bf16[4,128,512]{2,1,0:T(8,128)(2,1)}, bf16[4,128,512]{2,1,0:T(8,128)(2,1)}, u32[]{:S(2)}, u32[]{:S(2)}) %collective-permute-start.1) | collective-permute-done | bytes 524320 | tf_op jit(solution)/shard_map/ppermute | solution.py:14
  23.0 5.6 %collective-permute-done = bf16[4,128,512]{2,1,0:T(8,128)(2,1)} collective-permute-done((bf16[4,128,512]{2,1,0:T(8,128)(2,1)}, bf16[4,128,512]{2,1,0:T(8,128)(2,1)}, u32[]{:S(2)}, u32[]{:S(2)}) %collective-permute-start) | collective-permute-done | bytes 524320 | tf_op jit(solution)/shard_map/ppermute | solution.py:14
  28.6 1.5 pad_maximum_fusion.coeff_ref
  30.1 0.0 copy-done
  30.1 7.9 %shard_map.46 = bf16[1,12,4,128,512]{4,3,2,1,0:T(8,128)(2,1)} custom-call(s32[24]{0:T(128)S(1)} %get-tuple-element.8.left_ref, s32[24]{0:T(128)S(1)} %get-tuple-element.7.right_ref, s32[1]{0:T(128)S(6)} %copy.5.count_ref, bf16[24,4,128,128]{3,2,1,0:T(8,128)(2,1)S(1)} %copy-done, bf16[12,128,512]{2,1,0:T(8,128)(2,1)S(1)} %pad_maximum_fusion.coeff_ref), custom_call_target="tpu_custom_call" | custom-call | tf_op jit(solution)/shard_map/pallas_call | solution.py:113
  38.1 2.5 %slice_bitcast_fusion.2 = (bf16[4,4,128,512]{3,2,1,0:T(8,128)(2,1)S(1)}, bf16[4,4,128,512]{3,2,1,0:T(8,128)(2,1)S(1)}) fusion(bf16[1,12,4,128,512]{4,3,2,1,0:T(8,128)(2,1)} %shard_map.46), kind=kLoop, calls=%fused_computation.4 | loop fusion | bytes 8388608 | tf_op jit(solution)/shard_map/slice | solution.py:149
  40.6 1.9 collective-permute-start.2
  42.5 1.9 collective-permute-start.3
  44.4 44.1 %collective-permute-done.2 = bf16[4,4,128,512]{3,2,1,0:T(8,128)(2,1)S(1)} collective-permute-done((bf16[4,4,128,512]{3,2,1,0:T(8,128)(2,1)S(1)}, bf16[4,4,128,512]{3,2,1,0:T(8,128)(2,1)S(1)}, u32[]{:S(2)}, u32[]{:S(2)}) %collective-permute-start.2) | collective-permute-done | bytes 2097184 | tf_op jit(solution)/shard_map/ppermute | solution.py:14
  88.5 27.1 %collective-permute-done.3 = bf16[4,4,128,512]{3,2,1,0:T(8,128)(2,1)S(1)} collective-permute-done((bf16[4,4,128,512]{3,2,1,0:T(8,128)(2,1)S(1)}, bf16[4,4,128,512]{3,2,1,0:T(8,128)(2,1)S(1)}, u32[]{:S(2)}, u32[]{:S(2)}) %collective-permute-start.3) | collective-permute-done | bytes 2097184 | tf_op jit(solution)/shard_map/ppermute | solution.py:14
  115.5 2.6 %fusion.refs_0_ = bf16[4,4,128,512]{3,2,1,0:T(8,128)(2,1)S(1)} fusion(bf16[4,4,128,512]{3,2,1,0:T(8,128)(2,1)S(1)} %collective-permute-done.3, bf16[4,4,128,512]{3,2,1,0:T(8,128)(2,1)S(1)} %collective-permute-done.2, bf16[1,12,4,128,512]{4,3,2,1,0:T(8,128)(2,1)} %shard_map.46), kind=kLoop, calls=%fused_computation.1 | loop fusion | flops 6291456 | bytes 8388608 | tf_op jit(solution)/shard_map/convert_element_type | solution.py:153
  118.1 1.9 collective-permute-start.4
  120.1 2.0 collective-permute-start.6
  122.1 42.2 %collective-permute-done.4.refs_1_ = bf16[4,4,128,512]{3,2,1,0:T(8,128)(2,1)} collective-permute-done((bf16[4,4,128,512]{3,2,1,0:T(8,128)(2,1)S(1)}, bf16[4,4,128,512]{3,2,1,0:T(8,128)(2,1)}, u32[]{:S(2)}, u32[]{:S(2)}) %collective-permute-start.4) | collective-permute-done | bytes 2097184 | tf_op jit(solution)/shard_map/ppermute | solution.py:14
  164.3 1.3 collective-permute-start.5
  165.6 0.0 collective-permute-done.6
  165.6 5.1 %collective-permute-done.5 = bf16[4,4,128,512]{3,2,1,0:T(8,128)(2,1)} collective-permute-done((bf16[4,4,128,512]{3,2,1,0:T(8,128)(2,1)}, bf16[4,4,128,512]{3,2,1,0:T(8,128)(2,1)}, u32[]{:S(2)}, u32[]{:S(2)}) %collective-permute-start.5) | collective-permute-done | bytes 2097184 | tf_op jit(solution)/shard_map/ppermute | solution.py:157
  170.7 3.1 %broadcast_select_fusion.refs_2_ = bf16[4,4,128,512]{3,2,1,0:T(8,128)(2,1)} fusion(bf16[4,4,128,512]{3,2,1,0:T(8,128)(2,1)} %collective-permute-done.5, bf16[4,4,128,512]{3,2,1,0:T(8,128)(2,1)} %collective-permute-done.6, pred[]{:T(512)S(6)} %eq.5), kind=kLoop, calls=%fused_computation.5 | loop fusion | flops 1048576 | bytes 6291457 | tf_op jit(solution)/shard_map/jit(_where)/select_n | solution.py:159
  173.8 5.5 %shard_map.47 = f32[8,24,16,128]{3,2,1,0:T(8,128)S(1)} custom-call(s32[24]{0:T(128)S(1)} %get-tuple-element.8.left_ref, s32[24]{0:T(128)S(1)} %get-tuple-element.7.right_ref, s32[1]{0:T(128)S(6)} %copy.5.count_ref, bf16[4,4,128,512]{3,2,1,0:T(8,128)(2,1)S(1)} %fusion.refs_0_, bf16[4,4,128,512]{3,2,1,0:T(8,128)(2,1)} %collective-permute-done.4.refs_1_, ...), custom_call_target="tpu_custom_call" | custom-call | tf_op jit(solution)/shard_map/pallas_call | solution.py:164
  179.3 47.2 %all_to_all.5 = f32[8,24,16,128]{3,2,1,0:T(8,128)S(1)} all-to-all(f32[8,24,16,128]{3,2,1,0:T(8,128)S(1)} %shard_map.47), channel_id=1, replica_groups=mesh['aux'=8,'ao'=64] {'aux'}, dimensions={0} | all-to-all | bytes 3145728 | tf_op jit(solution)/shard_map/all_to_all | solution.py:182
  226.5 0.7 fusion.3
Async XLA Ops:
  0.0 30.1 %copy-start = (bf16[24,4,128,128]{3,2,1,0:T(8,128)(2,1)S(1)}, bf16[24,4,128,128]{3,2,1,0:T(8,128)(2,1)}, u32[]{:S(2)}) copy-start(bf16[24,4,128,128]{3,2,1,0:T(8,128)(2,1)} %tile_ref.1) | copy-start | bytes 9437188
  0.0 23.0 %collective-permute-start.1 = (bf16[4,128,512]{2,1,0:T(8,128)(2,1)}, bf16[4,128,512]{2,1,0:T(8,128)(2,1)}, u32[]{:S(2)}, u32[]{:S(2)}) collective-permute-start(bf16[4,128,512]{2,1,0:T(8,128)(2,1)} %bitcast.16), channel_id=1, source_target_pairs={{2,0},{3,1},{4,2},{5,3},{6,4},{7,5},{8,6},{9,7},{10,8},{11,9},{12,... | collective-permute-start | bytes 1572872 | tf_op jit(solution)/shard_map/ppermute | solution.py:14
  11.5 17.1 %collective-permute-start = (bf16[4,128,512]{2,1,0:T(8,128)(2,1)}, bf16[4,128,512]{2,1,0:T(8,128)(2,1)}, u32[]{:S(2)}, u32[]{:S(2)}) collective-permute-start(bf16[4,128,512]{2,1,0:T(8,128)(2,1)} %bitcast.17), channel_id=1, source_target_pairs={{1,0},{2,1},{3,2},{4,3},{5,4},{6,5},{7,6},{8,7},{9,8},{10,9},{11,1... | collective-permute-start | bytes 1572872 | tf_op jit(solution)/shard_map/ppermute | solution.py:14
  40.6 47.9 %collective-permute-start.2 = (bf16[4,4,128,512]{3,2,1,0:T(8,128)(2,1)S(1)}, bf16[4,4,128,512]{3,2,1,0:T(8,128)(2,1)S(1)}, u32[]{:S(2)}, u32[]{:S(2)}) collective-permute-start(bf16[4,4,128,512]{3,2,1,0:T(8,128)(2,1)S(1)} %get-tuple-element.5), channel_id=1, source_target_pairs={{0,2},{1,3},{2,4},{3,5},{4,6},{5,7},{6,8},{7,9},{8,10},{9,11},{10,... | collective-permute-start | bytes 6291464 | tf_op jit(solution)/shard_map/ppermute | solution.py:14
  42.5 73.1 %collective-permute-start.3 = (bf16[4,4,128,512]{3,2,1,0:T(8,128)(2,1)S(1)}, bf16[4,4,128,512]{3,2,1,0:T(8,128)(2,1)S(1)}, u32[]{:S(2)}, u32[]{:S(2)}) collective-permute-start(bf16[4,4,128,512]{3,2,1,0:T(8,128)(2,1)S(1)} %get-tuple-element.6), channel_id=1, source_target_pairs={{0,1},{1,2},{2,3},{3,4},{4,5},{5,6},{6,7},{7,8},{8,9},{9,10},{10,1... | collective-permute-start | bytes 6291464 | tf_op jit(solution)/shard_map/ppermute | solution.py:14
  118.1 46.2 %collective-permute-start.4 = (bf16[4,4,128,512]{3,2,1,0:T(8,128)(2,1)S(1)}, bf16[4,4,128,512]{3,2,1,0:T(8,128)(2,1)}, u32[]{:S(2)}, u32[]{:S(2)}) collective-permute-start(bf16[4,4,128,512]{3,2,1,0:T(8,128)(2,1)S(1)} %fusion.refs_0_), channel_id=1, source_target_pairs={{1,0},{2,1},{3,2},{4,3},{5,4},{6,5},{7,6},{8,7},{9,8},{10,9},{11,1... | collective-permute-start | bytes 6291464 | tf_op jit(solution)/shard_map/ppermute | solution.py:14
  120.1 45.6 %collective-permute-start.6 = (bf16[4,4,128,512]{3,2,1,0:T(8,128)(2,1)S(1)}, bf16[4,4,128,512]{3,2,1,0:T(8,128)(2,1)}, u32[]{:S(2)}, u32[]{:S(2)}) collective-permute-start(bf16[4,4,128,512]{3,2,1,0:T(8,128)(2,1)S(1)} %fusion.refs_0_), channel_id=1, source_target_pairs={{3,1},{5,3},{7,5},{9,7},{11,9},{13,11},{15,13},{17,15},{19,17},{21... | collective-permute-start | bytes 6291464 | tf_op jit(solution)/shard_map/ppermute | solution.py:158
  164.3 6.4 %collective-permute-start.5 = (bf16[4,4,128,512]{3,2,1,0:T(8,128)(2,1)}, bf16[4,4,128,512]{3,2,1,0:T(8,128)(2,1)}, u32[]{:S(2)}, u32[]{:S(2)}) collective-permute-start(bf16[4,4,128,512]{3,2,1,0:T(8,128)(2,1)} %collective-permute-done.4.refs_1_), channel_id=1, source_target_pairs={{1,0},{3,2},{5,4},{7,6},{9,8},{11,10},{13,12},{15,14},{17,16},{19,... | collective-permute-start | bytes 6291464 | tf_op jit(solution)/shard_map/ppermute | solution.py:157

commit v8 on v7

--- a/solution.py
+++ b/solution.py
@@ -137,27 +137,26 @@
         ),
     )(left_rel, right_rel, count, tiles, window_coeff)
 
-    odd_down_one = [(s, s - 1) for s in range(1, devices, 2)]
-    odd_down_two = [(s, s - 2) for s in range(3, devices, 2)]
-    is_even = (owner_index % 2) == 0
     block_shape = (own_blocks, aux_local, block_size, width)
     pieces = []
-    pending = halves[0]
     for c in range(CHUNKS):
-        chunk = pending
-        from_one = passed_along(chunk[own_blocks : 2 * own_blocks], "ao", 1)
-        from_two = passed_along(chunk[2 * own_blocks :], "ao", 2)
-        fitted = (
-            (from_two.astype(jnp.float32) + from_one.astype(jnp.float32))
-            + chunk[:own_blocks].astype(jnp.float32)
-        ).astype(jnp.bfloat16)
-        if c + 1 < CHUNKS:
-            fitted, pending = lax.optimization_barrier((fitted, halves[c + 1]))
-        near = passed_along(fitted, "ao", -1)
-        relayed = lax.ppermute(near, "ao", odd_down_one)
-        direct = lax.ppermute(fitted, "ao", odd_down_two)
-        far = jnp.where(is_even, relayed, direct)
-        pieces += [fitted, near, far]
+        chunk = halves[c]
+        behind_two = passed_along(chunk[2 * own_blocks :], "ao", 2)
+        behind_one = passed_along(chunk[own_blocks:], "ao", 1)
+        ahead_one = passed_along(chunk[: 2 * own_blocks], "ao", -1)
+        ahead_two = passed_along(chunk[:own_blocks], "ao", -2)
+
+        def owner_sum(first, second, third):
+            total = first.astype(jnp.float32) + second.astype(jnp.float32)
+            return (total + third.astype(jnp.float32)).astype(jnp.bfloat16)
+
+        pieces += [
+            owner_sum(behind_two, behind_one[:own_blocks], chunk[:own_blocks]),
+            owner_sum(
+                behind_one[own_blocks:], chunk[own_blocks : 2 * own_blocks], ahead_one[:own_blocks]
+            ),
+            owner_sum(chunk[2 * own_blocks :], ahead_one[own_blocks:], ahead_two),
+        ]
     aux_devices = lax.axis_size("aux")
     share = block_size // aux_devices
     whole = pl.BlockSpec(block_shape, lambda s, l, r, n: (0, 0, 0, 0))

time: 228 us -> 207 us (0.908)
  the two profiles are of different devices: /device:TPU:6 before, /device:TPU:5 now
where the time goes in v8:
time: 207 us
  waiting for transfers between devices  93.7 us (45%)
  blocking collectives  42.4 us (20%)
  starting transfers between devices  40.6 us (20%)
  Pallas kernels  17.3 us (8%)
  other arithmetic  7.43 us (4%)
  local copies, waits for them, and re-layouts  4.38 us (2%)
    ppermute x6, waiting for transfers between devices, passed_along(): lax.ppermute(value, axis, [(source, source + steps) for source in range(f...  93.7 us
    all_to_all x1, blocking collectives, on_device(): gathered = lax.all_to_all(partial_tiles, 'aux', 0, 0, tiled=True)  42.4 us
    ppermute x6, starting transfers between devices, passed_along(): lax.ppermute(value, axis, [(source, source + steps) for source in range(f...  40.6 us
    pallas_call x1, Pallas kernels, on_device(): pl.pallas_call(_half_kernel, grid_spec=pltpu.PrefetchScalarGridSpec(num_s...  10.4 us
    pallas_call x1, Pallas kernels, on_device(): pl.pallas_call(_contract_kernel, grid_spec=pltpu.PrefetchScalarGridSpec(n...  6.88 us
    convert_element_type x1, other arithmetic, owner_sum(): return (total + third.astype(jnp.float32)).astype(jnp.bfloat16)  4.4 us
  transfers between devices with their start and end apart: 6, of which 4 were waited for; matrix products, arithmetic and copies ran while one was open for 1% of the time, Pallas kernels for 0%

profile of v8, /device:TPU:5, one launch (start us, length us, event | category | flops | bytes accessed | tf_op | source)
XLA Modules:
  0.0 206.5 jit_solution(5826045249020186970)
XLA Ops:
  0.0 0.0 copy-start
  0.0 10.9 %collective-permute-start.1 = (bf16[4,128,512]{2,1,0:T(8,128)(2,1)}, bf16[4,128,512]{2,1,0:T(8,128)(2,1)}, u32[]{:S(2)}, u32[]{:S(2)}) collective-permute-start(bf16[4,128,512]{2,1,0:T(8,128)(2,1)} %bitcast.24), channel_id=1, source_target_pairs={{2,0},{3,1},{4,2},{5,3},{6,4},{7,5},{8,6},{9,7},{10,8},{11,9},{12,... | collective-permute-start | bytes 1572872 | tf_op jit(solution)/shard_map/ppermute | solution.py:14
  10.9 2.9 %collective-permute-start = (bf16[4,128,512]{2,1,0:T(8,128)(2,1)}, bf16[4,128,512]{2,1,0:T(8,128)(2,1)}, u32[]{:S(2)}, u32[]{:S(2)}) collective-permute-start(bf16[4,128,512]{2,1,0:T(8,128)(2,1)} %bitcast.25), channel_id=1, source_target_pairs={{1,0},{2,1},{3,2},{4,3},{5,4},{6,5},{7,6},{8,7},{9,8},{10,9},{11,1... | collective-permute-start | bytes 1572872 | tf_op jit(solution)/shard_map/ppermute | solution.py:14
  14.4 0.8 subtract_bitcast_fusion
  15.2 6.6 %collective-permute-done.1 = bf16[4,128,512]{2,1,0:T(8,128)(2,1)} collective-permute-done((bf16[4,128,512]{2,1,0:T(8,128)(2,1)}, bf16[4,128,512]{2,1,0:T(8,128)(2,1)}, u32[]{:S(2)}, u32[]{:S(2)}) %collective-permute-start.1) | collective-permute-done | bytes 524320 | tf_op jit(solution)/shard_map/ppermute | solution.py:14
  21.8 0.6 collective-permute-done
  22.4 1.5 pad_maximum_fusion.coeff_ref
  23.9 0.0 copy-done
  23.9 10.4 %shard_map.46 = bf16[1,12,4,128,512]{4,3,2,1,0:T(8,128)(2,1)} custom-call(s32[24]{0:T(128)S(1)} %get-tuple-element.13.left_ref, s32[24]{0:T(128)S(1)} %get-tuple-element.12.right_ref, s32[1]{0:T(128)S(6)} %copy.5.count_ref, bf16[24,4,128,128]{3,2,1,0:T(8,128)(2,1)S(1)} %copy-done, bf16[12,128,512]{2,1,0:T(8,128)(2,1)S(1)} %pad_maximum_fusion.coeff_ref), custom_call_target="tpu_custom_call" | custom-call | tf_op jit(solution)/shard_map/pallas_call | solution.py:113
  34.4 0.0 copy-start.1
  34.4 3.9 %slice_bitcast_fusion = (bf16[8,4,128,512]{3,2,1,0:T(8,128)(2,1)S(1)}, bf16[8,4,128,512]{3,2,1,0:T(8,128)(2,1)S(1)}) fusion(bf16[1,12,4,128,512]{4,3,2,1,0:T(8,128)(2,1)} %shard_map.46), kind=kLoop, calls=%fused_computation | loop fusion | bytes 16777216 | tf_op jit(solution)/shard_map/slice | solution.py:146
  38.3 8.6 %collective-permute-start.4 = (bf16[8,4,128,512]{3,2,1,0:T(8,128)(2,1)S(1)}, bf16[8,4,128,512]{3,2,1,0:T(8,128)(2,1)S(1)}, u32[]{:S(2)}, u32[]{:S(2)}) collective-permute-start(bf16[8,4,128,512]{3,2,1,0:T(8,128)(2,1)S(1)} %get-tuple-element.10), channel_id=1, source_target_pairs={{1,0},{2,1},{3,2},{4,3},{5,4},{6,5},{7,6},{8,7},{9,8},{10,9},{11,1... | collective-permute-start | bytes 12582920 | tf_op jit(solution)/shard_map/ppermute | solution.py:14
  46.9 1.9 collective-permute-start.3
  48.8 0.0 copy-done.1
  48.8 0.5 slice_bitcast_fusion.3
  49.3 14.4 %collective-permute-start.5 = (bf16[4,4,128,512]{3,2,1,0:T(8,128)(2,1)S(1)}, bf16[4,4,128,512]{3,2,1,0:T(8,128)(2,1)S(1)}, u32[]{:S(2)}, u32[]{:S(2)}) collective-permute-start(bf16[4,4,128,512]{3,2,1,0:T(8,128)(2,1)S(1)} %get-tuple-element.8), channel_id=1, source_target_pairs={{2,0},{3,1},{4,2},{5,3},{6,4},{7,5},{8,6},{9,7},{10,8},{11,9},{12,... | collective-permute-start | bytes 6291464 | tf_op jit(solution)/shard_map/ppermute | solution.py:14
  63.7 1.9 collective-permute-start.2
  65.6 43.5 %collective-permute-done.5 = bf16[4,4,128,512]{3,2,1,0:T(8,128)(2,1)S(1)} collective-permute-done((bf16[4,4,128,512]{3,2,1,0:T(8,128)(2,1)S(1)}, bf16[4,4,128,512]{3,2,1,0:T(8,128)(2,1)S(1)}, u32[]{:S(2)}, u32[]{:S(2)}) %collective-permute-start.5) | collective-permute-done | bytes 2097184 | tf_op jit(solution)/shard_map/ppermute | solution.py:14
  109.1 43.0 %collective-permute-done.2 = bf16[4,4,128,512]{3,2,1,0:T(8,128)(2,1)S(1)} collective-permute-done((bf16[4,4,128,512]{3,2,1,0:T(8,128)(2,1)S(1)}, bf16[4,4,128,512]{3,2,1,0:T(8,128)(2,1)S(1)}, u32[]{:S(2)}, u32[]{:S(2)}) %collective-permute-start.2) | collective-permute-done | bytes 2097184 | tf_op jit(solution)/shard_map/ppermute | solution.py:14
  152.1 0.0 collective-permute-done.4
  152.1 0.0 collective-permute-done.3
  152.1 4.4 %add_convert_fusion = (bf16[4,4,128,512]{3,2,1,0:T(8,128)(2,1)}, bf16[4,4,128,512]{3,2,1,0:T(8,128)(2,1)S(1)}, bf16[4,4,128,512]{3,2,1,0:T(8,128)(2,1)S(1)}) fusion(bf16[4,4,128,512]{3,2,1,0:T(8,128)(2,1)S(1)} %collective-permute-done.5, bf16[8,4,128,512]{3,2,1,0:T(8,128)(2,1)S(1)} %collective-permute-done.4, bf16[1,12,4,128,512]{4,3,2,1,0:T(8,128)(2,1)S(1)} %copy-done.1, ...), kind=kLoop, calls=%fused_computation.5 | loop fusion | flops 18874368 | bytes 25165824 | tf_op jit(solution)/shard_map/convert_element_type | solution.py:151
  156.5 6.9 %shard_map.47 = f32[8,24,16,128]{3,2,1,0:T(8,128)S(1)} custom-call(s32[24]{0:T(128)S(1)} %get-tuple-element.13.left_ref, s32[24]{0:T(128)S(1)} %get-tuple-element.12.right_ref, s32[1]{0:T(128)S(6)} %copy.5.count_ref, bf16[4,4,128,512]{3,2,1,0:T(8,128)(2,1)S(1)} %get-tuple-element.7.refs_0_, bf16[4,4,128,512]{3,2,1,0:T(8,128)(2,1)S(1)} %get-tuple-element.6.refs_1_, ...), custom_call_target="tpu_custom_call" | custom-call | tf_op jit(solution)/shard_map/pallas_call | solution.py:163
  163.4 42.4 %all_to_all.5 = f32[8,24,16,128]{3,2,1,0:T(8,128)S(1)} all-to-all(f32[8,24,16,128]{3,2,1,0:T(8,128)S(1)} %shard_map.47), channel_id=1, replica_groups=mesh['aux'=8,'ao'=64] {'aux'}, dimensions={0} | all-to-all | bytes 3145728 | tf_op jit(solution)/shard_map/all_to_all | solution.py:181
  205.8 0.7 fusion.4
Async XLA Ops:
  0.0 23.9 %copy-start = (bf16[24,4,128,128]{3,2,1,0:T(8,128)(2,1)S(1)}, bf16[24,4,128,128]{3,2,1,0:T(8,128)(2,1)}, u32[]{:S(2)}) copy-start(bf16[24,4,128,128]{3,2,1,0:T(8,128)(2,1)} %tile_ref.1) | copy-start | bytes 9437188
  0.0 21.8 %collective-permute-start.1 = (bf16[4,128,512]{2,1,0:T(8,128)(2,1)}, bf16[4,128,512]{2,1,0:T(8,128)(2,1)}, u32[]{:S(2)}, u32[]{:S(2)}) collective-permute-start(bf16[4,128,512]{2,1,0:T(8,128)(2,1)} %bitcast.24), channel_id=1, source_target_pairs={{2,0},{3,1},{4,2},{5,3},{6,4},{7,5},{8,6},{9,7},{10,8},{11,9},{12,... | collective-permute-start | bytes 1572872 | tf_op jit(solution)/shard_map/ppermute | solution.py:14
  10.9 11.5 %collective-permute-start = (bf16[4,128,512]{2,1,0:T(8,128)(2,1)}, bf16[4,128,512]{2,1,0:T(8,128)(2,1)}, u32[]{:S(2)}, u32[]{:S(2)}) collective-permute-start(bf16[4,128,512]{2,1,0:T(8,128)(2,1)} %bitcast.25), channel_id=1, source_target_pairs={{1,0},{2,1},{3,2},{4,3},{5,4},{6,5},{7,6},{8,7},{9,8},{10,9},{11,1... | collective-permute-start | bytes 1572872 | tf_op jit(solution)/shard_map/ppermute | solution.py:14
  34.4 14.5 %copy-start.1 = (bf16[1,12,4,128,512]{4,3,2,1,0:T(8,128)(2,1)S(1)}, bf16[1,12,4,128,512]{4,3,2,1,0:T(8,128)(2,1)}, u32[]{:S(2)}) copy-start(bf16[1,12,4,128,512]{4,3,2,1,0:T(8,128)(2,1)} %shard_map.46) | copy-start | bytes 18874372
  38.3 113.8 %collective-permute-start.4 = (bf16[8,4,128,512]{3,2,1,0:T(8,128)(2,1)S(1)}, bf16[8,4,128,512]{3,2,1,0:T(8,128)(2,1)S(1)}, u32[]{:S(2)}, u32[]{:S(2)}) collective-permute-start(bf16[8,4,128,512]{3,2,1,0:T(8,128)(2,1)S(1)} %get-tuple-element.10), channel_id=1, source_target_pairs={{1,0},{2,1},{3,2},{4,3},{5,4},{6,5},{7,6},{8,7},{9,8},{10,9},{11,1... | collective-permute-start | bytes 12582920 | tf_op jit(solution)/shard_map/ppermute | solution.py:14
  46.9 105.2 %collective-permute-start.3 = (bf16[8,4,128,512]{3,2,1,0:T(8,128)(2,1)S(1)}, bf16[8,4,128,512]{3,2,1,0:T(8,128)(2,1)S(1)}, u32[]{:S(2)}, u32[]{:S(2)}) collective-permute-start(bf16[8,4,128,512]{3,2,1,0:T(8,128)(2,1)S(1)} %get-tuple-element.11), channel_id=1, source_target_pairs={{0,1},{1,2},{2,3},{3,4},{4,5},{5,6},{6,7},{7,8},{8,9},{9,10},{10,1... | collective-permute-start | bytes 12582920 | tf_op jit(solution)/shard_map/ppermute | solution.py:14
  49.3 59.8 %collective-permute-start.5 = (bf16[4,4,128,512]{3,2,1,0:T(8,128)(2,1)S(1)}, bf16[4,4,128,512]{3,2,1,0:T(8,128)(2,1)S(1)}, u32[]{:S(2)}, u32[]{:S(2)}) collective-permute-start(bf16[4,4,128,512]{3,2,1,0:T(8,128)(2,1)S(1)} %get-tuple-element.8), channel_id=1, source_target_pairs={{2,0},{3,1},{4,2},{5,3},{6,4},{7,5},{8,6},{9,7},{10,8},{11,9},{12,... | collective-permute-start | bytes 6291464 | tf_op jit(solution)/shard_map/ppermute | solution.py:14
  63.7 88.4 %collective-permute-start.2 = (bf16[4,4,128,512]{3,2,1,0:T(8,128)(2,1)S(1)}, bf16[4,4,128,512]{3,2,1,0:T(8,128)(2,1)S(1)}, u32[]{:S(2)}, u32[]{:S(2)}) collective-permute-start(bf16[4,4,128,512]{3,2,1,0:T(8,128)(2,1)S(1)} %get-tuple-element.9), channel_id=1, source_target_pairs={{0,2},{1,3},{2,4},{3,5},{4,6},{5,7},{6,8},{7,9},{8,10},{9,11},{10,... | collective-permute-start | bytes 6291464 | tf_op jit(solution)/shard_map/ppermute | solution.py:14

commit v9 on v8

--- a/solution.py
+++ b/solution.py
@@ -79,7 +79,9 @@
                     preferred_element_type=jnp.float32,
                 )
                 total = part if total is None else total + part
-        out_ref[:, 0] = total.reshape(out_ref.shape[0], out_ref.shape[2], out_ref.shape[3])
+        out_ref[:, 0] = total.reshape(
+            out_ref.shape[0], out_ref.shape[2], out_ref.shape[3]
+        ).astype(out_ref.dtype)
 
     @pl.when(jnp.logical_not(live))
     def _():
@@ -171,7 +173,7 @@
             ),
         ),
         out_shape=jax.ShapeDtypeStruct(
-            (aux_devices, pair_slots, share, block_size), jnp.float32
+            (aux_devices, pair_slots, share, block_size), jnp.bfloat16
         ),
         compiler_params=pltpu.CompilerParams(
             dimension_semantics=("arbitrary",), vmem_limit_bytes=48 * 1024 * 1024
@@ -179,9 +181,9 @@
     )(left_rel, right_rel, count, *pieces)
 
     gathered = lax.all_to_all(partial_tiles, "aux", 0, 0, tiled=True)
-    summed = gathered[0]
+    summed = gathered[0].astype(jnp.float32)
     for source in range(1, aux_devices):
-        summed = summed + gathered[source]
+        summed = summed + gathered[source].astype(jnp.float32)
     norm_factor = (aux_local * lax.axis_size("aux") * orbitals) ** (-0.5)
     return (summed * norm_factor).astype(jnp.bfloat16)
 

time: 207 us -> 190 us (0.918)
  blocking collectives: 42.4 us -> 25.5 us
  Pallas kernels: 17.3 us -> 26.3 us
  starting transfers between devices: 40.6 us -> 31.6 us
    all_to_all x1, blocking collectives: 42.4 us -> 25.5 us  [on_device(): gathered = lax.all_to_all(partial_tiles, 'aux', 0, 0, tiled=True)]
    ppermute x6, starting transfers between devices: 40.6 us -> 31.6 us  [passed_along(): lax.ppermute(value, axis, [(source, source + steps) for source in range(f...]
    pallas_call x1, Pallas kernels: 10.4 us -> 15.4 us  [on_device(): pl.pallas_call(_half_kernel, grid_spec=pltpu.PrefetchScalarGridSpec(num_s...]
    pallas_call x1, Pallas kernels: 6.88 us -> 10.8 us  [on_device(): pl.pallas_call(_contract_kernel, grid_spec=pltpu.PrefetchScalarGridSpec(n...]
where the time goes in v9:
time: 190 us
  waiting for transfers between devices  93.7 us (49%)
  starting transfers between devices  31.6 us (17%)
  Pallas kernels  26.3 us (14%)
  blocking collectives  25.5 us (13%)
  other arithmetic  7.44 us (4%)
  local copies, waits for them, and re-layouts  4.38 us (2%)
    ppermute x6, waiting for transfers between devices, passed_along(): lax.ppermute(value, axis, [(source, source + steps) for source in range(f...  93.7 us
    ppermute x6, starting transfers between devices, passed_along(): lax.ppermute(value, axis, [(source, source + steps) for source in range(f...  31.6 us
    all_to_all x1, blocking collectives, on_device(): gathered = lax.all_to_all(partial_tiles, 'aux', 0, 0, tiled=True)  25.5 us
    pallas_call x1, Pallas kernels, on_device(): pl.pallas_call(_half_kernel, grid_spec=pltpu.PrefetchScalarGridSpec(num_s...  15.4 us
    pallas_call x1, Pallas kernels, on_device(): pl.pallas_call(_contract_kernel, grid_spec=pltpu.PrefetchScalarGridSpec(n...  10.8 us
    convert_element_type x1, other arithmetic, owner_sum(): return (total + third.astype(jnp.float32)).astype(jnp.bfloat16)  4.4 us
    slice x1, local copies, waits for them, and re-layouts, on_device(): ahead_one = passed_along(chunk[:2 * own_blocks], 'ao', -1)  3.92 us
  transfers between devices with their start and end apart: 6, of which 4 were waited for; matrix products, arithmetic and copies ran while one was open for 1% of the time, Pallas kernels for 0%

profile of v9, /device:TPU:5, one launch (start us, length us, event | category | flops | bytes accessed | tf_op | source)
XLA Modules:
  0.0 189.6 jit_solution(2167782228043837519)
XLA Ops:
  0.0 0.0 copy-start
  0.0 10.9 %collective-permute-start.1 = (bf16[4,128,512]{2,1,0:T(8,128)(2,1)}, bf16[4,128,512]{2,1,0:T(8,128)(2,1)}, u32[]{:S(2)}, u32[]{:S(2)}) collective-permute-start(bf16[4,128,512]{2,1,0:T(8,128)(2,1)} %bitcast.24), channel_id=1, source_target_pairs={{2,0},{3,1},{4,2},{5,3},{6,4},{7,5},{8,6},{9,7},{10,8},{11,9},{12,... | collective-permute-start | bytes 1572872 | tf_op jit(solution)/shard_map/ppermute | solution.py:14
  10.9 2.9 %collective-permute-start = (bf16[4,128,512]{2,1,0:T(8,128)(2,1)}, bf16[4,128,512]{2,1,0:T(8,128)(2,1)}, u32[]{:S(2)}, u32[]{:S(2)}) collective-permute-start(bf16[4,128,512]{2,1,0:T(8,128)(2,1)} %bitcast.25), channel_id=1, source_target_pairs={{1,0},{2,1},{3,2},{4,3},{5,4},{6,5},{7,6},{8,7},{9,8},{10,9},{11,1... | collective-permute-start | bytes 1572872 | tf_op jit(solution)/shard_map/ppermute | solution.py:14
  14.4 0.8 subtract_bitcast_fusion
  15.2 6.6 %collective-permute-done.1 = bf16[4,128,512]{2,1,0:T(8,128)(2,1)} collective-permute-done((bf16[4,128,512]{2,1,0:T(8,128)(2,1)}, bf16[4,128,512]{2,1,0:T(8,128)(2,1)}, u32[]{:S(2)}, u32[]{:S(2)}) %collective-permute-start.1) | collective-permute-done | bytes 524320 | tf_op jit(solution)/shard_map/ppermute | solution.py:14
  21.8 0.6 collective-permute-done
  22.4 1.5 pad_maximum_fusion.coeff_ref
  23.9 0.0 copy-done
  23.9 15.4 %shard_map.46 = bf16[1,12,4,128,512]{4,3,2,1,0:T(8,128)(2,1)} custom-call(s32[24]{0:T(128)S(1)} %get-tuple-element.13.left_ref, s32[24]{0:T(128)S(1)} %get-tuple-element.12.right_ref, s32[1]{0:T(128)S(6)} %copy.5.count_ref, bf16[24,4,128,128]{3,2,1,0:T(8,128)(2,1)S(1)} %copy-done, bf16[12,128,512]{2,1,0:T(8,128)(2,1)S(1)} %pad_maximum_fusion.coeff_ref), custom_call_target="tpu_custom_call" | custom-call | tf_op jit(solution)/shard_map/pallas_call | solution.py:115
  39.3 0.0 copy-start.1
  39.3 3.9 %slice_bitcast_fusion = (bf16[8,4,128,512]{3,2,1,0:T(8,128)(2,1)S(1)}, bf16[8,4,128,512]{3,2,1,0:T(8,128)(2,1)S(1)}) fusion(bf16[1,12,4,128,512]{4,3,2,1,0:T(8,128)(2,1)} %shard_map.46), kind=kLoop, calls=%fused_computation | loop fusion | bytes 16777216 | tf_op jit(solution)/shard_map/slice | solution.py:148
  43.3 8.6 %collective-permute-start.4 = (bf16[8,4,128,512]{3,2,1,0:T(8,128)(2,1)S(1)}, bf16[8,4,128,512]{3,2,1,0:T(8,128)(2,1)S(1)}, u32[]{:S(2)}, u32[]{:S(2)}) collective-permute-start(bf16[8,4,128,512]{3,2,1,0:T(8,128)(2,1)S(1)} %get-tuple-element.10), channel_id=1, source_target_pairs={{1,0},{2,1},{3,2},{4,3},{5,4},{6,5},{7,6},{8,7},{9,8},{10,9},{11,1... | collective-permute-start | bytes 12582920 | tf_op jit(solution)/shard_map/ppermute | solution.py:14
  51.9 1.9 %collective-permute-start.3 = (bf16[8,4,128,512]{3,2,1,0:T(8,128)(2,1)S(1)}, bf16[8,4,128,512]{3,2,1,0:T(8,128)(2,1)S(1)}, u32[]{:S(2)}, u32[]{:S(2)}) collective-permute-start(bf16[8,4,128,512]{3,2,1,0:T(8,128)(2,1)S(1)} %get-tuple-element.11), channel_id=1, source_target_pairs={{0,1},{1,2},{2,3},{3,4},{4,5},{5,6},{6,7},{7,8},{8,9},{9,10},{10,1... | collective-permute-start | bytes 12582920 | tf_op jit(solution)/shard_map/ppermute | solution.py:14
  53.8 0.0 copy-done.1
  53.8 0.5 slice_bitcast_fusion.3
  54.3 5.4 %collective-permute-start.5 = (bf16[4,4,128,512]{3,2,1,0:T(8,128)(2,1)S(1)}, bf16[4,4,128,512]{3,2,1,0:T(8,128)(2,1)S(1)}, u32[]{:S(2)}, u32[]{:S(2)}) collective-permute-start(bf16[4,4,128,512]{3,2,1,0:T(8,128)(2,1)S(1)} %get-tuple-element.8), channel_id=1, source_target_pairs={{2,0},{3,1},{4,2},{5,3},{6,4},{7,5},{8,6},{9,7},{10,8},{11,9},{12,... | collective-permute-start | bytes 6291464 | tf_op jit(solution)/shard_map/ppermute | solution.py:14
  59.7 1.9 %collective-permute-start.2 = (bf16[4,4,128,512]{3,2,1,0:T(8,128)(2,1)S(1)}, bf16[4,4,128,512]{3,2,1,0:T(8,128)(2,1)S(1)}, u32[]{:S(2)}, u32[]{:S(2)}) collective-permute-start(bf16[4,4,128,512]{3,2,1,0:T(8,128)(2,1)S(1)} %get-tuple-element.9), channel_id=1, source_target_pairs={{0,2},{1,3},{2,4},{3,5},{4,6},{5,7},{6,8},{7,9},{8,10},{9,11},{10,... | collective-permute-start | bytes 6291464 | tf_op jit(solution)/shard_map/ppermute | solution.py:14
  61.6 43.5 %collective-permute-done.5 = bf16[4,4,128,512]{3,2,1,0:T(8,128)(2,1)S(1)} collective-permute-done((bf16[4,4,128,512]{3,2,1,0:T(8,128)(2,1)S(1)}, bf16[4,4,128,512]{3,2,1,0:T(8,128)(2,1)S(1)}, u32[]{:S(2)}, u32[]{:S(2)}) %collective-permute-start.5) | collective-permute-done | bytes 2097184 | tf_op jit(solution)/shard_map/ppermute | solution.py:14
  105.1 43.0 %collective-permute-done.2 = bf16[4,4,128,512]{3,2,1,0:T(8,128)(2,1)S(1)} collective-permute-done((bf16[4,4,128,512]{3,2,1,0:T(8,128)(2,1)S(1)}, bf16[4,4,128,512]{3,2,1,0:T(8,128)(2,1)S(1)}, u32[]{:S(2)}, u32[]{:S(2)}) %collective-permute-start.2) | collective-permute-done | bytes 2097184 | tf_op jit(solution)/shard_map/ppermute | solution.py:14
  148.1 0.0 collective-permute-done.4
  148.1 0.0 collective-permute-done.3
  148.1 4.4 %add_convert_fusion = (bf16[4,4,128,512]{3,2,1,0:T(8,128)(2,1)}, bf16[4,4,128,512]{3,2,1,0:T(8,128)(2,1)S(1)}, bf16[4,4,128,512]{3,2,1,0:T(8,128)(2,1)S(1)}) fusion(bf16[4,4,128,512]{3,2,1,0:T(8,128)(2,1)S(1)} %collective-permute-done.5, bf16[8,4,128,512]{3,2,1,0:T(8,128)(2,1)S(1)} %collective-permute-done.4, bf16[1,12,4,128,512]{4,3,2,1,0:T(8,128)(2,1)S(1)} %copy-done.1, ...), kind=kLoop, calls=%fused_computation.5 | loop fusion | flops 18874368 | bytes 25165824 | tf_op jit(solution)/shard_map/convert_element_type | solution.py:153
  152.5 10.8 %shard_map.47 = bf16[8,24,16,128]{3,2,1,0:T(8,128)(2,1)S(1)} custom-call(s32[24]{0:T(128)S(1)} %get-tuple-element.13.left_ref, s32[24]{0:T(128)S(1)} %get-tuple-element.12.right_ref, s32[1]{0:T(128)S(6)} %copy.5.count_ref, bf16[4,4,128,512]{3,2,1,0:T(8,128)(2,1)S(1)} %get-tuple-element.7.refs_0_, bf16[4,4,128,512]{3,2,1,0:T(8,128)(2,1)S(1)} %get-tuple-element.6.refs_1_, ...), custom_call_target="tpu_custom_call" | custom-call | tf_op jit(solution)/shard_map/pallas_call | solution.py:165
  163.4 25.5 %all_to_all.5 = bf16[8,24,16,128]{3,2,1,0:T(8,128)(2,1)S(1)} all-to-all(bf16[8,24,16,128]{3,2,1,0:T(8,128)(2,1)S(1)} %shard_map.47), channel_id=1, replica_groups=mesh['aux'=8,'ao'=64] {'aux'}, dimensions={0} | all-to-all | bytes 1572864 | tf_op jit(solution)/shard_map/all_to_all | solution.py:183
  188.9 0.8 fusion.2
Async XLA Ops:
  0.0 23.9 %copy-start = (bf16[24,4,128,128]{3,2,1,0:T(8,128)(2,1)S(1)}, bf16[24,4,128,128]{3,2,1,0:T(8,128)(2,1)}, u32[]{:S(2)}) copy-start(bf16[24,4,128,128]{3,2,1,0:T(8,128)(2,1)} %tile_ref.1) | copy-start | bytes 9437188
  0.0 21.8 %collective-permute-start.1 = (bf16[4,128,512]{2,1,0:T(8,128)(2,1)}, bf16[4,128,512]{2,1,0:T(8,128)(2,1)}, u32[]{:S(2)}, u32[]{:S(2)}) collective-permute-start(bf16[4,128,512]{2,1,0:T(8,128)(2,1)} %bitcast.24), channel_id=1, source_target_pairs={{2,0},{3,1},{4,2},{5,3},{6,4},{7,5},{8,6},{9,7},{10,8},{11,9},{12,... | collective-permute-start | bytes 1572872 | tf_op jit(solution)/shard_map/ppermute | solution.py:14
  10.9 11.5 %collective-permute-start = (bf16[4,128,512]{2,1,0:T(8,128)(2,1)}, bf16[4,128,512]{2,1,0:T(8,128)(2,1)}, u32[]{:S(2)}, u32[]{:S(2)}) collective-permute-start(bf16[4,128,512]{2,1,0:T(8,128)(2,1)} %bitcast.25), channel_id=1, source_target_pairs={{1,0},{2,1},{3,2},{4,3},{5,4},{6,5},{7,6},{8,7},{9,8},{10,9},{11,1... | collective-permute-start | bytes 1572872 | tf_op jit(solution)/shard_map/ppermute | solution.py:14
  39.3 14.5 %copy-start.1 = (bf16[1,12,4,128,512]{4,3,2,1,0:T(8,128)(2,1)S(1)}, bf16[1,12,4,128,512]{4,3,2,1,0:T(8,128)(2,1)}, u32[]{:S(2)}) copy-start(bf16[1,12,4,128,512]{4,3,2,1,0:T(8,128)(2,1)} %shard_map.46) | copy-start | bytes 18874372
  43.3 104.8 %collective-permute-start.4 = (bf16[8,4,128,512]{3,2,1,0:T(8,128)(2,1)S(1)}, bf16[8,4,128,512]{3,2,1,0:T(8,128)(2,1)S(1)}, u32[]{:S(2)}, u32[]{:S(2)}) collective-permute-start(bf16[8,4,128,512]{3,2,1,0:T(8,128)(2,1)S(1)} %get-tuple-element.10), channel_id=1, source_target_pairs={{1,0},{2,1},{3,2},{4,3},{5,4},{6,5},{7,6},{8,7},{9,8},{10,9},{11,1... | collective-permute-start | bytes 12582920 | tf_op jit(solution)/shard_map/ppermute | solution.py:14
  51.9 96.2 %collective-permute-start.3 = (bf16[8,4,128,512]{3,2,1,0:T(8,128)(2,1)S(1)}, bf16[8,4,128,512]{3,2,1,0:T(8,128)(2,1)S(1)}, u32[]{:S(2)}, u32[]{:S(2)}) collective-permute-start(bf16[8,4,128,512]{3,2,1,0:T(8,128)(2,1)S(1)} %get-tuple-element.11), channel_id=1, source_target_pairs={{0,1},{1,2},{2,3},{3,4},{4,5},{5,6},{6,7},{7,8},{8,9},{9,10},{10,1... | collective-permute-start | bytes 12582920 | tf_op jit(solution)/shard_map/ppermute | solution.py:14
  54.3 50.8 %collective-permute-start.5 = (bf16[4,4,128,512]{3,2,1,0:T(8,128)(2,1)S(1)}, bf16[4,4,128,512]{3,2,1,0:T(8,128)(2,1)S(1)}, u32[]{:S(2)}, u32[]{:S(2)}) collective-permute-start(bf16[4,4,128,512]{3,2,1,0:T(8,128)(2,1)S(1)} %get-tuple-element.8), channel_id=1, source_target_pairs={{2,0},{3,1},{4,2},{5,3},{6,4},{7,5},{8,6},{9,7},{10,8},{11,9},{12,... | collective-permute-start | bytes 6291464 | tf_op jit(solution)/shard_map/ppermute | solution.py:14
  59.7 88.4 %collective-permute-start.2 = (bf16[4,4,128,512]{3,2,1,0:T(8,128)(2,1)S(1)}, bf16[4,4,128,512]{3,2,1,0:T(8,128)(2,1)S(1)}, u32[]{:S(2)}, u32[]{:S(2)}) collective-permute-start(bf16[4,4,128,512]{3,2,1,0:T(8,128)(2,1)S(1)} %get-tuple-element.9), channel_id=1, source_target_pairs={{0,2},{1,3},{2,4},{3,5},{4,6},{5,7},{6,8},{7,9},{8,10},{9,11},{10,... | collective-permute-start | bytes 6291464 | tf_op jit(solution)/shard_map/ppermute | solution.py:14

commit v10 on v9

--- a/solution.py
+++ b/solution.py
@@ -140,13 +140,22 @@
     )(left_rel, right_rel, count, tiles, window_coeff)
 
     block_shape = (own_blocks, aux_local, block_size, width)
+    is_even = (owner_index % 2) == 0
+    even_up_two = [(s, s + 2) for s in range(0, devices - 2, 2)]
+    odd_down_two = [(s, s - 2) for s in range(3, devices, 2)]
+    even_up_one = [(s, s + 1) for s in range(0, devices - 1, 2)]
+    odd_down_one = [(s, s - 1) for s in range(1, devices, 2)]
     pieces = []
     for c in range(CHUNKS):
         chunk = halves[c]
-        behind_two = passed_along(chunk[2 * own_blocks :], "ao", 2)
         behind_one = passed_along(chunk[own_blocks:], "ao", 1)
         ahead_one = passed_along(chunk[: 2 * own_blocks], "ao", -1)
-        ahead_two = passed_along(chunk[:own_blocks], "ao", -2)
+        even_two = lax.ppermute(chunk[2 * own_blocks :], "ao", even_up_two)
+        odd_two = lax.ppermute(chunk[:own_blocks], "ao", odd_down_two)
+        relay_behind = lax.ppermute(behind_one[own_blocks:], "ao", even_up_one)
+        relay_ahead = lax.ppermute(ahead_one[:own_blocks], "ao", odd_down_one)
+        behind_two = jnp.where(is_even, even_two, relay_behind)
+        ahead_two = jnp.where(is_even, relay_ahead, odd_two)
 
         def owner_sum(first, second, third):
             total = first.astype(jnp.float32) + second.astype(jnp.float32)

time: 190 us -> 186 us (0.979)
  the two profiles are of different devices: /device:TPU:5 before, /device:TPU:2 now
where the time goes in v10:
time: 186 us
  waiting for transfers between devices  79.4 us (43%)
  starting transfers between devices  29.3 us (16%)
  blocking collectives  26.9 us (14%)
  Pallas kernels  25.7 us (14%)
  other arithmetic  12.5 us (7%)
  local copies, waits for them, and re-layouts  11.1 us (6%)
    ppermute x4, waiting for transfers between devices, passed_along(): lax.ppermute(value, axis, [(source, source + steps) for source in range(f...  76.7 us
    all_to_all x1, blocking collectives, on_device(): gathered = lax.all_to_all(partial_tiles, 'aux', 0, 0, tiled=True)  26.9 us
    ppermute x4, starting transfers between devices, passed_along(): lax.ppermute(value, axis, [(source, source + steps) for source in range(f...  21.1 us
    pallas_call x1, Pallas kernels, on_device(): pl.pallas_call(_half_kernel, grid_spec=pltpu.PrefetchScalarGridSpec(num_s...  15.4 us
    pallas_call x1, Pallas kernels, on_device(): pl.pallas_call(_contract_kernel, grid_spec=pltpu.PrefetchScalarGridSpec(n...  10.3 us
    convert_element_type x1, other arithmetic, owner_sum(): return (total + third.astype(jnp.float32)).astype(jnp.bfloat16)  9.48 us
    slice x1, local copies, waits for them, and re-layouts, on_device(): ahead_one = passed_along(chunk[:2 * own_blocks], 'ao', -1)  3.96 us
  transfers between devices with their start and end apart: 8, of which 5 were waited for; matrix products, arithmetic and copies ran while one was open for 3% of the time, Pallas kernels for 0%

profile of v10, /device:TPU:2, one launch (start us, length us, event | category | flops | bytes accessed | tf_op | source)
XLA Modules:
  0.0 185.7 jit_solution(17989601620358175247)
XLA Ops:
  0.0 0.0 copy-start
  0.0 11.2 %collective-permute-start.1 = (bf16[4,128,512]{2,1,0:T(8,128)(2,1)}, bf16[4,128,512]{2,1,0:T(8,128)(2,1)}, u32[]{:S(2)}, u32[]{:S(2)}) collective-permute-start(bf16[4,128,512]{2,1,0:T(8,128)(2,1)} %bitcast.24), channel_id=1, source_target_pairs={{2,0},{3,1},{4,2},{5,3},{6,4},{7,5},{8,6},{9,7},{10,8},{11,9},{12,... | collective-permute-start | bytes 1572872 | tf_op jit(solution)/shard_map/ppermute | solution.py:14
  11.2 1.9 %collective-permute-start = (bf16[4,128,512]{2,1,0:T(8,128)(2,1)}, bf16[4,128,512]{2,1,0:T(8,128)(2,1)}, u32[]{:S(2)}, u32[]{:S(2)}) collective-permute-start(bf16[4,128,512]{2,1,0:T(8,128)(2,1)} %bitcast.25), channel_id=1, source_target_pairs={{1,0},{2,1},{3,2},{4,3},{5,4},{6,5},{7,6},{8,7},{9,8},{10,9},{11,1... | collective-permute-start | bytes 1572872 | tf_op jit(solution)/shard_map/ppermute | solution.py:14
  13.8 0.8 subtract_bitcast_fusion
  14.5 8.1 %collective-permute-done.1 = bf16[4,128,512]{2,1,0:T(8,128)(2,1)} collective-permute-done((bf16[4,128,512]{2,1,0:T(8,128)(2,1)}, bf16[4,128,512]{2,1,0:T(8,128)(2,1)}, u32[]{:S(2)}, u32[]{:S(2)}) %collective-permute-start.1) | collective-permute-done | bytes 524320 | tf_op jit(solution)/shard_map/ppermute | solution.py:14
  22.7 5.6 %collective-permute-done = bf16[4,128,512]{2,1,0:T(8,128)(2,1)} collective-permute-done((bf16[4,128,512]{2,1,0:T(8,128)(2,1)}, bf16[4,128,512]{2,1,0:T(8,128)(2,1)}, u32[]{:S(2)}, u32[]{:S(2)}) %collective-permute-start) | collective-permute-done | bytes 524320 | tf_op jit(solution)/shard_map/ppermute | solution.py:14
  28.3 1.5 pad_maximum_fusion.coeff_ref
  29.8 0.0 copy-done
  29.8 15.4 %shard_map.46 = bf16[1,12,4,128,512]{4,3,2,1,0:T(8,128)(2,1)} custom-call(s32[24]{0:T(128)S(1)} %get-tuple-element.13.left_ref, s32[24]{0:T(128)S(1)} %get-tuple-element.12.right_ref, s32[1]{0:T(128)S(6)} %copy.5.count_ref, bf16[24,4,128,128]{3,2,1,0:T(8,128)(2,1)S(1)} %copy-done, bf16[12,128,512]{2,1,0:T(8,128)(2,1)S(1)} %pad_maximum_fusion.coeff_ref), custom_call_target="tpu_custom_call" | custom-call | tf_op jit(solution)/shard_map/pallas_call | solution.py:115
  45.2 4.0 %slice_bitcast_fusion = (bf16[8,4,128,512]{3,2,1,0:T(8,128)(2,1)S(1)}, bf16[8,4,128,512]{3,2,1,0:T(8,128)(2,1)S(1)}) fusion(bf16[1,12,4,128,512]{4,3,2,1,0:T(8,128)(2,1)} %shard_map.46), kind=kLoop, calls=%fused_computation | loop fusion | bytes 16777216 | tf_op jit(solution)/shard_map/slice | solution.py:152
  49.2 6.1 %collective-permute-start.5 = (bf16[8,4,128,512]{3,2,1,0:T(8,128)(2,1)S(1)}, bf16[8,4,128,512]{3,2,1,0:T(8,128)(2,1)S(1)}, u32[]{:S(2)}, u32[]{:S(2)}) collective-permute-start(bf16[8,4,128,512]{3,2,1,0:T(8,128)(2,1)S(1)} %get-tuple-element.10), channel_id=1, source_target_pairs={{1,0},{2,1},{3,2},{4,3},{5,4},{6,5},{7,6},{8,7},{9,8},{10,9},{11,1... | collective-permute-start | bytes 12582920 | tf_op jit(solution)/shard_map/ppermute | solution.py:14
  55.3 1.9 %collective-permute-start.3 = (bf16[8,4,128,512]{3,2,1,0:T(8,128)(2,1)S(1)}, bf16[8,4,128,512]{3,2,1,0:T(8,128)(2,1)S(1)}, u32[]{:S(2)}, u32[]{:S(2)}) collective-permute-start(bf16[8,4,128,512]{3,2,1,0:T(8,128)(2,1)S(1)} %get-tuple-element.11), channel_id=1, source_target_pairs={{0,1},{1,2},{2,3},{3,4},{4,5},{5,6},{6,7},{7,8},{8,9},{9,10},{10,1... | collective-permute-start | bytes 12582920 | tf_op jit(solution)/shard_map/ppermute | solution.py:14
  57.2 0.0 copy-done.1
  57.2 2.3 %slice_bitcast_fusion.3 = (bf16[4,4,128,512]{3,2,1,0:T(8,128)(2,1)}, bf16[4,4,128,512]{3,2,1,0:T(8,128)(2,1)}) fusion(bf16[1,12,4,128,512]{4,3,2,1,0:T(8,128)(2,1)S(1)} %copy-done.1), kind=kLoop, calls=%fused_computation.8 | loop fusion | bytes 8388608 | tf_op jit(solution)/shard_map/slice | solution.py:165
  59.5 2.0 %collective-permute-start.7 = (bf16[4,4,128,512]{3,2,1,0:T(8,128)(2,1)}, bf16[4,4,128,512]{3,2,1,0:T(8,128)(2,1)}, u32[]{:S(2)}, u32[]{:S(2)}) collective-permute-start(bf16[4,4,128,512]{3,2,1,0:T(8,128)(2,1)} %get-tuple-element.8), channel_id=1, source_target_pairs={{3,1},{5,3},{7,5},{9,7},{11,9},{13,11},{15,13},{17,15},{19,17},{21... | collective-permute-start | bytes 6291464 | tf_op jit(solution)/shard_map/ppermute | solution.py:154
  61.5 1.9 %collective-permute-start.2 = (bf16[4,4,128,512]{3,2,1,0:T(8,128)(2,1)}, bf16[4,4,128,512]{3,2,1,0:T(8,128)(2,1)}, u32[]{:S(2)}, u32[]{:S(2)}) collective-permute-start(bf16[4,4,128,512]{3,2,1,0:T(8,128)(2,1)} %get-tuple-element.9), channel_id=1, source_target_pairs={{0,2},{2,4},{4,6},{6,8},{8,10},{10,12},{12,14},{14,16},{16,18},{18... | collective-permute-start | bytes 6291464 | tf_op jit(solution)/shard_map/ppermute | solution.py:153
  63.4 60.3 %collective-permute-done.5 = bf16[8,4,128,512]{3,2,1,0:T(8,128)(2,1)S(1)} collective-permute-done((bf16[8,4,128,512]{3,2,1,0:T(8,128)(2,1)S(1)}, bf16[8,4,128,512]{3,2,1,0:T(8,128)(2,1)S(1)}, u32[]{:S(2)}, u32[]{:S(2)}) %collective-permute-start.5) | collective-permute-done | bytes 4194336 | tf_op jit(solution)/shard_map/ppermute | solution.py:14
  123.8 0.1 slice.104
  123.9 1.9 %copy-done.2 = bf16[8,4,128,512]{3,2,1,0:T(8,128)(2,1)} copy-done((bf16[8,4,128,512]{3,2,1,0:T(8,128)(2,1)}, bf16[8,4,128,512]{3,2,1,0:T(8,128)(2,1)S(1)}, u32[]{:S(2)}) %copy-start.2) | copy-done | bytes 4194328
  125.8 1.3 collective-permute-start.6
  127.1 2.6 %collective-permute-done.3 = bf16[8,4,128,512]{3,2,1,0:T(8,128)(2,1)S(1)} collective-permute-done((bf16[8,4,128,512]{3,2,1,0:T(8,128)(2,1)S(1)}, bf16[8,4,128,512]{3,2,1,0:T(8,128)(2,1)S(1)}, u32[]{:S(2)}, u32[]{:S(2)}) %collective-permute-start.3) | collective-permute-done | bytes 4194336 | tf_op jit(solution)/shard_map/ppermute | solution.py:14
  129.7 1.6 slice.99
  131.3 1.2 copy-done.3
  132.5 3.1 %collective-permute-start.4 = (bf16[4,4,128,512]{3,2,1,0:T(8,128)(2,1)}, bf16[4,4,128,512]{3,2,1,0:T(8,128)(2,1)}, u32[]{:S(2)}, u32[]{:S(2)}) collective-permute-start(bf16[4,4,128,512]{3,2,1,0:T(8,128)(2,1)} %slice.99), channel_id=1, source_target_pairs={{0,1},{2,3},{4,5},{6,7},{8,9},{10,11},{12,13},{14,15},{16,17},{18,... | collective-permute-start | bytes 6291464 | tf_op jit(solution)/shard_map/ppermute | solution.py:155
  135.5 0.0 collective-permute-done.7
  135.5 0.0 collective-permute-done.2
  135.5 0.0 collective-permute-done.6
  135.5 2.8 %collective-permute-done.4 = bf16[4,4,128,512]{3,2,1,0:T(8,128)(2,1)} collective-permute-done((bf16[4,4,128,512]{3,2,1,0:T(8,128)(2,1)}, bf16[4,4,128,512]{3,2,1,0:T(8,128)(2,1)}, u32[]{:S(2)}, u32[]{:S(2)}) %collective-permute-start.4) | collective-permute-done | bytes 2097184 | tf_op jit(solution)/shard_map/ppermute | solution.py:155
  138.3 9.5 %add_convert_fusion = (bf16[4,4,128,512]{3,2,1,0:T(8,128)(2,1)}, bf16[4,4,128,512]{3,2,1,0:T(8,128)(2,1)S(1)}, bf16[4,4,128,512]{3,2,1,0:T(8,128)(2,1)S(1)}) fusion(bf16[8,4,128,512]{3,2,1,0:T(8,128)(2,1)} %copy-done.2, bf16[4,4,128,512]{3,2,1,0:T(8,128)(2,1)} %collective-permute-done.6, bf16[4,4,128,512]{3,2,1,0:T(8,128)(2,1)} %collective-permute-done.7, ...), kind=kLoop, calls=%fused_computation.5 | loop fusion | flops 20971520 | bytes 29360128 | tf_op jit(solution)/shard_map/convert_element_type | solution.py:162
  147.8 10.3 %shard_map.47 = bf16[8,24,16,128]{3,2,1,0:T(8,128)(2,1)S(1)} custom-call(s32[24]{0:T(128)S(1)} %get-tuple-element.13.left_ref, s32[24]{0:T(128)S(1)} %get-tuple-element.12.right_ref, s32[1]{0:T(128)S(6)} %copy.5.count_ref, bf16[4,4,128,512]{3,2,1,0:T(8,128)(2,1)S(1)} %get-tuple-element.7.refs_0_, bf16[4,4,128,512]{3,2,1,0:T(8,128)(2,1)S(1)} %get-tuple-element.6.refs_1_, ...), custom_call_target="tpu_custom_call" | custom-call | tf_op jit(solution)/shard_map/pallas_call | solution.py:174
  158.1 26.9 %all_to_all.5 = bf16[8,24,16,128]{3,2,1,0:T(8,128)(2,1)S(1)} all-to-all(bf16[8,24,16,128]{3,2,1,0:T(8,128)(2,1)S(1)} %shard_map.47), channel_id=1, replica_groups=mesh['aux'=8,'ao'=64] {'aux'}, dimensions={0} | all-to-all | bytes 1572864 | tf_op jit(solution)/shard_map/all_to_all | solution.py:192
  184.9 0.8 fusion.2
  (3 shorter events, 0.0 us)
Async XLA Ops:
  0.0 29.8 %copy-start = (bf16[24,4,128,128]{3,2,1,0:T(8,128)(2,1)S(1)}, bf16[24,4,128,128]{3,2,1,0:T(8,128)(2,1)}, u32[]{:S(2)}) copy-start(bf16[24,4,128,128]{3,2,1,0:T(8,128)(2,1)} %tile_ref.1) | copy-start | bytes 9437188
  0.0 22.7 %collective-permute-start.1 = (bf16[4,128,512]{2,1,0:T(8,128)(2,1)}, bf16[4,128,512]{2,1,0:T(8,128)(2,1)}, u32[]{:S(2)}, u32[]{:S(2)}) collective-permute-start(bf16[4,128,512]{2,1,0:T(8,128)(2,1)} %bitcast.24), channel_id=1, source_target_pairs={{2,0},{3,1},{4,2},{5,3},{6,4},{7,5},{8,6},{9,7},{10,8},{11,9},{12,... | collective-permute-start | bytes 1572872 | tf_op jit(solution)/shard_map/ppermute | solution.py:14
  11.2 17.1 %collective-permute-start = (bf16[4,128,512]{2,1,0:T(8,128)(2,1)}, bf16[4,128,512]{2,1,0:T(8,128)(2,1)}, u32[]{:S(2)}, u32[]{:S(2)}) collective-permute-start(bf16[4,128,512]{2,1,0:T(8,128)(2,1)} %bitcast.25), channel_id=1, source_target_pairs={{1,0},{2,1},{3,2},{4,3},{5,4},{6,5},{7,6},{8,7},{9,8},{10,9},{11,1... | collective-permute-start | bytes 1572872 | tf_op jit(solution)/shard_map/ppermute | solution.py:14
  45.2 12.0 %copy-start.1 = (bf16[1,12,4,128,512]{4,3,2,1,0:T(8,128)(2,1)S(1)}, bf16[1,12,4,128,512]{4,3,2,1,0:T(8,128)(2,1)}, u32[]{:S(2)}) copy-start(bf16[1,12,4,128,512]{4,3,2,1,0:T(8,128)(2,1)} %shard_map.46) | copy-start | bytes 18874372
  49.2 74.5 %collective-permute-start.5 = (bf16[8,4,128,512]{3,2,1,0:T(8,128)(2,1)S(1)}, bf16[8,4,128,512]{3,2,1,0:T(8,128)(2,1)S(1)}, u32[]{:S(2)}, u32[]{:S(2)}) collective-permute-start(bf16[8,4,128,512]{3,2,1,0:T(8,128)(2,1)S(1)} %get-tuple-element.10), channel_id=1, source_target_pairs={{1,0},{2,1},{3,2},{4,3},{5,4},{6,5},{7,6},{8,7},{9,8},{10,9},{11,1... | collective-permute-start | bytes 12582920 | tf_op jit(solution)/shard_map/ppermute | solution.py:14
  55.3 74.4 %collective-permute-start.3 = (bf16[8,4,128,512]{3,2,1,0:T(8,128)(2,1)S(1)}, bf16[8,4,128,512]{3,2,1,0:T(8,128)(2,1)S(1)}, u32[]{:S(2)}, u32[]{:S(2)}) collective-permute-start(bf16[8,4,128,512]{3,2,1,0:T(8,128)(2,1)S(1)} %get-tuple-element.11), channel_id=1, source_target_pairs={{0,1},{1,2},{2,3},{3,4},{4,5},{5,6},{6,7},{7,8},{8,9},{9,10},{10,1... | collective-permute-start | bytes 12582920 | tf_op jit(solution)/shard_map/ppermute | solution.py:14
  59.5 76.0 %collective-permute-start.7 = (bf16[4,4,128,512]{3,2,1,0:T(8,128)(2,1)}, bf16[4,4,128,512]{3,2,1,0:T(8,128)(2,1)}, u32[]{:S(2)}, u32[]{:S(2)}) collective-permute-start(bf16[4,4,128,512]{3,2,1,0:T(8,128)(2,1)} %get-tuple-element.8), channel_id=1, source_target_pairs={{3,1},{5,3},{7,5},{9,7},{11,9},{13,11},{15,13},{17,15},{19,17},{21... | collective-permute-start | bytes 6291464 | tf_op jit(solution)/shard_map/ppermute | solution.py:154
  61.5 74.0 %collective-permute-start.2 = (bf16[4,4,128,512]{3,2,1,0:T(8,128)(2,1)}, bf16[4,4,128,512]{3,2,1,0:T(8,128)(2,1)}, u32[]{:S(2)}, u32[]{:S(2)}) collective-permute-start(bf16[4,4,128,512]{3,2,1,0:T(8,128)(2,1)} %get-tuple-element.9), channel_id=1, source_target_pairs={{0,2},{2,4},{4,6},{6,8},{8,10},{10,12},{12,14},{14,16},{16,18},{18... | collective-permute-start | bytes 6291464 | tf_op jit(solution)/shard_map/ppermute | solution.py:153
  123.8 2.0 %copy-start.2 = (bf16[8,4,128,512]{3,2,1,0:T(8,128)(2,1)}, bf16[8,4,128,512]{3,2,1,0:T(8,128)(2,1)S(1)}, u32[]{:S(2)}) copy-start(bf16[8,4,128,512]{3,2,1,0:T(8,128)(2,1)S(1)} %collective-permute-done.5) | copy-start | bytes 12582916
  125.8 9.8 %collective-permute-start.6 = (bf16[4,4,128,512]{3,2,1,0:T(8,128)(2,1)S(1)}, bf16[4,4,128,512]{3,2,1,0:T(8,128)(2,1)}, u32[]{:S(2)}, u32[]{:S(2)}) collective-permute-start(bf16[4,4,128,512]{3,2,1,0:T(8,128)(2,1)S(1)} %slice.104), channel_id=1, source_target_pairs={{1,0},{3,2},{5,4},{7,6},{9,8},{11,10},{13,12},{15,14},{17,16},{19,... | collective-permute-start | bytes 6291464 | tf_op jit(solution)/shard_map/ppermute | solution.py:156
  129.7 2.8 %copy-start.3 = (bf16[8,4,128,512]{3,2,1,0:T(8,128)(2,1)}, bf16[8,4,128,512]{3,2,1,0:T(8,128)(2,1)S(1)}, u32[]{:S(2)}) copy-start(bf16[8,4,128,512]{3,2,1,0:T(8,128)(2,1)S(1)} %collective-permute-done.3) | copy-start | bytes 12582916
  132.5 5.8 %collective-permute-start.4 = (bf16[4,4,128,512]{3,2,1,0:T(8,128)(2,1)}, bf16[4,4,128,512]{3,2,1,0:T(8,128)(2,1)}, u32[]{:S(2)}, u32[]{:S(2)}) collective-permute-start(bf16[4,4,128,512]{3,2,1,0:T(8,128)(2,1)} %slice.99), channel_id=1, source_target_pairs={{0,1},{2,3},{4,5},{6,7},{8,9},{10,11},{12,13},{14,15},{16,17},{18,... | collective-permute-start | bytes 6291464 | tf_op jit(solution)/shard_map/ppermute | solution.py:155

commit v11 on v10

--- a/solution.py
+++ b/solution.py
@@ -14,8 +14,9 @@
     return lax.ppermute(value, axis, [(source, source + steps) for source in range(first, last)])
 
 
-def _half_kernel(left_ref, right_ref, count_ref, tile_ref, coeff_ref, out_ref, acc_ref):
+def _right_kernel(left_ref, right_ref, count_ref, tile_ref, coeff_ref, hi_ref, part_ref, acc_ref):
     slot = pl.program_id(0)
+    own_blocks = part_ref.shape[0]
 
     @pl.when(slot == 0)
     def _():
@@ -23,33 +24,48 @@
 
     @pl.when(slot < count_ref[0])
     def _():
-        left = left_ref[slot]
-        right = right_ref[slot]
         tile = tile_ref[0]
-        aux_local, block_size, _ = tile.shape
-        right_coeff = coeff_ref[right]
-        left_coeff = coeff_ref[left]
-        to_left = jnp.dot(
-            tile.reshape(aux_local * block_size, block_size),
-            right_coeff,
-            preferred_element_type=jnp.float32,
-        ).reshape(aux_local, block_size, -1)
-        acc_ref[left] += to_left
+        left_coeff = coeff_ref[left_ref[slot]]
         parts = [
             lax.dot_general(
                 tile[p], left_coeff, (((0,), (0,)), ((), ())),
                 preferred_element_type=jnp.float32,
             )
-            for p in range(aux_local)
+            for p in range(tile.shape[0])
         ]
+        right = right_ref[slot]
         acc_ref[right] += jnp.stack(parts, 0)
 
     @pl.when(slot == pl.num_programs(0) - 1)
     def _():
-        chunks = out_ref.shape[0]
-        width = out_ref.shape[-1]
-        for c in range(chunks):
-            out_ref[c] = acc_ref[:, :, :, c * width : (c + 1) * width].astype(out_ref.dtype)
+        part_ref[...] = acc_ref[:own_blocks]
+        hi_ref[...] = acc_ref[own_blocks:].astype(hi_ref.dtype)
+
+
+def _left_kernel(left_ref, right_ref, count_ref, tile_ref, coeff_ref, part_ref, hi_ref, lo_ref, acc_ref):
+    slot = pl.program_id(0)
+    own_blocks = part_ref.shape[0]
+
+    @pl.when(slot == 0)
+    def _():
+        acc_ref[...] = part_ref[...]
+
+    @pl.when(slot < count_ref[0])
+    def _():
+        tile = tile_ref[0]
+        aux_local, block_size, _ = tile.shape
+        to_left = jnp.dot(
+            tile.reshape(aux_local * block_size, block_size),
+            coeff_ref[right_ref[slot]],
+            preferred_element_type=jnp.float32,
+        ).reshape(aux_local, block_size, -1)
+        left = left_ref[slot]
+        acc_ref[left] += to_left
+
+    @pl.when(slot == pl.num_programs(0) - 1)
+    def _():
+        lo_ref[:own_blocks] = acc_ref[...].astype(lo_ref.dtype)
+        lo_ref[own_blocks:] = hi_ref[:own_blocks]
 
 
 def _contract_kernel(left_ref, right_ref, count_ref, *refs):
@@ -107,51 +123,65 @@
     count = pair_count.astype(jnp.int32)
     own_coeff = coeff.reshape(own_blocks, block_size, orbitals)
     ahead_coeff = [passed_along(own_coeff, "ao", -distance) for distance in range(1, BAND + 1)]
-    window_coeff = jnp.concatenate([own_coeff] + ahead_coeff, 0)
 
     def tile_map(slot, left, right, cnt):
         return (jnp.minimum(slot, jnp.maximum(cnt[0] - 1, 0)), 0, 0, 0)
 
-    halves = pl.pallas_call(
-        _half_kernel,
+    def fixed(shape):
+        return pl.BlockSpec(shape, lambda s, l, r, c: (0,) * len(shape))
+
+    tile_spec = pl.BlockSpec((1, aux_local, block_size, block_size), tile_map)
+    own_shape = (own_blocks, aux_local, block_size, orbitals)
+    wide_shape = (2 * own_blocks, aux_local, block_size, orbitals)
+    params = pltpu.CompilerParams(
+        dimension_semantics=("arbitrary",), vmem_limit_bytes=48 * 1024 * 1024
+    )
+    hi, part = pl.pallas_call(
+        _right_kernel,
+        grid_spec=pltpu.PrefetchScalarGridSpec(
+            num_scalar_prefetch=3,
+            grid=(pair_slots,),
+            in_specs=[tile_spec, fixed((own_blocks, block_size, orbitals))],
+            out_specs=[fixed(wide_shape), fixed(own_shape)],
+            scratch_shapes=[pltpu.VMEM((window_blocks,) + own_shape[1:], jnp.float32)],
+        ),
+        out_shape=[
+            jax.ShapeDtypeStruct(wide_shape, jnp.bfloat16),
+            jax.ShapeDtypeStruct(own_shape, jnp.float32),
+        ],
+        compiler_params=params,
+    )(left_rel, right_rel, count, tiles, own_coeff)
+    window_coeff = jnp.concatenate([own_coeff] + ahead_coeff, 0)
+    lo = pl.pallas_call(
+        _left_kernel,
         grid_spec=pltpu.PrefetchScalarGridSpec(
             num_scalar_prefetch=3,
             grid=(pair_slots,),
             in_specs=[
-                pl.BlockSpec((1, aux_local, block_size, block_size), tile_map),
-                pl.BlockSpec(
-                    (window_blocks, block_size, orbitals), lambda s, l, r, c: (0, 0, 0)
-                ),
+                tile_spec,
+                fixed((window_blocks, block_size, orbitals)),
+                fixed(own_shape),
+                fixed(wide_shape),
             ],
-            out_specs=pl.BlockSpec(
-                (CHUNKS, window_blocks, aux_local, block_size, width),
-                lambda s, l, r, c: (0, 0, 0, 0, 0),
-            ),
-            scratch_shapes=[
-                pltpu.VMEM((window_blocks, aux_local, block_size, orbitals), jnp.float32)
-            ],
-        ),
-        out_shape=jax.ShapeDtypeStruct(
-            (CHUNKS, window_blocks, aux_local, block_size, width), jnp.bfloat16
-        ),
-        compiler_params=pltpu.CompilerParams(
-            dimension_semantics=("arbitrary",), vmem_limit_bytes=48 * 1024 * 1024
-        ),
-    )(left_rel, right_rel, count, tiles, window_coeff)
-
-    block_shape = (own_blocks, aux_local, block_size, width)
+            out_specs=fixed(wide_shape),
+            scratch_shapes=[pltpu.VMEM(own_shape, jnp.float32)],
+        ),
+        out_shape=jax.ShapeDtypeStruct(wide_shape, jnp.bfloat16),
+        compiler_params=params,
+    )(left_rel, right_rel, count, tiles, window_coeff, part, hi)
+
+    block_shape = own_shape
     is_even = (owner_index % 2) == 0
     even_up_two = [(s, s + 2) for s in range(0, devices - 2, 2)]
     odd_down_two = [(s, s - 2) for s in range(3, devices, 2)]
     even_up_one = [(s, s + 1) for s in range(0, devices - 1, 2)]
     odd_down_one = [(s, s - 1) for s in range(1, devices, 2)]
     pieces = []
-    for c in range(CHUNKS):
-        chunk = halves[c]
-        behind_one = passed_along(chunk[own_blocks:], "ao", 1)
-        ahead_one = passed_along(chunk[: 2 * own_blocks], "ao", -1)
-        even_two = lax.ppermute(chunk[2 * own_blocks :], "ao", even_up_two)
-        odd_two = lax.ppermute(chunk[:own_blocks], "ao", odd_down_two)
+    for c in range(1):
+        behind_one = passed_along(hi, "ao", 1)
+        even_two = lax.ppermute(hi[own_blocks:], "ao", even_up_two)
+        ahead_one = passed_along(lo, "ao", -1)
+        odd_two = lax.ppermute(lo[:own_blocks], "ao", odd_down_two)
         relay_behind = lax.ppermute(behind_one[own_blocks:], "ao", even_up_one)
         relay_ahead = lax.ppermute(ahead_one[:own_blocks], "ao", odd_down_one)
         behind_two = jnp.where(is_even, even_two, relay_behind)
@@ -162,11 +192,11 @@
             return (total + third.astype(jnp.float32)).astype(jnp.bfloat16)
 
         pieces += [
-            owner_sum(behind_two, behind_one[:own_blocks], chunk[:own_blocks]),
+            owner_sum(behind_two, behind_one[:own_blocks], lo[:own_blocks]),
             owner_sum(
-                behind_one[own_blocks:], chunk[own_blocks : 2 * own_blocks], ahead_one[:own_blocks]
+                behind_one[own_blocks:], hi[:own_blocks], ahead_one[:own_blocks]
             ),
-            owner_sum(chunk[2 * own_blocks :], ahead_one[own_blocks:], ahead_two),
+            owner_sum(hi[own_blocks:], ahead_one[own_blocks:], ahead_two),
         ]
     aux_devices = lax.axis_size("aux")
     share = block_size // aux_devices

time: 186 us -> 179 us (0.962)
  the two profiles are of different devices: /device:TPU:2 before, /device:TPU:66 now
where the time goes in v11:
time: 179 us
  waiting for transfers between devices  62.8 us (35%)
  Pallas kernels  38.3 us (21%)
  blocking collectives  30.3 us (17%)
  starting transfers between devices  25.3 us (14%)
  other arithmetic  11.1 us (6%)
  local copies, waits for them, and re-layouts  10 us (6%)
    ppermute x4, waiting for transfers between devices, passed_along(): lax.ppermute(value, axis, [(source, source + steps) for source in range(f...  57.8 us
    all_to_all x1, blocking collectives, on_device(): gathered = lax.all_to_all(partial_tiles, 'aux', 0, 0, tiled=True)  30.3 us
    ppermute x4, starting transfers between devices, passed_along(): lax.ppermute(value, axis, [(source, source + steps) for source in range(f...  17.4 us
    pallas_call x1, Pallas kernels, on_device(): pl.pallas_call(_left_kernel, grid_spec=pltpu.PrefetchScalarGridSpec(num_s...  14.4 us
    pallas_call x1, Pallas kernels, on_device(): pl.pallas_call(_right_kernel, grid_spec=pltpu.PrefetchScalarGridSpec(num_...  13.6 us
    pallas_call x1, Pallas kernels, on_device(): pl.pallas_call(_contract_kernel, grid_spec=pltpu.PrefetchScalarGridSpec(n...  10.3 us
    convert_element_type x1, other arithmetic, owner_sum(): return (total + third.astype(jnp.float32)).astype(jnp.bfloat16)  9.44 us
    ppermute x1, waiting for transfers between devices, on_device(): relay_ahead = lax.ppermute(ahead_one[:own_blocks], 'ao', odd_down_one)  5.05 us
  transfers between devices with their start and end apart: 8, of which 3 were waited for; matrix products, arithmetic and copies ran while one was open for 3% of the time, Pallas kernels for 16%

profile of v11, /device:TPU:66, one launch (start us, length us, event | category | flops | bytes accessed | tf_op | source)
XLA Modules:
  0.0 178.7 jit_solution(7876814493806709502)
XLA Ops:
  0.0 1.9 %collective-permute-start.4 = (bf16[4,128,512]{2,1,0:T(8,128)(2,1)}, bf16[4,128,512]{2,1,0:T(8,128)(2,1)S(1)}, u32[]{:S(2)}, u32[]{:S(2)}) collective-permute-start(bf16[4,128,512]{2,1,0:T(8,128)(2,1)} %bitcast.7), channel_id=1, source_target_pairs={{2,0},{3,1},{4,2},{5,3},{6,4},{7,5},{8,6},{9,7},{10,8},{11,9},{12,... | collective-permute-start | bytes 1572872 | tf_op jit(solution)/shard_map/ppermute | solution.py:14
  1.9 9.7 %collective-permute-start.3 = (bf16[4,128,512]{2,1,0:T(8,128)(2,1)}, bf16[4,128,512]{2,1,0:T(8,128)(2,1)S(1)}, u32[]{:S(2)}, u32[]{:S(2)}) collective-permute-start(bf16[4,128,512]{2,1,0:T(8,128)(2,1)} %bitcast.8), channel_id=1, source_target_pairs={{1,0},{2,1},{3,2},{4,3},{5,4},{6,5},{7,6},{8,7},{9,8},{10,9},{11,1... | collective-permute-start | bytes 1572872 | tf_op jit(solution)/shard_map/ppermute | solution.py:14
  12.3 0.8 subtract_bitcast_fusion
  13.1 1.9 %copy-done = bf16[24,4,128,128]{3,2,1,0:T(8,128)(2,1)S(1)} copy-done((bf16[24,4,128,128]{3,2,1,0:T(8,128)(2,1)S(1)}, bf16[24,4,128,128]{3,2,1,0:T(8,128)(2,1)}, u32[]{:S(2)}) %copy-start) | copy-done | bytes 3145752
  15.0 1.0 copy-done.1
  16.0 13.6 %shard_map.46 = (bf16[8,4,128,512]{3,2,1,0:T(8,128)(2,1)}, f32[4,4,128,512]{3,2,1,0:T(8,128)}) custom-call(s32[24]{0:T(128)S(1)} %get-tuple-element.13.left_ref, s32[24]{0:T(128)S(1)} %get-tuple-element.12.right_ref, s32[1]{0:T(128)S(6)} %copy.5.count_ref, bf16[24,4,128,128]{3,2,1,0:T(8,128)(2,1)S(1)} %copy-done, bf16[4,128,512]{2,1,0:T(8,128)(2,1)S(1)} %bitcast.9), custom_call_target="tpu_custom_call" | custom-call | tf_op jit(solution)/shard_map/pallas_call | solution.py:139
  29.6 1.9 %collective-permute-start.1 = (bf16[8,4,128,512]{3,2,1,0:T(8,128)(2,1)}, bf16[8,4,128,512]{3,2,1,0:T(8,128)(2,1)S(1)}, u32[]{:S(2)}, u32[]{:S(2)}) collective-permute-start(bf16[8,4,128,512]{3,2,1,0:T(8,128)(2,1)} %get-tuple-element.7.hi_ref), channel_id=1, source_target_pairs={{0,1},{1,2},{2,3},{3,4},{4,5},{5,6},{6,7},{7,8},{8,9},{9,10},{10,1... | collective-permute-start | bytes 12582920 | tf_op jit(solution)/shard_map/ppermute | solution.py:14
  31.5 0.0 collective-permute-done.4
  31.5 0.0 collective-permute-done.3
  31.5 0.2 pad_maximum_fusion.coeff_ref
  31.7 14.4 %shard_map.47 = bf16[8,4,128,512]{3,2,1,0:T(8,128)(2,1)} custom-call(s32[24]{0:T(128)S(1)} %get-tuple-element.13.left_ref, s32[24]{0:T(128)S(1)} %get-tuple-element.12.right_ref, s32[1]{0:T(128)S(6)} %copy.5.count_ref, bf16[24,4,128,128]{3,2,1,0:T(8,128)(2,1)S(1)} %copy-done, bf16[12,128,512]{2,1,0:T(8,128)(2,1)S(1)} %pad_maximum_fusion.coeff_ref, ...), custom_call_target="tpu_custom_call" | custom-call | tf_op jit(solution)/shard_map/pallas_call | solution.py:155
  46.1 3.9 %collective-permute-start.5 = (bf16[8,4,128,512]{3,2,1,0:T(8,128)(2,1)}, bf16[8,4,128,512]{3,2,1,0:T(8,128)(2,1)S(1)}, u32[]{:S(2)}, u32[]{:S(2)}) collective-permute-start(bf16[8,4,128,512]{3,2,1,0:T(8,128)(2,1)} %shard_map.47), channel_id=1, source_target_pairs={{1,0},{2,1},{3,2},{4,3},{5,4},{6,5},{7,6},{8,7},{9,8},{10,9},{11,1... | collective-permute-start | bytes 12582920 | tf_op jit(solution)/shard_map/ppermute | solution.py:14
  50.0 0.2 slice.57
  50.2 1.9 %collective-permute-start = (bf16[4,4,128,512]{3,2,1,0:T(8,128)(2,1)S(1)}, bf16[4,4,128,512]{3,2,1,0:T(8,128)(2,1)}, u32[]{:S(2)}, u32[]{:S(2)}) collective-permute-start(bf16[4,4,128,512]{3,2,1,0:T(8,128)(2,1)S(1)} %slice.57), channel_id=1, source_target_pairs={{0,2},{2,4},{4,6},{6,8},{8,10},{10,12},{12,14},{14,16},{16,18},{18... | collective-permute-start | bytes 6291464 | tf_op jit(solution)/shard_map/ppermute | solution.py:182
  52.2 1.6 slice.74
  53.8 2.0 %collective-permute-start.7 = (bf16[4,4,128,512]{3,2,1,0:T(8,128)(2,1)}, bf16[4,4,128,512]{3,2,1,0:T(8,128)(2,1)}, u32[]{:S(2)}, u32[]{:S(2)}) collective-permute-start(bf16[4,4,128,512]{3,2,1,0:T(8,128)(2,1)} %slice.74), channel_id=1, source_target_pairs={{3,1},{5,3},{7,5},{9,7},{11,9},{13,11},{15,13},{17,15},{19,17},{21... | collective-permute-start | bytes 6291464 | tf_op jit(solution)/shard_map/ppermute | solution.py:184
  55.8 46.3 %collective-permute-done.1 = bf16[8,4,128,512]{3,2,1,0:T(8,128)(2,1)S(1)} collective-permute-done((bf16[8,4,128,512]{3,2,1,0:T(8,128)(2,1)}, bf16[8,4,128,512]{3,2,1,0:T(8,128)(2,1)S(1)}, u32[]{:S(2)}, u32[]{:S(2)}) %collective-permute-start.1) | collective-permute-done | bytes 4194336 | tf_op jit(solution)/shard_map/ppermute | solution.py:14
  102.1 1.6 slice.72
  103.7 1.0 copy-done.5
  104.7 2.6 %collective-permute-start.2 = (bf16[4,4,128,512]{3,2,1,0:T(8,128)(2,1)}, bf16[4,4,128,512]{3,2,1,0:T(8,128)(2,1)}, u32[]{:S(2)}, u32[]{:S(2)}) collective-permute-start(bf16[4,4,128,512]{3,2,1,0:T(8,128)(2,1)} %slice.72), channel_id=1, source_target_pairs={{0,1},{2,3},{4,5},{6,7},{8,9},{10,11},{12,13},{14,15},{16,17},{18,... | collective-permute-start | bytes 6291464 | tf_op jit(solution)/shard_map/ppermute | solution.py:185
  107.3 11.5 %collective-permute-done.5 = bf16[8,4,128,512]{3,2,1,0:T(8,128)(2,1)S(1)} collective-permute-done((bf16[8,4,128,512]{3,2,1,0:T(8,128)(2,1)}, bf16[8,4,128,512]{3,2,1,0:T(8,128)(2,1)S(1)}, u32[]{:S(2)}, u32[]{:S(2)}) %collective-permute-start.5) | collective-permute-done | bytes 4194336 | tf_op jit(solution)/shard_map/ppermute | solution.py:14
  118.8 1.8 %slice.75 = bf16[4,4,128,512]{3,2,1,0:T(8,128)(2,1)} slice(bf16[8,4,128,512]{3,2,1,0:T(8,128)(2,1)S(1)} %collective-permute-done.5), slice={[0:4], [0:4], [0:128], [0:512]} | slice | bytes 4194304 | tf_op jit(solution)/shard_map/slice | solution.py:197
  120.6 0.9 copy-done.6
  121.5 1.3 collective-permute-start.6
  122.8 0.0 collective-permute-done
  122.8 0.0 collective-permute-done.7
  122.8 0.0 collective-permute-done.2
  122.8 5.1 %collective-permute-done.6 = bf16[4,4,128,512]{3,2,1,0:T(8,128)(2,1)} collective-permute-done((bf16[4,4,128,512]{3,2,1,0:T(8,128)(2,1)}, bf16[4,4,128,512]{3,2,1,0:T(8,128)(2,1)}, u32[]{:S(2)}, u32[]{:S(2)}) %collective-permute-start.6) | collective-permute-done | bytes 2097184 | tf_op jit(solution)/shard_map/ppermute | solution.py:186
  127.9 9.4 %add_convert_fusion = (bf16[4,4,128,512]{3,2,1,0:T(8,128)(2,1)}, bf16[4,4,128,512]{3,2,1,0:T(8,128)(2,1)S(1)}, bf16[4,4,128,512]{3,2,1,0:T(8,128)(2,1)S(1)}) fusion(bf16[8,4,128,512]{3,2,1,0:T(8,128)(2,1)} %copy-done.6, bf16[4,4,128,512]{3,2,1,0:T(8,128)(2,1)} %collective-permute-done.6, bf16[4,4,128,512]{3,2,1,0:T(8,128)(2,1)} %collective-permute-done.7, ...), kind=kLoop, calls=%fused_computation | loop fusion | flops 20971520 | bytes 29360128 | tf_op jit(solution)/shard_map/convert_element_type | solution.py:192
  137.3 10.3 %shard_map.48 = bf16[8,24,16,128]{3,2,1,0:T(8,128)(2,1)S(1)} custom-call(s32[24]{0:T(128)S(1)} %get-tuple-element.13.left_ref, s32[24]{0:T(128)S(1)} %get-tuple-element.12.right_ref, s32[1]{0:T(128)S(6)} %copy.5.count_ref, bf16[4,4,128,512]{3,2,1,0:T(8,128)(2,1)S(1)} %get-tuple-element.11.refs_0_, bf16[4,4,128,512]{3,2,1,0:T(8,128)(2,1)S(1)} %get-tuple-element.10.refs_1_, ...), custom_call_target="tpu_custom_call" | custom-call | tf_op jit(solution)/shard_map/pallas_call | solution.py:204
  147.6 30.3 %all_to_all.5 = bf16[8,24,16,128]{3,2,1,0:T(8,128)(2,1)S(1)} all-to-all(bf16[8,24,16,128]{3,2,1,0:T(8,128)(2,1)S(1)} %shard_map.48), channel_id=1, replica_groups=mesh['aux'=8,'ao'=64] {'aux'}, dimensions={0} | all-to-all | bytes 1572864 | tf_op jit(solution)/shard_map/all_to_all | solution.py:222
  177.9 0.8 fusion
  (10 shorter events, 0.0 us)
Async XLA Ops:
  0.0 31.5 %collective-permute-start.4 = (bf16[4,128,512]{2,1,0:T(8,128)(2,1)}, bf16[4,128,512]{2,1,0:T(8,128)(2,1)S(1)}, u32[]{:S(2)}, u32[]{:S(2)}) collective-permute-start(bf16[4,128,512]{2,1,0:T(8,128)(2,1)} %bitcast.7), channel_id=1, source_target_pairs={{2,0},{3,1},{4,2},{5,3},{6,4},{7,5},{8,6},{9,7},{10,8},{11,9},{12,... | collective-permute-start | bytes 1572872 | tf_op jit(solution)/shard_map/ppermute | solution.py:14
  1.9 29.6 %collective-permute-start.3 = (bf16[4,128,512]{2,1,0:T(8,128)(2,1)}, bf16[4,128,512]{2,1,0:T(8,128)(2,1)S(1)}, u32[]{:S(2)}, u32[]{:S(2)}) collective-permute-start(bf16[4,128,512]{2,1,0:T(8,128)(2,1)} %bitcast.8), channel_id=1, source_target_pairs={{1,0},{2,1},{3,2},{4,3},{5,4},{6,5},{7,6},{8,7},{9,8},{10,9},{11,1... | collective-permute-start | bytes 1572872 | tf_op jit(solution)/shard_map/ppermute | solution.py:14
  13.1 1.9 %copy-start = (bf16[24,4,128,128]{3,2,1,0:T(8,128)(2,1)S(1)}, bf16[24,4,128,128]{3,2,1,0:T(8,128)(2,1)}, u32[]{:S(2)}) copy-start(bf16[24,4,128,128]{3,2,1,0:T(8,128)(2,1)} %tile_ref.3) | copy-start | bytes 9437188
  15.0 1.0 copy-start.1
  16.0 15.5 %copy-start.2 = (bf16[512,512]{1,0:T(8,128)(2,1)S(1)}, bf16[512,512]{1,0:T(8,128)(2,1)}, u32[]{:S(2)}) copy-start(bf16[512,512]{1,0:T(8,128)(2,1)} %param.7) | copy-start | bytes 1572868
  29.6 72.5 %collective-permute-start.1 = (bf16[8,4,128,512]{3,2,1,0:T(8,128)(2,1)}, bf16[8,4,128,512]{3,2,1,0:T(8,128)(2,1)S(1)}, u32[]{:S(2)}, u32[]{:S(2)}) collective-permute-start(bf16[8,4,128,512]{3,2,1,0:T(8,128)(2,1)} %get-tuple-element.7.hi_ref), channel_id=1, source_target_pairs={{0,1},{1,2},{2,3},{3,4},{4,5},{5,6},{6,7},{7,8},{8,9},{9,10},{10,1... | collective-permute-start | bytes 12582920 | tf_op jit(solution)/shard_map/ppermute | solution.py:14
  31.7 18.3 %copy-start.3 = (bf16[8,4,128,512]{3,2,1,0:T(8,128)(2,1)S(1)}, bf16[8,4,128,512]{3,2,1,0:T(8,128)(2,1)}, u32[]{:S(2)}) copy-start(bf16[8,4,128,512]{3,2,1,0:T(8,128)(2,1)} %get-tuple-element.7.hi_ref) | copy-start | bytes 12582916
  46.1 6.1 %copy-start.4 = (bf16[8,4,128,512]{3,2,1,0:T(8,128)(2,1)S(1)}, bf16[8,4,128,512]{3,2,1,0:T(8,128)(2,1)}, u32[]{:S(2)}) copy-start(bf16[8,4,128,512]{3,2,1,0:T(8,128)(2,1)} %shard_map.47) | copy-start | bytes 12582916
  46.1 72.7 %collective-permute-start.5 = (bf16[8,4,128,512]{3,2,1,0:T(8,128)(2,1)}, bf16[8,4,128,512]{3,2,1,0:T(8,128)(2,1)S(1)}, u32[]{:S(2)}, u32[]{:S(2)}) collective-permute-start(bf16[8,4,128,512]{3,2,1,0:T(8,128)(2,1)} %shard_map.47), channel_id=1, source_target_pairs={{1,0},{2,1},{3,2},{4,3},{5,4},{6,5},{7,6},{8,7},{9,8},{10,9},{11,1... | collective-permute-start | bytes 12582920 | tf_op jit(solution)/shard_map/ppermute | solution.py:14
  50.2 72.5 %collective-permute-start = (bf16[4,4,128,512]{3,2,1,0:T(8,128)(2,1)S(1)}, bf16[4,4,128,512]{3,2,1,0:T(8,128)(2,1)}, u32[]{:S(2)}, u32[]{:S(2)}) collective-permute-start(bf16[4,4,128,512]{3,2,1,0:T(8,128)(2,1)S(1)} %slice.57), channel_id=1, source_target_pairs={{0,2},{2,4},{4,6},{6,8},{8,10},{10,12},{12,14},{14,16},{16,18},{18... | collective-permute-start | bytes 6291464 | tf_op jit(solution)/shard_map/ppermute | solution.py:182
  53.8 69.0 %collective-permute-start.7 = (bf16[4,4,128,512]{3,2,1,0:T(8,128)(2,1)}, bf16[4,4,128,512]{3,2,1,0:T(8,128)(2,1)}, u32[]{:S(2)}, u32[]{:S(2)}) collective-permute-start(bf16[4,4,128,512]{3,2,1,0:T(8,128)(2,1)} %slice.74), channel_id=1, source_target_pairs={{3,1},{5,3},{7,5},{9,7},{11,9},{13,11},{15,13},{17,15},{19,17},{21... | collective-permute-start | bytes 6291464 | tf_op jit(solution)/shard_map/ppermute | solution.py:184
  102.1 2.6 %copy-start.5 = (bf16[8,4,128,512]{3,2,1,0:T(8,128)(2,1)}, bf16[8,4,128,512]{3,2,1,0:T(8,128)(2,1)S(1)}, u32[]{:S(2)}) copy-start(bf16[8,4,128,512]{3,2,1,0:T(8,128)(2,1)S(1)} %collective-permute-done.1) | copy-start | bytes 12582916
  104.7 18.1 %collective-permute-start.2 = (bf16[4,4,128,512]{3,2,1,0:T(8,128)(2,1)}, bf16[4,4,128,512]{3,2,1,0:T(8,128)(2,1)}, u32[]{:S(2)}, u32[]{:S(2)}) collective-permute-start(bf16[4,4,128,512]{3,2,1,0:T(8,128)(2,1)} %slice.72), channel_id=1, source_target_pairs={{0,1},{2,3},{4,5},{6,7},{8,9},{10,11},{12,13},{14,15},{16,17},{18,... | collective-permute-start | bytes 6291464 | tf_op jit(solution)/shard_map/ppermute | solution.py:185
  118.8 2.7 %copy-start.6 = (bf16[8,4,128,512]{3,2,1,0:T(8,128)(2,1)}, bf16[8,4,128,512]{3,2,1,0:T(8,128)(2,1)S(1)}, u32[]{:S(2)}) copy-start(bf16[8,4,128,512]{3,2,1,0:T(8,128)(2,1)S(1)} %collective-permute-done.5) | copy-start | bytes 12582916
  121.5 6.4 %collective-permute-start.6 = (bf16[4,4,128,512]{3,2,1,0:T(8,128)(2,1)}, bf16[4,4,128,512]{3,2,1,0:T(8,128)(2,1)}, u32[]{:S(2)}, u32[]{:S(2)}) collective-permute-start(bf16[4,4,128,512]{3,2,1,0:T(8,128)(2,1)} %slice.75), channel_id=1, source_target_pairs={{1,0},{3,2},{5,4},{7,6},{9,8},{11,10},{13,12},{15,14},{17,16},{19,... | collective-permute-start | bytes 6291464 | tf_op jit(solution)/shard_map/ppermute | solution.py:186

commit v12 on v11

--- a/solution.py
+++ b/solution.py
@@ -171,33 +171,43 @@
     )(left_rel, right_rel, count, tiles, window_coeff, part, hi)
 
     block_shape = own_shape
+    nb = own_blocks
     is_even = (owner_index % 2) == 0
-    even_up_two = [(s, s + 2) for s in range(0, devices - 2, 2)]
-    odd_down_two = [(s, s - 2) for s in range(3, devices, 2)]
-    even_up_one = [(s, s + 1) for s in range(0, devices - 1, 2)]
-    odd_down_one = [(s, s - 1) for s in range(1, devices, 2)]
-    pieces = []
-    for c in range(1):
-        behind_one = passed_along(hi, "ao", 1)
-        even_two = lax.ppermute(hi[own_blocks:], "ao", even_up_two)
-        ahead_one = passed_along(lo, "ao", -1)
-        odd_two = lax.ppermute(lo[:own_blocks], "ao", odd_down_two)
-        relay_behind = lax.ppermute(behind_one[own_blocks:], "ao", even_up_one)
-        relay_ahead = lax.ppermute(ahead_one[:own_blocks], "ao", odd_down_one)
-        behind_two = jnp.where(is_even, even_two, relay_behind)
-        ahead_two = jnp.where(is_even, relay_ahead, odd_two)
-
-        def owner_sum(first, second, third):
-            total = first.astype(jnp.float32) + second.astype(jnp.float32)
-            return (total + third.astype(jnp.float32)).astype(jnp.bfloat16)
-
-        pieces += [
-            owner_sum(behind_two, behind_one[:own_blocks], lo[:own_blocks]),
-            owner_sum(
-                behind_one[own_blocks:], hi[:own_blocks], ahead_one[:own_blocks]
-            ),
-            owner_sum(hi[own_blocks:], ahead_one[own_blocks:], ahead_two),
-        ]
+    even_up = [(s, s + 1) for s in range(0, devices - 1, 2)]
+    odd_down = [(s, s - 1) for s in range(1, devices, 2)]
+    odd_up = [(s, s + 1) for s in range(1, devices - 1, 2)]
+    even_down = [(s, s - 1) for s in range(2, devices, 2)]
+
+    def f32(value):
+        return value.astype(jnp.float32)
+
+    def bf16(value):
+        return value.astype(jnp.bfloat16)
+
+    mate_behind = lax.ppermute(hi, "ao", even_up)
+    mate_ahead = lax.ppermute(lo, "ao", odd_down)
+    up_package = jnp.concatenate([bf16(f32(mate_behind[nb:]) + f32(hi[:nb])), hi[nb:]], 0)
+    down_package = jnp.concatenate([lo[:nb], bf16(f32(hi[:nb]) + f32(mate_ahead[:nb]))], 0)
+    from_behind = lax.ppermute(up_package, "ao", odd_up)
+    from_ahead = lax.ppermute(down_package, "ao", even_down)
+    relay_behind = lax.ppermute(from_behind[nb:], "ao", even_up)
+    relay_ahead = lax.ppermute(from_ahead[:nb], "ao", odd_down)
+
+    def even_sums(_):
+        return (
+            bf16(f32(from_behind[:nb]) + f32(lo[:nb])),
+            bf16((f32(from_behind[nb:]) + f32(hi[:nb])) + f32(mate_ahead[:nb])),
+            bf16((f32(hi[nb:]) + f32(mate_ahead[nb:])) + f32(relay_ahead)),
+        )
+
+    def odd_sums(_):
+        return (
+            bf16((f32(relay_behind) + f32(mate_behind[:nb])) + f32(lo[:nb])),
+            bf16((f32(mate_behind[nb:]) + f32(hi[:nb])) + f32(from_ahead[:nb])),
+            bf16(f32(hi[nb:]) + f32(from_ahead[nb:])),
+        )
+
+    pieces = list(lax.cond(is_even, even_sums, odd_sums, None))
     aux_devices = lax.axis_size("aux")
     share = block_size // aux_devices
     whole = pl.BlockSpec(block_shape, lambda s, l, r, n: (0, 0, 0, 0))

time: 179 us -> 176 us (0.983)
  the two profiles are of different devices: /device:TPU:66 before, /device:TPU:6 now
where the time goes in v12:
time: 176 us
  waiting for transfers between devices  55.5 us (32%)
  Pallas kernels  33.9 us (19%)
  starting transfers between devices  30.9 us (18%)
  blocking collectives  30.3 us (17%)
  other arithmetic  15.1 us (9%)
  local copies, waits for them, and re-layouts  9.23 us (5%)
    ppermute x1, waiting for transfers between devices, on_device(): from_behind = lax.ppermute(up_package, 'ao', odd_up)  43.3 us
    all_to_all x1, blocking collectives, on_device(): gathered = lax.all_to_all(partial_tiles, 'aux', 0, 0, tiled=True)  30.3 us
    ppermute x2, starting transfers between devices, passed_along(): lax.ppermute(value, axis, [(source, source + steps) for source in range(f...  13.1 us
    pallas_call x1, Pallas kernels, on_device(): pl.pallas_call(_right_kernel, grid_spec=pltpu.PrefetchScalarGridSpec(num_...  12.3 us
    convert_element_type x2, other arithmetic, bf16(): return value.astype(jnp.bfloat16)  11.7 us
    pallas_call x1, Pallas kernels, on_device(): pl.pallas_call(_contract_kernel, grid_spec=pltpu.PrefetchScalarGridSpec(n...  10.9 us
    pallas_call x1, Pallas kernels, on_device(): pl.pallas_call(_left_kernel, grid_spec=pltpu.PrefetchScalarGridSpec(num_s...  10.7 us
    unnamed x18, local copies, waits for them, and re-layouts  7.14 us
  transfers between devices with their start and end apart: 8, of which 3 were waited for; matrix products, arithmetic and copies ran while one was open for 3% of the time, Pallas kernels for 13%

profile of v12, /device:TPU:6, one launch (start us, length us, event | category | flops | bytes accessed | tf_op | source)
XLA Modules:
  0.0 175.8 jit_solution(16020624302971041433)
XLA Ops:
  0.0 11.2 %collective-permute-start.4 = (bf16[4,128,512]{2,1,0:T(8,128)(2,1)}, bf16[4,128,512]{2,1,0:T(8,128)(2,1)S(1)}, u32[]{:S(2)}, u32[]{:S(2)}) collective-permute-start(bf16[4,128,512]{2,1,0:T(8,128)(2,1)} %bitcast.7), channel_id=1, source_target_pairs={{2,0},{3,1},{4,2},{5,3},{6,4},{7,5},{8,6},{9,7},{10,8},{11,9},{12,... | collective-permute-start | bytes 1572872 | tf_op jit(solution)/shard_map/ppermute | solution.py:14
  11.2 1.9 %collective-permute-start.3 = (bf16[4,128,512]{2,1,0:T(8,128)(2,1)}, bf16[4,128,512]{2,1,0:T(8,128)(2,1)S(1)}, u32[]{:S(2)}, u32[]{:S(2)}) collective-permute-start(bf16[4,128,512]{2,1,0:T(8,128)(2,1)} %bitcast.8), channel_id=1, source_target_pairs={{1,0},{2,1},{3,2},{4,3},{5,4},{6,5},{7,6},{8,7},{9,8},{10,9},{11,1... | collective-permute-start | bytes 1572872 | tf_op jit(solution)/shard_map/ppermute | solution.py:14
  13.8 0.8 subtract_bitcast_fusion
  14.6 1.9 %copy-done = bf16[24,4,128,128]{3,2,1,0:T(8,128)(2,1)S(1)} copy-done((bf16[24,4,128,128]{3,2,1,0:T(8,128)(2,1)S(1)}, bf16[24,4,128,128]{3,2,1,0:T(8,128)(2,1)}, u32[]{:S(2)}) %copy-start) | copy-done | bytes 3145752
  16.4 1.0 copy-done.1
  17.5 12.3 %shard_map.46 = (bf16[8,4,128,512]{3,2,1,0:T(8,128)(2,1)S(1)}, f32[4,4,128,512]{3,2,1,0:T(8,128)}) custom-call(s32[24]{0:T(128)S(1)} %get-tuple-element.81.left_ref, s32[24]{0:T(128)S(1)} %get-tuple-element.80.right_ref, s32[1]{0:T(128)S(6)} %copy.11.count_ref, bf16[24,4,128,128]{3,2,1,0:T(8,128)(2,1)S(1)} %copy-done, bf16[4,128,512]{2,1,0:T(8,128)(2,1)S(1)} %bitcast.10), custom_call_target="tpu_custom_call" | custom-call | tf_op jit(solution)/shard_map/pallas_call | solution.py:139
  29.8 4.3 %collective-permute-start = (bf16[8,4,128,512]{3,2,1,0:T(8,128)(2,1)S(1)}, bf16[8,4,128,512]{3,2,1,0:T(8,128)(2,1)}, u32[]{:S(2)}, u32[]{:S(2)}) collective-permute-start(bf16[8,4,128,512]{3,2,1,0:T(8,128)(2,1)S(1)} %get-tuple-element.58.hi_ref), channel_id=1, source_target_pairs={{0,1},{2,3},{4,5},{6,7},{8,9},{10,11},{12,13},{14,15},{16,17},{18,... | collective-permute-start | bytes 12582920 | tf_op jit(solution)/shard_map/ppermute | solution.py:187
  34.1 1.2 pad_maximum_fusion.2.coeff_ref
  35.4 10.7 %shard_map.47 = bf16[8,4,128,512]{3,2,1,0:T(8,128)(2,1)S(1)} custom-call(s32[24]{0:T(128)S(1)} %get-tuple-element.81.left_ref, s32[24]{0:T(128)S(1)} %get-tuple-element.80.right_ref, s32[1]{0:T(128)S(6)} %copy.11.count_ref, bf16[24,4,128,128]{3,2,1,0:T(8,128)(2,1)S(1)} %copy-done, bf16[12,128,512]{2,1,0:T(8,128)(2,1)S(1)} %pad_maximum_fusion.2.coeff_ref, ...), custom_call_target="tpu_custom_call" | custom-call | tf_op jit(solution)/shard_map/pallas_call | solution.py:155
  46.1 1.3 collective-permute-start.5
  47.4 0.2 slice.98
  47.7 0.3 copy-done.3
  48.0 7.1 %collective-permute-done.5 = bf16[8,4,128,512]{3,2,1,0:T(8,128)(2,1)S(1)} collective-permute-done((bf16[8,4,128,512]{3,2,1,0:T(8,128)(2,1)S(1)}, bf16[8,4,128,512]{3,2,1,0:T(8,128)(2,1)S(1)}, u32[]{:S(2)}, u32[]{:S(2)}) %collective-permute-start.5) | collective-permute-done | bytes 4194336 | tf_op jit(solution)/shard_map/ppermute | solution.py:188
  55.1 4.4 %fusion.1 = (bf16[4,4,128,512]{3,2,1,0:T(8,128)(2,1)S(1)}, bf16[4,4,128,512]{3,2,1,0:T(8,128)(2,1)S(1)}) fusion(bf16[8,4,128,512]{3,2,1,0:T(8,128)(2,1)S(1)} %collective-permute-done.5, bf16[8,4,128,512]{3,2,1,0:T(8,128)(2,1)S(1)} %get-tuple-element.58.hi_ref, bf16[8,4,128,512]{3,2,1,0:T(8,128)(2,1)} %collective-permute-done), kind=kLoop, calls=%fused_computation.9 | loop fusion | flops 7340032 | bytes 10485760 | tf_op jit(solution)/shard_map/convert_element_type | solution.py:185
  59.6 0.4 pad_maximum_fusion
  59.9 1.3 collective-permute-start.1
  61.2 0.4 pad_maximum_fusion.1
  61.6 6.9 %collective-permute-start.6 = (bf16[8,4,128,512]{3,2,1,0:T(8,128)(2,1)S(1)}, bf16[8,4,128,512]{3,2,1,0:T(8,128)(2,1)S(1)}, u32[]{:S(2)}, u32[]{:S(2)}) collective-permute-start(bf16[8,4,128,512]{3,2,1,0:T(8,128)(2,1)S(1)} %pad_maximum_fusion.1), channel_id=1, source_target_pairs={{2,1},{4,3},{6,5},{8,7},{10,9},{12,11},{14,13},{16,15},{18,17},{20... | collective-permute-start | bytes 12582920 | tf_op jit(solution)/shard_map/ppermute | solution.py:192
  68.5 43.3 %collective-permute-done.1 = bf16[8,4,128,512]{3,2,1,0:T(8,128)(2,1)S(1)} collective-permute-done((bf16[8,4,128,512]{3,2,1,0:T(8,128)(2,1)S(1)}, bf16[8,4,128,512]{3,2,1,0:T(8,128)(2,1)S(1)}, u32[]{:S(2)}, u32[]{:S(2)}) %collective-permute-start.1) | collective-permute-done | bytes 4194336 | tf_op jit(solution)/shard_map/ppermute | solution.py:191
  111.9 0.2 slice.112
  112.1 2.7 %collective-permute-start.2 = (bf16[4,4,128,512]{3,2,1,0:T(8,128)(2,1)S(1)}, bf16[4,4,128,512]{3,2,1,0:T(8,128)(2,1)}, u32[]{:S(2)}, u32[]{:S(2)}) collective-permute-start(bf16[4,4,128,512]{3,2,1,0:T(8,128)(2,1)S(1)} %slice.112), channel_id=1, source_target_pairs={{0,1},{2,3},{4,5},{6,7},{8,9},{10,11},{12,13},{14,15},{16,17},{18,... | collective-permute-start | bytes 6291464 | tf_op jit(solution)/shard_map/ppermute | solution.py:193
  114.8 1.9 %copy-done.6 = bf16[8,4,128,512]{3,2,1,0:T(8,128)(2,1)} copy-done((bf16[8,4,128,512]{3,2,1,0:T(8,128)(2,1)}, bf16[8,4,128,512]{3,2,1,0:T(8,128)(2,1)S(1)}, u32[]{:S(2)}) %copy-start.6) | copy-done | bytes 4194328
  116.7 1.5 slice.115
  118.2 1.3 collective-permute-start.7
  119.6 5.1 %collective-permute-done.7 = bf16[4,4,128,512]{3,2,1,0:T(8,128)(2,1)} collective-permute-done((bf16[4,4,128,512]{3,2,1,0:T(8,128)(2,1)}, bf16[4,4,128,512]{3,2,1,0:T(8,128)(2,1)}, u32[]{:S(2)}, u32[]{:S(2)}) %collective-permute-start.7) | collective-permute-done | bytes 2097184 | tf_op jit(solution)/shard_map/ppermute | solution.py:194
  124.6 7.3 %conditional.4 = (bf16[4,4,128,512]{3,2,1,0:T(8,128)(2,1)S(1)}, bf16[4,4,128,512]{3,2,1,0:T(8,128)(2,1)S(1)}, bf16[4,4,128,512]{3,2,1,0:T(8,128)(2,1)S(1)}) conditional(s32[]{:T(128)} %convert_element_type.146, (bf16[4,4,128,512]{3,2,1,0:T(8,128)(2,1)}, bf16[8,4,128,512]{3,2,1,0:T(8,128)(2,1)}, bf16[8,4,128,512]{3,2,1,0:T(8,128)(2,1)}, ...), branch_computations={%region_0.1_spmd, %region_1.2_spmd} | conditional | flops 16777216 | bytes 23068696
  124.6 7.3 %add_convert_fusion.3 = (bf16[4,4,128,512]{3,2,1,0:T(8,128)(2,1)S(1)}, bf16[4,4,128,512]{3,2,1,0:T(8,128)(2,1)S(1)}, bf16[4,4,128,512]{3,2,1,0:T(8,128)(2,1)S(1)}) fusion(bf16[4,4,128,512]{3,2,1,0:T(8,128)(2,1)} %get-tuple-element.52, bf16[8,4,128,512]{3,2,1,0:T(8,128)(2,1)} %get-tuple-element.51, bf16[8,4,128,512]{3,2,1,0:T(8,128)(2,1)} %get-tuple-element.50, ...), kind=kLoop, calls=%fused_computation.3 | loop fusion | flops 16777216 | bytes 23068672 | tf_op jit(solution)/shard_map/cond/branch_0_fun/convert_element_type | solution.py:185
  131.9 1.3 copy-done.7
  133.2 0.7 copy-done.8
  133.9 10.9 %shard_map.48 = bf16[8,24,16,128]{3,2,1,0:T(8,128)(2,1)S(1)} custom-call(s32[24]{0:T(128)S(1)} %get-tuple-element.81.left_ref, s32[24]{0:T(128)S(1)} %get-tuple-element.80.right_ref, s32[1]{0:T(128)S(6)} %copy.11.count_ref, bf16[4,4,128,512]{3,2,1,0:T(8,128)(2,1)} %copy-done.8, bf16[4,4,128,512]{3,2,1,0:T(8,128)(2,1)} %copy-done.7, ...), custom_call_target="tpu_custom_call" | custom-call | tf_op jit(solution)/shard_map/pallas_call | solution.py:214
  144.7 30.3 %all_to_all.5 = bf16[8,24,16,128]{3,2,1,0:T(8,128)(2,1)S(1)} all-to-all(bf16[8,24,16,128]{3,2,1,0:T(8,128)(2,1)S(1)} %shard_map.48), channel_id=1, replica_groups=mesh['aux'=8,'ao'=64] {'aux'}, dimensions={0} | all-to-all | bytes 1572864 | tf_op jit(solution)/shard_map/all_to_all | solution.py:232
  175.1 0.8 fusion.2
  (18 shorter events, 0.2 us)
Async XLA Ops:
  0.0 34.1 %collective-permute-start.4 = (bf16[4,128,512]{2,1,0:T(8,128)(2,1)}, bf16[4,128,512]{2,1,0:T(8,128)(2,1)S(1)}, u32[]{:S(2)}, u32[]{:S(2)}) collective-permute-start(bf16[4,128,512]{2,1,0:T(8,128)(2,1)} %bitcast.7), channel_id=1, source_target_pairs={{2,0},{3,1},{4,2},{5,3},{6,4},{7,5},{8,6},{9,7},{10,8},{11,9},{12,... | collective-permute-start | bytes 1572872 | tf_op jit(solution)/shard_map/ppermute | solution.py:14
  11.2 22.9 %collective-permute-start.3 = (bf16[4,128,512]{2,1,0:T(8,128)(2,1)}, bf16[4,128,512]{2,1,0:T(8,128)(2,1)S(1)}, u32[]{:S(2)}, u32[]{:S(2)}) collective-permute-start(bf16[4,128,512]{2,1,0:T(8,128)(2,1)} %bitcast.8), channel_id=1, source_target_pairs={{1,0},{2,1},{3,2},{4,3},{5,4},{6,5},{7,6},{8,7},{9,8},{10,9},{11,1... | collective-permute-start | bytes 1572872 | tf_op jit(solution)/shard_map/ppermute | solution.py:14
  14.6 1.9 %copy-start = (bf16[24,4,128,128]{3,2,1,0:T(8,128)(2,1)S(1)}, bf16[24,4,128,128]{3,2,1,0:T(8,128)(2,1)}, u32[]{:S(2)}) copy-start(bf16[24,4,128,128]{3,2,1,0:T(8,128)(2,1)} %tile_ref.3) | copy-start | bytes 9437188
  16.4 1.0 copy-start.1
  29.8 25.3 %copy-start.2 = (bf16[8,4,128,512]{3,2,1,0:T(8,128)(2,1)}, bf16[8,4,128,512]{3,2,1,0:T(8,128)(2,1)S(1)}, u32[]{:S(2)}) copy-start(bf16[8,4,128,512]{3,2,1,0:T(8,128)(2,1)S(1)} %get-tuple-element.58.hi_ref) | copy-start | bytes 12582916
  29.8 18.3 %collective-permute-start = (bf16[8,4,128,512]{3,2,1,0:T(8,128)(2,1)S(1)}, bf16[8,4,128,512]{3,2,1,0:T(8,128)(2,1)}, u32[]{:S(2)}, u32[]{:S(2)}) collective-permute-start(bf16[8,4,128,512]{3,2,1,0:T(8,128)(2,1)S(1)} %get-tuple-element.58.hi_ref), channel_id=1, source_target_pairs={{0,1},{2,3},{4,5},{6,7},{8,9},{10,11},{12,13},{14,15},{16,17},{18,... | collective-permute-start | bytes 12582920 | tf_op jit(solution)/shard_map/ppermute | solution.py:187
  46.0 2.0 %copy-start.3 = (bf16[8,4,128,512]{3,2,1,0:T(8,128)(2,1)}, bf16[8,4,128,512]{3,2,1,0:T(8,128)(2,1)S(1)}, u32[]{:S(2)}) copy-start(bf16[8,4,128,512]{3,2,1,0:T(8,128)(2,1)S(1)} %shard_map.47) | copy-start | bytes 12582916
  46.1 9.1 %collective-permute-start.5 = (bf16[8,4,128,512]{3,2,1,0:T(8,128)(2,1)S(1)}, bf16[8,4,128,512]{3,2,1,0:T(8,128)(2,1)S(1)}, u32[]{:S(2)}, u32[]{:S(2)}) collective-permute-start(bf16[8,4,128,512]{3,2,1,0:T(8,128)(2,1)S(1)} %shard_map.47), channel_id=1, source_target_pairs={{1,0},{3,2},{5,4},{7,6},{9,8},{11,10},{13,12},{15,14},{17,16},{19,... | collective-permute-start | bytes 12582920 | tf_op jit(solution)/shard_map/ppermute | solution.py:188
  55.1 4.4 %copy-start.4 = (bf16[8,4,128,512]{3,2,1,0:T(8,128)(2,1)}, bf16[8,4,128,512]{3,2,1,0:T(8,128)(2,1)S(1)}, u32[]{:S(2)}) copy-start(bf16[8,4,128,512]{3,2,1,0:T(8,128)(2,1)S(1)} %collective-permute-done.5) | copy-start | bytes 12582916
  59.9 51.9 %collective-permute-start.1 = (bf16[8,4,128,512]{3,2,1,0:T(8,128)(2,1)S(1)}, bf16[8,4,128,512]{3,2,1,0:T(8,128)(2,1)S(1)}, u32[]{:S(2)}, u32[]{:S(2)}) collective-permute-start(bf16[8,4,128,512]{3,2,1,0:T(8,128)(2,1)S(1)} %pad_maximum_fusion), channel_id=1, source_target_pairs={{1,2},{3,4},{5,6},{7,8},{9,10},{11,12},{13,14},{15,16},{17,18},{19... | collective-permute-start | bytes 12582920 | tf_op jit(solution)/shard_map/ppermute | solution.py:191
  61.6 53.2 %collective-permute-start.6 = (bf16[8,4,128,512]{3,2,1,0:T(8,128)(2,1)S(1)}, bf16[8,4,128,512]{3,2,1,0:T(8,128)(2,1)S(1)}, u32[]{:S(2)}, u32[]{:S(2)}) collective-permute-start(bf16[8,4,128,512]{3,2,1,0:T(8,128)(2,1)S(1)} %pad_maximum_fusion.1), channel_id=1, source_target_pairs={{2,1},{4,3},{6,5},{8,7},{10,9},{12,11},{14,13},{16,15},{18,17},{20... | collective-permute-start | bytes 12582920 | tf_op jit(solution)/shard_map/ppermute | solution.py:192
  111.9 6.4 %copy-start.5 = (bf16[8,4,128,512]{3,2,1,0:T(8,128)(2,1)}, bf16[8,4,128,512]{3,2,1,0:T(8,128)(2,1)S(1)}, u32[]{:S(2)}) copy-start(bf16[8,4,128,512]{3,2,1,0:T(8,128)(2,1)S(1)} %collective-permute-done.1) | copy-start | bytes 12582916
  112.1 7.5 %collective-permute-start.2 = (bf16[4,4,128,512]{3,2,1,0:T(8,128)(2,1)S(1)}, bf16[4,4,128,512]{3,2,1,0:T(8,128)(2,1)}, u32[]{:S(2)}, u32[]{:S(2)}) collective-permute-start(bf16[4,4,128,512]{3,2,1,0:T(8,128)(2,1)S(1)} %slice.112), channel_id=1, source_target_pairs={{0,1},{2,3},{4,5},{6,7},{8,9},{10,11},{12,13},{14,15},{16,17},{18,... | collective-permute-start | bytes 6291464 | tf_op jit(solution)/shard_map/ppermute | solution.py:193
  114.8 1.9 %copy-start.6 = (bf16[8,4,128,512]{3,2,1,0:T(8,128)(2,1)}, bf16[8,4,128,512]{3,2,1,0:T(8,128)(2,1)S(1)}, u32[]{:S(2)}) copy-start(bf16[8,4,128,512]{3,2,1,0:T(8,128)(2,1)S(1)} %collective-permute-done.6) | copy-start | bytes 12582916
  118.2 6.4 %collective-permute-start.7 = (bf16[4,4,128,512]{3,2,1,0:T(8,128)(2,1)}, bf16[4,4,128,512]{3,2,1,0:T(8,128)(2,1)}, u32[]{:S(2)}, u32[]{:S(2)}) collective-permute-start(bf16[4,4,128,512]{3,2,1,0:T(8,128)(2,1)} %slice.115), channel_id=1, source_target_pairs={{1,0},{3,2},{5,4},{7,6},{9,8},{11,10},{13,12},{15,14},{17,16},{19,... | collective-permute-start | bytes 6291464 | tf_op jit(solution)/shard_map/ppermute | solution.py:194
  131.9 1.3 copy-start.7
  131.9 2.0 %copy-start.8 = (bf16[4,4,128,512]{3,2,1,0:T(8,128)(2,1)}, bf16[4,4,128,512]{3,2,1,0:T(8,128)(2,1)S(1)}, u32[]{:S(2)}) copy-start(bf16[4,4,128,512]{3,2,1,0:T(8,128)(2,1)S(1)} %get-tuple-element.69.refs_0_) | copy-start | bytes 6291460

commit v13 on v11

--- a/solution.py
+++ b/solution.py
@@ -39,7 +39,9 @@
     @pl.when(slot == pl.num_programs(0) - 1)
     def _():
         part_ref[...] = acc_ref[:own_blocks]
-        hi_ref[...] = acc_ref[own_blocks:].astype(hi_ref.dtype)
+        width = hi_ref.shape[-1]
+        for c in range(hi_ref.shape[0]):
+            hi_ref[c] = acc_ref[own_blocks:, :, :, c * width : (c + 1) * width].astype(hi_ref.dtype)
 
 
 def _left_kernel(left_ref, right_ref, count_ref, tile_ref, coeff_ref, part_ref, hi_ref, lo_ref, acc_ref):
@@ -64,8 +66,10 @@
 
     @pl.when(slot == pl.num_programs(0) - 1)
     def _():
-        lo_ref[:own_blocks] = acc_ref[...].astype(lo_ref.dtype)
-        lo_ref[own_blocks:] = hi_ref[:own_blocks]
+        width = lo_ref.shape[-1]
+        for c in range(lo_ref.shape[0]):
+            lo_ref[c, :own_blocks] = acc_ref[:, :, :, c * width : (c + 1) * width].astype(lo_ref.dtype)
+            lo_ref[c, own_blocks:] = hi_ref[c, :own_blocks]
 
 
 def _contract_kernel(left_ref, right_ref, count_ref, *refs):
@@ -104,7 +108,7 @@
         out_ref[...] = jnp.zeros_like(out_ref)
 
 
-CHUNKS = 1
+CHUNKS = 2
 
 
 def on_device(pair_list, pair_count, tiles, coeff):
@@ -132,7 +136,7 @@
 
     tile_spec = pl.BlockSpec((1, aux_local, block_size, block_size), tile_map)
     own_shape = (own_blocks, aux_local, block_size, orbitals)
-    wide_shape = (2 * own_blocks, aux_local, block_size, orbitals)
+    wide_shape = (CHUNKS, 2 * own_blocks, aux_local, block_size, width)
     params = pltpu.CompilerParams(
         dimension_semantics=("arbitrary",), vmem_limit_bytes=48 * 1024 * 1024
     )
@@ -170,18 +174,24 @@
         compiler_params=params,
     )(left_rel, right_rel, count, tiles, window_coeff, part, hi)
 
-    block_shape = own_shape
+    block_shape = (own_blocks, aux_local, block_size, width)
     is_even = (owner_index % 2) == 0
     even_up_two = [(s, s + 2) for s in range(0, devices - 2, 2)]
     odd_down_two = [(s, s - 2) for s in range(3, devices, 2)]
     even_up_one = [(s, s + 1) for s in range(0, devices - 1, 2)]
     odd_down_one = [(s, s - 1) for s in range(1, devices, 2)]
     pieces = []
-    for c in range(1):
-        behind_one = passed_along(hi, "ao", 1)
-        even_two = lax.ppermute(hi[own_blocks:], "ao", even_up_two)
-        ahead_one = passed_along(lo, "ao", -1)
-        odd_two = lax.ppermute(lo[:own_blocks], "ao", odd_down_two)
+    hi_next, lo_next = hi[0], lo[0]
+    for c in range(CHUNKS):
+        hi_c, lo_c = hi_next, lo_next
+        behind_one = passed_along(hi_c, "ao", 1)
+        even_two = lax.ppermute(hi_c[own_blocks:], "ao", even_up_two)
+        ahead_one = passed_along(lo_c, "ao", -1)
+        odd_two = lax.ppermute(lo_c[:own_blocks], "ao", odd_down_two)
+        if c + 1 < CHUNKS:
+            behind_one, even_two, ahead_one, odd_two, hi_next, lo_next = lax.optimization_barrier(
+                (behind_one, even_two, ahead_one, odd_two, hi[c + 1], lo[c + 1])
+            )
         relay_behind = lax.ppermute(behind_one[own_blocks:], "ao", even_up_one)
         relay_ahead = lax.ppermute(ahead_one[:own_blocks], "ao", odd_down_one)
         behind_two = jnp.where(is_even, even_two, relay_behind)
@@ -192,11 +202,9 @@
             return (total + third.astype(jnp.float32)).astype(jnp.bfloat16)
 
         pieces += [
-            owner_sum(behind_two, behind_one[:own_blocks], lo[:own_blocks]),
-            owner_sum(
-                behind_one[own_blocks:], hi[:own_blocks], ahead_one[:own_blocks]
-            ),
-            owner_sum(hi[own_blocks:], ahead_one[own_blocks:], ahead_two),
+            owner_sum(behind_two, behind_one[:own_blocks], lo_c[:own_blocks]),
+            owner_sum(behind_one[own_blocks:], hi_c[:own_blocks], ahead_one[:own_blocks]),
+            owner_sum(hi_c[own_blocks:], ahead_one[own_blocks:], ahead_two),
         ]
     aux_devices = lax.axis_size("aux")
     share = block_size // aux_devices

time: 179 us -> 190 us (1.061)
  the two profiles are of different devices: /device:TPU:66 before, /device:TPU:4 now
where the time goes in v13:
time: 190 us; the launch traced here: 189 us
  waiting for transfers between devices  51.1 us (27%)
  starting transfers between devices  44.6 us (23%)
  Pallas kernels  37.8 us (20%)
  blocking collectives  26.5 us (14%)
  local copies, waits for them, and re-layouts  17.6 us (9%)
  other arithmetic  10.3 us (5%)
    ppermute x6, waiting for transfers between devices, passed_along(): lax.ppermute(value, axis, [(source, source + steps) for source in range(f...  34.7 us
    all_to_all x1, blocking collectives, on_device(): gathered = lax.all_to_all(partial_tiles, 'aux', 0, 0, tiled=True)  26.5 us
    ppermute x6, starting transfers between devices, passed_along(): lax.ppermute(value, axis, [(source, source + steps) for source in range(f...  25 us
    ppermute x2, waiting for transfers between devices, on_device(): even_two = lax.ppermute(hi_c[own_blocks:], 'ao', even_up_two)  16.3 us
    pallas_call x1, Pallas kernels, on_device(): pl.pallas_call(_left_kernel, grid_spec=pltpu.PrefetchScalarGridSpec(num_s...  14.3 us
    pallas_call x1, Pallas kernels, on_device(): pl.pallas_call(_right_kernel, grid_spec=pltpu.PrefetchScalarGridSpec(num_...  13.7 us
    pallas_call x1, Pallas kernels, on_device(): pl.pallas_call(_contract_kernel, grid_spec=pltpu.PrefetchScalarGridSpec(n...  9.86 us
    ppermute x2, starting transfers between devices, on_device(): relay_behind = lax.ppermute(behind_one[own_blocks:], 'ao', even_up_one)  9.11 us
  transfers between devices with their start and end apart: 14, of which 4 were waited for; matrix products, arithmetic and copies ran while one was open for 10% of the time, Pallas kernels for 15%

profile of v13, /device:TPU:4, one launch (start us, length us, event | category | flops | bytes accessed | tf_op | source)
XLA Modules:
  0.0 188.8 jit_solution(15147737249840078970)
XLA Ops:
  0.0 10.9 %collective-permute-start.3 = (bf16[4,128,512]{2,1,0:T(8,128)(2,1)}, bf16[4,128,512]{2,1,0:T(8,128)(2,1)S(1)}, u32[]{:S(2)}, u32[]{:S(2)}) collective-permute-start(bf16[4,128,512]{2,1,0:T(8,128)(2,1)} %bitcast.26), channel_id=1, source_target_pairs={{2,0},{3,1},{4,2},{5,3},{6,4},{7,5},{8,6},{9,7},{10,8},{11,9},{12,... | collective-permute-start | bytes 1572872 | tf_op jit(solution)/shard_map/ppermute | solution.py:14
  10.9 1.9 %collective-permute-start.2 = (bf16[4,128,512]{2,1,0:T(8,128)(2,1)}, bf16[4,128,512]{2,1,0:T(8,128)(2,1)S(1)}, u32[]{:S(2)}, u32[]{:S(2)}) collective-permute-start(bf16[4,128,512]{2,1,0:T(8,128)(2,1)} %bitcast.27), channel_id=1, source_target_pairs={{1,0},{2,1},{3,2},{4,3},{5,4},{6,5},{7,6},{8,7},{9,8},{10,9},{11,1... | collective-permute-start | bytes 1572872 | tf_op jit(solution)/shard_map/ppermute | solution.py:14
  14.3 1.9 copy-done
  17.2 13.7 %shard_map.46 = (bf16[2,8,4,128,256]{4,3,2,1,0:T(8,128)(2,1)}, f32[4,4,128,512]{3,2,1,0:T(8,128)}) custom-call(s32[24]{0:T(128)S(1)} %get-tuple-element.32.left_ref, s32[24]{0:T(128)S(1)} %get-tuple-element.31.right_ref, s32[1]{0:T(128)S(6)} %copy.5.count_ref, bf16[24,4,128,128]{3,2,1,0:T(8,128)(2,1)S(1)} %copy-done, bf16[4,128,512]{2,1,0:T(8,128)(2,1)S(1)} %bitcast.28), custom_call_target="tpu_custom_call" | custom-call | tf_op jit(solution)/shard_map/pallas_call | solution.py:143
  30.9 2.8 %slice_bitcast_fusion.2 = (bf16[8,4,128,256]{3,2,1,0:T(8,128)(2,1)S(1)}, bf16[8,4,128,256]{3,2,1,0:T(8,128)(2,1)S(1)}) fusion(bf16[2,8,4,128,256]{4,3,2,1,0:T(8,128)(2,1)} %get-tuple-element.13.hi_ref), kind=kLoop, calls=%fused_computation.10 | loop fusion | bytes 8388608 | tf_op jit(solution)/shard_map/squeeze | solution.py:193
  33.7 2.4 %collective-permute-start = (bf16[8,4,128,256]{3,2,1,0:T(8,128)(2,1)S(1)}, bf16[8,4,128,256]{3,2,1,0:T(8,128)(2,1)S(1)}, u32[]{:S(2)}, u32[]{:S(2)}) collective-permute-start(bf16[8,4,128,256]{3,2,1,0:T(8,128)(2,1)S(1)} %get-tuple-element.28), channel_id=1, source_target_pairs={{0,1},{1,2},{2,3},{3,4},{4,5},{5,6},{6,7},{7,8},{8,9},{9,10},{10,1... | collective-permute-start | bytes 6291464 | tf_op jit(solution)/shard_map/ppermute | solution.py:14
  36.3 14.3 %shard_map.47 = bf16[2,8,4,128,256]{4,3,2,1,0:T(8,128)(2,1)} custom-call(s32[24]{0:T(128)S(1)} %get-tuple-element.32.left_ref, s32[24]{0:T(128)S(1)} %get-tuple-element.31.right_ref, s32[1]{0:T(128)S(6)} %copy.5.count_ref, bf16[24,4,128,128]{3,2,1,0:T(8,128)(2,1)S(1)} %copy-done, bf16[12,128,512]{2,1,0:T(8,128)(2,1)S(1)} %pad_maximum_fusion.coeff_ref, ...), custom_call_target="tpu_custom_call" | custom-call | tf_op jit(solution)/shard_map/pallas_call | solution.py:159
  50.5 2.7 %slice_bitcast_fusion = (bf16[8,4,128,256]{3,2,1,0:T(8,128)(2,1)S(1)}, bf16[8,4,128,256]{3,2,1,0:T(8,128)(2,1)S(1)}) fusion(bf16[2,8,4,128,256]{4,3,2,1,0:T(8,128)(2,1)} %shard_map.47), kind=kLoop, calls=%fused_computation | loop fusion | bytes 8388608 | tf_op jit(solution)/shard_map/squeeze | solution.py:193
  53.3 2.0 %collective-permute-start.4 = (bf16[8,4,128,256]{3,2,1,0:T(8,128)(2,1)S(1)}, bf16[8,4,128,256]{3,2,1,0:T(8,128)(2,1)S(1)}, u32[]{:S(2)}, u32[]{:S(2)}) collective-permute-start(bf16[8,4,128,256]{3,2,1,0:T(8,128)(2,1)S(1)} %get-tuple-element.26), channel_id=1, source_target_pairs={{1,0},{2,1},{3,2},{4,3},{5,4},{6,5},{7,6},{8,7},{9,8},{10,9},{11,1... | collective-permute-start | bytes 6291464 | tf_op jit(solution)/shard_map/ppermute | solution.py:14
  55.2 1.3 slice_bitcast_fusion.5
  56.6 3.5 %collective-permute-start.1 = (bf16[4,4,128,256]{3,2,1,0:T(8,128)(2,1)S(1)}, bf16[4,4,128,256]{3,2,1,0:T(8,128)(2,1)S(1)}, u32[]{:S(2)}, u32[]{:S(2)}) collective-permute-start(bf16[4,4,128,256]{3,2,1,0:T(8,128)(2,1)S(1)} %slice_bitcast_fusion.5), channel_id=1, source_target_pairs={{0,2},{2,4},{4,6},{6,8},{8,10},{10,12},{12,14},{14,16},{16,18},{18... | collective-permute-start | bytes 3145736 | tf_op jit(solution)/shard_map/ppermute | solution.py:188
  60.1 1.3 slice_bitcast_fusion.4
  62.1 13.2 %collective-permute-done.1 = bf16[4,4,128,256]{3,2,1,0:T(8,128)(2,1)S(1)} collective-permute-done((bf16[4,4,128,256]{3,2,1,0:T(8,128)(2,1)S(1)}, bf16[4,4,128,256]{3,2,1,0:T(8,128)(2,1)S(1)}, u32[]{:S(2)}, u32[]{:S(2)}) %collective-permute-start.1) | collective-permute-done | bytes 1048608 | tf_op jit(solution)/shard_map/ppermute | solution.py:188
  75.4 14.6 %collective-permute-done.4 = bf16[8,4,128,256]{3,2,1,0:T(8,128)(2,1)S(1)} collective-permute-done((bf16[8,4,128,256]{3,2,1,0:T(8,128)(2,1)S(1)}, bf16[8,4,128,256]{3,2,1,0:T(8,128)(2,1)S(1)}, u32[]{:S(2)}, u32[]{:S(2)}) %collective-permute-start.4) | collective-permute-done | bytes 2097184 | tf_op jit(solution)/shard_map/ppermute | solution.py:14
  90.0 5.9 %collective-permute-start.11 = (bf16[8,4,128,256]{3,2,1,0:T(8,128)(2,1)S(1)}, bf16[8,4,128,256]{3,2,1,0:T(8,128)(2,1)S(1)}, u32[]{:S(2)}, u32[]{:S(2)}) collective-permute-start(bf16[8,4,128,256]{3,2,1,0:T(8,128)(2,1)S(1)} %get-tuple-element.20), channel_id=1, source_target_pairs={{1,0},{2,1},{3,2},{4,3},{5,4},{6,5},{7,6},{8,7},{9,8},{10,9},{11,1... | collective-permute-start | bytes 6291464 | tf_op jit(solution)/shard_map/ppermute | solution.py:14
  95.9 1.9 %collective-permute-start.9 = (bf16[8,4,128,256]{3,2,1,0:T(8,128)(2,1)S(1)}, bf16[8,4,128,256]{3,2,1,0:T(8,128)(2,1)S(1)}, u32[]{:S(2)}, u32[]{:S(2)}) collective-permute-start(bf16[8,4,128,256]{3,2,1,0:T(8,128)(2,1)S(1)} %get-tuple-element.19), channel_id=1, source_target_pairs={{0,1},{1,2},{2,3},{3,4},{4,5},{5,6},{6,7},{7,8},{8,9},{9,10},{10,1... | collective-permute-start | bytes 6291464 | tf_op jit(solution)/shard_map/ppermute | solution.py:14
  97.9 1.3 collective-permute-start.7
  99.2 1.1 slice.112
  100.3 4.1 %collective-permute-start.6 = (bf16[4,4,128,256]{3,2,1,0:T(8,128)(2,1)}, bf16[4,4,128,256]{3,2,1,0:T(8,128)(2,1)}, u32[]{:S(2)}, u32[]{:S(2)}) collective-permute-start(bf16[4,4,128,256]{3,2,1,0:T(8,128)(2,1)} %slice.112), channel_id=1, source_target_pairs={{0,1},{2,3},{4,5},{6,7},{8,9},{10,11},{12,13},{14,15},{16,17},{18,... | collective-permute-start | bytes 3145736 | tf_op jit(solution)/shard_map/ppermute | solution.py:195
  104.4 1.2 slice.120
  105.6 1.1 slice.117
  106.7 1.7 collective-permute-start.13
  108.4 20.1 %collective-permute-done.11 = bf16[8,4,128,256]{3,2,1,0:T(8,128)(2,1)S(1)} collective-permute-done((bf16[8,4,128,256]{3,2,1,0:T(8,128)(2,1)S(1)}, bf16[8,4,128,256]{3,2,1,0:T(8,128)(2,1)S(1)}, u32[]{:S(2)}, u32[]{:S(2)}) %collective-permute-start.11) | collective-permute-done | bytes 2097184 | tf_op jit(solution)/shard_map/ppermute | solution.py:14
  128.5 2.0 %collective-permute-start.8 = (bf16[4,4,128,256]{3,2,1,0:T(8,128)(2,1)}, bf16[4,4,128,256]{3,2,1,0:T(8,128)(2,1)}, u32[]{:S(2)}, u32[]{:S(2)}) collective-permute-start(bf16[4,4,128,256]{3,2,1,0:T(8,128)(2,1)} %slice.117), channel_id=1, source_target_pairs={{0,2},{2,4},{4,6},{6,8},{8,10},{10,12},{12,14},{14,16},{16,18},{18... | collective-permute-start | bytes 3145736 | tf_op jit(solution)/shard_map/ppermute | solution.py:188
  131.5 1.3 collective-permute-start.12
  132.8 1.1 slice.135
  134.9 5.0 %collective-permute-start.10 = (bf16[4,4,128,256]{3,2,1,0:T(8,128)(2,1)}, bf16[4,4,128,256]{3,2,1,0:T(8,128)(2,1)}, u32[]{:S(2)}, u32[]{:S(2)}) collective-permute-start(bf16[4,4,128,256]{3,2,1,0:T(8,128)(2,1)} %slice.135), channel_id=1, source_target_pairs={{0,1},{2,3},{4,5},{6,7},{8,9},{10,11},{12,13},{14,15},{16,17},{18,... | collective-permute-start | bytes 3145736 | tf_op jit(solution)/shard_map/ppermute | solution.py:195
  139.9 4.6 %add_convert_fusion.3 = (bf16[4,4,128,256]{3,2,1,0:T(8,128)(2,1)S(1)}, bf16[4,4,128,256]{3,2,1,0:T(8,128)(2,1)S(1)}, bf16[4,4,128,256]{3,2,1,0:T(8,128)(2,1)S(1)}) fusion(bf16[4,4,128,256]{3,2,1,0:T(8,128)(2,1)} %copy-done.12, bf16[4,4,128,256]{3,2,1,0:T(8,128)(2,1)} %copy-done.11, bf16[8,4,128,256]{3,2,1,0:T(8,128)(2,1)} %copy-done.6, pred[]{:T(512)S(6)} %eq.5, ...), kind=kLoop, calls=%fused_computation.8 | loop fusion | flops 10485760 | bytes 14680065 | tf_op jit(solution)/shard_map/convert_element_type | solution.py:202
  144.5 3.1 %collective-permute-done.8 = bf16[4,4,128,256]{3,2,1,0:T(8,128)(2,1)} collective-permute-done((bf16[4,4,128,256]{3,2,1,0:T(8,128)(2,1)}, bf16[4,4,128,256]{3,2,1,0:T(8,128)(2,1)}, u32[]{:S(2)}, u32[]{:S(2)}) %collective-permute-start.8) | collective-permute-done | bytes 1048608 | tf_op jit(solution)/shard_map/ppermute | solution.py:188
  147.6 4.1 %add_convert_fusion = (bf16[4,4,128,256]{3,2,1,0:T(8,128)(2,1)}, bf16[4,4,128,256]{3,2,1,0:T(8,128)(2,1)S(1)}, bf16[4,4,128,256]{3,2,1,0:T(8,128)(2,1)S(1)}) fusion(bf16[8,4,128,256]{3,2,1,0:T(8,128)(2,1)S(1)} %copy-done.8, bf16[4,4,128,256]{3,2,1,0:T(8,128)(2,1)} %collective-permute-done.12, bf16[4,4,128,256]{3,2,1,0:T(8,128)(2,1)} %collective-permute-done.13, ...), kind=kLoop, calls=%fused_computation.5 | loop fusion | flops 10485760 | bytes 14680065 | tf_op jit(solution)/shard_map/convert_element_type | solution.py:202
  151.7 9.9 %shard_map.48 = bf16[8,24,16,128]{3,2,1,0:T(8,128)(2,1)S(1)} custom-call(s32[24]{0:T(128)S(1)} %get-tuple-element.32.left_ref, s32[24]{0:T(128)S(1)} %get-tuple-element.31.right_ref, s32[1]{0:T(128)S(6)} %copy.5.count_ref, bf16[4,4,128,256]{3,2,1,0:T(8,128)(2,1)S(1)} %get-tuple-element.30.refs_0_, bf16[4,4,128,256]{3,2,1,0:T(8,128)(2,1)S(1)} %get-tuple-element.22.refs_1_, ...), custom_call_target="tpu_custom_call" | custom-call | tf_op jit(solution)/shard_map/pallas_call | solution.py:212
  161.6 26.5 %all_to_all.5 = bf16[8,24,16,128]{3,2,1,0:T(8,128)(2,1)S(1)} all-to-all(bf16[8,24,16,128]{3,2,1,0:T(8,128)(2,1)S(1)} %shard_map.48), channel_id=1, replica_groups=mesh['aux'=8,'ao'=64] {'aux'}, dimensions={0} | all-to-all | bytes 1572864 | tf_op jit(solution)/shard_map/all_to_all | solution.py:230
  (41 shorter events, 5.6 us)
Async XLA Ops:
  0.0 36.1 %collective-permute-start.3 = (bf16[4,128,512]{2,1,0:T(8,128)(2,1)}, bf16[4,128,512]{2,1,0:T(8,128)(2,1)S(1)}, u32[]{:S(2)}, u32[]{:S(2)}) collective-permute-start(bf16[4,128,512]{2,1,0:T(8,128)(2,1)} %bitcast.26), channel_id=1, source_target_pairs={{2,0},{3,1},{4,2},{5,3},{6,4},{7,5},{8,6},{9,7},{10,8},{11,9},{12,... | collective-permute-start | bytes 1572872 | tf_op jit(solution)/shard_map/ppermute | solution.py:14
  10.9 25.2 %collective-permute-start.2 = (bf16[4,128,512]{2,1,0:T(8,128)(2,1)}, bf16[4,128,512]{2,1,0:T(8,128)(2,1)S(1)}, u32[]{:S(2)}, u32[]{:S(2)}) collective-permute-start(bf16[4,128,512]{2,1,0:T(8,128)(2,1)} %bitcast.27), channel_id=1, source_target_pairs={{1,0},{2,1},{3,2},{4,3},{5,4},{6,5},{7,6},{8,7},{9,8},{10,9},{11,1... | collective-permute-start | bytes 1572872 | tf_op jit(solution)/shard_map/ppermute | solution.py:14
  14.3 1.9 %copy-start = (bf16[24,4,128,128]{3,2,1,0:T(8,128)(2,1)S(1)}, bf16[24,4,128,128]{3,2,1,0:T(8,128)(2,1)}, u32[]{:S(2)}) copy-start(bf16[24,4,128,128]{3,2,1,0:T(8,128)(2,1)} %tile_ref.3) | copy-start | bytes 9437188
  16.1 1.0 copy-start.1
  30.9 5.2 %copy-start.2 = (bf16[512,512]{1,0:T(8,128)(2,1)S(1)}, bf16[512,512]{1,0:T(8,128)(2,1)}, u32[]{:S(2)}) copy-start(bf16[512,512]{1,0:T(8,128)(2,1)} %param.7) | copy-start | bytes 1572868
  33.7 41.7 %collective-permute-start = (bf16[8,4,128,256]{3,2,1,0:T(8,128)(2,1)S(1)}, bf16[8,4,128,256]{3,2,1,0:T(8,128)(2,1)S(1)}, u32[]{:S(2)}, u32[]{:S(2)}) collective-permute-start(bf16[8,4,128,256]{3,2,1,0:T(8,128)(2,1)S(1)} %get-tuple-element.28), channel_id=1, source_target_pairs={{0,1},{1,2},{2,3},{3,4},{4,5},{5,6},{6,7},{7,8},{8,9},{9,10},{10,1... | collective-permute-start | bytes 6291464 | tf_op jit(solution)/shard_map/ppermute | solution.py:14
  53.3 51.2 %copy-start.3 = (bf16[8,4,128,256]{3,2,1,0:T(8,128)(2,1)}, bf16[8,4,128,256]{3,2,1,0:T(8,128)(2,1)S(1)}, u32[]{:S(2)}) copy-start(bf16[8,4,128,256]{3,2,1,0:T(8,128)(2,1)S(1)} %get-tuple-element.20) | copy-start | bytes 6291460
  53.3 36.7 %collective-permute-start.4 = (bf16[8,4,128,256]{3,2,1,0:T(8,128)(2,1)S(1)}, bf16[8,4,128,256]{3,2,1,0:T(8,128)(2,1)S(1)}, u32[]{:S(2)}, u32[]{:S(2)}) collective-permute-start(bf16[8,4,128,256]{3,2,1,0:T(8,128)(2,1)S(1)} %get-tuple-element.26), channel_id=1, source_target_pairs={{1,0},{2,1},{3,2},{4,3},{5,4},{6,5},{7,6},{8,7},{9,8},{10,9},{11,1... | collective-permute-start | bytes 6291464 | tf_op jit(solution)/shard_map/ppermute | solution.py:14
  56.6 18.8 %collective-permute-start.1 = (bf16[4,4,128,256]{3,2,1,0:T(8,128)(2,1)S(1)}, bf16[4,4,128,256]{3,2,1,0:T(8,128)(2,1)S(1)}, u32[]{:S(2)}, u32[]{:S(2)}) collective-permute-start(bf16[4,4,128,256]{3,2,1,0:T(8,128)(2,1)S(1)} %slice_bitcast_fusion.5), channel_id=1, source_target_pairs={{0,2},{2,4},{4,6},{6,8},{8,10},{10,12},{12,14},{14,16},{16,18},{18... | collective-permute-start | bytes 3145736 | tf_op jit(solution)/shard_map/ppermute | solution.py:188
  61.4 14.0 %collective-permute-start.5 = (bf16[4,4,128,256]{3,2,1,0:T(8,128)(2,1)S(1)}, bf16[4,4,128,256]{3,2,1,0:T(8,128)(2,1)S(1)}, u32[]{:S(2)}, u32[]{:S(2)}) collective-permute-start(bf16[4,4,128,256]{3,2,1,0:T(8,128)(2,1)S(1)} %slice_bitcast_fusion.4), channel_id=1, source_target_pairs={{3,1},{5,3},{7,5},{9,7},{11,9},{13,11},{15,13},{17,15},{19,17},{21... | collective-permute-start | bytes 3145736 | tf_op jit(solution)/shard_map/ppermute | solution.py:190
  75.4 58.5 %copy-start.11 = (bf16[4,4,128,256]{3,2,1,0:T(8,128)(2,1)}, bf16[4,4,128,256]{3,2,1,0:T(8,128)(2,1)S(1)}, u32[]{:S(2)}) copy-start(bf16[4,4,128,256]{3,2,1,0:T(8,128)(2,1)S(1)} %collective-permute-done.5) | copy-start | bytes 3145732
  75.4 25.0 %copy-start.5 = (bf16[8,4,128,256]{3,2,1,0:T(8,128)(2,1)}, bf16[8,4,128,256]{3,2,1,0:T(8,128)(2,1)S(1)}, u32[]{:S(2)}) copy-start(bf16[8,4,128,256]{3,2,1,0:T(8,128)(2,1)S(1)} %collective-permute-done) | copy-start | bytes 6291460
  90.0 10.3 %copy-start.6 = (bf16[8,4,128,256]{3,2,1,0:T(8,128)(2,1)}, bf16[8,4,128,256]{3,2,1,0:T(8,128)(2,1)S(1)}, u32[]{:S(2)}) copy-start(bf16[8,4,128,256]{3,2,1,0:T(8,128)(2,1)S(1)} %collective-permute-done.4) | copy-start | bytes 6291460
  90.0 38.5 %collective-permute-start.11 = (bf16[8,4,128,256]{3,2,1,0:T(8,128)(2,1)S(1)}, bf16[8,4,128,256]{3,2,1,0:T(8,128)(2,1)S(1)}, u32[]{:S(2)}, u32[]{:S(2)}) collective-permute-start(bf16[8,4,128,256]{3,2,1,0:T(8,128)(2,1)S(1)} %get-tuple-element.20), channel_id=1, source_target_pairs={{1,0},{2,1},{3,2},{4,3},{5,4},{6,5},{7,6},{8,7},{9,8},{10,9},{11,1... | collective-permute-start | bytes 6291464 | tf_op jit(solution)/shard_map/ppermute | solution.py:14
  95.9 35.6 %collective-permute-start.9 = (bf16[8,4,128,256]{3,2,1,0:T(8,128)(2,1)S(1)}, bf16[8,4,128,256]{3,2,1,0:T(8,128)(2,1)S(1)}, u32[]{:S(2)}, u32[]{:S(2)}) collective-permute-start(bf16[8,4,128,256]{3,2,1,0:T(8,128)(2,1)S(1)} %get-tuple-element.19), channel_id=1, source_target_pairs={{0,1},{1,2},{2,3},{3,4},{4,5},{5,6},{6,7},{7,8},{8,9},{9,10},{10,1... | collective-permute-start | bytes 6291464 | tf_op jit(solution)/shard_map/ppermute | solution.py:14
  97.9 36.0 %collective-permute-start.7 = (bf16[4,4,128,256]{3,2,1,0:T(8,128)(2,1)S(1)}, bf16[4,4,128,256]{3,2,1,0:T(8,128)(2,1)S(1)}, u32[]{:S(2)}, u32[]{:S(2)}) collective-permute-start(bf16[4,4,128,256]{3,2,1,0:T(8,128)(2,1)S(1)} %slice.115), channel_id=1, source_target_pairs={{1,0},{3,2},{5,4},{7,6},{9,8},{11,10},{13,12},{15,14},{17,16},{19,... | collective-permute-start | bytes 3145736 | tf_op jit(solution)/shard_map/ppermute | solution.py:196
  100.3 39.6 %collective-permute-start.6 = (bf16[4,4,128,256]{3,2,1,0:T(8,128)(2,1)}, bf16[4,4,128,256]{3,2,1,0:T(8,128)(2,1)}, u32[]{:S(2)}, u32[]{:S(2)}) collective-permute-start(bf16[4,4,128,256]{3,2,1,0:T(8,128)(2,1)} %slice.112), channel_id=1, source_target_pairs={{0,1},{2,3},{4,5},{6,7},{8,9},{10,11},{12,13},{14,15},{16,17},{18,... | collective-permute-start | bytes 3145736 | tf_op jit(solution)/shard_map/ppermute | solution.py:195
  106.7 37.8 %collective-permute-start.13 = (bf16[4,4,128,256]{3,2,1,0:T(8,128)(2,1)}, bf16[4,4,128,256]{3,2,1,0:T(8,128)(2,1)}, u32[]{:S(2)}, u32[]{:S(2)}) collective-permute-start(bf16[4,4,128,256]{3,2,1,0:T(8,128)(2,1)} %slice.120), channel_id=1, source_target_pairs={{3,1},{5,3},{7,5},{9,7},{11,9},{13,11},{15,13},{17,15},{19,17},{21... | collective-permute-start | bytes 3145736 | tf_op jit(solution)/shard_map/ppermute | solution.py:190
  128.5 5.4 %copy-start.7 = (bf16[8,4,128,256]{3,2,1,0:T(8,128)(2,1)}, bf16[8,4,128,256]{3,2,1,0:T(8,128)(2,1)S(1)}, u32[]{:S(2)}) copy-start(bf16[8,4,128,256]{3,2,1,0:T(8,128)(2,1)S(1)} %collective-permute-done.11) | copy-start | bytes 6291460
  128.5 19.1 %collective-permute-start.8 = (bf16[4,4,128,256]{3,2,1,0:T(8,128)(2,1)}, bf16[4,4,128,256]{3,2,1,0:T(8,128)(2,1)}, u32[]{:S(2)}, u32[]{:S(2)}) collective-permute-start(bf16[4,4,128,256]{3,2,1,0:T(8,128)(2,1)} %slice.117), channel_id=1, source_target_pairs={{0,2},{2,4},{4,6},{6,8},{8,10},{10,12},{12,14},{14,16},{16,18},{18... | collective-permute-start | bytes 3145736 | tf_op jit(solution)/shard_map/ppermute | solution.py:188
  131.5 2.4 %copy-start.9 = (bf16[8,4,128,256]{3,2,1,0:T(8,128)(2,1)}, bf16[8,4,128,256]{3,2,1,0:T(8,128)(2,1)S(1)}, u32[]{:S(2)}) copy-start(bf16[8,4,128,256]{3,2,1,0:T(8,128)(2,1)S(1)} %collective-permute-done.9) | copy-start | bytes 6291460
  131.5 16.1 %collective-permute-start.12 = (bf16[4,4,128,256]{3,2,1,0:T(8,128)(2,1)}, bf16[4,4,128,256]{3,2,1,0:T(8,128)(2,1)}, u32[]{:S(2)}, u32[]{:S(2)}) collective-permute-start(bf16[4,4,128,256]{3,2,1,0:T(8,128)(2,1)} %slice.137), channel_id=1, source_target_pairs={{1,0},{3,2},{5,4},{7,6},{9,8},{11,10},{13,12},{15,14},{17,16},{19,... | collective-permute-start | bytes 3145736 | tf_op jit(solution)/shard_map/ppermute | solution.py:196
  133.9 1.0 copy-start.12
  134.9 12.7 %collective-permute-start.10 = (bf16[4,4,128,256]{3,2,1,0:T(8,128)(2,1)}, bf16[4,4,128,256]{3,2,1,0:T(8,128)(2,1)}, u32[]{:S(2)}, u32[]{:S(2)}) collective-permute-start(bf16[4,4,128,256]{3,2,1,0:T(8,128)(2,1)} %slice.135), channel_id=1, source_target_pairs={{0,1},{2,3},{4,5},{6,7},{8,9},{10,11},{12,13},{14,15},{16,17},{18,... | collective-permute-start | bytes 3145736 | tf_op jit(solution)/shard_map/ppermute | solution.py:195
  139.9 7.7 %copy-start.4 = (bf16[8,4,128,256]{3,2,1,0:T(8,128)(2,1)S(1)}, bf16[8,4,128,256]{3,2,1,0:T(8,128)(2,1)}, u32[]{:S(2)}) copy-start(bf16[8,4,128,256]{3,2,1,0:T(8,128)(2,1)} %copy-done.3) | copy-start | bytes 6291460
  139.9 7.7 %copy-start.8 = (bf16[8,4,128,256]{3,2,1,0:T(8,128)(2,1)S(1)}, bf16[8,4,128,256]{3,2,1,0:T(8,128)(2,1)}, u32[]{:S(2)}) copy-start(bf16[8,4,128,256]{3,2,1,0:T(8,128)(2,1)} %copy-done.7) | copy-start | bytes 6291460
  139.9 7.7 %copy-start.10 = (bf16[8,4,128,256]{3,2,1,0:T(8,128)(2,1)S(1)}, bf16[8,4,128,256]{3,2,1,0:T(8,128)(2,1)}, u32[]{:S(2)}) copy-start(bf16[8,4,128,256]{3,2,1,0:T(8,128)(2,1)} %copy-done.9) | copy-start | bytes 6291460

commit v14 on v11

--- a/solution.py
+++ b/solution.py
@@ -179,9 +179,12 @@
     pieces = []
     for c in range(1):
         behind_one = passed_along(hi, "ao", 1)
-        even_two = lax.ppermute(hi[own_blocks:], "ao", even_up_two)
         ahead_one = passed_along(lo, "ao", -1)
-        odd_two = lax.ppermute(lo[:own_blocks], "ao", odd_down_two)
+        behind_one, ahead_one, hi_tail, lo_head = lax.optimization_barrier(
+            (behind_one, ahead_one, hi[own_blocks:], lo[:own_blocks])
+        )
+        even_two = lax.ppermute(hi_tail, "ao", even_up_two)
+        odd_two = lax.ppermute(lo_head, "ao", odd_down_two)
         relay_behind = lax.ppermute(behind_one[own_blocks:], "ao", even_up_one)
         relay_ahead = lax.ppermute(ahead_one[:own_blocks], "ao", odd_down_one)
         behind_two = jnp.where(is_even, even_two, relay_behind)

time: 179 us -> 186 us (1.039)
  the two profiles are of different devices: /device:TPU:66 before, /device:TPU:6 now
where the time goes in v14:
time: 186 us; the launch traced here: 184 us
  waiting for transfers between devices  70 us (38%)
  starting transfers between devices  41.5 us (22%)
  blocking collectives  29.8 us (16%)
  Pallas kernels  22.2 us (12%)
  other arithmetic  11.1 us (6%)
  local copies, waits for them, and re-layouts  8.12 us (4%)
    ppermute x4, waiting for transfers between devices, passed_along(): lax.ppermute(value, axis, [(source, source + steps) for source in range(f...  44.5 us
    all_to_all x1, blocking collectives, on_device(): gathered = lax.all_to_all(partial_tiles, 'aux', 0, 0, tiled=True)  29.8 us
    ppermute x1, waiting for transfers between devices, on_device(): even_two = lax.ppermute(hi_tail, 'ao', even_up_two)  25.5 us
    ppermute x4, starting transfers between devices, passed_along(): lax.ppermute(value, axis, [(source, source + steps) for source in range(f...  23.2 us
    ppermute x1, starting transfers between devices, on_device(): relay_behind = lax.ppermute(behind_one[own_blocks:], 'ao', even_up_one)  12.1 us
    pallas_call x1, Pallas kernels, on_device(): pl.pallas_call(_left_kernel, grid_spec=pltpu.PrefetchScalarGridSpec(num_s...  9.48 us
    convert_element_type x1, other arithmetic, owner_sum(): return (total + third.astype(jnp.float32)).astype(jnp.bfloat16)  9.45 us
    pallas_call x1, Pallas kernels, on_device(): pl.pallas_call(_right_kernel, grid_spec=pltpu.PrefetchScalarGridSpec(num_...  8.03 us
  transfers between devices with their start and end apart: 8, of which 3 were waited for; matrix products, arithmetic and copies ran while one was open for 1% of the time, Pallas kernels for 10%

profile of v14, /device:TPU:6, one launch (start us, length us, event | category | flops | bytes accessed | tf_op | source)
XLA Modules:
  0.0 183.6 jit_solution(5744359732870816316)
XLA Ops:
  0.0 11.2 %collective-permute-start.2 = (bf16[4,128,512]{2,1,0:T(8,128)(2,1)}, bf16[4,128,512]{2,1,0:T(8,128)(2,1)S(1)}, u32[]{:S(2)}, u32[]{:S(2)}) collective-permute-start(bf16[4,128,512]{2,1,0:T(8,128)(2,1)} %bitcast.7), channel_id=1, source_target_pairs={{2,0},{3,1},{4,2},{5,3},{6,4},{7,5},{8,6},{9,7},{10,8},{11,9},{12,... | collective-permute-start | bytes 1572872 | tf_op jit(solution)/shard_map/ppermute | solution.py:14
  11.2 1.9 %collective-permute-start.1 = (bf16[4,128,512]{2,1,0:T(8,128)(2,1)}, bf16[4,128,512]{2,1,0:T(8,128)(2,1)S(1)}, u32[]{:S(2)}, u32[]{:S(2)}) collective-permute-start(bf16[4,128,512]{2,1,0:T(8,128)(2,1)} %bitcast.8), channel_id=1, source_target_pairs={{1,0},{2,1},{3,2},{4,3},{5,4},{6,5},{7,6},{8,7},{9,8},{10,9},{11,1... | collective-permute-start | bytes 1572872 | tf_op jit(solution)/shard_map/ppermute | solution.py:14
  13.8 0.8 subtract_bitcast_fusion
  14.6 1.9 %copy-done = bf16[24,4,128,128]{3,2,1,0:T(8,128)(2,1)S(1)} copy-done((bf16[24,4,128,128]{3,2,1,0:T(8,128)(2,1)S(1)}, bf16[24,4,128,128]{3,2,1,0:T(8,128)(2,1)}, u32[]{:S(2)}) %copy-start) | copy-done | bytes 3145752
  16.4 1.0 copy-done.1
  17.5 8.0 %shard_map.46 = (bf16[8,4,128,512]{3,2,1,0:T(8,128)(2,1)}, f32[4,4,128,512]{3,2,1,0:T(8,128)}) custom-call(s32[24]{0:T(128)S(1)} %get-tuple-element.21.left_ref, s32[24]{0:T(128)S(1)} %get-tuple-element.20.right_ref, s32[1]{0:T(128)S(6)} %copy.5.count_ref, bf16[24,4,128,128]{3,2,1,0:T(8,128)(2,1)S(1)} %copy-done, bf16[4,128,512]{2,1,0:T(8,128)(2,1)S(1)} %bitcast.9), custom_call_target="tpu_custom_call" | custom-call | tf_op jit(solution)/shard_map/pallas_call | solution.py:139
  25.5 7.9 %collective-permute-start = (bf16[8,4,128,512]{3,2,1,0:T(8,128)(2,1)}, bf16[8,4,128,512]{3,2,1,0:T(8,128)(2,1)S(1)}, u32[]{:S(2)}, u32[]{:S(2)}) collective-permute-start(bf16[8,4,128,512]{3,2,1,0:T(8,128)(2,1)} %get-tuple-element.11.hi_ref), channel_id=1, source_target_pairs={{0,1},{1,2},{2,3},{3,4},{4,5},{5,6},{6,7},{7,8},{8,9},{9,10},{10,1... | collective-permute-start | bytes 12582920 | tf_op jit(solution)/shard_map/ppermute | solution.py:14
  33.5 0.0 collective-permute-done.2
  33.5 0.0 collective-permute-done.1
  33.5 0.0 copy-done.2
  33.5 0.2 pad_maximum_fusion.coeff_ref
  33.7 0.0 copy-start.3
  33.7 9.5 %shard_map.47 = bf16[8,4,128,512]{3,2,1,0:T(8,128)(2,1)} custom-call(s32[24]{0:T(128)S(1)} %get-tuple-element.21.left_ref, s32[24]{0:T(128)S(1)} %get-tuple-element.20.right_ref, s32[1]{0:T(128)S(6)} %copy.5.count_ref, bf16[24,4,128,128]{3,2,1,0:T(8,128)(2,1)S(1)} %copy-done, bf16[12,128,512]{2,1,0:T(8,128)(2,1)S(1)} %pad_maximum_fusion.coeff_ref, ...), custom_call_target="tpu_custom_call" | custom-call | tf_op jit(solution)/shard_map/pallas_call | solution.py:155
  43.2 2.2 %collective-permute-start.3 = (bf16[8,4,128,512]{3,2,1,0:T(8,128)(2,1)}, bf16[8,4,128,512]{3,2,1,0:T(8,128)(2,1)S(1)}, u32[]{:S(2)}, u32[]{:S(2)}) collective-permute-start(bf16[8,4,128,512]{3,2,1,0:T(8,128)(2,1)} %shard_map.47), channel_id=1, source_target_pairs={{1,0},{2,1},{3,2},{4,3},{5,4},{6,5},{7,6},{8,7},{9,8},{10,9},{11,1... | collective-permute-start | bytes 12582920 | tf_op jit(solution)/shard_map/ppermute | solution.py:14
  45.3 1.6 slice.57
  46.9 0.2 slice.72
  47.1 30.5 %collective-permute-done = bf16[8,4,128,512]{3,2,1,0:T(8,128)(2,1)S(1)} collective-permute-done((bf16[8,4,128,512]{3,2,1,0:T(8,128)(2,1)}, bf16[8,4,128,512]{3,2,1,0:T(8,128)(2,1)S(1)}, u32[]{:S(2)}, u32[]{:S(2)}) %collective-permute-start) | collective-permute-done | bytes 4194336 | tf_op jit(solution)/shard_map/ppermute | solution.py:14
  77.6 14.0 %collective-permute-done.3 = bf16[8,4,128,512]{3,2,1,0:T(8,128)(2,1)S(1)} collective-permute-done((bf16[8,4,128,512]{3,2,1,0:T(8,128)(2,1)}, bf16[8,4,128,512]{3,2,1,0:T(8,128)(2,1)S(1)}, u32[]{:S(2)}, u32[]{:S(2)}) %collective-permute-start.3) | collective-permute-done | bytes 4194336 | tf_op jit(solution)/shard_map/ppermute | solution.py:14
  91.7 1.6 slice.59
  93.3 1.8 slice.62
  95.1 1.3 collective-permute-start.6
  96.4 12.1 %collective-permute-start.5 = (bf16[4,4,128,512]{3,2,1,0:T(8,128)(2,1)}, bf16[4,4,128,512]{3,2,1,0:T(8,128)(2,1)}, u32[]{:S(2)}, u32[]{:S(2)}) collective-permute-start(bf16[4,4,128,512]{3,2,1,0:T(8,128)(2,1)} %slice.59), channel_id=1, source_target_pairs={{0,1},{2,3},{4,5},{6,7},{8,9},{10,11},{12,13},{14,15},{16,17},{18,... | collective-permute-start | bytes 6291464 | tf_op jit(solution)/shard_map/ppermute | solution.py:188
  108.5 2.9 %collective-permute-start.4 = (bf16[4,4,128,512]{3,2,1,0:T(8,128)(2,1)}, bf16[4,4,128,512]{3,2,1,0:T(8,128)(2,1)}, u32[]{:S(2)}, u32[]{:S(2)}) collective-permute-start(bf16[4,4,128,512]{3,2,1,0:T(8,128)(2,1)} %slice.57), channel_id=1, source_target_pairs={{0,2},{2,4},{4,6},{6,8},{8,10},{10,12},{12,14},{14,16},{16,18},{18... | collective-permute-start | bytes 6291464 | tf_op jit(solution)/shard_map/ppermute | solution.py:186
  111.3 2.0 %collective-permute-start.7 = (bf16[4,4,128,512]{3,2,1,0:T(8,128)(2,1)S(1)}, bf16[4,4,128,512]{3,2,1,0:T(8,128)(2,1)}, u32[]{:S(2)}, u32[]{:S(2)}) collective-permute-start(bf16[4,4,128,512]{3,2,1,0:T(8,128)(2,1)S(1)} %slice.72), channel_id=1, source_target_pairs={{3,1},{5,3},{7,5},{9,7},{11,9},{13,11},{15,13},{17,15},{19,17},{21... | collective-permute-start | bytes 6291464 | tf_op jit(solution)/shard_map/ppermute | solution.py:187
  113.3 0.0 collective-permute-done.6
  113.3 0.0 collective-permute-done.5
  113.3 25.5 %collective-permute-done.4 = bf16[4,4,128,512]{3,2,1,0:T(8,128)(2,1)} collective-permute-done((bf16[4,4,128,512]{3,2,1,0:T(8,128)(2,1)}, bf16[4,4,128,512]{3,2,1,0:T(8,128)(2,1)}, u32[]{:S(2)}, u32[]{:S(2)}) %collective-permute-start.4) | collective-permute-done | bytes 2097184 | tf_op jit(solution)/shard_map/ppermute | solution.py:186
  138.8 0.0 collective-permute-done.7
  138.8 9.4 %add_convert_fusion = (bf16[4,4,128,512]{3,2,1,0:T(8,128)(2,1)}, bf16[4,4,128,512]{3,2,1,0:T(8,128)(2,1)S(1)}, bf16[4,4,128,512]{3,2,1,0:T(8,128)(2,1)S(1)}) fusion(bf16[4,4,128,512]{3,2,1,0:T(8,128)(2,1)} %collective-permute-done.6, bf16[4,4,128,512]{3,2,1,0:T(8,128)(2,1)} %collective-permute-done.7, bf16[8,4,128,512]{3,2,1,0:T(8,128)(2,1)} %copy-done.6, ...), kind=kLoop, calls=%fused_computation | loop fusion | flops 20971520 | bytes 29360128 | tf_op jit(solution)/shard_map/convert_element_type | solution.py:195
  148.3 4.7 %shard_map.48 = bf16[8,24,16,128]{3,2,1,0:T(8,128)(2,1)S(1)} custom-call(s32[24]{0:T(128)S(1)} %get-tuple-element.21.left_ref, s32[24]{0:T(128)S(1)} %get-tuple-element.20.right_ref, s32[1]{0:T(128)S(6)} %copy.5.count_ref, bf16[4,4,128,512]{3,2,1,0:T(8,128)(2,1)S(1)} %get-tuple-element.19.refs_0_, bf16[4,4,128,512]{3,2,1,0:T(8,128)(2,1)S(1)} %get-tuple-element.18.refs_1_, ...), custom_call_target="tpu_custom_call" | custom-call | tf_op jit(solution)/shard_map/pallas_call | solution.py:207
  153.0 29.8 %all_to_all.5 = bf16[8,24,16,128]{3,2,1,0:T(8,128)(2,1)S(1)} all-to-all(bf16[8,24,16,128]{3,2,1,0:T(8,128)(2,1)S(1)} %shard_map.48), channel_id=1, replica_groups=mesh['aux'=8,'ao'=64] {'aux'}, dimensions={0} | all-to-all | bytes 1572864 | tf_op jit(solution)/shard_map/all_to_all | solution.py:225
  182.8 0.8 fusion
  (10 shorter events, 0.0 us)
Async XLA Ops:
  0.0 33.5 %collective-permute-start.2 = (bf16[4,128,512]{2,1,0:T(8,128)(2,1)}, bf16[4,128,512]{2,1,0:T(8,128)(2,1)S(1)}, u32[]{:S(2)}, u32[]{:S(2)}) collective-permute-start(bf16[4,128,512]{2,1,0:T(8,128)(2,1)} %bitcast.7), channel_id=1, source_target_pairs={{2,0},{3,1},{4,2},{5,3},{6,4},{7,5},{8,6},{9,7},{10,8},{11,9},{12,... | collective-permute-start | bytes 1572872 | tf_op jit(solution)/shard_map/ppermute | solution.py:14
  11.2 22.3 %collective-permute-start.1 = (bf16[4,128,512]{2,1,0:T(8,128)(2,1)}, bf16[4,128,512]{2,1,0:T(8,128)(2,1)S(1)}, u32[]{:S(2)}, u32[]{:S(2)}) collective-permute-start(bf16[4,128,512]{2,1,0:T(8,128)(2,1)} %bitcast.8), channel_id=1, source_target_pairs={{1,0},{2,1},{3,2},{4,3},{5,4},{6,5},{7,6},{8,7},{9,8},{10,9},{11,1... | collective-permute-start | bytes 1572872 | tf_op jit(solution)/shard_map/ppermute | solution.py:14
  14.6 1.9 %copy-start = (bf16[24,4,128,128]{3,2,1,0:T(8,128)(2,1)S(1)}, bf16[24,4,128,128]{3,2,1,0:T(8,128)(2,1)}, u32[]{:S(2)}) copy-start(bf16[24,4,128,128]{3,2,1,0:T(8,128)(2,1)} %tile_ref.3) | copy-start | bytes 9437188
  16.4 1.0 copy-start.1
  17.5 16.0 %copy-start.2 = (bf16[512,512]{1,0:T(8,128)(2,1)S(1)}, bf16[512,512]{1,0:T(8,128)(2,1)}, u32[]{:S(2)}) copy-start(bf16[512,512]{1,0:T(8,128)(2,1)} %param.7) | copy-start | bytes 1572868
  25.5 52.1 %collective-permute-start = (bf16[8,4,128,512]{3,2,1,0:T(8,128)(2,1)}, bf16[8,4,128,512]{3,2,1,0:T(8,128)(2,1)S(1)}, u32[]{:S(2)}, u32[]{:S(2)}) collective-permute-start(bf16[8,4,128,512]{3,2,1,0:T(8,128)(2,1)} %get-tuple-element.11.hi_ref), channel_id=1, source_target_pairs={{0,1},{1,2},{2,3},{3,4},{4,5},{5,6},{6,7},{7,8},{8,9},{9,10},{10,1... | collective-permute-start | bytes 12582920 | tf_op jit(solution)/shard_map/ppermute | solution.py:14
  33.7 11.7 %copy-start.3 = (bf16[8,4,128,512]{3,2,1,0:T(8,128)(2,1)S(1)}, bf16[8,4,128,512]{3,2,1,0:T(8,128)(2,1)}, u32[]{:S(2)}) copy-start(bf16[8,4,128,512]{3,2,1,0:T(8,128)(2,1)} %get-tuple-element.11.hi_ref) | copy-start | bytes 12582916
  43.2 3.8 %copy-start.4 = (bf16[8,4,128,512]{3,2,1,0:T(8,128)(2,1)S(1)}, bf16[8,4,128,512]{3,2,1,0:T(8,128)(2,1)}, u32[]{:S(2)}) copy-start(bf16[8,4,128,512]{3,2,1,0:T(8,128)(2,1)} %shard_map.47) | copy-start | bytes 12582916
  43.2 48.5 %collective-permute-start.3 = (bf16[8,4,128,512]{3,2,1,0:T(8,128)(2,1)}, bf16[8,4,128,512]{3,2,1,0:T(8,128)(2,1)S(1)}, u32[]{:S(2)}, u32[]{:S(2)}) collective-permute-start(bf16[8,4,128,512]{3,2,1,0:T(8,128)(2,1)} %shard_map.47), channel_id=1, source_target_pairs={{1,0},{2,1},{3,2},{4,3},{5,4},{6,5},{7,6},{8,7},{9,8},{10,9},{11,1... | collective-permute-start | bytes 12582920 | tf_op jit(solution)/shard_map/ppermute | solution.py:14
  77.6 15.7 %copy-start.5 = (bf16[8,4,128,512]{3,2,1,0:T(8,128)(2,1)}, bf16[8,4,128,512]{3,2,1,0:T(8,128)(2,1)S(1)}, u32[]{:S(2)}) copy-start(bf16[8,4,128,512]{3,2,1,0:T(8,128)(2,1)S(1)} %collective-permute-done) | copy-start | bytes 12582916
  91.7 3.4 %copy-start.6 = (bf16[8,4,128,512]{3,2,1,0:T(8,128)(2,1)}, bf16[8,4,128,512]{3,2,1,0:T(8,128)(2,1)S(1)}, u32[]{:S(2)}) copy-start(bf16[8,4,128,512]{3,2,1,0:T(8,128)(2,1)S(1)} %collective-permute-done.3) | copy-start | bytes 12582916
  95.1 18.3 %collective-permute-start.6 = (bf16[4,4,128,512]{3,2,1,0:T(8,128)(2,1)}, bf16[4,4,128,512]{3,2,1,0:T(8,128)(2,1)}, u32[]{:S(2)}, u32[]{:S(2)}) collective-permute-start(bf16[4,4,128,512]{3,2,1,0:T(8,128)(2,1)} %slice.62), channel_id=1, source_target_pairs={{1,0},{3,2},{5,4},{7,6},{9,8},{11,10},{13,12},{15,14},{17,16},{19,... | collective-permute-start | bytes 6291464 | tf_op jit(solution)/shard_map/ppermute | solution.py:189
  96.4 17.0 %collective-permute-start.5 = (bf16[4,4,128,512]{3,2,1,0:T(8,128)(2,1)}, bf16[4,4,128,512]{3,2,1,0:T(8,128)(2,1)}, u32[]{:S(2)}, u32[]{:S(2)}) collective-permute-start(bf16[4,4,128,512]{3,2,1,0:T(8,128)(2,1)} %slice.59), channel_id=1, source_target_pairs={{0,1},{2,3},{4,5},{6,7},{8,9},{10,11},{12,13},{14,15},{16,17},{18,... | collective-permute-start | bytes 6291464 | tf_op jit(solution)/shard_map/ppermute | solution.py:188
  108.5 30.3 %collective-permute-start.4 = (bf16[4,4,128,512]{3,2,1,0:T(8,128)(2,1)}, bf16[4,4,128,512]{3,2,1,0:T(8,128)(2,1)}, u32[]{:S(2)}, u32[]{:S(2)}) collective-permute-start(bf16[4,4,128,512]{3,2,1,0:T(8,128)(2,1)} %slice.57), channel_id=1, source_target_pairs={{0,2},{2,4},{4,6},{6,8},{8,10},{10,12},{12,14},{14,16},{16,18},{18... | collective-permute-start | bytes 6291464 | tf_op jit(solution)/shard_map/ppermute | solution.py:186
  111.3 27.5 %collective-permute-start.7 = (bf16[4,4,128,512]{3,2,1,0:T(8,128)(2,1)S(1)}, bf16[4,4,128,512]{3,2,1,0:T(8,128)(2,1)}, u32[]{:S(2)}, u32[]{:S(2)}) collective-permute-start(bf16[4,4,128,512]{3,2,1,0:T(8,128)(2,1)S(1)} %slice.72), channel_id=1, source_target_pairs={{3,1},{5,3},{7,5},{9,7},{11,9},{13,11},{15,13},{17,15},{19,17},{21... | collective-permute-start | bytes 6291464 | tf_op jit(solution)/shard_map/ppermute | solution.py:187

commit v15 on v11

--- a/solution.py
+++ b/solution.py
@@ -184,20 +184,26 @@
         odd_two = lax.ppermute(lo[:own_blocks], "ao", odd_down_two)
         relay_behind = lax.ppermute(behind_one[own_blocks:], "ao", even_up_one)
         relay_ahead = lax.ppermute(ahead_one[:own_blocks], "ao", odd_down_one)
-        behind_two = jnp.where(is_even, even_two, relay_behind)
-        ahead_two = jnp.where(is_even, relay_ahead, odd_two)
 
         def owner_sum(first, second, third):
             total = first.astype(jnp.float32) + second.astype(jnp.float32)
             return (total + third.astype(jnp.float32)).astype(jnp.bfloat16)
 
-        pieces += [
-            owner_sum(behind_two, behind_one[:own_blocks], lo[:own_blocks]),
-            owner_sum(
-                behind_one[own_blocks:], hi[:own_blocks], ahead_one[:own_blocks]
-            ),
-            owner_sum(hi[own_blocks:], ahead_one[own_blocks:], ahead_two),
-        ]
+        def sums(behind_two, ahead_two):
+            return (
+                owner_sum(behind_two, behind_one[:own_blocks], lo[:own_blocks]),
+                owner_sum(behind_one[own_blocks:], hi[:own_blocks], ahead_one[:own_blocks]),
+                owner_sum(hi[own_blocks:], ahead_one[own_blocks:], ahead_two),
+            )
+
+        pieces += list(
+            lax.cond(
+                is_even,
+                lambda _: sums(even_two, relay_ahead),
+                lambda _: sums(relay_behind, odd_two),
+                None,
+            )
+        )
     aux_devices = lax.axis_size("aux")
     share = block_size // aux_devices
     whole = pl.BlockSpec(block_shape, lambda s, l, r, n: (0, 0, 0, 0))

time: 179 us -> 172 us (0.961)
  the two profiles are of different devices: /device:TPU:66 before, /device:TPU:3 now
where the time goes in v15:
time: 172 us; the launch traced here: 171 us
  waiting for transfers between devices  62.6 us (36%)
  Pallas kernels  33.8 us (20%)
  blocking collectives  26.1 us (15%)
  starting transfers between devices  24.2 us (14%)
  local copies, waits for them, and re-layouts  13.8 us (8%)
  other arithmetic  9.72 us (6%)
    ppermute x4, waiting for transfers between devices, passed_along(): lax.ppermute(value, axis, [(source, source + steps) for source in range(f...  59.8 us
    all_to_all x1, blocking collectives, on_device(): gathered = lax.all_to_all(partial_tiles, 'aux', 0, 0, tiled=True)  26.1 us
    ppermute x4, starting transfers between devices, passed_along(): lax.ppermute(value, axis, [(source, source + steps) for source in range(f...  17.3 us
    pallas_call x1, Pallas kernels, on_device(): pl.pallas_call(_right_kernel, grid_spec=pltpu.PrefetchScalarGridSpec(num_...  12.3 us
    pallas_call x1, Pallas kernels, on_device(): pl.pallas_call(_contract_kernel, grid_spec=pltpu.PrefetchScalarGridSpec(n...  10.9 us
    pallas_call x1, Pallas kernels, on_device(): pl.pallas_call(_left_kernel, grid_spec=pltpu.PrefetchScalarGridSpec(num_s...  10.7 us
    convert_element_type x1, other arithmetic, owner_sum(): return (total + third.astype(jnp.float32)).astype(jnp.bfloat16)  8.03 us
    unnamed x16, local copies, waits for them, and re-layouts  5.76 us
  transfers between devices with their start and end apart: 8, of which 3 were waited for; matrix products, arithmetic and copies ran while one was open for 5% of the time, Pallas kernels for 13%

profile of v15, /device:TPU:3, one launch (start us, length us, event | category | flops | bytes accessed | tf_op | source)
XLA Modules:
  0.0 171.1 jit_solution(2534398530207754820)
XLA Ops:
  0.0 10.6 %collective-permute-start.3 = (bf16[4,128,512]{2,1,0:T(8,128)(2,1)}, bf16[4,128,512]{2,1,0:T(8,128)(2,1)S(1)}, u32[]{:S(2)}, u32[]{:S(2)}) collective-permute-start(bf16[4,128,512]{2,1,0:T(8,128)(2,1)} %bitcast.7), channel_id=1, source_target_pairs={{2,0},{3,1},{4,2},{5,3},{6,4},{7,5},{8,6},{9,7},{10,8},{11,9},{12,... | collective-permute-start | bytes 1572872 | tf_op jit(solution)/shard_map/ppermute | solution.py:14
  10.6 2.9 %collective-permute-start.2 = (bf16[4,128,512]{2,1,0:T(8,128)(2,1)}, bf16[4,128,512]{2,1,0:T(8,128)(2,1)S(1)}, u32[]{:S(2)}, u32[]{:S(2)}) collective-permute-start(bf16[4,128,512]{2,1,0:T(8,128)(2,1)} %bitcast.8), channel_id=1, source_target_pairs={{1,0},{2,1},{3,2},{4,3},{5,4},{6,5},{7,6},{8,7},{9,8},{10,9},{11,1... | collective-permute-start | bytes 1572872 | tf_op jit(solution)/shard_map/ppermute | solution.py:14
  14.2 0.8 subtract_bitcast_fusion
  14.9 1.9 %copy-done = bf16[24,4,128,128]{3,2,1,0:T(8,128)(2,1)S(1)} copy-done((bf16[24,4,128,128]{3,2,1,0:T(8,128)(2,1)S(1)}, bf16[24,4,128,128]{3,2,1,0:T(8,128)(2,1)}, u32[]{:S(2)}) %copy-start) | copy-done | bytes 3145752
  16.8 1.0 copy-done.1
  17.9 12.3 %shard_map.46 = (bf16[8,4,128,512]{3,2,1,0:T(8,128)(2,1)S(1)}, f32[4,4,128,512]{3,2,1,0:T(8,128)}) custom-call(s32[24]{0:T(128)S(1)} %get-tuple-element.85.left_ref, s32[24]{0:T(128)S(1)} %get-tuple-element.84.right_ref, s32[1]{0:T(128)S(6)} %copy.11.count_ref, bf16[24,4,128,128]{3,2,1,0:T(8,128)(2,1)S(1)} %copy-done, bf16[4,128,512]{2,1,0:T(8,128)(2,1)S(1)} %bitcast.9), custom_call_target="tpu_custom_call" | custom-call | tf_op jit(solution)/shard_map/pallas_call | solution.py:139
  30.1 1.9 %collective-permute-start = (bf16[8,4,128,512]{3,2,1,0:T(8,128)(2,1)S(1)}, bf16[8,4,128,512]{3,2,1,0:T(8,128)(2,1)}, u32[]{:S(2)}, u32[]{:S(2)}) collective-permute-start(bf16[8,4,128,512]{3,2,1,0:T(8,128)(2,1)S(1)} %get-tuple-element.64.hi_ref), channel_id=1, source_target_pairs={{0,1},{1,2},{2,3},{3,4},{4,5},{5,6},{6,7},{7,8},{8,9},{9,10},{10,1... | collective-permute-start | bytes 12582920 | tf_op jit(solution)/shard_map/ppermute | solution.py:14
  32.1 0.0 collective-permute-done.3
  32.1 0.0 collective-permute-done.2
  32.1 0.2 pad_maximum_fusion.coeff_ref
  32.3 10.7 %shard_map.47 = bf16[8,4,128,512]{3,2,1,0:T(8,128)(2,1)S(1)} custom-call(s32[24]{0:T(128)S(1)} %get-tuple-element.85.left_ref, s32[24]{0:T(128)S(1)} %get-tuple-element.84.right_ref, s32[1]{0:T(128)S(6)} %copy.11.count_ref, bf16[24,4,128,128]{3,2,1,0:T(8,128)(2,1)S(1)} %copy-done, bf16[12,128,512]{2,1,0:T(8,128)(2,1)S(1)} %pad_maximum_fusion.coeff_ref, ...), custom_call_target="tpu_custom_call" | custom-call | tf_op jit(solution)/shard_map/pallas_call | solution.py:155
  43.0 1.9 %collective-permute-start.4 = (bf16[8,4,128,512]{3,2,1,0:T(8,128)(2,1)S(1)}, bf16[8,4,128,512]{3,2,1,0:T(8,128)(2,1)S(1)}, u32[]{:S(2)}, u32[]{:S(2)}) collective-permute-start(bf16[8,4,128,512]{3,2,1,0:T(8,128)(2,1)S(1)} %shard_map.47), channel_id=1, source_target_pairs={{1,0},{2,1},{3,2},{4,3},{5,4},{6,5},{7,6},{8,7},{9,8},{10,9},{11,1... | collective-permute-start | bytes 12582920 | tf_op jit(solution)/shard_map/ppermute | solution.py:14
  44.9 1.6 slice.88
  46.5 0.8 collective-permute-start.6
  47.3 1.6 slice.99
  48.9 2.2 %collective-permute-start.5 = (bf16[4,4,128,512]{3,2,1,0:T(8,128)(2,1)}, bf16[4,4,128,512]{3,2,1,0:T(8,128)(2,1)}, u32[]{:S(2)}, u32[]{:S(2)}) collective-permute-start(bf16[4,4,128,512]{3,2,1,0:T(8,128)(2,1)} %slice.99), channel_id=1, source_target_pairs={{3,1},{5,3},{7,5},{9,7},{11,9},{13,11},{15,13},{17,15},{19,17},{21... | collective-permute-start | bytes 6291464 | tf_op jit(solution)/shard_map/ppermute | solution.py:184
  51.0 48.9 %collective-permute-done = bf16[8,4,128,512]{3,2,1,0:T(8,128)(2,1)} collective-permute-done((bf16[8,4,128,512]{3,2,1,0:T(8,128)(2,1)S(1)}, bf16[8,4,128,512]{3,2,1,0:T(8,128)(2,1)}, u32[]{:S(2)}, u32[]{:S(2)}) %collective-permute-start) | collective-permute-done | bytes 4194336 | tf_op jit(solution)/shard_map/ppermute | solution.py:14
  100.0 3.1 %slice.98 = bf16[4,4,128,512]{3,2,1,0:T(8,128)(2,1)} slice(bf16[8,4,128,512]{3,2,1,0:T(8,128)(2,1)} %collective-permute-done), slice={[4:8], [0:4], [0:128], [0:512]} | slice | bytes 4194304 | tf_op jit(solution)/shard_map/slice | solution.py:185
  103.1 1.3 collective-permute-start.1
  104.4 10.9 %collective-permute-done.4 = bf16[8,4,128,512]{3,2,1,0:T(8,128)(2,1)S(1)} collective-permute-done((bf16[8,4,128,512]{3,2,1,0:T(8,128)(2,1)S(1)}, bf16[8,4,128,512]{3,2,1,0:T(8,128)(2,1)S(1)}, u32[]{:S(2)}, u32[]{:S(2)}) %collective-permute-start.4) | collective-permute-done | bytes 4194336 | tf_op jit(solution)/shard_map/ppermute | solution.py:14
  115.3 1.8 %slice.100 = bf16[4,4,128,512]{3,2,1,0:T(8,128)(2,1)} slice(bf16[8,4,128,512]{3,2,1,0:T(8,128)(2,1)S(1)} %collective-permute-done.4), slice={[0:4], [0:4], [0:128], [0:512]} | slice | bytes 4194304 | tf_op jit(solution)/shard_map/slice | solution.py:186
  117.1 0.9 copy-done.5
  117.9 2.6 %collective-permute-start.7 = (bf16[4,4,128,512]{3,2,1,0:T(8,128)(2,1)}, bf16[4,4,128,512]{3,2,1,0:T(8,128)(2,1)}, u32[]{:S(2)}, u32[]{:S(2)}) collective-permute-start(bf16[4,4,128,512]{3,2,1,0:T(8,128)(2,1)} %slice.100), channel_id=1, source_target_pairs={{1,0},{3,2},{5,4},{7,6},{9,8},{11,10},{13,12},{15,14},{17,16},{19,... | collective-permute-start | bytes 6291464 | tf_op jit(solution)/shard_map/ppermute | solution.py:186
  120.6 0.0 collective-permute-done.5
  120.6 2.8 %collective-permute-done.7 = bf16[4,4,128,512]{3,2,1,0:T(8,128)(2,1)} collective-permute-done((bf16[4,4,128,512]{3,2,1,0:T(8,128)(2,1)}, bf16[4,4,128,512]{3,2,1,0:T(8,128)(2,1)}, u32[]{:S(2)}, u32[]{:S(2)}) %collective-permute-start.7) | collective-permute-done | bytes 2097184 | tf_op jit(solution)/shard_map/ppermute | solution.py:186
  123.3 8.0 %conditional.4 = (bf16[4,4,128,512]{3,2,1,0:T(8,128)(2,1)S(1)}, bf16[4,4,128,512]{3,2,1,0:T(8,128)(2,1)S(1)}, bf16[4,4,128,512]{3,2,1,0:T(8,128)(2,1)S(1)}) conditional(s32[]{:T(128)} %convert_element_type.136, (bf16[4,4,128,512]{3,2,1,0:T(8,128)(2,1)}, bf16[8,4,128,512]{3,2,1,0:T(8,128)(2,1)}, bf16[8,4,128,512]{3,2,1,0:T(8,128)(2,1)}, ...), branch_computations={%region_0.1_spmd, %region_1.2_spmd} | conditional | flops 18874368 | bytes 33554484
  123.3 8.0 %add_convert_fusion = (bf16[4,4,128,512]{3,2,1,0:T(8,128)(2,1)S(1)}, bf16[4,4,128,512]{3,2,1,0:T(8,128)(2,1)S(1)}, bf16[4,4,128,512]{3,2,1,0:T(8,128)(2,1)S(1)}) fusion(bf16[4,4,128,512]{3,2,1,0:T(8,128)(2,1)} %get-tuple-element.52, bf16[8,4,128,512]{3,2,1,0:T(8,128)(2,1)} %get-tuple-element.51, bf16[8,4,128,512]{3,2,1,0:T(8,128)(2,1)} %get-tuple-element.50, ...), kind=kLoop, calls=%fused_computation | loop fusion | flops 18874368 | bytes 25165824 | tf_op jit(solution)/shard_map/cond/branch_0_fun/convert_element_type | solution.py:190
  131.4 1.3 copy-done.6
  132.7 0.7 copy-done.7
  133.4 10.9 %shard_map.48 = bf16[8,24,16,128]{3,2,1,0:T(8,128)(2,1)S(1)} custom-call(s32[24]{0:T(128)S(1)} %get-tuple-element.85.left_ref, s32[24]{0:T(128)S(1)} %get-tuple-element.84.right_ref, s32[1]{0:T(128)S(6)} %copy.11.count_ref, bf16[4,4,128,512]{3,2,1,0:T(8,128)(2,1)} %copy-done.7, bf16[4,4,128,512]{3,2,1,0:T(8,128)(2,1)} %copy-done.6, ...), custom_call_target="tpu_custom_call" | custom-call | tf_op jit(solution)/shard_map/pallas_call | solution.py:210
  144.2 26.1 %all_to_all.5 = bf16[8,24,16,128]{3,2,1,0:T(8,128)(2,1)S(1)} all-to-all(bf16[8,24,16,128]{3,2,1,0:T(8,128)(2,1)S(1)} %shard_map.48), channel_id=1, replica_groups=mesh['aux'=8,'ao'=64] {'aux'}, dimensions={0} | all-to-all | bytes 1572864 | tf_op jit(solution)/shard_map/all_to_all | solution.py:228
  170.3 0.8 fusion
  (13 shorter events, 0.0 us)
Async XLA Ops:
  0.0 32.1 %collective-permute-start.3 = (bf16[4,128,512]{2,1,0:T(8,128)(2,1)}, bf16[4,128,512]{2,1,0:T(8,128)(2,1)S(1)}, u32[]{:S(2)}, u32[]{:S(2)}) collective-permute-start(bf16[4,128,512]{2,1,0:T(8,128)(2,1)} %bitcast.7), channel_id=1, source_target_pairs={{2,0},{3,1},{4,2},{5,3},{6,4},{7,5},{8,6},{9,7},{10,8},{11,9},{12,... | collective-permute-start | bytes 1572872 | tf_op jit(solution)/shard_map/ppermute | solution.py:14
  10.6 21.4 %collective-permute-start.2 = (bf16[4,128,512]{2,1,0:T(8,128)(2,1)}, bf16[4,128,512]{2,1,0:T(8,128)(2,1)S(1)}, u32[]{:S(2)}, u32[]{:S(2)}) collective-permute-start(bf16[4,128,512]{2,1,0:T(8,128)(2,1)} %bitcast.8), channel_id=1, source_target_pairs={{1,0},{2,1},{3,2},{4,3},{5,4},{6,5},{7,6},{8,7},{9,8},{10,9},{11,1... | collective-permute-start | bytes 1572872 | tf_op jit(solution)/shard_map/ppermute | solution.py:14
  14.9 1.9 %copy-start = (bf16[24,4,128,128]{3,2,1,0:T(8,128)(2,1)S(1)}, bf16[24,4,128,128]{3,2,1,0:T(8,128)(2,1)}, u32[]{:S(2)}) copy-start(bf16[24,4,128,128]{3,2,1,0:T(8,128)(2,1)} %tile_ref.3) | copy-start | bytes 9437188
  16.8 1.0 copy-start.1
  17.9 14.2 %copy-start.2 = (bf16[512,512]{1,0:T(8,128)(2,1)S(1)}, bf16[512,512]{1,0:T(8,128)(2,1)}, u32[]{:S(2)}) copy-start(bf16[512,512]{1,0:T(8,128)(2,1)} %param.9) | copy-start | bytes 1572868
  30.1 14.8 %copy-start.3 = (bf16[8,4,128,512]{3,2,1,0:T(8,128)(2,1)}, bf16[8,4,128,512]{3,2,1,0:T(8,128)(2,1)S(1)}, u32[]{:S(2)}) copy-start(bf16[8,4,128,512]{3,2,1,0:T(8,128)(2,1)S(1)} %get-tuple-element.64.hi_ref) | copy-start | bytes 12582916
  30.1 69.8 %collective-permute-start = (bf16[8,4,128,512]{3,2,1,0:T(8,128)(2,1)S(1)}, bf16[8,4,128,512]{3,2,1,0:T(8,128)(2,1)}, u32[]{:S(2)}, u32[]{:S(2)}) collective-permute-start(bf16[8,4,128,512]{3,2,1,0:T(8,128)(2,1)S(1)} %get-tuple-element.64.hi_ref), channel_id=1, source_target_pairs={{0,1},{1,2},{2,3},{3,4},{4,5},{5,6},{6,7},{7,8},{8,9},{9,10},{10,1... | collective-permute-start | bytes 12582920 | tf_op jit(solution)/shard_map/ppermute | solution.py:14
  43.0 4.3 %copy-start.4 = (bf16[8,4,128,512]{3,2,1,0:T(8,128)(2,1)}, bf16[8,4,128,512]{3,2,1,0:T(8,128)(2,1)S(1)}, u32[]{:S(2)}) copy-start(bf16[8,4,128,512]{3,2,1,0:T(8,128)(2,1)S(1)} %shard_map.47) | copy-start | bytes 12582916
  43.0 72.3 %collective-permute-start.4 = (bf16[8,4,128,512]{3,2,1,0:T(8,128)(2,1)S(1)}, bf16[8,4,128,512]{3,2,1,0:T(8,128)(2,1)S(1)}, u32[]{:S(2)}, u32[]{:S(2)}) collective-permute-start(bf16[8,4,128,512]{3,2,1,0:T(8,128)(2,1)S(1)} %shard_map.47), channel_id=1, source_target_pairs={{1,0},{2,1},{3,2},{4,3},{5,4},{6,5},{7,6},{8,7},{9,8},{10,9},{11,1... | collective-permute-start | bytes 12582920 | tf_op jit(solution)/shard_map/ppermute | solution.py:14
  46.5 74.1 %collective-permute-start.6 = (bf16[4,4,128,512]{3,2,1,0:T(8,128)(2,1)}, bf16[4,4,128,512]{3,2,1,0:T(8,128)(2,1)S(1)}, u32[]{:S(2)}, u32[]{:S(2)}) collective-permute-start(bf16[4,4,128,512]{3,2,1,0:T(8,128)(2,1)} %slice.88), channel_id=1, source_target_pairs={{0,2},{2,4},{4,6},{6,8},{8,10},{10,12},{12,14},{14,16},{16,18},{18... | collective-permute-start | bytes 6291464 | tf_op jit(solution)/shard_map/ppermute | solution.py:182
  48.9 71.7 %collective-permute-start.5 = (bf16[4,4,128,512]{3,2,1,0:T(8,128)(2,1)}, bf16[4,4,128,512]{3,2,1,0:T(8,128)(2,1)}, u32[]{:S(2)}, u32[]{:S(2)}) collective-permute-start(bf16[4,4,128,512]{3,2,1,0:T(8,128)(2,1)} %slice.99), channel_id=1, source_target_pairs={{3,1},{5,3},{7,5},{9,7},{11,9},{13,11},{15,13},{17,15},{19,17},{21... | collective-permute-start | bytes 6291464 | tf_op jit(solution)/shard_map/ppermute | solution.py:184
  103.1 17.5 %collective-permute-start.1 = (bf16[4,4,128,512]{3,2,1,0:T(8,128)(2,1)}, bf16[4,4,128,512]{3,2,1,0:T(8,128)(2,1)}, u32[]{:S(2)}, u32[]{:S(2)}) collective-permute-start(bf16[4,4,128,512]{3,2,1,0:T(8,128)(2,1)} %slice.98), channel_id=1, source_target_pairs={{0,1},{2,3},{4,5},{6,7},{8,9},{10,11},{12,13},{14,15},{16,17},{18,... | collective-permute-start | bytes 6291464 | tf_op jit(solution)/shard_map/ppermute | solution.py:185
  115.3 2.7 %copy-start.5 = (bf16[8,4,128,512]{3,2,1,0:T(8,128)(2,1)}, bf16[8,4,128,512]{3,2,1,0:T(8,128)(2,1)S(1)}, u32[]{:S(2)}) copy-start(bf16[8,4,128,512]{3,2,1,0:T(8,128)(2,1)S(1)} %collective-permute-done.4) | copy-start | bytes 12582916
  117.9 5.4 %collective-permute-start.7 = (bf16[4,4,128,512]{3,2,1,0:T(8,128)(2,1)}, bf16[4,4,128,512]{3,2,1,0:T(8,128)(2,1)}, u32[]{:S(2)}, u32[]{:S(2)}) collective-permute-start(bf16[4,4,128,512]{3,2,1,0:T(8,128)(2,1)} %slice.100), channel_id=1, source_target_pairs={{1,0},{3,2},{5,4},{7,6},{9,8},{11,10},{13,12},{15,14},{17,16},{19,... | collective-permute-start | bytes 6291464 | tf_op jit(solution)/shard_map/ppermute | solution.py:186
  131.4 1.3 copy-start.6
  131.4 2.0 %copy-start.7 = (bf16[4,4,128,512]{3,2,1,0:T(8,128)(2,1)}, bf16[4,4,128,512]{3,2,1,0:T(8,128)(2,1)S(1)}, u32[]{:S(2)}) copy-start(bf16[4,4,128,512]{3,2,1,0:T(8,128)(2,1)S(1)} %get-tuple-element.75.refs_0_) | copy-start | bytes 6291460

commit v16 on v15

--- a/solution.py
+++ b/solution.py
@@ -14,7 +14,7 @@
     return lax.ppermute(value, axis, [(source, source + steps) for source in range(first, last)])
 
 
-def _right_kernel(left_ref, right_ref, count_ref, tile_ref, coeff_ref, hi_ref, part_ref, acc_ref):
+def _right_kernel(left_ref, right_ref, count_ref, tile_ref, coeff_ref, near_ref, far_ref, part_ref, acc_ref):
     slot = pl.program_id(0)
     own_blocks = part_ref.shape[0]
 
@@ -39,10 +39,11 @@
     @pl.when(slot == pl.num_programs(0) - 1)
     def _():
         part_ref[...] = acc_ref[:own_blocks]
-        hi_ref[...] = acc_ref[own_blocks:].astype(hi_ref.dtype)
-
-
-def _left_kernel(left_ref, right_ref, count_ref, tile_ref, coeff_ref, part_ref, hi_ref, lo_ref, acc_ref):
+        near_ref[...] = acc_ref[own_blocks : 2 * own_blocks].astype(near_ref.dtype)
+        far_ref[...] = acc_ref[2 * own_blocks :].astype(far_ref.dtype)
+
+
+def _left_kernel(left_ref, right_ref, count_ref, tile_ref, coeff_ref, part_ref, lo_ref, acc_ref):
     slot = pl.program_id(0)
     own_blocks = part_ref.shape[0]
 
@@ -64,8 +65,7 @@
 
     @pl.when(slot == pl.num_programs(0) - 1)
     def _():
-        lo_ref[:own_blocks] = acc_ref[...].astype(lo_ref.dtype)
-        lo_ref[own_blocks:] = hi_ref[:own_blocks]
+        lo_ref[...] = acc_ref[...].astype(lo_ref.dtype)
 
 
 def _contract_kernel(left_ref, right_ref, count_ref, *refs):
@@ -136,17 +136,18 @@
     params = pltpu.CompilerParams(
         dimension_semantics=("arbitrary",), vmem_limit_bytes=48 * 1024 * 1024
     )
-    hi, part = pl.pallas_call(
+    hi_near, hi_far, part = pl.pallas_call(
         _right_kernel,
         grid_spec=pltpu.PrefetchScalarGridSpec(
             num_scalar_prefetch=3,
             grid=(pair_slots,),
             in_specs=[tile_spec, fixed((own_blocks, block_size, orbitals))],
-            out_specs=[fixed(wide_shape), fixed(own_shape)],
+            out_specs=[fixed(own_shape), fixed(own_shape), fixed(own_shape)],
             scratch_shapes=[pltpu.VMEM((window_blocks,) + own_shape[1:], jnp.float32)],
         ),
         out_shape=[
-            jax.ShapeDtypeStruct(wide_shape, jnp.bfloat16),
+            jax.ShapeDtypeStruct(own_shape, jnp.bfloat16),
+            jax.ShapeDtypeStruct(own_shape, jnp.bfloat16),
             jax.ShapeDtypeStruct(own_shape, jnp.float32),
         ],
         compiler_params=params,
@@ -161,14 +162,13 @@
                 tile_spec,
                 fixed((window_blocks, block_size, orbitals)),
                 fixed(own_shape),
-                fixed(wide_shape),
             ],
-            out_specs=fixed(wide_shape),
+            out_specs=fixed(own_shape),
             scratch_shapes=[pltpu.VMEM(own_shape, jnp.float32)],
         ),
-        out_shape=jax.ShapeDtypeStruct(wide_shape, jnp.bfloat16),
+        out_shape=jax.ShapeDtypeStruct(own_shape, jnp.bfloat16),
         compiler_params=params,
-    )(left_rel, right_rel, count, tiles, window_coeff, part, hi)
+    )(left_rel, right_rel, count, tiles, window_coeff, part)
 
     block_shape = own_shape
     is_even = (owner_index % 2) == 0
@@ -178,12 +178,14 @@
     odd_down_one = [(s, s - 1) for s in range(1, devices, 2)]
     pieces = []
     for c in range(1):
-        behind_one = passed_along(hi, "ao", 1)
-        even_two = lax.ppermute(hi[own_blocks:], "ao", even_up_two)
-        ahead_one = passed_along(lo, "ao", -1)
-        odd_two = lax.ppermute(lo[:own_blocks], "ao", odd_down_two)
-        relay_behind = lax.ppermute(behind_one[own_blocks:], "ao", even_up_one)
-        relay_ahead = lax.ppermute(ahead_one[:own_blocks], "ao", odd_down_one)
+        behind_near = passed_along(hi_near, "ao", 1)
+        behind_far = passed_along(hi_far, "ao", 1)
+        even_two = lax.ppermute(hi_far, "ao", even_up_two)
+        ahead_own = passed_along(lo, "ao", -1)
+        ahead_near = passed_along(hi_near, "ao", -1)
+        odd_two = lax.ppermute(lo, "ao", odd_down_two)
+        relay_behind = lax.ppermute(behind_far, "ao", even_up_one)
+        relay_ahead = lax.ppermute(ahead_own, "ao", odd_down_one)
 
         def owner_sum(first, second, third):
             total = first.astype(jnp.float32) + second.astype(jnp.float32)
@@ -191,9 +193,9 @@
 
         def sums(behind_two, ahead_two):
             return (
-                owner_sum(behind_two, behind_one[:own_blocks], lo[:own_blocks]),
-                owner_sum(behind_one[own_blocks:], hi[:own_blocks], ahead_one[:own_blocks]),
-                owner_sum(hi[own_blocks:], ahead_one[own_blocks:], ahead_two),
+                owner_sum(behind_two, behind_near, lo),
+                owner_sum(behind_far, hi_near, ahead_own),
+                owner_sum(hi_far, ahead_near, ahead_two),
             )
 
         pieces += list(

time: 172 us -> 166 us (0.965)
  the two profiles are of different devices: /device:TPU:3 before, /device:TPU:2 now
where the time goes in v16:
time: 166 us
  waiting for transfers between devices  52.1 us (31%)
  Pallas kernels  34.5 us (21%)
  starting transfers between devices  32.6 us (20%)
  blocking collectives  23 us (14%)
  other arithmetic  13.3 us (8%)
  local copies, waits for them, and re-layouts  9.15 us (6%)
    ppermute x6, waiting for transfers between devices, passed_along(): lax.ppermute(value, axis, [(source, source + steps) for source in range(f...  47 us
    ppermute x6, starting transfers between devices, passed_along(): lax.ppermute(value, axis, [(source, source + steps) for source in range(f...  24.8 us
    all_to_all x1, blocking collectives, on_device(): gathered = lax.all_to_all(partial_tiles, 'aux', 0, 0, tiled=True)  23 us
    pallas_call x1, Pallas kernels, on_device(): pl.pallas_call(_right_kernel, grid_spec=pltpu.PrefetchScalarGridSpec(num_...  13.7 us
    convert_element_type x2, other arithmetic, owner_sum(): return (total + third.astype(jnp.float32)).astype(jnp.bfloat16)  11.6 us
    pallas_call x1, Pallas kernels, on_device(): pl.pallas_call(_left_kernel, grid_spec=pltpu.PrefetchScalarGridSpec(num_s...  10.5 us
    pallas_call x1, Pallas kernels, on_device(): pl.pallas_call(_contract_kernel, grid_spec=pltpu.PrefetchScalarGridSpec(n...  10.3 us
    another operation x2, local copies, waits for them, and re-layouts  6.21 us
  transfers between devices with their start and end apart: 10, of which 4 were waited for; matrix products, arithmetic and copies ran while one was open for 1% of the time, Pallas kernels for 15%

profile of v16, /device:TPU:2, one launch (start us, length us, event | category | flops | bytes accessed | tf_op | source)
XLA Modules:
  0.0 165.6 jit_solution(18179463704409734106)
XLA Ops:
  0.0 10.9 %collective-permute-start.1 = (bf16[4,128,512]{2,1,0:T(8,128)(2,1)}, bf16[4,128,512]{2,1,0:T(8,128)(2,1)S(1)}, u32[]{:S(2)}, u32[]{:S(2)}) collective-permute-start(bf16[4,128,512]{2,1,0:T(8,128)(2,1)} %bitcast.7), channel_id=1, source_target_pairs={{2,0},{3,1},{4,2},{5,3},{6,4},{7,5},{8,6},{9,7},{10,8},{11,9},{12,... | collective-permute-start | bytes 1572872 | tf_op jit(solution)/shard_map/ppermute | solution.py:14
  10.9 1.9 %collective-permute-start = (bf16[4,128,512]{2,1,0:T(8,128)(2,1)}, bf16[4,128,512]{2,1,0:T(8,128)(2,1)S(1)}, u32[]{:S(2)}, u32[]{:S(2)}) collective-permute-start(bf16[4,128,512]{2,1,0:T(8,128)(2,1)} %bitcast.8), channel_id=1, source_target_pairs={{1,0},{2,1},{3,2},{4,3},{5,4},{6,5},{7,6},{8,7},{9,8},{10,9},{11,1... | collective-permute-start | bytes 1572872 | tf_op jit(solution)/shard_map/ppermute | solution.py:14
  13.5 0.8 subtract_bitcast_fusion
  14.3 1.9 %copy-done = bf16[24,4,128,128]{3,2,1,0:T(8,128)(2,1)S(1)} copy-done((bf16[24,4,128,128]{3,2,1,0:T(8,128)(2,1)S(1)}, bf16[24,4,128,128]{3,2,1,0:T(8,128)(2,1)}, u32[]{:S(2)}) %copy-start) | copy-done | bytes 3145752
  16.2 1.0 copy-done.1
  17.2 13.7 %shard_map.46 = (bf16[4,4,128,512]{3,2,1,0:T(8,128)(2,1)}, bf16[4,4,128,512]{3,2,1,0:T(8,128)(2,1)}, f32[4,4,128,512]{3,2,1,0:T(8,128)}) custom-call(s32[24]{0:T(128)S(1)} %get-tuple-element.144.left_ref, s32[24]{0:T(128)S(1)} %get-tuple-element.143.right_ref, s32[1]{0:T(128)S(6)} %copy.9.count_ref, bf16[24,4,128,128]{3,2,1,0:T(8,128)(2,1)S(1)} %copy-done, ...), custom_call_target="tpu_custom_call" | custom-call | tf_op jit(solution)/shard_map/pallas_call | solution.py:139
  30.9 1.9 %collective-permute-start.4 = (bf16[4,4,128,512]{3,2,1,0:T(8,128)(2,1)}, bf16[4,4,128,512]{3,2,1,0:T(8,128)(2,1)}, u32[]{:S(2)}, u32[]{:S(2)}) collective-permute-start(bf16[4,4,128,512]{3,2,1,0:T(8,128)(2,1)} %get-tuple-element.69), channel_id=1, source_target_pairs={{0,1},{1,2},{2,3},{3,4},{4,5},{5,6},{6,7},{7,8},{8,9},{9,10},{10,1... | collective-permute-start | bytes 6291464 | tf_op jit(solution)/shard_map/ppermute | solution.py:14
  32.8 5.8 %collective-permute-start.7 = (bf16[4,4,128,512]{3,2,1,0:T(8,128)(2,1)}, bf16[4,4,128,512]{3,2,1,0:T(8,128)(2,1)S(1)}, u32[]{:S(2)}, u32[]{:S(2)}) collective-permute-start(bf16[4,4,128,512]{3,2,1,0:T(8,128)(2,1)} %get-tuple-element.70), channel_id=1, source_target_pairs={{1,0},{2,1},{3,2},{4,3},{5,4},{6,5},{7,6},{8,7},{9,8},{10,9},{11,1... | collective-permute-start | bytes 6291464 | tf_op jit(solution)/shard_map/ppermute | solution.py:14
  38.6 0.0 collective-permute-done.1
  38.6 0.0 collective-permute-done
  38.6 0.2 pad_maximum_fusion.coeff_ref
  38.8 10.5 %shard_map.47 = bf16[4,4,128,512]{3,2,1,0:T(8,128)(2,1)S(1)} custom-call(s32[24]{0:T(128)S(1)} %get-tuple-element.144.left_ref, s32[24]{0:T(128)S(1)} %get-tuple-element.143.right_ref, s32[1]{0:T(128)S(6)} %copy.9.count_ref, bf16[24,4,128,128]{3,2,1,0:T(8,128)(2,1)S(1)} %copy-done, bf16[12,128,512]{2,1,0:T(8,128)(2,1)S(1)} %pad_maximum_fusion.coeff_ref, ...), custom_call_target="tpu_custom_call" | custom-call | tf_op jit(solution)/shard_map/pallas_call | solution.py:156
  49.3 1.9 %collective-permute-start.2 = (bf16[4,4,128,512]{3,2,1,0:T(8,128)(2,1)S(1)}, bf16[4,4,128,512]{3,2,1,0:T(8,128)(2,1)}, u32[]{:S(2)}, u32[]{:S(2)}) collective-permute-start(bf16[4,4,128,512]{3,2,1,0:T(8,128)(2,1)S(1)} %shard_map.47), channel_id=1, source_target_pairs={{1,0},{2,1},{3,2},{4,3},{5,4},{6,5},{7,6},{8,7},{9,8},{10,9},{11,1... | collective-permute-start | bytes 6291464 | tf_op jit(solution)/shard_map/ppermute | solution.py:14
  51.3 2.4 %collective-permute-start.6 = (bf16[4,4,128,512]{3,2,1,0:T(8,128)(2,1)}, bf16[4,4,128,512]{3,2,1,0:T(8,128)(2,1)}, u32[]{:S(2)}, u32[]{:S(2)}) collective-permute-start(bf16[4,4,128,512]{3,2,1,0:T(8,128)(2,1)} %get-tuple-element.70), channel_id=1, source_target_pairs={{0,1},{1,2},{2,3},{3,4},{4,5},{5,6},{6,7},{7,8},{8,9},{9,10},{10,1... | collective-permute-start | bytes 6291464 | tf_op jit(solution)/shard_map/ppermute | solution.py:14
  53.7 2.0 %collective-permute-start.3 = (bf16[4,4,128,512]{3,2,1,0:T(8,128)(2,1)S(1)}, bf16[4,4,128,512]{3,2,1,0:T(8,128)(2,1)}, u32[]{:S(2)}, u32[]{:S(2)}) collective-permute-start(bf16[4,4,128,512]{3,2,1,0:T(8,128)(2,1)S(1)} %shard_map.47), channel_id=1, source_target_pairs={{3,1},{5,3},{7,5},{9,7},{11,9},{13,11},{15,13},{17,15},{19,17},{21... | collective-permute-start | bytes 6291464 | tf_op jit(solution)/shard_map/ppermute | solution.py:186
  55.7 5.0 %collective-permute-done.4 = bf16[4,4,128,512]{3,2,1,0:T(8,128)(2,1)} collective-permute-done((bf16[4,4,128,512]{3,2,1,0:T(8,128)(2,1)}, bf16[4,4,128,512]{3,2,1,0:T(8,128)(2,1)}, u32[]{:S(2)}, u32[]{:S(2)}) %collective-permute-start.4) | collective-permute-done | bytes 2097184 | tf_op jit(solution)/shard_map/ppermute | solution.py:14
  60.7 2.6 %collective-permute-start.5 = (bf16[4,4,128,512]{3,2,1,0:T(8,128)(2,1)}, bf16[4,4,128,512]{3,2,1,0:T(8,128)(2,1)}, u32[]{:S(2)}, u32[]{:S(2)}) collective-permute-start(bf16[4,4,128,512]{3,2,1,0:T(8,128)(2,1)} %collective-permute-done.4), channel_id=1, source_target_pairs={{0,1},{2,3},{4,5},{6,7},{8,9},{10,11},{12,13},{14,15},{16,17},{18,... | collective-permute-start | bytes 6291464 | tf_op jit(solution)/shard_map/ppermute | solution.py:187
  63.3 2.0 %collective-permute-done.7 = bf16[4,4,128,512]{3,2,1,0:T(8,128)(2,1)S(1)} collective-permute-done((bf16[4,4,128,512]{3,2,1,0:T(8,128)(2,1)}, bf16[4,4,128,512]{3,2,1,0:T(8,128)(2,1)S(1)}, u32[]{:S(2)}, u32[]{:S(2)}) %collective-permute-start.7) | collective-permute-done | bytes 2097184 | tf_op jit(solution)/shard_map/ppermute | solution.py:14
  65.3 1.9 %collective-permute-start.9 = (bf16[4,4,128,512]{3,2,1,0:T(8,128)(2,1)}, bf16[4,4,128,512]{3,2,1,0:T(8,128)(2,1)}, u32[]{:S(2)}, u32[]{:S(2)}) collective-permute-start(bf16[4,4,128,512]{3,2,1,0:T(8,128)(2,1)} %get-tuple-element.69), channel_id=1, source_target_pairs={{0,2},{2,4},{4,6},{6,8},{8,10},{10,12},{12,14},{14,16},{16,18},{18... | collective-permute-start | bytes 6291464 | tf_op jit(solution)/shard_map/ppermute | solution.py:183
  67.2 40.1 %collective-permute-done.2 = bf16[4,4,128,512]{3,2,1,0:T(8,128)(2,1)} collective-permute-done((bf16[4,4,128,512]{3,2,1,0:T(8,128)(2,1)S(1)}, bf16[4,4,128,512]{3,2,1,0:T(8,128)(2,1)}, u32[]{:S(2)}, u32[]{:S(2)}) %collective-permute-start.2) | collective-permute-done | bytes 2097184 | tf_op jit(solution)/shard_map/ppermute | solution.py:14
  107.3 1.3 collective-permute-start.8
  108.6 0.0 collective-permute-done.6
  108.6 0.0 collective-permute-done.5
  108.6 5.0 %collective-permute-done.8 = bf16[4,4,128,512]{3,2,1,0:T(8,128)(2,1)} collective-permute-done((bf16[4,4,128,512]{3,2,1,0:T(8,128)(2,1)}, bf16[4,4,128,512]{3,2,1,0:T(8,128)(2,1)}, u32[]{:S(2)}, u32[]{:S(2)}) %collective-permute-start.8) | collective-permute-done | bytes 2097184 | tf_op jit(solution)/shard_map/ppermute | solution.py:188
  113.6 6.2 %conditional.2 = ((bf16[4,4,128,512]{3,2,1,0:T(8,128)(2,1)S(1)}, bf16[4,4,128,512]{3,2,1,0:T(8,128)(2,1)}, bf16[4,4,128,512]{3,2,1,0:T(8,128)(2,1)}, bf16[4,4,12...) conditional(s32[]{:T(128)} %convert_element_type.106, ...), branch_computations={%region_0.1_spmd.clone, %region_1.2_spmd.clone} | conditional | bytes 8388688
  113.6 3.1 %copy.7 = bf16[4,4,128,512]{3,2,1,0:T(8,128)(2,1)} copy(bf16[4,4,128,512]{3,2,1,0:T(8,128)(2,1)} %get-tuple-element.158) | data formatting | bytes 4194304 | tf_op jit(solution)/shard_map/conditional
  116.7 3.1 %copy.8 = bf16[4,4,128,512]{3,2,1,0:T(8,128)(2,1)} copy(bf16[4,4,128,512]{3,2,1,0:T(8,128)(2,1)} %get-tuple-element.159) | data formatting | bytes 4194304 | tf_op jit(solution)/shard_map/conditional
  119.9 5.2 %fusion.2.refs_2_ = bf16[4,4,128,512]{3,2,1,0:T(8,128)(2,1)} fusion(bf16[4,4,128,512]{3,2,1,0:T(8,128)(2,1)} %get-tuple-element.141, bf16[4,4,128,512]{3,2,1,0:T(8,128)(2,1)} %get-tuple-element.142, bf16[4,4,128,512]{3,2,1,0:T(8,128)(2,1)} %get-tuple-element.136), kind=kLoop, calls=%fused_computation.5 | loop fusion | flops 6291456 | bytes 8388608 | tf_op jit(solution)/shard_map/cond/branch_0_fun/convert_element_type | solution.py:192
  125.1 6.4 %fusion = (bf16[4,4,128,512]{3,2,1,0:T(8,128)(2,1)S(1)}, bf16[4,4,128,512]{3,2,1,0:T(8,128)(2,1)S(1)}) fusion(bf16[4,4,128,512]{3,2,1,0:T(8,128)(2,1)} %get-tuple-element.137, bf16[4,4,128,512]{3,2,1,0:T(8,128)(2,1)} %get-tuple-element.138, bf16[4,4,128,512]{3,2,1,0:T(8,128)(2,1)S(1)} %get-tuple-element.134, bf16[4,4,128,512]{3,2,1,0:T(8,128)(2,1)} %get-tuple-element.135, ...), kind=kLoop, calls=%fused_computation.1 | loop fusion | flops 12582912 | bytes 16777216 | tf_op jit(solution)/shard_map/cond/branch_0_fun/convert_element_type | solution.py:192
  131.5 10.3 %shard_map.48 = bf16[8,24,16,128]{3,2,1,0:T(8,128)(2,1)S(1)} custom-call(s32[24]{0:T(128)S(1)} %get-tuple-element.144.left_ref, s32[24]{0:T(128)S(1)} %get-tuple-element.143.right_ref, s32[1]{0:T(128)S(6)} %copy.9.count_ref, bf16[4,4,128,512]{3,2,1,0:T(8,128)(2,1)S(1)} %get-tuple-element.145.refs_0_, ...), custom_call_target="tpu_custom_call" | custom-call | tf_op jit(solution)/shard_map/pallas_call | solution.py:212
  141.8 23.0 %all_to_all.5 = bf16[8,24,16,128]{3,2,1,0:T(8,128)(2,1)S(1)} all-to-all(bf16[8,24,16,128]{3,2,1,0:T(8,128)(2,1)S(1)} %shard_map.48), channel_id=1, replica_groups=mesh['aux'=8,'ao'=64] {'aux'}, dimensions={0} | all-to-all | bytes 1572864 | tf_op jit(solution)/shard_map/all_to_all | solution.py:230
  164.8 0.8 fusion.3
  (8 shorter events, 0.0 us)
Async XLA Ops:
  0.0 38.6 %collective-permute-start.1 = (bf16[4,128,512]{2,1,0:T(8,128)(2,1)}, bf16[4,128,512]{2,1,0:T(8,128)(2,1)S(1)}, u32[]{:S(2)}, u32[]{:S(2)}) collective-permute-start(bf16[4,128,512]{2,1,0:T(8,128)(2,1)} %bitcast.7), channel_id=1, source_target_pairs={{2,0},{3,1},{4,2},{5,3},{6,4},{7,5},{8,6},{9,7},{10,8},{11,9},{12,... | collective-permute-start | bytes 1572872 | tf_op jit(solution)/shard_map/ppermute | solution.py:14
  10.9 27.7 %collective-permute-start = (bf16[4,128,512]{2,1,0:T(8,128)(2,1)}, bf16[4,128,512]{2,1,0:T(8,128)(2,1)S(1)}, u32[]{:S(2)}, u32[]{:S(2)}) collective-permute-start(bf16[4,128,512]{2,1,0:T(8,128)(2,1)} %bitcast.8), channel_id=1, source_target_pairs={{1,0},{2,1},{3,2},{4,3},{5,4},{6,5},{7,6},{8,7},{9,8},{10,9},{11,1... | collective-permute-start | bytes 1572872 | tf_op jit(solution)/shard_map/ppermute | solution.py:14
  14.3 1.9 %copy-start = (bf16[24,4,128,128]{3,2,1,0:T(8,128)(2,1)S(1)}, bf16[24,4,128,128]{3,2,1,0:T(8,128)(2,1)}, u32[]{:S(2)}) copy-start(bf16[24,4,128,128]{3,2,1,0:T(8,128)(2,1)} %tile_ref.3) | copy-start | bytes 9437188
  16.1 1.0 copy-start.1
  17.2 21.4 %copy-start.2 = (bf16[512,512]{1,0:T(8,128)(2,1)S(1)}, bf16[512,512]{1,0:T(8,128)(2,1)}, u32[]{:S(2)}) copy-start(bf16[512,512]{1,0:T(8,128)(2,1)} %param.9) | copy-start | bytes 1572868
  30.9 29.8 %collective-permute-start.4 = (bf16[4,4,128,512]{3,2,1,0:T(8,128)(2,1)}, bf16[4,4,128,512]{3,2,1,0:T(8,128)(2,1)}, u32[]{:S(2)}, u32[]{:S(2)}) collective-permute-start(bf16[4,4,128,512]{3,2,1,0:T(8,128)(2,1)} %get-tuple-element.69), channel_id=1, source_target_pairs={{0,1},{1,2},{2,3},{3,4},{4,5},{5,6},{6,7},{7,8},{8,9},{9,10},{10,1... | collective-permute-start | bytes 6291464 | tf_op jit(solution)/shard_map/ppermute | solution.py:14
  32.8 32.5 %collective-permute-start.7 = (bf16[4,4,128,512]{3,2,1,0:T(8,128)(2,1)}, bf16[4,4,128,512]{3,2,1,0:T(8,128)(2,1)S(1)}, u32[]{:S(2)}, u32[]{:S(2)}) collective-permute-start(bf16[4,4,128,512]{3,2,1,0:T(8,128)(2,1)} %get-tuple-element.70), channel_id=1, source_target_pairs={{1,0},{2,1},{3,2},{4,3},{5,4},{6,5},{7,6},{8,7},{9,8},{10,9},{11,1... | collective-permute-start | bytes 6291464 | tf_op jit(solution)/shard_map/ppermute | solution.py:14
  49.3 57.9 %collective-permute-start.2 = (bf16[4,4,128,512]{3,2,1,0:T(8,128)(2,1)S(1)}, bf16[4,4,128,512]{3,2,1,0:T(8,128)(2,1)}, u32[]{:S(2)}, u32[]{:S(2)}) collective-permute-start(bf16[4,4,128,512]{3,2,1,0:T(8,128)(2,1)S(1)} %shard_map.47), channel_id=1, source_target_pairs={{1,0},{2,1},{3,2},{4,3},{5,4},{6,5},{7,6},{8,7},{9,8},{10,9},{11,1... | collective-permute-start | bytes 6291464 | tf_op jit(solution)/shard_map/ppermute | solution.py:14
  51.3 57.3 %collective-permute-start.6 = (bf16[4,4,128,512]{3,2,1,0:T(8,128)(2,1)}, bf16[4,4,128,512]{3,2,1,0:T(8,128)(2,1)}, u32[]{:S(2)}, u32[]{:S(2)}) collective-permute-start(bf16[4,4,128,512]{3,2,1,0:T(8,128)(2,1)} %get-tuple-element.70), channel_id=1, source_target_pairs={{0,1},{1,2},{2,3},{3,4},{4,5},{5,6},{6,7},{7,8},{8,9},{9,10},{10,1... | collective-permute-start | bytes 6291464 | tf_op jit(solution)/shard_map/ppermute | solution.py:14
  53.7 54.9 %collective-permute-start.3 = (bf16[4,4,128,512]{3,2,1,0:T(8,128)(2,1)S(1)}, bf16[4,4,128,512]{3,2,1,0:T(8,128)(2,1)}, u32[]{:S(2)}, u32[]{:S(2)}) collective-permute-start(bf16[4,4,128,512]{3,2,1,0:T(8,128)(2,1)S(1)} %shard_map.47), channel_id=1, source_target_pairs={{3,1},{5,3},{7,5},{9,7},{11,9},{13,11},{15,13},{17,15},{19,17},{21... | collective-permute-start | bytes 6291464 | tf_op jit(solution)/shard_map/ppermute | solution.py:186
  60.7 47.9 %collective-permute-start.5 = (bf16[4,4,128,512]{3,2,1,0:T(8,128)(2,1)}, bf16[4,4,128,512]{3,2,1,0:T(8,128)(2,1)}, u32[]{:S(2)}, u32[]{:S(2)}) collective-permute-start(bf16[4,4,128,512]{3,2,1,0:T(8,128)(2,1)} %collective-permute-done.4), channel_id=1, source_target_pairs={{0,1},{2,3},{4,5},{6,7},{8,9},{10,11},{12,13},{14,15},{16,17},{18,... | collective-permute-start | bytes 6291464 | tf_op jit(solution)/shard_map/ppermute | solution.py:187
  65.3 42.0 %copy-start.3 = (bf16[4,4,128,512]{3,2,1,0:T(8,128)(2,1)}, bf16[4,4,128,512]{3,2,1,0:T(8,128)(2,1)S(1)}, u32[]{:S(2)}) copy-start(bf16[4,4,128,512]{3,2,1,0:T(8,128)(2,1)S(1)} %collective-permute-done.7) | copy-start | bytes 6291460
  65.3 43.3 %collective-permute-start.9 = (bf16[4,4,128,512]{3,2,1,0:T(8,128)(2,1)}, bf16[4,4,128,512]{3,2,1,0:T(8,128)(2,1)}, u32[]{:S(2)}, u32[]{:S(2)}) collective-permute-start(bf16[4,4,128,512]{3,2,1,0:T(8,128)(2,1)} %get-tuple-element.69), channel_id=1, source_target_pairs={{0,2},{2,4},{4,6},{6,8},{8,10},{10,12},{12,14},{14,16},{16,18},{18... | collective-permute-start | bytes 6291464 | tf_op jit(solution)/shard_map/ppermute | solution.py:183
  107.3 6.4 %collective-permute-start.8 = (bf16[4,4,128,512]{3,2,1,0:T(8,128)(2,1)}, bf16[4,4,128,512]{3,2,1,0:T(8,128)(2,1)}, u32[]{:S(2)}, u32[]{:S(2)}) collective-permute-start(bf16[4,4,128,512]{3,2,1,0:T(8,128)(2,1)} %collective-permute-done.2), channel_id=1, source_target_pairs={{1,0},{3,2},{5,4},{7,6},{9,8},{11,10},{13,12},{15,14},{17,16},{19,... | collective-permute-start | bytes 6291464 | tf_op jit(solution)/shard_map/ppermute | solution.py:188

commit v17 on v16

--- a/solution.py
+++ b/solution.py
@@ -43,7 +43,7 @@
         far_ref[...] = acc_ref[2 * own_blocks :].astype(far_ref.dtype)
 
 
-def _left_kernel(left_ref, right_ref, count_ref, tile_ref, coeff_ref, part_ref, lo_ref, acc_ref):
+def _left_kernel(left_ref, right_ref, count_ref, tile_ref, own_ref, near_ref, far_ref, part_ref, lo_ref, acc_ref):
     slot = pl.program_id(0)
     own_blocks = part_ref.shape[0]
 
@@ -55,9 +55,15 @@
     def _():
         tile = tile_ref[0]
         aux_local, block_size, _ = tile.shape
+        right = right_ref[slot]
+        group = right // own_ref.shape[0]
+        index = right % own_ref.shape[0]
+        right_coeff = jnp.where(
+            group == 0, own_ref[index], jnp.where(group == 1, near_ref[index], far_ref[index])
+        )
         to_left = jnp.dot(
             tile.reshape(aux_local * block_size, block_size),
-            coeff_ref[right_ref[slot]],
+            right_coeff,
             preferred_element_type=jnp.float32,
         ).reshape(aux_local, block_size, -1)
         left = left_ref[slot]
@@ -152,7 +158,6 @@
         ],
         compiler_params=params,
     )(left_rel, right_rel, count, tiles, own_coeff)
-    window_coeff = jnp.concatenate([own_coeff] + ahead_coeff, 0)
     lo = pl.pallas_call(
         _left_kernel,
         grid_spec=pltpu.PrefetchScalarGridSpec(
@@ -160,7 +165,9 @@
             grid=(pair_slots,),
             in_specs=[
                 tile_spec,
-                fixed((window_blocks, block_size, orbitals)),
+                fixed((own_blocks, block_size, orbitals)),
+                fixed((own_blocks, block_size, orbitals)),
+                fixed((own_blocks, block_size, orbitals)),
                 fixed(own_shape),
             ],
             out_specs=fixed(own_shape),
@@ -168,7 +175,7 @@
         ),
         out_shape=jax.ShapeDtypeStruct(own_shape, jnp.bfloat16),
         compiler_params=params,
-    )(left_rel, right_rel, count, tiles, window_coeff, part)
+    )(left_rel, right_rel, count, tiles, own_coeff, *ahead_coeff, part)
 
     block_shape = own_shape
     is_even = (owner_index % 2) == 0

time: 166 us -> 166 us (level)
  the two profiles are of different devices: /device:TPU:2 before, /device:TPU:6 now
where the time goes in v17:
time: 166 us
  waiting for transfers between devices  51.9 us (31%)
  Pallas kernels  34.9 us (21%)
  starting transfers between devices  32.9 us (20%)
  blocking collectives  23 us (14%)
  other arithmetic  13.1 us (8%)
  local copies, waits for them, and re-layouts  9.14 us (6%)
    ppermute x6, waiting for transfers between devices, passed_along(): lax.ppermute(value, axis, [(source, source + steps) for source in range(f...  46.9 us
    ppermute x6, starting transfers between devices, passed_along(): lax.ppermute(value, axis, [(source, source + steps) for source in range(f...  25.1 us
    all_to_all x1, blocking collectives, on_device(): gathered = lax.all_to_all(partial_tiles, 'aux', 0, 0, tiled=True)  23 us
    pallas_call x1, Pallas kernels, on_device(): pl.pallas_call(_right_kernel, grid_spec=pltpu.PrefetchScalarGridSpec(num_...  13.7 us
    convert_element_type x2, other arithmetic, owner_sum(): return (total + third.astype(jnp.float32)).astype(jnp.bfloat16)  11.6 us
    pallas_call x1, Pallas kernels, on_device(): pl.pallas_call(_left_kernel, grid_spec=pltpu.PrefetchScalarGridSpec(num_s...  10.9 us
    pallas_call x1, Pallas kernels, on_device(): pl.pallas_call(_contract_kernel, grid_spec=pltpu.PrefetchScalarGridSpec(n...  10.3 us
    another operation x2, local copies, waits for them, and re-layouts  6.21 us
  transfers between devices with their start and end apart: 10, of which 4 were waited for; matrix products, arithmetic and copies ran while one was open for 0% of the time, Pallas kernels for 15%

profile of v17, /device:TPU:6, one launch (start us, length us, event | category | flops | bytes accessed | tf_op | source)
XLA Modules:
  0.0 165.8 jit_solution(3074308695725877553)
XLA Ops:
  0.0 11.2 %collective-permute-start.1 = (bf16[4,128,512]{2,1,0:T(8,128)(2,1)}, bf16[4,128,512]{2,1,0:T(8,128)(2,1)S(1)}, u32[]{:S(2)}, u32[]{:S(2)}) collective-permute-start(bf16[4,128,512]{2,1,0:T(8,128)(2,1)} %bitcast.7), channel_id=1, source_target_pairs={{2,0},{3,1},{4,2},{5,3},{6,4},{7,5},{8,6},{9,7},{10,8},{11,9},{12,... | collective-permute-start | bytes 1572872 | tf_op jit(solution)/shard_map/ppermute | solution.py:14
  11.2 1.9 %collective-permute-start = (bf16[4,128,512]{2,1,0:T(8,128)(2,1)}, bf16[4,128,512]{2,1,0:T(8,128)(2,1)S(1)}, u32[]{:S(2)}, u32[]{:S(2)}) collective-permute-start(bf16[4,128,512]{2,1,0:T(8,128)(2,1)} %bitcast.8), channel_id=1, source_target_pairs={{1,0},{2,1},{3,2},{4,3},{5,4},{6,5},{7,6},{8,7},{9,8},{10,9},{11,1... | collective-permute-start | bytes 1572872 | tf_op jit(solution)/shard_map/ppermute | solution.py:14
  13.8 0.8 subtract_bitcast_fusion
  14.6 1.9 %copy-done = bf16[24,4,128,128]{3,2,1,0:T(8,128)(2,1)S(1)} copy-done((bf16[24,4,128,128]{3,2,1,0:T(8,128)(2,1)S(1)}, bf16[24,4,128,128]{3,2,1,0:T(8,128)(2,1)}, u32[]{:S(2)}) %copy-start) | copy-done | bytes 3145752
  16.4 1.0 copy-done.1
  17.5 13.7 %shard_map.46 = (bf16[4,4,128,512]{3,2,1,0:T(8,128)(2,1)}, bf16[4,4,128,512]{3,2,1,0:T(8,128)(2,1)}, f32[4,4,128,512]{3,2,1,0:T(8,128)}) custom-call(s32[24]{0:T(128)S(1)} %get-tuple-element.144.left_ref, s32[24]{0:T(128)S(1)} %get-tuple-element.143.right_ref, s32[1]{0:T(128)S(6)} %copy.9.count_ref, bf16[24,4,128,128]{3,2,1,0:T(8,128)(2,1)S(1)} %copy-done, ...), custom_call_target="tpu_custom_call" | custom-call | tf_op jit(solution)/shard_map/pallas_call | solution.py:145
  31.2 1.9 %collective-permute-start.4 = (bf16[4,4,128,512]{3,2,1,0:T(8,128)(2,1)}, bf16[4,4,128,512]{3,2,1,0:T(8,128)(2,1)}, u32[]{:S(2)}, u32[]{:S(2)}) collective-permute-start(bf16[4,4,128,512]{3,2,1,0:T(8,128)(2,1)} %get-tuple-element.69), channel_id=1, source_target_pairs={{0,1},{1,2},{2,3},{3,4},{4,5},{5,6},{6,7},{7,8},{8,9},{9,10},{10,1... | collective-permute-start | bytes 6291464 | tf_op jit(solution)/shard_map/ppermute | solution.py:14
  33.1 5.8 %collective-permute-start.7 = (bf16[4,4,128,512]{3,2,1,0:T(8,128)(2,1)}, bf16[4,4,128,512]{3,2,1,0:T(8,128)(2,1)S(1)}, u32[]{:S(2)}, u32[]{:S(2)}) collective-permute-start(bf16[4,4,128,512]{3,2,1,0:T(8,128)(2,1)} %get-tuple-element.70), channel_id=1, source_target_pairs={{1,0},{2,1},{3,2},{4,3},{5,4},{6,5},{7,6},{8,7},{9,8},{10,9},{11,1... | collective-permute-start | bytes 6291464 | tf_op jit(solution)/shard_map/ppermute | solution.py:14
  38.9 0.0 collective-permute-done.1.far_ref
  38.9 0.0 collective-permute-done.near_ref
  38.9 10.9 %shard_map.47 = bf16[4,4,128,512]{3,2,1,0:T(8,128)(2,1)S(1)} custom-call(s32[24]{0:T(128)S(1)} %get-tuple-element.144.left_ref, s32[24]{0:T(128)S(1)} %get-tuple-element.143.right_ref, s32[1]{0:T(128)S(6)} %copy.9.count_ref, bf16[24,4,128,128]{3,2,1,0:T(8,128)(2,1)S(1)} %copy-done, bf16[4,128,512]{2,1,0:T(8,128)(2,1)S(1)} %bitcast.10, ...), custom_call_target="tpu_custom_call" | custom-call | tf_op jit(solution)/shard_map/pallas_call | solution.py:161
  49.8 1.9 %collective-permute-start.2 = (bf16[4,4,128,512]{3,2,1,0:T(8,128)(2,1)S(1)}, bf16[4,4,128,512]{3,2,1,0:T(8,128)(2,1)}, u32[]{:S(2)}, u32[]{:S(2)}) collective-permute-start(bf16[4,4,128,512]{3,2,1,0:T(8,128)(2,1)S(1)} %shard_map.47), channel_id=1, source_target_pairs={{1,0},{2,1},{3,2},{4,3},{5,4},{6,5},{7,6},{8,7},{9,8},{10,9},{11,1... | collective-permute-start | bytes 6291464 | tf_op jit(solution)/shard_map/ppermute | solution.py:14
  51.7 2.4 %collective-permute-start.6 = (bf16[4,4,128,512]{3,2,1,0:T(8,128)(2,1)}, bf16[4,4,128,512]{3,2,1,0:T(8,128)(2,1)}, u32[]{:S(2)}, u32[]{:S(2)}) collective-permute-start(bf16[4,4,128,512]{3,2,1,0:T(8,128)(2,1)} %get-tuple-element.70), channel_id=1, source_target_pairs={{0,1},{1,2},{2,3},{3,4},{4,5},{5,6},{6,7},{7,8},{8,9},{9,10},{10,1... | collective-permute-start | bytes 6291464 | tf_op jit(solution)/shard_map/ppermute | solution.py:14
  54.1 2.0 %collective-permute-start.3 = (bf16[4,4,128,512]{3,2,1,0:T(8,128)(2,1)S(1)}, bf16[4,4,128,512]{3,2,1,0:T(8,128)(2,1)}, u32[]{:S(2)}, u32[]{:S(2)}) collective-permute-start(bf16[4,4,128,512]{3,2,1,0:T(8,128)(2,1)S(1)} %shard_map.47), channel_id=1, source_target_pairs={{3,1},{5,3},{7,5},{9,7},{11,9},{13,11},{15,13},{17,15},{19,17},{21... | collective-permute-start | bytes 6291464 | tf_op jit(solution)/shard_map/ppermute | solution.py:193
  56.1 4.8 %collective-permute-done.4 = bf16[4,4,128,512]{3,2,1,0:T(8,128)(2,1)} collective-permute-done((bf16[4,4,128,512]{3,2,1,0:T(8,128)(2,1)}, bf16[4,4,128,512]{3,2,1,0:T(8,128)(2,1)}, u32[]{:S(2)}, u32[]{:S(2)}) %collective-permute-start.4) | collective-permute-done | bytes 2097184 | tf_op jit(solution)/shard_map/ppermute | solution.py:14
  61.0 2.6 %collective-permute-start.5 = (bf16[4,4,128,512]{3,2,1,0:T(8,128)(2,1)}, bf16[4,4,128,512]{3,2,1,0:T(8,128)(2,1)}, u32[]{:S(2)}, u32[]{:S(2)}) collective-permute-start(bf16[4,4,128,512]{3,2,1,0:T(8,128)(2,1)} %collective-permute-done.4), channel_id=1, source_target_pairs={{0,1},{2,3},{4,5},{6,7},{8,9},{10,11},{12,13},{14,15},{16,17},{18,... | collective-permute-start | bytes 6291464 | tf_op jit(solution)/shard_map/ppermute | solution.py:194
  63.6 1.8 %collective-permute-done.7 = bf16[4,4,128,512]{3,2,1,0:T(8,128)(2,1)S(1)} collective-permute-done((bf16[4,4,128,512]{3,2,1,0:T(8,128)(2,1)}, bf16[4,4,128,512]{3,2,1,0:T(8,128)(2,1)S(1)}, u32[]{:S(2)}, u32[]{:S(2)}) %collective-permute-start.7) | collective-permute-done | bytes 2097184 | tf_op jit(solution)/shard_map/ppermute | solution.py:14
  65.4 1.9 %collective-permute-start.9 = (bf16[4,4,128,512]{3,2,1,0:T(8,128)(2,1)}, bf16[4,4,128,512]{3,2,1,0:T(8,128)(2,1)}, u32[]{:S(2)}, u32[]{:S(2)}) collective-permute-start(bf16[4,4,128,512]{3,2,1,0:T(8,128)(2,1)} %get-tuple-element.69), channel_id=1, source_target_pairs={{0,2},{2,4},{4,6},{6,8},{8,10},{10,12},{12,14},{14,16},{16,18},{18... | collective-permute-start | bytes 6291464 | tf_op jit(solution)/shard_map/ppermute | solution.py:190
  67.3 40.2 %collective-permute-done.2 = bf16[4,4,128,512]{3,2,1,0:T(8,128)(2,1)} collective-permute-done((bf16[4,4,128,512]{3,2,1,0:T(8,128)(2,1)S(1)}, bf16[4,4,128,512]{3,2,1,0:T(8,128)(2,1)}, u32[]{:S(2)}, u32[]{:S(2)}) %collective-permute-start.2) | collective-permute-done | bytes 2097184 | tf_op jit(solution)/shard_map/ppermute | solution.py:14
  107.6 1.3 collective-permute-start.8
  108.9 0.0 collective-permute-done.6
  108.9 0.0 collective-permute-done.3
  108.9 0.0 collective-permute-done.5
  108.9 5.0 %collective-permute-done.8 = bf16[4,4,128,512]{3,2,1,0:T(8,128)(2,1)} collective-permute-done((bf16[4,4,128,512]{3,2,1,0:T(8,128)(2,1)}, bf16[4,4,128,512]{3,2,1,0:T(8,128)(2,1)}, u32[]{:S(2)}, u32[]{:S(2)}) %collective-permute-start.8) | collective-permute-done | bytes 2097184 | tf_op jit(solution)/shard_map/ppermute | solution.py:195
  113.9 6.2 %conditional.2 = ((bf16[4,4,128,512]{3,2,1,0:T(8,128)(2,1)S(1)}, bf16[4,4,128,512]{3,2,1,0:T(8,128)(2,1)}, bf16[4,4,128,512]{3,2,1,0:T(8,128)(2,1)}, bf16[4,4,12...) conditional(s32[]{:T(128)} %convert_element_type.106, ...), branch_computations={%region_0.1_spmd.clone, %region_1.2_spmd.clone} | conditional | bytes 8388688
  113.9 3.1 %copy.7 = bf16[4,4,128,512]{3,2,1,0:T(8,128)(2,1)} copy(bf16[4,4,128,512]{3,2,1,0:T(8,128)(2,1)} %get-tuple-element.158) | data formatting | bytes 4194304 | tf_op jit(solution)/shard_map/conditional
  117.0 3.1 %copy.8 = bf16[4,4,128,512]{3,2,1,0:T(8,128)(2,1)} copy(bf16[4,4,128,512]{3,2,1,0:T(8,128)(2,1)} %get-tuple-element.159) | data formatting | bytes 4194304 | tf_op jit(solution)/shard_map/conditional
  120.2 5.2 %fusion.2.refs_2_ = bf16[4,4,128,512]{3,2,1,0:T(8,128)(2,1)} fusion(bf16[4,4,128,512]{3,2,1,0:T(8,128)(2,1)} %get-tuple-element.141, bf16[4,4,128,512]{3,2,1,0:T(8,128)(2,1)} %get-tuple-element.142, bf16[4,4,128,512]{3,2,1,0:T(8,128)(2,1)} %get-tuple-element.136), kind=kLoop, calls=%fused_computation.5 | loop fusion | flops 6291456 | bytes 8388608 | tf_op jit(solution)/shard_map/cond/branch_0_fun/convert_element_type | solution.py:199
  125.4 6.4 %fusion = (bf16[4,4,128,512]{3,2,1,0:T(8,128)(2,1)S(1)}, bf16[4,4,128,512]{3,2,1,0:T(8,128)(2,1)S(1)}) fusion(bf16[4,4,128,512]{3,2,1,0:T(8,128)(2,1)} %get-tuple-element.137, bf16[4,4,128,512]{3,2,1,0:T(8,128)(2,1)} %get-tuple-element.138, bf16[4,4,128,512]{3,2,1,0:T(8,128)(2,1)S(1)} %get-tuple-element.134, bf16[4,4,128,512]{3,2,1,0:T(8,128)(2,1)} %get-tuple-element.135, ...), kind=kLoop, calls=%fused_computation.1 | loop fusion | flops 12582912 | bytes 16777216 | tf_op jit(solution)/shard_map/cond/branch_0_fun/convert_element_type | solution.py:199
  131.8 10.3 %shard_map.48 = bf16[8,24,16,128]{3,2,1,0:T(8,128)(2,1)S(1)} custom-call(s32[24]{0:T(128)S(1)} %get-tuple-element.144.left_ref, s32[24]{0:T(128)S(1)} %get-tuple-element.143.right_ref, s32[1]{0:T(128)S(6)} %copy.9.count_ref, bf16[4,4,128,512]{3,2,1,0:T(8,128)(2,1)S(1)} %get-tuple-element.145.refs_0_, ...), custom_call_target="tpu_custom_call" | custom-call | tf_op jit(solution)/shard_map/pallas_call | solution.py:219
  142.1 23.0 %all_to_all.5 = bf16[8,24,16,128]{3,2,1,0:T(8,128)(2,1)S(1)} all-to-all(bf16[8,24,16,128]{3,2,1,0:T(8,128)(2,1)S(1)} %shard_map.48), channel_id=1, replica_groups=mesh['aux'=8,'ao'=64] {'aux'}, dimensions={0} | all-to-all | bytes 1572864 | tf_op jit(solution)/shard_map/all_to_all | solution.py:237
  165.1 0.8 fusion.3
  (5 shorter events, 0.0 us)
Async XLA Ops:
  0.0 38.9 %collective-permute-start.1 = (bf16[4,128,512]{2,1,0:T(8,128)(2,1)}, bf16[4,128,512]{2,1,0:T(8,128)(2,1)S(1)}, u32[]{:S(2)}, u32[]{:S(2)}) collective-permute-start(bf16[4,128,512]{2,1,0:T(8,128)(2,1)} %bitcast.7), channel_id=1, source_target_pairs={{2,0},{3,1},{4,2},{5,3},{6,4},{7,5},{8,6},{9,7},{10,8},{11,9},{12,... | collective-permute-start | bytes 1572872 | tf_op jit(solution)/shard_map/ppermute | solution.py:14
  11.2 27.7 %collective-permute-start = (bf16[4,128,512]{2,1,0:T(8,128)(2,1)}, bf16[4,128,512]{2,1,0:T(8,128)(2,1)S(1)}, u32[]{:S(2)}, u32[]{:S(2)}) collective-permute-start(bf16[4,128,512]{2,1,0:T(8,128)(2,1)} %bitcast.8), channel_id=1, source_target_pairs={{1,0},{2,1},{3,2},{4,3},{5,4},{6,5},{7,6},{8,7},{9,8},{10,9},{11,1... | collective-permute-start | bytes 1572872 | tf_op jit(solution)/shard_map/ppermute | solution.py:14
  14.6 1.9 %copy-start = (bf16[24,4,128,128]{3,2,1,0:T(8,128)(2,1)S(1)}, bf16[24,4,128,128]{3,2,1,0:T(8,128)(2,1)}, u32[]{:S(2)}) copy-start(bf16[24,4,128,128]{3,2,1,0:T(8,128)(2,1)} %tile_ref.3) | copy-start | bytes 9437188
  16.4 1.0 copy-start.1
  31.2 29.8 %collective-permute-start.4 = (bf16[4,4,128,512]{3,2,1,0:T(8,128)(2,1)}, bf16[4,4,128,512]{3,2,1,0:T(8,128)(2,1)}, u32[]{:S(2)}, u32[]{:S(2)}) collective-permute-start(bf16[4,4,128,512]{3,2,1,0:T(8,128)(2,1)} %get-tuple-element.69), channel_id=1, source_target_pairs={{0,1},{1,2},{2,3},{3,4},{4,5},{5,6},{6,7},{7,8},{8,9},{9,10},{10,1... | collective-permute-start | bytes 6291464 | tf_op jit(solution)/shard_map/ppermute | solution.py:14
  33.1 32.3 %collective-permute-start.7 = (bf16[4,4,128,512]{3,2,1,0:T(8,128)(2,1)}, bf16[4,4,128,512]{3,2,1,0:T(8,128)(2,1)S(1)}, u32[]{:S(2)}, u32[]{:S(2)}) collective-permute-start(bf16[4,4,128,512]{3,2,1,0:T(8,128)(2,1)} %get-tuple-element.70), channel_id=1, source_target_pairs={{1,0},{2,1},{3,2},{4,3},{5,4},{6,5},{7,6},{8,7},{9,8},{10,9},{11,1... | collective-permute-start | bytes 6291464 | tf_op jit(solution)/shard_map/ppermute | solution.py:14
  49.8 57.8 %collective-permute-start.2 = (bf16[4,4,128,512]{3,2,1,0:T(8,128)(2,1)S(1)}, bf16[4,4,128,512]{3,2,1,0:T(8,128)(2,1)}, u32[]{:S(2)}, u32[]{:S(2)}) collective-permute-start(bf16[4,4,128,512]{3,2,1,0:T(8,128)(2,1)S(1)} %shard_map.47), channel_id=1, source_target_pairs={{1,0},{2,1},{3,2},{4,3},{5,4},{6,5},{7,6},{8,7},{9,8},{10,9},{11,1... | collective-permute-start | bytes 6291464 | tf_op jit(solution)/shard_map/ppermute | solution.py:14
  51.7 57.1 %collective-permute-start.6 = (bf16[4,4,128,512]{3,2,1,0:T(8,128)(2,1)}, bf16[4,4,128,512]{3,2,1,0:T(8,128)(2,1)}, u32[]{:S(2)}, u32[]{:S(2)}) collective-permute-start(bf16[4,4,128,512]{3,2,1,0:T(8,128)(2,1)} %get-tuple-element.70), channel_id=1, source_target_pairs={{0,1},{1,2},{2,3},{3,4},{4,5},{5,6},{6,7},{7,8},{8,9},{9,10},{10,1... | collective-permute-start | bytes 6291464 | tf_op jit(solution)/shard_map/ppermute | solution.py:14
  54.1 54.7 %collective-permute-start.3 = (bf16[4,4,128,512]{3,2,1,0:T(8,128)(2,1)S(1)}, bf16[4,4,128,512]{3,2,1,0:T(8,128)(2,1)}, u32[]{:S(2)}, u32[]{:S(2)}) collective-permute-start(bf16[4,4,128,512]{3,2,1,0:T(8,128)(2,1)S(1)} %shard_map.47), channel_id=1, source_target_pairs={{3,1},{5,3},{7,5},{9,7},{11,9},{13,11},{15,13},{17,15},{19,17},{21... | collective-permute-start | bytes 6291464 | tf_op jit(solution)/shard_map/ppermute | solution.py:193
  61.0 47.9 %collective-permute-start.5 = (bf16[4,4,128,512]{3,2,1,0:T(8,128)(2,1)}, bf16[4,4,128,512]{3,2,1,0:T(8,128)(2,1)}, u32[]{:S(2)}, u32[]{:S(2)}) collective-permute-start(bf16[4,4,128,512]{3,2,1,0:T(8,128)(2,1)} %collective-permute-done.4), channel_id=1, source_target_pairs={{0,1},{2,3},{4,5},{6,7},{8,9},{10,11},{12,13},{14,15},{16,17},{18,... | collective-permute-start | bytes 6291464 | tf_op jit(solution)/shard_map/ppermute | solution.py:194
  65.4 42.1 %copy-start.2 = (bf16[4,4,128,512]{3,2,1,0:T(8,128)(2,1)}, bf16[4,4,128,512]{3,2,1,0:T(8,128)(2,1)S(1)}, u32[]{:S(2)}) copy-start(bf16[4,4,128,512]{3,2,1,0:T(8,128)(2,1)S(1)} %collective-permute-done.7) | copy-start | bytes 6291460
  65.4 43.5 %collective-permute-start.9 = (bf16[4,4,128,512]{3,2,1,0:T(8,128)(2,1)}, bf16[4,4,128,512]{3,2,1,0:T(8,128)(2,1)}, u32[]{:S(2)}, u32[]{:S(2)}) collective-permute-start(bf16[4,4,128,512]{3,2,1,0:T(8,128)(2,1)} %get-tuple-element.69), channel_id=1, source_target_pairs={{0,2},{2,4},{4,6},{6,8},{8,10},{10,12},{12,14},{14,16},{16,18},{18... | collective-permute-start | bytes 6291464 | tf_op jit(solution)/shard_map/ppermute | solution.py:190
  107.6 6.4 %collective-permute-start.8 = (bf16[4,4,128,512]{3,2,1,0:T(8,128)(2,1)}, bf16[4,4,128,512]{3,2,1,0:T(8,128)(2,1)}, u32[]{:S(2)}, u32[]{:S(2)}) collective-permute-start(bf16[4,4,128,512]{3,2,1,0:T(8,128)(2,1)} %collective-permute-done.2), channel_id=1, source_target_pairs={{1,0},{3,2},{5,4},{7,6},{9,8},{11,10},{13,12},{15,14},{17,16},{19,... | collective-permute-start | bytes 6291464 | tf_op jit(solution)/shard_map/ppermute | solution.py:195

commit v18 on v17

--- a/solution.py
+++ b/solution.py
@@ -26,15 +26,11 @@
     def _():
         tile = tile_ref[0]
         left_coeff = coeff_ref[left_ref[slot]]
-        parts = [
-            lax.dot_general(
-                tile[p], left_coeff, (((0,), (0,)), ((), ())),
-                preferred_element_type=jnp.float32,
-            )
-            for p in range(tile.shape[0])
-        ]
+        aux_local, block_size, _ = tile.shape
+        turned = jnp.swapaxes(tile, 1, 2).reshape(aux_local * block_size, block_size)
+        to_right = jnp.dot(turned, left_coeff, preferred_element_type=jnp.float32)
         right = right_ref[slot]
-        acc_ref[right] += jnp.stack(parts, 0)
+        acc_ref[right] += to_right.reshape(aux_local, block_size, -1)
 
     @pl.when(slot == pl.num_programs(0) - 1)
     def _():

time: 166 us -> 166 us (level)
  Pallas kernels: 34.9 us -> 24 us
  starting transfers between devices: 32.9 us -> 38.4 us
  blocking collectives: 23 us -> 27.8 us
    all_to_all x1, blocking collectives: 23 us -> 27.8 us  [on_device(): gathered = lax.all_to_all(partial_tiles, 'aux', 0, 0, tiled=True)]
    pallas_call x1, Pallas kernels: 13.7 us -> 9.93 us  [on_device(): pl.pallas_call(_right_kernel, grid_spec=pltpu.PrefetchScalarGridSpec(num_...]
    ppermute x6, starting transfers between devices: 25.1 us -> 28.9 us  [passed_along(): lax.ppermute(value, axis, [(source, source + steps) for source in range(f...]
    pallas_call x1, Pallas kernels: 10.3 us -> 6.59 us  [on_device(): pl.pallas_call(_contract_kernel, grid_spec=pltpu.PrefetchScalarGridSpec(n...]
    pallas_call x1, Pallas kernels: 10.9 us -> 7.47 us  [on_device(): pl.pallas_call(_left_kernel, grid_spec=pltpu.PrefetchScalarGridSpec(num_s...]
    ppermute x6, waiting for transfers between devices: 46.9 us -> 45.2 us  [passed_along(): lax.ppermute(value, axis, [(source, source + steps) for source in range(f...]
  transfers between devices with their start and end apart: 10 -> 10, of which waited for: 4 -> 4; matrix products, arithmetic and copies ran while one was open for 0% -> 0% of each run, Pallas kernels for 15% -> 11%
where the time goes in v18:
time: 166 us; the launch traced here: 164 us
  waiting for transfers between devices  51.1 us (31%)
  starting transfers between devices  38.4 us (23%)
  blocking collectives  27.8 us (17%)
  Pallas kernels  24 us (14%)
  other arithmetic  13.1 us (8%)
  local copies, waits for them, and re-layouts  9.14 us (6%)
    ppermute x6, waiting for transfers between devices, passed_along(): lax.ppermute(value, axis, [(source, source + steps) for source in range(f...  45.2 us
    ppermute x6, starting transfers between devices, passed_along(): lax.ppermute(value, axis, [(source, source + steps) for source in range(f...  28.9 us
    all_to_all x1, blocking collectives, on_device(): gathered = lax.all_to_all(partial_tiles, 'aux', 0, 0, tiled=True)  27.8 us
    convert_element_type x2, other arithmetic, owner_sum(): return (total + third.astype(jnp.float32)).astype(jnp.bfloat16)  11.6 us
    pallas_call x1, Pallas kernels, on_device(): pl.pallas_call(_right_kernel, grid_spec=pltpu.PrefetchScalarGridSpec(num_...  9.93 us
    pallas_call x1, Pallas kernels, on_device(): pl.pallas_call(_left_kernel, grid_spec=pltpu.PrefetchScalarGridSpec(num_s...  7.47 us
    pallas_call x1, Pallas kernels, on_device(): pl.pallas_call(_contract_kernel, grid_spec=pltpu.PrefetchScalarGridSpec(n...  6.59 us
    another operation x2, local copies, waits for them, and re-layouts  6.21 us
  transfers between devices with their start and end apart: 10, of which 4 were waited for; matrix products, arithmetic and copies ran while one was open for 0% of the time, Pallas kernels for 11%

profile of v18, /device:TPU:6, one launch (start us, length us, event | category | flops | bytes accessed | tf_op | source)
XLA Modules:
  0.0 164.4 jit_solution(8010259707540671845)
XLA Ops:
  0.0 11.2 %collective-permute-start.1 = (bf16[4,128,512]{2,1,0:T(8,128)(2,1)}, bf16[4,128,512]{2,1,0:T(8,128)(2,1)S(1)}, u32[]{:S(2)}, u32[]{:S(2)}) collective-permute-start(bf16[4,128,512]{2,1,0:T(8,128)(2,1)} %bitcast.7), channel_id=1, source_target_pairs={{2,0},{3,1},{4,2},{5,3},{6,4},{7,5},{8,6},{9,7},{10,8},{11,9},{12,... | collective-permute-start | bytes 1572872 | tf_op jit(solution)/shard_map/ppermute | solution.py:14
  11.2 1.9 %collective-permute-start = (bf16[4,128,512]{2,1,0:T(8,128)(2,1)}, bf16[4,128,512]{2,1,0:T(8,128)(2,1)S(1)}, u32[]{:S(2)}, u32[]{:S(2)}) collective-permute-start(bf16[4,128,512]{2,1,0:T(8,128)(2,1)} %bitcast.8), channel_id=1, source_target_pairs={{1,0},{2,1},{3,2},{4,3},{5,4},{6,5},{7,6},{8,7},{9,8},{10,9},{11,1... | collective-permute-start | bytes 1572872 | tf_op jit(solution)/shard_map/ppermute | solution.py:14
  13.8 0.8 subtract_bitcast_fusion
  14.6 1.9 %copy-done = bf16[24,4,128,128]{3,2,1,0:T(8,128)(2,1)S(1)} copy-done((bf16[24,4,128,128]{3,2,1,0:T(8,128)(2,1)S(1)}, bf16[24,4,128,128]{3,2,1,0:T(8,128)(2,1)}, u32[]{:S(2)}) %copy-start) | copy-done | bytes 3145752
  16.4 1.0 copy-done.1
  17.5 9.9 %shard_map.46 = (bf16[4,4,128,512]{3,2,1,0:T(8,128)(2,1)}, bf16[4,4,128,512]{3,2,1,0:T(8,128)(2,1)}, f32[4,4,128,512]{3,2,1,0:T(8,128)}) custom-call(s32[24]{0:T(128)S(1)} %get-tuple-element.144.left_ref, s32[24]{0:T(128)S(1)} %get-tuple-element.143.right_ref, s32[1]{0:T(128)S(6)} %copy.9.count_ref, bf16[24,4,128,128]{3,2,1,0:T(8,128)(2,1)S(1)} %copy-done, ...), custom_call_target="tpu_custom_call" | custom-call | tf_op jit(solution)/shard_map/pallas_call | solution.py:141
  27.4 6.1 %collective-permute-start.4 = (bf16[4,4,128,512]{3,2,1,0:T(8,128)(2,1)}, bf16[4,4,128,512]{3,2,1,0:T(8,128)(2,1)}, u32[]{:S(2)}, u32[]{:S(2)}) collective-permute-start(bf16[4,4,128,512]{3,2,1,0:T(8,128)(2,1)} %get-tuple-element.69), channel_id=1, source_target_pairs={{0,1},{1,2},{2,3},{3,4},{4,5},{5,6},{6,7},{7,8},{8,9},{9,10},{10,1... | collective-permute-start | bytes 6291464 | tf_op jit(solution)/shard_map/ppermute | solution.py:14
  33.5 1.9 %collective-permute-start.7 = (bf16[4,4,128,512]{3,2,1,0:T(8,128)(2,1)}, bf16[4,4,128,512]{3,2,1,0:T(8,128)(2,1)S(1)}, u32[]{:S(2)}, u32[]{:S(2)}) collective-permute-start(bf16[4,4,128,512]{3,2,1,0:T(8,128)(2,1)} %get-tuple-element.70), channel_id=1, source_target_pairs={{1,0},{2,1},{3,2},{4,3},{5,4},{6,5},{7,6},{8,7},{9,8},{10,9},{11,1... | collective-permute-start | bytes 6291464 | tf_op jit(solution)/shard_map/ppermute | solution.py:14
  35.4 0.0 collective-permute-done.1.far_ref
  35.4 0.0 collective-permute-done.near_ref
  35.4 7.5 %shard_map.47 = bf16[4,4,128,512]{3,2,1,0:T(8,128)(2,1)S(1)} custom-call(s32[24]{0:T(128)S(1)} %get-tuple-element.144.left_ref, s32[24]{0:T(128)S(1)} %get-tuple-element.143.right_ref, s32[1]{0:T(128)S(6)} %copy.9.count_ref, bf16[24,4,128,128]{3,2,1,0:T(8,128)(2,1)S(1)} %copy-done, bf16[4,128,512]{2,1,0:T(8,128)(2,1)S(1)} %bitcast.10, ...), custom_call_target="tpu_custom_call" | custom-call | tf_op jit(solution)/shard_map/pallas_call | solution.py:157
  42.9 2.1 %collective-permute-start.2 = (bf16[4,4,128,512]{3,2,1,0:T(8,128)(2,1)S(1)}, bf16[4,4,128,512]{3,2,1,0:T(8,128)(2,1)}, u32[]{:S(2)}, u32[]{:S(2)}) collective-permute-start(bf16[4,4,128,512]{3,2,1,0:T(8,128)(2,1)S(1)} %shard_map.47), channel_id=1, source_target_pairs={{1,0},{2,1},{3,2},{4,3},{5,4},{6,5},{7,6},{8,7},{9,8},{10,9},{11,1... | collective-permute-start | bytes 6291464 | tf_op jit(solution)/shard_map/ppermute | solution.py:14
  45.0 5.7 %collective-permute-start.6 = (bf16[4,4,128,512]{3,2,1,0:T(8,128)(2,1)}, bf16[4,4,128,512]{3,2,1,0:T(8,128)(2,1)}, u32[]{:S(2)}, u32[]{:S(2)}) collective-permute-start(bf16[4,4,128,512]{3,2,1,0:T(8,128)(2,1)} %get-tuple-element.70), channel_id=1, source_target_pairs={{0,1},{1,2},{2,3},{3,4},{4,5},{5,6},{6,7},{7,8},{8,9},{9,10},{10,1... | collective-permute-start | bytes 6291464 | tf_op jit(solution)/shard_map/ppermute | solution.py:14
  50.7 2.0 %collective-permute-start.3 = (bf16[4,4,128,512]{3,2,1,0:T(8,128)(2,1)S(1)}, bf16[4,4,128,512]{3,2,1,0:T(8,128)(2,1)}, u32[]{:S(2)}, u32[]{:S(2)}) collective-permute-start(bf16[4,4,128,512]{3,2,1,0:T(8,128)(2,1)S(1)} %shard_map.47), channel_id=1, source_target_pairs={{3,1},{5,3},{7,5},{9,7},{11,9},{13,11},{15,13},{17,15},{19,17},{21... | collective-permute-start | bytes 6291464 | tf_op jit(solution)/shard_map/ppermute | solution.py:189
  52.7 4.5 %collective-permute-done.4 = bf16[4,4,128,512]{3,2,1,0:T(8,128)(2,1)} collective-permute-done((bf16[4,4,128,512]{3,2,1,0:T(8,128)(2,1)}, bf16[4,4,128,512]{3,2,1,0:T(8,128)(2,1)}, u32[]{:S(2)}, u32[]{:S(2)}) %collective-permute-start.4) | collective-permute-done | bytes 2097184 | tf_op jit(solution)/shard_map/ppermute | solution.py:14
  57.2 2.8 %collective-permute-start.5 = (bf16[4,4,128,512]{3,2,1,0:T(8,128)(2,1)}, bf16[4,4,128,512]{3,2,1,0:T(8,128)(2,1)}, u32[]{:S(2)}, u32[]{:S(2)}) collective-permute-start(bf16[4,4,128,512]{3,2,1,0:T(8,128)(2,1)} %collective-permute-done.4), channel_id=1, source_target_pairs={{0,1},{2,3},{4,5},{6,7},{8,9},{10,11},{12,13},{14,15},{16,17},{18,... | collective-permute-start | bytes 6291464 | tf_op jit(solution)/shard_map/ppermute | solution.py:190
  60.0 3.7 %collective-permute-done.7 = bf16[4,4,128,512]{3,2,1,0:T(8,128)(2,1)S(1)} collective-permute-done((bf16[4,4,128,512]{3,2,1,0:T(8,128)(2,1)}, bf16[4,4,128,512]{3,2,1,0:T(8,128)(2,1)S(1)}, u32[]{:S(2)}, u32[]{:S(2)}) %collective-permute-start.7) | collective-permute-done | bytes 2097184 | tf_op jit(solution)/shard_map/ppermute | solution.py:14
  63.7 3.4 %collective-permute-start.9 = (bf16[4,4,128,512]{3,2,1,0:T(8,128)(2,1)}, bf16[4,4,128,512]{3,2,1,0:T(8,128)(2,1)}, u32[]{:S(2)}, u32[]{:S(2)}) collective-permute-start(bf16[4,4,128,512]{3,2,1,0:T(8,128)(2,1)} %get-tuple-element.69), channel_id=1, source_target_pairs={{0,2},{2,4},{4,6},{6,8},{8,10},{10,12},{12,14},{14,16},{16,18},{18... | collective-permute-start | bytes 6291464 | tf_op jit(solution)/shard_map/ppermute | solution.py:186
  67.1 37.0 %collective-permute-done.2 = bf16[4,4,128,512]{3,2,1,0:T(8,128)(2,1)} collective-permute-done((bf16[4,4,128,512]{3,2,1,0:T(8,128)(2,1)S(1)}, bf16[4,4,128,512]{3,2,1,0:T(8,128)(2,1)}, u32[]{:S(2)}, u32[]{:S(2)}) %collective-permute-start.2) | collective-permute-done | bytes 2097184 | tf_op jit(solution)/shard_map/ppermute | solution.py:14
  104.1 1.3 collective-permute-start.8
  105.4 0.0 collective-permute-done.6
  105.4 0.0 collective-permute-done.3
  105.4 0.0 collective-permute-done.9
  105.5 5.9 %collective-permute-done.8 = bf16[4,4,128,512]{3,2,1,0:T(8,128)(2,1)} collective-permute-done((bf16[4,4,128,512]{3,2,1,0:T(8,128)(2,1)}, bf16[4,4,128,512]{3,2,1,0:T(8,128)(2,1)}, u32[]{:S(2)}, u32[]{:S(2)}) %collective-permute-start.8) | collective-permute-done | bytes 2097184 | tf_op jit(solution)/shard_map/ppermute | solution.py:191
  111.4 6.2 %conditional.2 = ((bf16[4,4,128,512]{3,2,1,0:T(8,128)(2,1)S(1)}, bf16[4,4,128,512]{3,2,1,0:T(8,128)(2,1)}, bf16[4,4,128,512]{3,2,1,0:T(8,128)(2,1)}, bf16[4,4,12...) conditional(s32[]{:T(128)} %convert_element_type.106, ...), branch_computations={%region_0.1_spmd.clone, %region_1.2_spmd.clone} | conditional | bytes 8388688
  111.4 3.1 %copy.7 = bf16[4,4,128,512]{3,2,1,0:T(8,128)(2,1)} copy(bf16[4,4,128,512]{3,2,1,0:T(8,128)(2,1)} %get-tuple-element.158) | data formatting | bytes 4194304 | tf_op jit(solution)/shard_map/conditional
  114.5 3.1 %copy.8 = bf16[4,4,128,512]{3,2,1,0:T(8,128)(2,1)} copy(bf16[4,4,128,512]{3,2,1,0:T(8,128)(2,1)} %get-tuple-element.159) | data formatting | bytes 4194304 | tf_op jit(solution)/shard_map/conditional
  117.6 5.2 %fusion.2.refs_2_ = bf16[4,4,128,512]{3,2,1,0:T(8,128)(2,1)} fusion(bf16[4,4,128,512]{3,2,1,0:T(8,128)(2,1)} %get-tuple-element.141, bf16[4,4,128,512]{3,2,1,0:T(8,128)(2,1)} %get-tuple-element.142, bf16[4,4,128,512]{3,2,1,0:T(8,128)(2,1)} %get-tuple-element.136), kind=kLoop, calls=%fused_computation.5 | loop fusion | flops 6291456 | bytes 8388608 | tf_op jit(solution)/shard_map/cond/branch_0_fun/convert_element_type | solution.py:195
  122.8 6.4 %fusion = (bf16[4,4,128,512]{3,2,1,0:T(8,128)(2,1)S(1)}, bf16[4,4,128,512]{3,2,1,0:T(8,128)(2,1)S(1)}) fusion(bf16[4,4,128,512]{3,2,1,0:T(8,128)(2,1)} %get-tuple-element.137, bf16[4,4,128,512]{3,2,1,0:T(8,128)(2,1)} %get-tuple-element.138, bf16[4,4,128,512]{3,2,1,0:T(8,128)(2,1)S(1)} %get-tuple-element.134, bf16[4,4,128,512]{3,2,1,0:T(8,128)(2,1)} %get-tuple-element.135, ...), kind=kLoop, calls=%fused_computation.1 | loop fusion | flops 12582912 | bytes 16777216 | tf_op jit(solution)/shard_map/cond/branch_0_fun/convert_element_type | solution.py:195
  129.2 6.6 %shard_map.48 = bf16[8,24,16,128]{3,2,1,0:T(8,128)(2,1)S(1)} custom-call(s32[24]{0:T(128)S(1)} %get-tuple-element.144.left_ref, s32[24]{0:T(128)S(1)} %get-tuple-element.143.right_ref, s32[1]{0:T(128)S(6)} %copy.9.count_ref, bf16[4,4,128,512]{3,2,1,0:T(8,128)(2,1)S(1)} %get-tuple-element.145.refs_0_, ...), custom_call_target="tpu_custom_call" | custom-call | tf_op jit(solution)/shard_map/pallas_call | solution.py:215
  135.8 27.8 %all_to_all.5 = bf16[8,24,16,128]{3,2,1,0:T(8,128)(2,1)S(1)} all-to-all(bf16[8,24,16,128]{3,2,1,0:T(8,128)(2,1)S(1)} %shard_map.48), channel_id=1, replica_groups=mesh['aux'=8,'ao'=64] {'aux'}, dimensions={0} | all-to-all | bytes 1572864 | tf_op jit(solution)/shard_map/all_to_all | solution.py:233
  163.6 0.8 fusion.3
  (5 shorter events, 0.0 us)
Async XLA Ops:
  0.0 35.4 %collective-permute-start.1 = (bf16[4,128,512]{2,1,0:T(8,128)(2,1)}, bf16[4,128,512]{2,1,0:T(8,128)(2,1)S(1)}, u32[]{:S(2)}, u32[]{:S(2)}) collective-permute-start(bf16[4,128,512]{2,1,0:T(8,128)(2,1)} %bitcast.7), channel_id=1, source_target_pairs={{2,0},{3,1},{4,2},{5,3},{6,4},{7,5},{8,6},{9,7},{10,8},{11,9},{12,... | collective-permute-start | bytes 1572872 | tf_op jit(solution)/shard_map/ppermute | solution.py:14
  11.2 24.2 %collective-permute-start = (bf16[4,128,512]{2,1,0:T(8,128)(2,1)}, bf16[4,128,512]{2,1,0:T(8,128)(2,1)S(1)}, u32[]{:S(2)}, u32[]{:S(2)}) collective-permute-start(bf16[4,128,512]{2,1,0:T(8,128)(2,1)} %bitcast.8), channel_id=1, source_target_pairs={{1,0},{2,1},{3,2},{4,3},{5,4},{6,5},{7,6},{8,7},{9,8},{10,9},{11,1... | collective-permute-start | bytes 1572872 | tf_op jit(solution)/shard_map/ppermute | solution.py:14
  14.6 1.9 %copy-start = (bf16[24,4,128,128]{3,2,1,0:T(8,128)(2,1)S(1)}, bf16[24,4,128,128]{3,2,1,0:T(8,128)(2,1)}, u32[]{:S(2)}) copy-start(bf16[24,4,128,128]{3,2,1,0:T(8,128)(2,1)} %tile_ref.3) | copy-start | bytes 9437188
  16.4 1.0 copy-start.1
  27.4 29.8 %collective-permute-start.4 = (bf16[4,4,128,512]{3,2,1,0:T(8,128)(2,1)}, bf16[4,4,128,512]{3,2,1,0:T(8,128)(2,1)}, u32[]{:S(2)}, u32[]{:S(2)}) collective-permute-start(bf16[4,4,128,512]{3,2,1,0:T(8,128)(2,1)} %get-tuple-element.69), channel_id=1, source_target_pairs={{0,1},{1,2},{2,3},{3,4},{4,5},{5,6},{6,7},{7,8},{8,9},{9,10},{10,1... | collective-permute-start | bytes 6291464 | tf_op jit(solution)/shard_map/ppermute | solution.py:14
  33.5 30.2 %collective-permute-start.7 = (bf16[4,4,128,512]{3,2,1,0:T(8,128)(2,1)}, bf16[4,4,128,512]{3,2,1,0:T(8,128)(2,1)S(1)}, u32[]{:S(2)}, u32[]{:S(2)}) collective-permute-start(bf16[4,4,128,512]{3,2,1,0:T(8,128)(2,1)} %get-tuple-element.70), channel_id=1, source_target_pairs={{1,0},{2,1},{3,2},{4,3},{5,4},{6,5},{7,6},{8,7},{9,8},{10,9},{11,1... | collective-permute-start | bytes 6291464 | tf_op jit(solution)/shard_map/ppermute | solution.py:14
  42.9 61.2 %collective-permute-start.2 = (bf16[4,4,128,512]{3,2,1,0:T(8,128)(2,1)S(1)}, bf16[4,4,128,512]{3,2,1,0:T(8,128)(2,1)}, u32[]{:S(2)}, u32[]{:S(2)}) collective-permute-start(bf16[4,4,128,512]{3,2,1,0:T(8,128)(2,1)S(1)} %shard_map.47), channel_id=1, source_target_pairs={{1,0},{2,1},{3,2},{4,3},{5,4},{6,5},{7,6},{8,7},{9,8},{10,9},{11,1... | collective-permute-start | bytes 6291464 | tf_op jit(solution)/shard_map/ppermute | solution.py:14
  45.0 60.4 %collective-permute-start.6 = (bf16[4,4,128,512]{3,2,1,0:T(8,128)(2,1)}, bf16[4,4,128,512]{3,2,1,0:T(8,128)(2,1)}, u32[]{:S(2)}, u32[]{:S(2)}) collective-permute-start(bf16[4,4,128,512]{3,2,1,0:T(8,128)(2,1)} %get-tuple-element.70), channel_id=1, source_target_pairs={{0,1},{1,2},{2,3},{3,4},{4,5},{5,6},{6,7},{7,8},{8,9},{9,10},{10,1... | collective-permute-start | bytes 6291464 | tf_op jit(solution)/shard_map/ppermute | solution.py:14
  50.7 54.7 %collective-permute-start.3 = (bf16[4,4,128,512]{3,2,1,0:T(8,128)(2,1)S(1)}, bf16[4,4,128,512]{3,2,1,0:T(8,128)(2,1)}, u32[]{:S(2)}, u32[]{:S(2)}) collective-permute-start(bf16[4,4,128,512]{3,2,1,0:T(8,128)(2,1)S(1)} %shard_map.47), channel_id=1, source_target_pairs={{3,1},{5,3},{7,5},{9,7},{11,9},{13,11},{15,13},{17,15},{19,17},{21... | collective-permute-start | bytes 6291464 | tf_op jit(solution)/shard_map/ppermute | solution.py:189
  57.2 48.3 %collective-permute-start.5 = (bf16[4,4,128,512]{3,2,1,0:T(8,128)(2,1)}, bf16[4,4,128,512]{3,2,1,0:T(8,128)(2,1)}, u32[]{:S(2)}, u32[]{:S(2)}) collective-permute-start(bf16[4,4,128,512]{3,2,1,0:T(8,128)(2,1)} %collective-permute-done.4), channel_id=1, source_target_pairs={{0,1},{2,3},{4,5},{6,7},{8,9},{10,11},{12,13},{14,15},{16,17},{18,... | collective-permute-start | bytes 6291464 | tf_op jit(solution)/shard_map/ppermute | solution.py:190
  63.7 40.4 %copy-start.2 = (bf16[4,4,128,512]{3,2,1,0:T(8,128)(2,1)}, bf16[4,4,128,512]{3,2,1,0:T(8,128)(2,1)S(1)}, u32[]{:S(2)}) copy-start(bf16[4,4,128,512]{3,2,1,0:T(8,128)(2,1)S(1)} %collective-permute-done.7) | copy-start | bytes 6291460
  63.7 41.7 %collective-permute-start.9 = (bf16[4,4,128,512]{3,2,1,0:T(8,128)(2,1)}, bf16[4,4,128,512]{3,2,1,0:T(8,128)(2,1)}, u32[]{:S(2)}, u32[]{:S(2)}) collective-permute-start(bf16[4,4,128,512]{3,2,1,0:T(8,128)(2,1)} %get-tuple-element.69), channel_id=1, source_target_pairs={{0,2},{2,4},{4,6},{6,8},{8,10},{10,12},{12,14},{14,16},{16,18},{18... | collective-permute-start | bytes 6291464 | tf_op jit(solution)/shard_map/ppermute | solution.py:186
  104.1 7.3 %collective-permute-start.8 = (bf16[4,4,128,512]{3,2,1,0:T(8,128)(2,1)}, bf16[4,4,128,512]{3,2,1,0:T(8,128)(2,1)}, u32[]{:S(2)}, u32[]{:S(2)}) collective-permute-start(bf16[4,4,128,512]{3,2,1,0:T(8,128)(2,1)} %collective-permute-done.2), channel_id=1, source_target_pairs={{1,0},{3,2},{5,4},{7,6},{9,8},{11,10},{13,12},{15,14},{17,16},{19,... | collective-permute-start | bytes 6291464 | tf_op jit(solution)/shard_map/ppermute | solution.py:191
